TPU v7x, 256 devices: a whole 4x4x8 slice. The times are simulated.
256 devices in a mesh: node: 4 (over x), space: 64 (over z, y, core).
Axes of the slice: x: 4, y: 4, z: 8, core: 2. Of those that a mesh axis runs over, the one named last changes fastest.
Arguments:
- snapshots: bfloat16 [512, 128, 8192], P('node', 'space'), may hold values from -8 to 8
- kappa: bfloat16 [128, 8192], P('space'), may hold values from 0.099609375 to 10
Outputs:
- gram: float32 [512, 512], P('node', 'space')
All inputs are finite; a program needn't handle non-finite values.
Results may differ from a plain program's by a relative error of at most 0.0003.
Values may be sent and summed in bfloat16 or wider, within the bound.
No kernel may reach another device: no remote copies, remote signals or barrier semaphores. Data moves between devices by JAX's collectives and lax.ppermute only.
A program may use at most 128 MiB of HBM per device.

v0:
```python
import math

import jax
import jax.numpy as jnp
from jax import lax
from jax.sharding import PartitionSpec as P

NY = 128
NZ = 64


def extended(value, sides, width):
    for axis, dim in sides:
        size, length = (lax.axis_size(axis), value.shape[dim])
        up = [(i, (i + 1) % size) for i in range(size - 1)]
        down = [(j, i) for i, j in up]
        last = lax.slice_in_dim(value, length - width, length, axis=dim)
        first = lax.slice_in_dim(value, 0, width, axis=dim)
        before = lax.ppermute(last, axis, up)
        after = lax.ppermute(first, axis, down)
        value = jnp.concatenate([before, value, after], axis=dim)
    return value


def shifted(value, axis, by):
    length = lax.axis_size(axis)
    return lax.ppermute(value, axis, [(i, (i + by) % length) for i in range(length)])


def ahead(values, offset):
    tail = jnp.zeros(values.shape[:-1] + (offset,), values.dtype)
    return jnp.concatenate([values[..., offset:], tail], axis=-1)


def behind(values, offset):
    head = jnp.zeros(values.shape[:-1] + (offset,), values.dtype)
    return jnp.concatenate([head, values[..., :-offset]], axis=-1)


def flat_terms(field, kap_mid):
    width = field.shape[-1]
    zpos = jnp.arange(width, dtype=jnp.int32) % NZ
    up_ok = zpos != NZ - 1
    down_ok = zpos != 0
    near = jnp.where(up_ok, ahead(field, 1), 0.0)
    near_k = jnp.where(up_ok, ahead(kap_mid, 1), 0.0)
    total = 0.5 * (kap_mid + near_k) * (field - near)
    near = jnp.where(down_ok, behind(field, 1), 0.0)
    near_k = jnp.where(down_ok, behind(kap_mid, 1), 0.0)
    total = total + 0.5 * (kap_mid + near_k) * (field - near)
    total = total + 0.5 * (kap_mid + ahead(kap_mid, NZ)) * (field - ahead(field, NZ))
    total = total + 0.5 * (kap_mid + behind(kap_mid, NZ)) * (field - behind(field, NZ))
    return total


def per_device(snapshots, kappa):
    snap_rows, planes, width = snapshots.shape
    stacked = jnp.concatenate([snapshots, kappa[None]], axis=0)
    padded = extended(stacked, (("space", 1),), 1)
    field = padded[:snap_rows, 1:-1].astype(jnp.float32)
    kap_all = padded[snap_rows].astype(jnp.float32)
    kap_mid = kap_all[1:-1]
    total = flat_terms(field, kap_mid)
    total = total + 0.5 * (kap_mid + kap_all[:-2]) * (
        field - padded[:snap_rows, :-2].astype(jnp.float32)
    )
    total = total + 0.5 * (kap_mid + kap_all[2:]) * (
        field - padded[:snap_rows, 2:].astype(jnp.float32)
    )
    image = total.astype(jnp.bfloat16).reshape(snap_rows, planes * width)
    owned = snapshots.reshape(snap_rows, planes * width)
    scale = jnp.float32(1.0 / math.sqrt(planes * lax.axis_size("space") * NY * NZ))
    nodes = lax.axis_size("node")
    where_am = lax.axis_index("node")

    def place(carry_total, block, turn):
        source = (where_am - turn) % nodes
        tile = jnp.einsum("ic,jc->ij", image, block, preferred_element_type=jnp.float32)
        return lax.dynamic_update_slice(carry_total, tile, (jnp.int32(0), source * snap_rows))

    def advance(turn, carry):
        partial_rows, block = carry
        partial_rows = place(partial_rows, block, turn)
        block = shifted(block, "node", 1)
        return (partial_rows, block)

    start = jnp.zeros((snap_rows, nodes * snap_rows), jnp.float32)
    partial_rows, block = lax.fori_loop(0, nodes - 1, advance, (start, owned))
    partial_rows = place(partial_rows, block, nodes - 1)
    gram = lax.psum_scatter(partial_rows, "space", scatter_dimension=1, tiled=True)
    return gram * scale


def solution(mesh):
    placed = (P("node", "space", None), P("space", None))
    return jax.shard_map(
        per_device, mesh=mesh, in_specs=placed, out_specs=P("node", "space"), check_vma=False
    )
```

profile of v0, /device:TPU:8, one launch (start us, length us, event | category | flops | bytes accessed | tf_op | source)
XLA Modules:
  0.0 657.8 jit_solution(820837370051495960)
XLA Ops:
  6.5 0.0 all-reduce.11.cloned.1.call-start
  6.5 12.0 %slice_maximum_fusion = (bf16[129,1,8192]{2,1,0:T(2,128)(2,1)S(1)}, bf16[129,1,8192]{2,1,0:T(2,128)(2,1)S(1)}) fusion(bf16[1,2,8192]{2,1,0:T(2,128)(2,1)} %bitcast.45, bf16[128,2,8192]{2,1,0:T(2,128)(2,1)} %param.4), kind=kLoop, calls=%fused_computation.20 | loop fusion | flops 8454144 | bytes 8454144 | tf_op jit(solution)/shard_map/concatenate | solution.py:58
  18.6 2.3 copy.11
  20.9 0.0 copy-start
  20.9 2.2 collective-permute-start.1
  23.1 3.7 copy.12
  26.8 3.6 collective-permute-start.2
  30.4 0.0 copy-done
  30.4 9.6 %fusion.22 = (f32[128,2,8191]{2,1,0:T(2,128)}, f32[128,2,8191]{2,1,0:T(2,128)}) fusion(bf16[128,2,8192]{2,1,0:T(2,128)(2,1)S(1)} %copy-done), kind=kLoop, calls=%fused_computation.49 | loop fusion | bytes 33550336 | tf_op jit(solution)/shard_map/slice | solution.py:32
  40.0 6.8 %copy.32 = bf16[16,8,2,8192]{3,1,2,0:T(8,128)(2,1)} copy(bf16[16,8,2,8192]{3,2,1,0:T(2,128)(2,1)} %bitcast.40) | data formatting | bytes 8388608
  46.8 12.0 %fusion.23 = (f32[128,2,8128]{2,1,0:T(2,128)}, f32[128,2,8128]{2,1,0:T(2,128)}) fusion(bf16[128,2,8192]{2,1,0:T(2,128)(2,1)} %param.4), kind=kLoop, calls=%fused_computation.50 | loop fusion | bytes 33292288 | tf_op jit(solution)/shard_map/slice | solution.py:32
  58.8 0.0 collective-permute-done.1
  58.8 6.4 copy.13
  65.2 0.0 copy-start.1
  65.2 0.0 copy-start.4
  65.2 0.0 collective-permute-done.2
  65.2 8.6 %copy.14 = bf16[129,1,8192]{2,1,0:T(2,128)(2,1)} copy(bf16[129,1,8192]{2,0,1:T(8,128)(2,1)} %collective-permute-done.2) | data formatting | bytes 4227072 | tf_op jit(solution)/shard_map/ppermute | solution.py:20
  73.8 0.0 copy-done.1
  73.8 0.0 copy-done.4
  73.8 0.0 copy-start.2
  73.8 1.0 fusion.16
  74.8 0.1 fusion.24
  75.0 0.1 fusion.25
  75.1 0.3 add_multiply_fusion.3
  75.4 0.7 copy-done.2
  76.0 83.4 %fusion.11 = bf16[128,2,8192]{2,1,0:T(2,128)(2,1)} fusion(f32[128,2,8128]{2,1,0:T(2,128)} %get-tuple-element.161, f32[128,2,8128]{2,1,0:T(2,128)} %get-tuple-element.160, f32[128,2,8191]{2,1,0:T(2,128)} %get-tuple-element.159, pred[8192]{0:T(1024)(128)(4,1)S(1)} %get-tuple-element.172, f32[128,2,8191]{2,1,0:T(2,128)} %get-tuple-element.158, ...), kind=kLoop, calls=%fused_computation.18 | loop fusion | flops 69206016 | bytes 46479360 | tf_op jit(solution)/shard_map/convert_element_type | solution.py:70
  159.4 11.2 %copy.17 = bf16[128,2,8192]{0,2,1:T(8,128)(2,1)} copy(bf16[128,2,8192]{2,1,0:T(2,128)(2,1)} %fusion.11) | data formatting | bytes 8388608 | tf_op jit(solution)/shard_map/convert_element_type | solution.py:70
  170.6 6.5 copy.18
  177.1 292.7 %while.17 = (s32[]{:T(128)}, f32[128,512]{0,1:T(8,128)S(1)}, bf16[128,16384]{1,0:T(8,128)(2,1)}, bf16[128,16384]{1,0:T(8,128)(2,1)}, s32[]{:T(128)}, /*index=5*/...) while((s32[]{:T(128)}, f32[128,512]{0,1:T(8,128)S(1)}, ...), condition=%wide.region_1.2_spmd, body=%wide.region_0.1_spmd.sunk | while | flops 536870912 | bytes 33620288 | solution.py:88
  177.1 4.5 copy.39
  181.6 1.5 collective-permute-start
  183.1 4.7 convolution_dynamic-update-slice_fusion.3
  187.8 87.8 %collective-permute-done = bf16[128,16384]{1,0:T(8,128)(2,1)} collective-permute-done((bf16[128,16384]{1,0:T(8,128)(2,1)}, bf16[128,16384]{1,0:T(8,128)(2,1)}, u32[]{:S(2)}, u32[]{:S(2)}) %collective-permute-start) | collective-permute-done | bytes 4194336 | tf_op jit(solution)/shard_map/while/body/eval_jaxpr/ppermute | solution.py:27
  275.6 4.5 copy.39
  280.0 0.3 collective-permute-start
  280.3 4.7 convolution_dynamic-update-slice_fusion.3
  285.0 88.1 %collective-permute-done = bf16[128,16384]{1,0:T(8,128)(2,1)} collective-permute-done((bf16[128,16384]{1,0:T(8,128)(2,1)}, bf16[128,16384]{1,0:T(8,128)(2,1)}, u32[]{:S(2)}, u32[]{:S(2)}) %collective-permute-start) | collective-permute-done | bytes 4194336 | tf_op jit(solution)/shard_map/while/body/eval_jaxpr/ppermute | solution.py:27
  373.2 4.5 copy.39
  377.6 0.0 collective-permute-start
  377.6 4.7 convolution_dynamic-update-slice_fusion.3
  382.4 87.5 %collective-permute-done = bf16[128,16384]{1,0:T(8,128)(2,1)} collective-permute-done((bf16[128,16384]{1,0:T(8,128)(2,1)}, bf16[128,16384]{1,0:T(8,128)(2,1)}, u32[]{:S(2)}, u32[]{:S(2)}) %collective-permute-start) | collective-permute-done | bytes 4194336 | tf_op jit(solution)/shard_map/while/body/eval_jaxpr/ppermute | solution.py:27
  469.8 0.0 copy-start.5
  469.8 4.7 convolution_dynamic-update-slice_fusion.1
  474.5 0.0 copy-start.3
  474.6 0.7 copy-done.3
  475.2 0.0 all-reduce.11.cloned.1.call-update
  475.3 0.0 copy-done.5
  475.3 0.6 dynamic-slice
  476.5 173.2 %all-reduce.11.cloned.1.call-done = f32[128,512]{0,1:T(8,128)} async-done(((f32[128,512]{0,1:T(8,128)}), f32[128,512]{0,1:T(8,128)}) %all-reduce.11.cloned.1.call-update) | async-done | bytes 262160
  649.7 1.3 dynamic-slice_multiply_fusion
  (2 shorter events, 0.0 us)
Async XLA Ops:
  6.5 643.2 %all-reduce.11.cloned.1.call-start = ((), (), s32[]{:S(2)}) async-start(), calls=%async_computation | async-start | bytes 524288
  20.9 9.6 %copy-start = (bf16[128,2,8192]{2,1,0:T(2,128)(2,1)S(1)}, bf16[128,2,8192]{2,1,0:T(2,128)(2,1)}, u32[]{:S(2)}) copy-start(bf16[128,2,8192]{2,1,0:T(2,128)(2,1)} %param.4) | copy-start | bytes 12582916
  20.9 37.9 %collective-permute-start.1 = (bf16[129,1,8192]{2,0,1:T(8,128)(2,1)S(1)}, bf16[129,1,8192]{2,0,1:T(8,128)(2,1)}, u32[]{:S(2)}, u32[]{:S(2)}) collective-permute-start(bf16[129,1,8192]{2,0,1:T(8,128)(2,1)S(1)} %copy.11), channel_id=1, source_target_pairs={{0,1},{1,2},{2,3},{3,4},{4,5},{5,6},{6,7},{7,8},{8,9},{9,10},{10,1... | collective-permute-start | bytes 6340616 | tf_op jit(solution)/shard_map/ppermute | solution.py:19
  26.8 38.4 %collective-permute-start.2 = (bf16[129,1,8192]{2,0,1:T(8,128)(2,1)}, bf16[129,1,8192]{2,0,1:T(8,128)(2,1)}, u32[]{:S(2)}, u32[]{:S(2)}) collective-permute-start(bf16[129,1,8192]{2,0,1:T(8,128)(2,1)} %copy.12), channel_id=1, source_target_pairs={{1,0},{2,1},{3,2},{4,3},{5,4},{6,5},{7,6},{8,7},{9,8},{10,9},{11,1... | collective-permute-start | bytes 6340616 | tf_op jit(solution)/shard_map/ppermute | solution.py:20
  65.2 8.6 %copy-start.1 = (bf16[128,2,8192]{2,1,0:T(2,128)(2,1)S(1)}, bf16[128,2,8192]{2,1,0:T(2,128)(2,1)}, u32[]{:S(2)}) copy-start(bf16[128,2,8192]{2,1,0:T(2,128)(2,1)} %param.4) | copy-start | bytes 12582916
  65.2 8.6 %copy-start.4 = (bf16[2,8192]{1,0:T(2,128)(2,1)S(1)}, bf16[2,8192]{1,0:T(2,128)(2,1)}, u32[]{:S(2)}) copy-start(bf16[2,8192]{1,0:T(2,128)(2,1)} %param.5) | copy-start | bytes 98308
  73.8 2.2 copy-start.2
  181.6 94.0 %collective-permute-start = (bf16[128,16384]{1,0:T(8,128)(2,1)}, bf16[128,16384]{1,0:T(8,128)(2,1)}, u32[]{:S(2)}, u32[]{:S(2)}) collective-permute-start(bf16[128,16384]{1,0:T(8,128)(2,1)} %copy.39), channel_id=1, source_target_pairs={{0,64},{64,128},{128,192},{192,0},{1,65},{65,129},{129,193},{193,1... | collective-permute-start | bytes 12582920 | tf_op jit(solution)/shard_map/while/body/eval_jaxpr/ppermute | solution.py:27
  280.0 93.1 %collective-permute-start = (bf16[128,16384]{1,0:T(8,128)(2,1)}, bf16[128,16384]{1,0:T(8,128)(2,1)}, u32[]{:S(2)}, u32[]{:S(2)}) collective-permute-start(bf16[128,16384]{1,0:T(8,128)(2,1)} %copy.39), channel_id=1, source_target_pairs={{0,64},{64,128},{128,192},{192,0},{1,65},{65,129},{129,193},{193,1... | collective-permute-start | bytes 12582920 | tf_op jit(solution)/shard_map/while/body/eval_jaxpr/ppermute | solution.py:27
  377.6 92.2 %collective-permute-start = (bf16[128,16384]{1,0:T(8,128)(2,1)}, bf16[128,16384]{1,0:T(8,128)(2,1)}, u32[]{:S(2)}, u32[]{:S(2)}) collective-permute-start(bf16[128,16384]{1,0:T(8,128)(2,1)} %copy.39), channel_id=1, source_target_pairs={{0,64},{64,128},{128,192},{192,0},{1,65},{65,129},{129,193},{193,1... | collective-permute-start | bytes 12582920 | tf_op jit(solution)/shard_map/while/body/eval_jaxpr/ppermute | solution.py:27
  469.8 5.4 copy-start.5
  474.5 0.7 copy-start.3
Sparse Core Ops, SparseCore 0:
  475.4 174.2 all-reduce.10
where the time goes:
time: 661 us; the launch traced here: 658 us
  waiting for transfers between devices  437 us (66%)
  other arithmetic  97.9 us (15%)
  local copies, waits for them, and re-layouts  82.7 us (13%)
  matrix products  18.8 us (3%)
  between operations  14.2 us (2%)
  starting transfers between devices  7.57 us (1%)
    ppermute x3, waiting for transfers between devices, shifted(): lax.ppermute(value, axis, [(i, (i + by) % length) for i in range(length)])  263 us
    unnamed x2, waiting for transfers between devices  173 us
    convert_element_type x1, other arithmetic, per_device(): image = total.astype(jnp.bfloat16).reshape(snap_rows, planes * width)  83.4 us
    slice x4, local copies, waits for them, and re-layouts, ahead(): return jnp.concatenate([values[..., offset:], tail], axis=-1)  21.8 us
    dynamic_update_slice x3, matrix products, place(): lax.dynamic_update_slice(carry_total, tile, (jnp.int32(0), source * snap_...  14.1 us
    another operation x3, local copies, waits for them, and re-layouts  13.5 us
  transfers between devices with their start and end apart: 6, of which 4 were waited for; matrix products, arithmetic and copies ran while one was open for 8% of the time, Pallas kernels for 0%

commit v1 on v0

v1 whole, which is shorter than its diff:
```python
import math

import jax
import jax.numpy as jnp
from jax import lax
from jax.experimental import pallas as pl
from jax.experimental.pallas import tpu as pltpu
from jax.sharding import PartitionSpec as P

NY = 128
NZ = 64
ROWS = 32


def ahead(values, offset):
    tail = jnp.zeros(values.shape[:-1] + (offset,), values.dtype)
    return jnp.concatenate([values[..., offset:], tail], axis=-1)


def behind(values, offset):
    head = jnp.zeros(values.shape[:-1] + (offset,), values.dtype)
    return jnp.concatenate([head, values[..., :-offset]], axis=-1)


def stencil_kernel(x_ref, below_ref, above_ref, coef_ref, out_ref):
    span = below_ref.shape[1]
    lane = lax.broadcasted_iota(jnp.int32, (1, span), 1)
    zpos = lane % NZ
    up_ok = zpos != NZ - 1
    down_ok = zpos != 0
    inner = (lane >= NZ) & (lane < span - NZ)
    planes = [x_ref[:, p * span:(p + 1) * span].astype(jnp.float32) for p in range(2)]
    below = below_ref[...].astype(jnp.float32)
    above = above_ref[...].astype(jnp.float32)
    for p in range(2):
        v = planes[p]

        def coef(t):
            return coef_ref[t:t + 1, p * span:(p + 1) * span]

        near = jnp.where(up_ok, pltpu.roll(v, span - 1, 1), 0.0)
        total = coef(0) * (v - near)
        near = jnp.where(down_ok, pltpu.roll(v, 1, 1), 0.0)
        total = total + coef(1) * (v - near)
        total = total + coef(2) * (v - pltpu.roll(v, span - NZ, 1))
        total = total + coef(3) * (v - pltpu.roll(v, NZ, 1))
        total = total + coef(4) * (v - (below if p == 0 else planes[0]))
        total = total + coef(5) * (v - (planes[1] if p == 0 else above))
        out_ref[:, p * span:(p + 1) * span] = jnp.where(inner, total, 0.0).astype(out_ref.dtype)


def stencil(field, below, above, coef):
    snaps, width = field.shape
    span = below.shape[1]
    return pl.pallas_call(
        stencil_kernel,
        grid=(snaps // ROWS,),
        in_specs=[
            pl.BlockSpec((ROWS, width), lambda i: (i, 0)),
            pl.BlockSpec((ROWS, span), lambda i: (i, 0)),
            pl.BlockSpec((ROWS, span), lambda i: (i, 0)),
            pl.BlockSpec(coef.shape, lambda i: (0, 0)),
        ],
        out_specs=pl.BlockSpec((ROWS, width), lambda i: (i, 0)),
        out_shape=jax.ShapeDtypeStruct(field.shape, jnp.bfloat16),
    )(field, below, above, coef)


def weights(kap_chunk, kap_below, kap_above):
    span = kap_chunk.shape[-1]
    kc = kap_chunk.astype(jnp.float32)
    zpos = jnp.arange(span, dtype=jnp.int32) % NZ
    k_zp = jnp.where(zpos != NZ - 1, ahead(kc, 1), 0.0)
    k_zm = jnp.where(zpos != 0, behind(kc, 1), 0.0)
    k_xm = jnp.stack([kap_below.astype(jnp.float32), kc[0]])
    k_xp = jnp.stack([kc[1], kap_above.astype(jnp.float32)])
    near = [k_zp, k_zm, ahead(kc, NZ), behind(kc, NZ), k_xm, k_xp]
    return jnp.stack([0.5 * (kc + k) for k in near]).reshape(6, 2 * span)


def space_coords(s):
    return s // 8, (s // 2) % 4, s % 2


def space_index(z, y, c):
    return z * 8 + y * 2 + c


def per_device(snapshots, kappa):
    rows, planes, width = snapshots.shape
    nodes = lax.axis_size("node")
    spaces = lax.axis_size("space")
    me = lax.axis_index("node")
    sp = lax.axis_index("space")
    chunk = width // nodes
    span = chunk + 2 * NZ
    snaps = rows * nodes

    up = [(i, i + 1) for i in range(spaces - 1)]
    down = [(j, i) for i, j in up]

    kpad = jnp.pad(kappa, ((0, 0), (NZ, NZ)))
    kap_chunk = lax.dynamic_slice_in_dim(kpad, me * chunk, span, axis=1)
    kap_below = lax.ppermute(kap_chunk[1], "space", up)
    kap_above = lax.ppermute(kap_chunk[0], "space", down)
    coef = weights(kap_chunk, kap_below, kap_above)

    spad = jnp.pad(snapshots, ((0, 0), (0, 0), (NZ, NZ)))
    pieces = jnp.stack([spad[:, :, q * chunk:q * chunk + span] for q in range(nodes)])
    pieces = pieces.reshape(nodes, rows, planes * span)
    field = lax.all_to_all(pieces, "node", 0, 0, tiled=True).reshape(snaps, planes * span)

    below = lax.ppermute(field[:, span:], "space", up)
    above = lax.ppermute(field[:, :span], "space", down)
    image = stencil(field, below, above, coef)
    part = lax.dot_general(image, field, (((1,), (1,)), ((), ())), preferred_element_type=jnp.float32)

    z, y, c = space_coords(sp)
    part = part.reshape(snaps, 8, 4, 2, 8)
    keep = jnp.take(part, c, axis=3)
    give = jnp.take(part, 1 - c, axis=3)
    pairs = [(s, s ^ 1) for s in range(spaces)]
    acc = (keep + lax.ppermute(give, "space", pairs)).reshape(nodes, rows, 8, 4, 8)

    total = jnp.take(acc, me, axis=0)
    for d in range(1, nodes):
        blk = jnp.take(acc, (me + d) % nodes, axis=0)
        total = total + lax.ppermute(blk, "node", [(i, (i + d) % nodes) for i in range(nodes)])

    acc = jnp.take(total, y, axis=2)
    for d in range(1, 4):
        blk = jnp.take(total, (y + d) % 4, axis=2)
        pairs = []
        for s in range(spaces):
            zz, yy, cc = space_coords(s)
            pairs.append((s, space_index(zz, (yy + d) % 4, cc)))
        acc = acc + lax.ppermute(blk, "space", pairs)

    out = jnp.take(acc, z, axis=1)
    for d in range(1, 8):
        blk = jnp.take(acc, (z + d) % 8, axis=1)
        pairs = []
        for s in range(spaces):
            zz, yy, cc = space_coords(s)
            pairs.append((s, space_index((zz + d) % 8, yy, cc)))
        out = out + lax.ppermute(blk, "space", pairs)

    scale = jnp.float32(1.0 / math.sqrt(planes * spaces * NY * NZ))
    return out * scale


def solution(mesh):
    placed = (P("node", "space", None), P("space", None))
    return jax.shard_map(
        per_device, mesh=mesh, in_specs=placed, out_specs=P("node", "space"), check_vma=False
    )
```

time: 661 us -> 183 us (0.28)
  waiting for transfers between devices: 437 us -> 87.1 us
  other arithmetic: 97.9 us -> 4.56 us
  local copies, waits for them, and re-layouts: 82.7 us -> 22.4 us
  starting transfers between devices: 7.57 us -> 44.8 us
  Pallas kernels: 0 us -> 15.9 us
  between operations: 14.2 us -> 0.42 us
  matrix products: 18.8 us -> 6.11 us
    ppermute x5 -> x18, waiting for transfers between devices: 263 us -> 39.7 us  [the longest x1 22 us: per_device(): below = lax.ppermute(field[:, span:], 'space', up)]
    unnamed x2 -> x0, waiting for transfers between devices: 173 us -> none
    convert_element_type x2 -> x1, other arithmetic: 84.4 us -> 0.09 us  [weights(): kc = kap_chunk.astype(jnp.float32)]
    all_to_all x0 -> x1, waiting for transfers between devices: none -> 47.4 us  [per_device(): lax.all_to_all(pieces, 'node', 0, 0, tiled=True)]
    ppermute x5 -> x18, starting transfers between devices: 7.57 us -> 39.8 us  [the longest x7 17.7 us: per_device(): out = out + lax.ppermute(blk, 'space', pairs)]
    pallas_call x0 -> x1, Pallas kernels: none -> 15.9 us  [stencil(): pl.pallas_call(stencil_kernel, grid=(snaps // ROWS,), in_specs=[pl.BlockS...]
    ppermute x2 -> x0, local copies, waits for them, and re-layouts: 15 us -> none  [the longest x1 8.58 us: extended(): after = lax.ppermute(first, axis, down)]
    dynamic_update_slice x3 -> x0, matrix products: 14.1 us -> none  [place(): lax.dynamic_update_slice(carry_total, tile, (jnp.int32(0), source * snap_...]
  transfers between devices with their start and end apart: 6 -> 19, of which waited for: 4 -> 11; matrix products, arithmetic and copies ran while one was open for 8% -> 3% of each run, Pallas kernels for 0% -> 0%
where the time goes in v1:
time: 183 us; the launch traced here: 181 us
  waiting for transfers between devices  87.1 us (48%)
  starting transfers between devices  44.8 us (24%)
  local copies, waits for them, and re-layouts  22.4 us (12%)
  Pallas kernels  15.9 us (9%)
  matrix products  6.11 us (3%)
  other arithmetic  4.56 us (2%)
    all_to_all x1, waiting for transfers between devices, per_device(): lax.all_to_all(pieces, 'node', 0, 0, tiled=True)  47.4 us
    ppermute x1, waiting for transfers between devices, per_device(): below = lax.ppermute(field[:, span:], 'space', up)  22 us
    ppermute x7, starting transfers between devices, per_device(): out = out + lax.ppermute(blk, 'space', pairs)  17.7 us
    pallas_call x1, Pallas kernels, stencil(): pl.pallas_call(stencil_kernel, grid=(snaps // ROWS,), in_specs=[pl.BlockS...  15.9 us
    slice x1, local copies, waits for them, and re-layouts, per_device(): spad[:, :, q * chunk:q * chunk + span]  10.6 us
    ppermute x3, waiting for transfers between devices, per_device(): lax.ppermute(blk, 'node', [(i, (i + d) % nodes) for i in range(nodes)])  7.93 us
    ppermute x3, starting transfers between devices, per_device(): acc = acc + lax.ppermute(blk, 'space', pairs)  7.12 us
    dot_general x1, matrix products, per_device(): lax.dot_general(image, field, (((1,), (1,)), ((), ())), preferred_element...  6.11 us
  transfers between devices with their start and end apart: 19, of which 11 were waited for; matrix products, arithmetic and copies ran while one was open for 3% of the time, Pallas kernels for 0%

profile of v1, /device:TPU:8, one launch (start us, length us, event | category | flops | bytes accessed | tf_op | source)
XLA Modules:
  0.0 181.4 jit_solution(17581867063916041542)
XLA Ops:
  0.0 10.6 %pad_slice_fusion.1 = (bf16[128,2,2176]{2,1,0:T(2,128)(2,1)}, bf16[128,2,2176]{2,1,0:T(2,128)(2,1)S(1)}, bf16[128,2,2176]{2,1,0:T(2,128)(2,1)S(1)}, bf16[128,2,2176]{2,1,0:T(2,128)(2,1)}) fusion(bf16[128,2,8192]{2,1,0:T(2,128)(2,1)} %param.10), kind=kLoop, calls=%fused_computation.4 | loop fusion | bytes 10878976 | tf_op jit(solution)/shard_map/slice | solution.py:109
  10.6 0.7 stack.57
  11.3 0.8 stack.56
  12.1 1.8 stack.55
  13.9 2.6 %stack.54 = bf16[1,128,4352]{2,1,0:T(8,128)(2,1)} reshape(bf16[128,2,2176]{2,1,0:T(2,128)(2,1)} %get-tuple-element.57) | data formatting | bytes 2228224 | tf_op jit(solution)/shard_map/stack | solution.py:109
  16.4 3.4 %pad_maximum_fusion = bf16[4,128,4352]{2,1,0:T(8,128)(2,1)} fusion(bf16[1,128,4352]{2,1,0:T(8,128)(2,1)S(1)} %stack.57, bf16[1,128,4352]{2,1,0:T(8,128)(2,1)S(1)} %stack.56, bf16[1,128,4352]{2,1,0:T(8,128)(2,1)S(1)} %stack.55, bf16[1,128,4352]{2,1,0:T(8,128)(2,1)} %stack.54), kind=kLoop, calls=%fused_computation | loop fusion | flops 6684672 | bytes 8912896 | tf_op jit(solution)/shard_map/stack | solution.py:109
  19.9 0.0 copy-start.1
  19.9 5.0 %all-to-all-start = ((bf16[4,128,4352]{2,1,0:T(8,128)(2,1)}), bf16[4,128,4352]{2,1,0:T(8,128)(2,1)}, u32[]{:S(2)}, u32[]{:S(2)}) async-start(bf16[4,128,4352]{2,1,0:T(8,128)(2,1)} %pad_maximum_fusion), calls=%async_computation | async-start | bytes 8912896 | tf_op jit(solution)/shard_map/all_to_all | solution.py:111
  24.9 0.0 copy-done.1
  24.9 0.1 dynamic-slice_reduce_fusion
  25.1 1.9 %collective-permute-start.3 = (bf16[2176]{0:T(1024)(128)(2,1)S(1)}, bf16[2176]{0:T(1024)(128)(2,1)S(1)}, u32[]{:S(2)}, u32[]{:S(2)}) collective-permute-start(bf16[2176]{0:T(1024)(128)(2,1)S(1)} %get-tuple-element.53), channel_id=1, source_target_pairs={{1,0},{2,1},{3,2},{4,3},{5,4},{6,5},{7,6},{8,7},{9,8},{10,9},{11,1... | collective-permute-start | bytes 13064 | tf_op jit(solution)/shard_map/ppermute | solution.py:105
  27.0 2.4 %collective-permute-start.2 = (bf16[2176]{0:T(1024)(128)(2,1)S(1)}, bf16[2176]{0:T(1024)(128)(2,1)S(1)}, u32[]{:S(2)}, u32[]{:S(2)}) collective-permute-start(bf16[2176]{0:T(1024)(128)(2,1)S(1)} %get-tuple-element.54), channel_id=1, source_target_pairs={{0,1},{1,2},{2,3},{3,4},{4,5},{5,6},{6,7},{7,8},{8,9},{9,10},{10,1... | collective-permute-start | bytes 13064 | tf_op jit(solution)/shard_map/ppermute | solution.py:104
  29.4 0.1 fusion.55
  29.5 47.4 %all-to-all-done = bf16[4,128,4352]{2,1,0:T(8,128)(2,1)} async-done(((bf16[4,128,4352]{2,1,0:T(8,128)(2,1)}), bf16[4,128,4352]{2,1,0:T(8,128)(2,1)}, u32[]{:S(2)}, u32[]{:S(2)}) %all-to-all-start) | async-done | bytes 4456480 | tf_op jit(solution)/shard_map/all_to_all | solution.py:111
  76.9 4.7 %fusion.56 = (bf16[512,2176]{1,0:T(8,128)(2,1)}, bf16[512,2176]{1,0:T(8,128)(2,1)}) fusion(bf16[512,4352]{1,0:T(8,128)(2,1)} %bitcast.x_ref), kind=kLoop, calls=%fused_computation.92 | loop fusion | bytes 8912896 | tf_op jit(solution)/shard_map/slice | solution.py:114
  81.5 1.9 %collective-permute-start = (bf16[512,2176]{1,0:T(8,128)(2,1)}, bf16[512,2176]{1,0:T(8,128)(2,1)S(1)}, u32[]{:S(2)}, u32[]{:S(2)}) collective-permute-start(bf16[512,2176]{1,0:T(8,128)(2,1)} %get-tuple-element.56), channel_id=1, source_target_pairs={{0,1},{1,2},{2,3},{3,4},{4,5},{5,6},{6,7},{7,8},{8,9},{9,10},{10,1... | collective-permute-start | bytes 6684680 | tf_op jit(solution)/shard_map/ppermute | solution.py:113
  83.5 3.6 %collective-permute-start.1 = (bf16[512,2176]{1,0:T(8,128)(2,1)}, bf16[512,2176]{1,0:T(8,128)(2,1)}, u32[]{:S(2)}, u32[]{:S(2)}) collective-permute-start(bf16[512,2176]{1,0:T(8,128)(2,1)} %get-tuple-element.55), channel_id=1, source_target_pairs={{1,0},{2,1},{3,2},{4,3},{5,4},{6,5},{7,6},{8,7},{9,8},{10,9},{11,1... | collective-permute-start | bytes 6684680 | tf_op jit(solution)/shard_map/ppermute | solution.py:114
  87.1 0.1 fusion.58
  87.2 0.1 fusion.59
  87.4 0.0 collective-permute-done.3
  87.4 0.0 collective-permute-done.2
  87.4 0.2 fusion.25
  87.7 0.8 stack.71.coef_ref
  88.5 22.0 %collective-permute-done.below_ref = bf16[512,2176]{1,0:T(8,128)(2,1)S(1)} collective-permute-done((bf16[512,2176]{1,0:T(8,128)(2,1)}, bf16[512,2176]{1,0:T(8,128)(2,1)S(1)}, u32[]{:S(2)}, u32[]{:S(2)}) %collective-permute-start) | collective-permute-done | bytes 2228256 | tf_op jit(solution)/shard_map/ppermute | solution.py:113
  110.5 0.0 copy-start
  110.5 1.9 %collective-permute-done.1.above_ref = bf16[512,2176]{1,0:T(8,128)(2,1)} collective-permute-done((bf16[512,2176]{1,0:T(8,128)(2,1)}, bf16[512,2176]{1,0:T(8,128)(2,1)}, u32[]{:S(2)}, u32[]{:S(2)}) %collective-permute-start.1) | collective-permute-done | bytes 2228256 | tf_op jit(solution)/shard_map/ppermute | solution.py:114
  112.4 0.0 copy-done
  112.4 15.9 %shard_map.28 = bf16[512,4352]{1,0:T(8,128)(2,1)} custom-call(bf16[512,4352]{1,0:T(8,128)(2,1)} %bitcast.x_ref, bf16[512,2176]{1,0:T(8,128)(2,1)} %copy-done, bf16[512,2176]{1,0:T(8,128)(2,1)} %collective-permute-done.1.above_ref, f32[6,4352]{1,0:T(8,128)} %stack.71.coef_ref), custom_call_target="tpu_custom_call" | custom-call | tf_op jit(solution)/shard_map/pallas_call | solution.py:55
  128.3 6.1 %fusion = f32[512,8,4,2,8]{0,4,3,2,1:T(8,128)S(1)} fusion(bf16[8,4,2,8,4352]{4,3,2,1,0:T(8,128)(2,1)} %bitcast.3, bf16[512,4352]{1,0:T(8,128)(2,1)} %shard_map.28), kind=kOutput, calls=%fused_computation.1 | convolution fusion | flops 2281701376 | bytes 9961472 | tf_op jit(solution)/shard_map/dot_general | solution.py:116
  134.5 2.0 %collective-permute-start.4 = (f32[512,8,4,8]{0,3,2,1:T(8,128)S(1)}, f32[512,8,4,8]{0,3,2,1:T(8,128)S(1)}, u32[]{:S(2)}, u32[]{:S(2)}) collective-permute-start(f32[512,8,4,8]{0,3,2,1:T(8,128)S(1)} %select_bitcast_fusion), channel_id=1, source_target_pairs={{0,1},{1,0},{2,3},{3,2},{4,5},{5,4},{6,7},{7,6},{8,9},{9,8},{10,11... | collective-permute-start | bytes 1572872 | tf_op jit(solution)/shard_map/ppermute | solution.py:123
  136.4 1.5 collective-permute-done.4
  138.0 0.1 fusion.4
  138.1 0.1 constant_dynamic-slice_fusion.11
  138.2 1.3 collective-permute-start.7
  139.5 1.6 collective-permute-start.6
  141.0 0.3 collective-permute-start.5
  141.4 3.2 %collective-permute-done.7 = f32[128,8,4,8]{0,3,1,2:T(8,128)S(1)} collective-permute-done((f32[128,8,4,8]{0,3,1,2:T(8,128)S(1)}, f32[128,8,4,8]{0,3,1,2:T(8,128)S(1)}, u32[]{:S(2)}, u32[]{:S(2)}) %collective-permute-start.7) | collective-permute-done | bytes 131104 | tf_op jit(solution)/shard_map/ppermute | solution.py:128
  144.6 2.8 %collective-permute-done.6 = f32[128,8,4,8]{0,3,1,2:T(8,128)S(1)} collective-permute-done((f32[128,8,4,8]{0,3,1,2:T(8,128)S(1)}, f32[128,8,4,8]{0,3,1,2:T(8,128)S(1)}, u32[]{:S(2)}, u32[]{:S(2)}) %collective-permute-start.6) | collective-permute-done | bytes 131104 | tf_op jit(solution)/shard_map/ppermute | solution.py:128
  147.4 1.9 %collective-permute-done.5 = f32[128,8,4,8]{0,3,1,2:T(8,128)S(1)} collective-permute-done((f32[128,8,4,8]{0,3,1,2:T(8,128)S(1)}, f32[128,8,4,8]{0,3,1,2:T(8,128)S(1)}, u32[]{:S(2)}, u32[]{:S(2)}) %collective-permute-start.5) | collective-permute-done | bytes 131104 | tf_op jit(solution)/shard_map/ppermute | solution.py:128
  149.4 0.5 collective-permute-start.10
  149.9 4.1 %collective-permute-start.9 = (f32[128,8,8]{0,2,1:T(8,128)S(1)}, f32[128,8,8]{0,2,1:T(8,128)S(1)}, u32[]{:S(2)}, u32[]{:S(2)}) collective-permute-start(f32[128,8,8]{0,2,1:T(8,128)S(1)} %get-tuple-element.67), channel_id=1, source_target_pairs={{0,4},{1,5},{2,6},{3,7},{4,0},{5,1},{6,2},{7,3},{8,12},{9,13},{10,... | collective-permute-start | bytes 98312 | tf_op jit(solution)/shard_map/ppermute | solution.py:137
  154.0 2.5 %collective-permute-start.8 = (f32[128,8,8]{0,2,1:T(8,128)S(1)}, f32[128,8,8]{0,2,1:T(8,128)S(1)}, u32[]{:S(2)}, u32[]{:S(2)}) collective-permute-start(f32[128,8,8]{0,2,1:T(8,128)S(1)} %get-tuple-element.65), channel_id=1, source_target_pairs={{0,2},{1,3},{2,4},{3,5},{4,6},{5,7},{6,0},{7,1},{8,10},{9,11},{10,... | collective-permute-start | bytes 98312 | tf_op jit(solution)/shard_map/ppermute | solution.py:137
  156.5 0.0 collective-permute-done.10
  156.5 0.0 collective-permute-done.9
  156.5 1.6 collective-permute-done.8
  158.2 3.9 %collective-permute-start.17 = (f32[128,8]{0,1:T(8,128)S(1)}, f32[128,8]{0,1:T(8,128)S(1)}, u32[]{:S(2)}, u32[]{:S(2)}) collective-permute-start(f32[128,8]{0,1:T(8,128)S(1)} %get-tuple-element.69), channel_id=1, source_target_pairs={{0,56},{1,57},{2,58},{3,59},{4,60},{5,61},{6,62},{7,63},{8,0},{9,1... | collective-permute-start | bytes 12296 | tf_op jit(solution)/shard_map/ppermute | solution.py:146
  162.1 2.5 %collective-permute-start.16 = (f32[128,8]{0,1:T(8,128)S(1)}, f32[128,8]{0,1:T(8,128)S(1)}, u32[]{:S(2)}, u32[]{:S(2)}) collective-permute-start(f32[128,8]{0,1:T(8,128)S(1)} %get-tuple-element.70), channel_id=1, source_target_pairs={{0,48},{1,49},{2,50},{3,51},{4,52},{5,53},{6,54},{7,55},{8,56},{9,... | collective-permute-start | bytes 12296 | tf_op jit(solution)/shard_map/ppermute | solution.py:146
  164.7 3.4 %collective-permute-start.15 = (f32[128,8]{0,1:T(8,128)S(1)}, f32[128,8]{0,1:T(8,128)S(1)}, u32[]{:S(2)}, u32[]{:S(2)}) collective-permute-start(f32[128,8]{0,1:T(8,128)S(1)} %get-tuple-element.71), channel_id=1, source_target_pairs={{0,40},{1,41},{2,42},{3,43},{4,44},{5,45},{6,46},{7,47},{8,48},{9,... | collective-permute-start | bytes 12296 | tf_op jit(solution)/shard_map/ppermute | solution.py:146
  168.0 2.1 %collective-permute-start.14 = (f32[128,8]{0,1:T(8,128)S(1)}, f32[128,8]{0,1:T(8,128)S(1)}, u32[]{:S(2)}, u32[]{:S(2)}) collective-permute-start(f32[128,8]{0,1:T(8,128)S(1)} %get-tuple-element.72), channel_id=1, source_target_pairs={{0,32},{1,33},{2,34},{3,35},{4,36},{5,37},{6,38},{7,39},{8,40},{9,... | collective-permute-start | bytes 12296 | tf_op jit(solution)/shard_map/ppermute | solution.py:146
  170.1 1.6 collective-permute-start.13
  171.8 0.0 collective-permute-done.17
  171.8 4.1 %collective-permute-start.12 = (f32[128,8]{0,1:T(8,128)S(1)}, f32[128,8]{0,1:T(8,128)S(1)}, u32[]{:S(2)}, u32[]{:S(2)}) collective-permute-start(f32[128,8]{0,1:T(8,128)S(1)} %get-tuple-element.74), channel_id=1, source_target_pairs={{0,16},{1,17},{2,18},{3,19},{4,20},{5,21},{6,22},{7,23},{8,24},{9,... | collective-permute-start | bytes 12296 | tf_op jit(solution)/shard_map/ppermute | solution.py:146
  175.9 0.0 collective-permute-done.16
  175.9 0.0 collective-permute-start.11
  175.9 0.0 collective-permute-done.15
  175.9 0.0 collective-permute-done.14
  175.9 0.8 collective-permute-done.13
  176.8 0.8 collective-permute-done.12
  177.6 3.2 %collective-permute-done.11 = f32[128,8]{0,1:T(8,128)S(1)} collective-permute-done((f32[128,8]{0,1:T(8,128)S(1)}, f32[128,8]{0,1:T(8,128)S(1)}, u32[]{:S(2)}, u32[]{:S(2)}) %collective-permute-start.11) | collective-permute-done | bytes 4128 | tf_op jit(solution)/shard_map/ppermute | solution.py:146
  180.7 0.6 fusion.40
  (18 shorter events, 0.3 us)
Async XLA Ops:
  19.9 5.1 %copy-start.1 = (bf16[2,8192]{1,0:T(2,128)(2,1)S(1)}, bf16[2,8192]{1,0:T(2,128)(2,1)}, u32[]{:S(2)}) copy-start(bf16[2,8192]{1,0:T(2,128)(2,1)} %param.11) | copy-start | bytes 98308
  19.9 57.0 %all-to-all-start = ((bf16[4,128,4352]{2,1,0:T(8,128)(2,1)}), bf16[4,128,4352]{2,1,0:T(8,128)(2,1)}, u32[]{:S(2)}, u32[]{:S(2)}) async-start(bf16[4,128,4352]{2,1,0:T(8,128)(2,1)} %pad_maximum_fusion), calls=%async_computation | async-start | bytes 8912896 | tf_op jit(solution)/shard_map/all_to_all | solution.py:111
  25.1 62.3 %collective-permute-start.3 = (bf16[2176]{0:T(1024)(128)(2,1)S(1)}, bf16[2176]{0:T(1024)(128)(2,1)S(1)}, u32[]{:S(2)}, u32[]{:S(2)}) collective-permute-start(bf16[2176]{0:T(1024)(128)(2,1)S(1)} %get-tuple-element.53), channel_id=1, source_target_pairs={{1,0},{2,1},{3,2},{4,3},{5,4},{6,5},{7,6},{8,7},{9,8},{10,9},{11,1... | collective-permute-start | bytes 13064 | tf_op jit(solution)/shard_map/ppermute | solution.py:105
  27.0 60.4 %collective-permute-start.2 = (bf16[2176]{0:T(1024)(128)(2,1)S(1)}, bf16[2176]{0:T(1024)(128)(2,1)S(1)}, u32[]{:S(2)}, u32[]{:S(2)}) collective-permute-start(bf16[2176]{0:T(1024)(128)(2,1)S(1)} %get-tuple-element.54), channel_id=1, source_target_pairs={{0,1},{1,2},{2,3},{3,4},{4,5},{5,6},{6,7},{7,8},{8,9},{9,10},{10,1... | collective-permute-start | bytes 13064 | tf_op jit(solution)/shard_map/ppermute | solution.py:104
  81.5 29.0 %collective-permute-start = (bf16[512,2176]{1,0:T(8,128)(2,1)}, bf16[512,2176]{1,0:T(8,128)(2,1)S(1)}, u32[]{:S(2)}, u32[]{:S(2)}) collective-permute-start(bf16[512,2176]{1,0:T(8,128)(2,1)} %get-tuple-element.56), channel_id=1, source_target_pairs={{0,1},{1,2},{2,3},{3,4},{4,5},{5,6},{6,7},{7,8},{8,9},{9,10},{10,1... | collective-permute-start | bytes 6684680 | tf_op jit(solution)/shard_map/ppermute | solution.py:113
  83.5 28.9 %collective-permute-start.1 = (bf16[512,2176]{1,0:T(8,128)(2,1)}, bf16[512,2176]{1,0:T(8,128)(2,1)}, u32[]{:S(2)}, u32[]{:S(2)}) collective-permute-start(bf16[512,2176]{1,0:T(8,128)(2,1)} %get-tuple-element.55), channel_id=1, source_target_pairs={{1,0},{2,1},{3,2},{4,3},{5,4},{6,5},{7,6},{8,7},{9,8},{10,9},{11,1... | collective-permute-start | bytes 6684680 | tf_op jit(solution)/shard_map/ppermute | solution.py:114
  110.5 1.9 %copy-start = (bf16[512,2176]{1,0:T(8,128)(2,1)}, bf16[512,2176]{1,0:T(8,128)(2,1)S(1)}, u32[]{:S(2)}) copy-start(bf16[512,2176]{1,0:T(8,128)(2,1)S(1)} %collective-permute-done.below_ref) | copy-start | bytes 6684676
  134.5 3.5 %collective-permute-start.4 = (f32[512,8,4,8]{0,3,2,1:T(8,128)S(1)}, f32[512,8,4,8]{0,3,2,1:T(8,128)S(1)}, u32[]{:S(2)}, u32[]{:S(2)}) collective-permute-start(f32[512,8,4,8]{0,3,2,1:T(8,128)S(1)} %select_bitcast_fusion), channel_id=1, source_target_pairs={{0,1},{1,0},{2,3},{3,2},{4,5},{5,4},{6,7},{7,6},{8,9},{9,8},{10,11... | collective-permute-start | bytes 1572872 | tf_op jit(solution)/shard_map/ppermute | solution.py:123
  138.2 6.4 %collective-permute-start.7 = (f32[128,8,4,8]{0,3,1,2:T(8,128)S(1)}, f32[128,8,4,8]{0,3,1,2:T(8,128)S(1)}, u32[]{:S(2)}, u32[]{:S(2)}) collective-permute-start(f32[128,8,4,8]{0,3,1,2:T(8,128)S(1)} %fusion.5), channel_id=1, source_target_pairs={{0,192},{64,0},{128,64},{192,128},{1,193},{65,1},{129,65},{193,129... | collective-permute-start | bytes 393224 | tf_op jit(solution)/shard_map/ppermute | solution.py:128
  139.5 7.9 %collective-permute-start.6 = (f32[128,8,4,8]{0,3,1,2:T(8,128)S(1)}, f32[128,8,4,8]{0,3,1,2:T(8,128)S(1)}, u32[]{:S(2)}, u32[]{:S(2)}) collective-permute-start(f32[128,8,4,8]{0,3,1,2:T(8,128)S(1)} %fusion.6), channel_id=1, source_target_pairs={{0,128},{64,192},{128,0},{192,64},{1,129},{65,193},{129,1},{193,65... | collective-permute-start | bytes 393224 | tf_op jit(solution)/shard_map/ppermute | solution.py:128
  141.0 8.3 %collective-permute-start.5 = (f32[128,8,4,8]{0,3,1,2:T(8,128)S(1)}, f32[128,8,4,8]{0,3,1,2:T(8,128)S(1)}, u32[]{:S(2)}, u32[]{:S(2)}) collective-permute-start(f32[128,8,4,8]{0,3,1,2:T(8,128)S(1)} %fusion.7), channel_id=1, source_target_pairs={{0,64},{64,128},{128,192},{192,0},{1,65},{65,129},{129,193},{193,1... | collective-permute-start | bytes 393224 | tf_op jit(solution)/shard_map/ppermute | solution.py:128
  149.4 7.1 %collective-permute-start.10 = (f32[128,8,8]{0,2,1:T(8,128)S(1)}, f32[128,8,8]{0,2,1:T(8,128)S(1)}, u32[]{:S(2)}, u32[]{:S(2)}) collective-permute-start(f32[128,8,8]{0,2,1:T(8,128)S(1)} %get-tuple-element.66), channel_id=1, source_target_pairs={{0,6},{1,7},{2,0},{3,1},{4,2},{5,3},{6,4},{7,5},{8,14},{9,15},{10,... | collective-permute-start | bytes 98312 | tf_op jit(solution)/shard_map/ppermute | solution.py:137
  149.9 6.6 %collective-permute-start.9 = (f32[128,8,8]{0,2,1:T(8,128)S(1)}, f32[128,8,8]{0,2,1:T(8,128)S(1)}, u32[]{:S(2)}, u32[]{:S(2)}) collective-permute-start(f32[128,8,8]{0,2,1:T(8,128)S(1)} %get-tuple-element.67), channel_id=1, source_target_pairs={{0,4},{1,5},{2,6},{3,7},{4,0},{5,1},{6,2},{7,3},{8,12},{9,13},{10,... | collective-permute-start | bytes 98312 | tf_op jit(solution)/shard_map/ppermute | solution.py:137
  154.0 4.1 %collective-permute-start.8 = (f32[128,8,8]{0,2,1:T(8,128)S(1)}, f32[128,8,8]{0,2,1:T(8,128)S(1)}, u32[]{:S(2)}, u32[]{:S(2)}) collective-permute-start(f32[128,8,8]{0,2,1:T(8,128)S(1)} %get-tuple-element.65), channel_id=1, source_target_pairs={{0,2},{1,3},{2,4},{3,5},{4,6},{5,7},{6,0},{7,1},{8,10},{9,11},{10,... | collective-permute-start | bytes 98312 | tf_op jit(solution)/shard_map/ppermute | solution.py:137
  158.2 13.6 %collective-permute-start.17 = (f32[128,8]{0,1:T(8,128)S(1)}, f32[128,8]{0,1:T(8,128)S(1)}, u32[]{:S(2)}, u32[]{:S(2)}) collective-permute-start(f32[128,8]{0,1:T(8,128)S(1)} %get-tuple-element.69), channel_id=1, source_target_pairs={{0,56},{1,57},{2,58},{3,59},{4,60},{5,61},{6,62},{7,63},{8,0},{9,1... | collective-permute-start | bytes 12296 | tf_op jit(solution)/shard_map/ppermute | solution.py:146
  162.1 13.8 %collective-permute-start.16 = (f32[128,8]{0,1:T(8,128)S(1)}, f32[128,8]{0,1:T(8,128)S(1)}, u32[]{:S(2)}, u32[]{:S(2)}) collective-permute-start(f32[128,8]{0,1:T(8,128)S(1)} %get-tuple-element.70), channel_id=1, source_target_pairs={{0,48},{1,49},{2,50},{3,51},{4,52},{5,53},{6,54},{7,55},{8,56},{9,... | collective-permute-start | bytes 12296 | tf_op jit(solution)/shard_map/ppermute | solution.py:146
  164.7 11.3 %collective-permute-start.15 = (f32[128,8]{0,1:T(8,128)S(1)}, f32[128,8]{0,1:T(8,128)S(1)}, u32[]{:S(2)}, u32[]{:S(2)}) collective-permute-start(f32[128,8]{0,1:T(8,128)S(1)} %get-tuple-element.71), channel_id=1, source_target_pairs={{0,40},{1,41},{2,42},{3,43},{4,44},{5,45},{6,46},{7,47},{8,48},{9,... | collective-permute-start | bytes 12296 | tf_op jit(solution)/shard_map/ppermute | solution.py:146
  168.0 7.9 %collective-permute-start.14 = (f32[128,8]{0,1:T(8,128)S(1)}, f32[128,8]{0,1:T(8,128)S(1)}, u32[]{:S(2)}, u32[]{:S(2)}) collective-permute-start(f32[128,8]{0,1:T(8,128)S(1)} %get-tuple-element.72), channel_id=1, source_target_pairs={{0,32},{1,33},{2,34},{3,35},{4,36},{5,37},{6,38},{7,39},{8,40},{9,... | collective-permute-start | bytes 12296 | tf_op jit(solution)/shard_map/ppermute | solution.py:146
  170.1 6.6 %collective-permute-start.13 = (f32[128,8]{0,1:T(8,128)S(1)}, f32[128,8]{0,1:T(8,128)S(1)}, u32[]{:S(2)}, u32[]{:S(2)}) collective-permute-start(f32[128,8]{0,1:T(8,128)S(1)} %get-tuple-element.73), channel_id=1, source_target_pairs={{0,24},{1,25},{2,26},{3,27},{4,28},{5,29},{6,30},{7,31},{8,32},{9,... | collective-permute-start | bytes 12296 | tf_op jit(solution)/shard_map/ppermute | solution.py:146
  171.8 5.8 %collective-permute-start.12 = (f32[128,8]{0,1:T(8,128)S(1)}, f32[128,8]{0,1:T(8,128)S(1)}, u32[]{:S(2)}, u32[]{:S(2)}) collective-permute-start(f32[128,8]{0,1:T(8,128)S(1)} %get-tuple-element.74), channel_id=1, source_target_pairs={{0,16},{1,17},{2,18},{3,19},{4,20},{5,21},{6,22},{7,23},{8,24},{9,... | collective-permute-start | bytes 12296 | tf_op jit(solution)/shard_map/ppermute | solution.py:146
  175.9 4.8 %collective-permute-start.11 = (f32[128,8]{0,1:T(8,128)S(1)}, f32[128,8]{0,1:T(8,128)S(1)}, u32[]{:S(2)}, u32[]{:S(2)}) collective-permute-start(f32[128,8]{0,1:T(8,128)S(1)} %get-tuple-element.68), channel_id=1, source_target_pairs={{0,8},{1,9},{2,10},{3,11},{4,12},{5,13},{6,14},{7,15},{8,16},{9,17... | collective-permute-start | bytes 12296 | tf_op jit(solution)/shard_map/ppermute | solution.py:146

commit v2 on v1

--- a/solution.py
+++ b/solution.py
@@ -78,20 +78,11 @@
     return jnp.stack([0.5 * (kc + k) for k in near]).reshape(6, 2 * span)
 
 
-def space_coords(s):
-    return s // 8, (s // 2) % 4, s % 2
-
-
-def space_index(z, y, c):
-    return z * 8 + y * 2 + c
-
-
 def per_device(snapshots, kappa):
     rows, planes, width = snapshots.shape
     nodes = lax.axis_size("node")
     spaces = lax.axis_size("space")
     me = lax.axis_index("node")
-    sp = lax.axis_index("space")
     chunk = width // nodes
     span = chunk + 2 * NZ
     snaps = rows * nodes
@@ -115,35 +106,10 @@
     image = stencil(field, below, above, coef)
     part = lax.dot_general(image, field, (((1,), (1,)), ((), ())), preferred_element_type=jnp.float32)
 
-    z, y, c = space_coords(sp)
-    part = part.reshape(snaps, 8, 4, 2, 8)
-    keep = jnp.take(part, c, axis=3)
-    give = jnp.take(part, 1 - c, axis=3)
-    pairs = [(s, s ^ 1) for s in range(spaces)]
-    acc = (keep + lax.ppermute(give, "space", pairs)).reshape(nodes, rows, 8, 4, 8)
-
-    total = jnp.take(acc, me, axis=0)
-    for d in range(1, nodes):
-        blk = jnp.take(acc, (me + d) % nodes, axis=0)
-        total = total + lax.ppermute(blk, "node", [(i, (i + d) % nodes) for i in range(nodes)])
-
-    acc = jnp.take(total, y, axis=2)
-    for d in range(1, 4):
-        blk = jnp.take(total, (y + d) % 4, axis=2)
-        pairs = []
-        for s in range(spaces):
-            zz, yy, cc = space_coords(s)
-            pairs.append((s, space_index(zz, (yy + d) % 4, cc)))
-        acc = acc + lax.ppermute(blk, "space", pairs)
-
-    out = jnp.take(acc, z, axis=1)
-    for d in range(1, 8):
-        blk = jnp.take(acc, (z + d) % 8, axis=1)
-        pairs = []
-        for s in range(spaces):
-            zz, yy, cc = space_coords(s)
-            pairs.append((s, space_index((zz + d) % 8, yy, cc)))
-        out = out + lax.ppermute(blk, "space", pairs)
+    part = part.reshape(nodes, rows, snaps)
+    part = lax.all_to_all(part, "node", 0, 0, tiled=True).sum(axis=0)
+    part = part.reshape(rows, spaces, snaps // spaces).transpose(1, 0, 2)
+    out = lax.all_to_all(part, "space", 0, 0, tiled=True).sum(axis=0)
 
     scale = jnp.float32(1.0 / math.sqrt(planes * spaces * NY * NZ))
     return out * scale

time: 183 us -> 181 us (0.989)
  blocking collectives: 0 us -> 42.4 us
  starting transfers between devices: 44.8 us -> 13.7 us
  waiting for transfers between devices: 87.1 us -> 72.6 us
    all_to_all x0 -> x2, blocking collectives: none -> 42.4 us  [the longest x1 24.7 us: per_device(): out = lax.all_to_all(part, 'space', 0, 0, tiled=True).sum(axis=0)]
    ppermute x14 -> x0, starting transfers between devices: 29.9 us -> none  [the longest x7 17.7 us: per_device(): out = out + lax.ppermute(blk, 'space', pairs)]
    ppermute x1, waiting for transfers between devices: 1.86 us -> 21.4 us  [per_device(): above = lax.ppermute(field[:, :span], 'space', down)]
    ppermute x1, waiting for transfers between devices: 22 us -> 3.82 us  [per_device(): below = lax.ppermute(field[:, span:], 'space', up)]
    ppermute x14 -> x0, waiting for transfers between devices: 15.9 us -> none  [the longest x3 7.93 us: per_device(): lax.ppermute(blk, 'node', [(i, (i + d) % nodes) for i in range(nodes)])]
  transfers between devices with their start and end apart: 19 -> 5, of which waited for: 11 -> 3; matrix products, arithmetic and copies ran while one was open for 3% -> 3% of each run, Pallas kernels for 0% -> 0%
where the time goes in v2:
time: 181 us; the launch traced here: 178 us
  waiting for transfers between devices  72.6 us (40%)
  blocking collectives  42.4 us (23%)
  local copies, waits for them, and re-layouts  22.5 us (12%)
  Pallas kernels  15.9 us (9%)
  starting transfers between devices  13.7 us (8%)
  matrix products  6.11 us (3%)
  other arithmetic  4.49 us (2%)
    all_to_all x1, waiting for transfers between devices, per_device(): lax.all_to_all(pieces, 'node', 0, 0, tiled=True)  47.4 us
    all_to_all x1, blocking collectives, per_device(): out = lax.all_to_all(part, 'space', 0, 0, tiled=True).sum(axis=0)  24.7 us
    ppermute x1, waiting for transfers between devices, per_device(): above = lax.ppermute(field[:, :span], 'space', down)  21.4 us
    all_to_all x1, blocking collectives, per_device(): part = lax.all_to_all(part, 'node', 0, 0, tiled=True).sum(axis=0)  17.7 us
    pallas_call x1, Pallas kernels, stencil(): pl.pallas_call(stencil_kernel, grid=(snaps // ROWS,), in_specs=[pl.BlockS...  15.9 us
    slice x1, local copies, waits for them, and re-layouts, per_device(): spad[:, :, q * chunk:q * chunk + span]  10.6 us
    dot_general x1, matrix products, per_device(): lax.dot_general(image, field, (((1,), (1,)), ((), ())), preferred_element...  6.11 us
    another operation x4, local copies, waits for them, and re-layouts, per_device(): jnp.stack([spad[:, :, q * chunk:q * chunk + span] for q in range(nodes)])  5.86 us
  transfers between devices with their start and end apart: 5, of which 3 were waited for; matrix products, arithmetic and copies ran while one was open for 3% of the time, Pallas kernels for 0%

profile of v2, /device:TPU:8, one launch (start us, length us, event | category | flops | bytes accessed | tf_op | source)
XLA Modules:
  0.0 177.9 jit_solution(15086771719528866285)
XLA Ops:
  0.0 10.6 %pad_slice_fusion.1 = (bf16[128,2,2176]{2,1,0:T(2,128)(2,1)S(1)}, bf16[128,2,2176]{2,1,0:T(2,128)(2,1)S(1)}, bf16[128,2,2176]{2,1,0:T(2,128)(2,1)}, bf16[128,2,2176]{2,1,0:T(2,128)(2,1)}) fusion(bf16[128,2,8192]{2,1,0:T(2,128)(2,1)} %param.2), kind=kLoop, calls=%fused_computation.2 | loop fusion | bytes 10878976 | tf_op jit(solution)/shard_map/slice | solution.py:100
  10.6 0.7 stack.54
  11.3 0.8 stack.57
  12.1 1.8 %stack.56 = bf16[1,128,4352]{2,1,0:T(8,128)(2,1)S(1)} reshape(bf16[128,2,2176]{2,1,0:T(2,128)(2,1)} %get-tuple-element.11) | data formatting | bytes 2228224 | tf_op jit(solution)/shard_map/stack | solution.py:100
  13.8 2.6 %stack.55 = bf16[1,128,4352]{2,1,0:T(8,128)(2,1)} reshape(bf16[128,2,2176]{2,1,0:T(2,128)(2,1)} %get-tuple-element.12) | data formatting | bytes 2228224 | tf_op jit(solution)/shard_map/stack | solution.py:100
  16.4 3.5 %pad_maximum_fusion = bf16[4,128,4352]{2,1,0:T(8,128)(2,1)} fusion(bf16[1,128,4352]{2,1,0:T(8,128)(2,1)S(1)} %stack.57, bf16[1,128,4352]{2,1,0:T(8,128)(2,1)S(1)} %stack.56, bf16[1,128,4352]{2,1,0:T(8,128)(2,1)} %stack.55, bf16[1,128,4352]{2,1,0:T(8,128)(2,1)S(1)} %stack.54), kind=kLoop, calls=%fused_computation | loop fusion | flops 6684672 | bytes 8912896 | tf_op jit(solution)/shard_map/stack | solution.py:100
  19.9 0.0 copy-start.1
  19.9 5.0 %all-to-all-start = ((bf16[4,128,4352]{2,1,0:T(8,128)(2,1)}), bf16[4,128,4352]{2,1,0:T(8,128)(2,1)}, u32[]{:S(2)}, u32[]{:S(2)}) async-start(bf16[4,128,4352]{2,1,0:T(8,128)(2,1)} %pad_maximum_fusion), calls=%async_computation | async-start | bytes 8912896 | tf_op jit(solution)/shard_map/all_to_all | solution.py:102
  24.9 0.0 copy-done.1
  24.9 0.1 dynamic-slice_reduce_fusion
  25.1 1.9 %collective-permute-start.3 = (bf16[2176]{0:T(1024)(128)(2,1)S(1)}, bf16[2176]{0:T(1024)(128)(2,1)S(1)}, u32[]{:S(2)}, u32[]{:S(2)}) collective-permute-start(bf16[2176]{0:T(1024)(128)(2,1)S(1)} %get-tuple-element.5), channel_id=1, source_target_pairs={{1,0},{2,1},{3,2},{4,3},{5,4},{6,5},{7,6},{8,7},{9,8},{10,9},{11,1... | collective-permute-start | bytes 13064 | tf_op jit(solution)/shard_map/ppermute | solution.py:96
  27.0 2.4 %collective-permute-start.2 = (bf16[2176]{0:T(1024)(128)(2,1)S(1)}, bf16[2176]{0:T(1024)(128)(2,1)S(1)}, u32[]{:S(2)}, u32[]{:S(2)}) collective-permute-start(bf16[2176]{0:T(1024)(128)(2,1)S(1)} %get-tuple-element.6), channel_id=1, source_target_pairs={{0,1},{1,2},{2,3},{3,4},{4,5},{5,6},{6,7},{7,8},{8,9},{9,10},{10,1... | collective-permute-start | bytes 13064 | tf_op jit(solution)/shard_map/ppermute | solution.py:95
  29.4 0.1 fusion.17
  29.5 47.4 %all-to-all-done = bf16[4,128,4352]{2,1,0:T(8,128)(2,1)} async-done(((bf16[4,128,4352]{2,1,0:T(8,128)(2,1)}), bf16[4,128,4352]{2,1,0:T(8,128)(2,1)}, u32[]{:S(2)}, u32[]{:S(2)}) %all-to-all-start) | async-done | bytes 4456480 | tf_op jit(solution)/shard_map/all_to_all | solution.py:102
  76.9 4.7 %fusion.18 = (bf16[512,2176]{1,0:T(8,128)(2,1)}, bf16[512,2176]{1,0:T(8,128)(2,1)}) fusion(bf16[512,4352]{1,0:T(8,128)(2,1)} %bitcast.x_ref), kind=kLoop, calls=%fused_computation.33 | loop fusion | bytes 8912896 | tf_op jit(solution)/shard_map/slice | solution.py:105
  81.6 1.9 %collective-permute-start.1 = (bf16[512,2176]{1,0:T(8,128)(2,1)}, bf16[512,2176]{1,0:T(8,128)(2,1)S(1)}, u32[]{:S(2)}, u32[]{:S(2)}) collective-permute-start(bf16[512,2176]{1,0:T(8,128)(2,1)} %get-tuple-element.7), channel_id=1, source_target_pairs={{1,0},{2,1},{3,2},{4,3},{5,4},{6,5},{7,6},{8,7},{9,8},{10,9},{11,1... | collective-permute-start | bytes 6684680 | tf_op jit(solution)/shard_map/ppermute | solution.py:105
  83.5 2.4 %collective-permute-start = (bf16[512,2176]{1,0:T(8,128)(2,1)}, bf16[512,2176]{1,0:T(8,128)(2,1)}, u32[]{:S(2)}, u32[]{:S(2)}) collective-permute-start(bf16[512,2176]{1,0:T(8,128)(2,1)} %get-tuple-element.8), channel_id=1, source_target_pairs={{0,1},{1,2},{2,3},{3,4},{4,5},{5,6},{6,7},{7,8},{8,9},{9,10},{10,1... | collective-permute-start | bytes 6684680 | tf_op jit(solution)/shard_map/ppermute | solution.py:104
  85.9 0.1 fusion.21
  86.0 0.1 fusion.20
  86.1 0.0 collective-permute-done.3
  86.1 0.0 collective-permute-done.2
  86.2 0.2 fusion.11
  86.5 0.8 stack.71.coef_ref
  87.3 21.4 %collective-permute-done.1.above_ref = bf16[512,2176]{1,0:T(8,128)(2,1)S(1)} collective-permute-done((bf16[512,2176]{1,0:T(8,128)(2,1)}, bf16[512,2176]{1,0:T(8,128)(2,1)S(1)}, u32[]{:S(2)}, u32[]{:S(2)}) %collective-permute-start.1) | collective-permute-done | bytes 2228256 | tf_op jit(solution)/shard_map/ppermute | solution.py:105
  108.7 0.0 copy-start
  108.7 3.8 %collective-permute-done.below_ref = bf16[512,2176]{1,0:T(8,128)(2,1)} collective-permute-done((bf16[512,2176]{1,0:T(8,128)(2,1)}, bf16[512,2176]{1,0:T(8,128)(2,1)}, u32[]{:S(2)}, u32[]{:S(2)}) %collective-permute-start) | collective-permute-done | bytes 2228256 | tf_op jit(solution)/shard_map/ppermute | solution.py:104
  112.6 0.0 copy-done
  112.6 15.9 %shard_map.28 = bf16[512,4352]{1,0:T(8,128)(2,1)} custom-call(bf16[512,4352]{1,0:T(8,128)(2,1)} %bitcast.x_ref, bf16[512,2176]{1,0:T(8,128)(2,1)} %collective-permute-done.below_ref, bf16[512,2176]{1,0:T(8,128)(2,1)} %copy-done, f32[6,4352]{1,0:T(8,128)} %stack.71.coef_ref), custom_call_target="tpu_custom_call" | custom-call | tf_op jit(solution)/shard_map/pallas_call | solution.py:55
  128.5 6.1 %fusion.22 = f32[4,128,512]{2,1,0:T(8,128)S(1)} fusion(bf16[4,128,4352]{2,1,0:T(8,128)(2,1)} %bitcast.33, bf16[512,4352,1]{1,0,2:T(8,128)(2,1)} %bitcast.2), kind=kOutput, calls=%fused_computation.37 | convolution fusion | flops 2281701376 | bytes 9961472 | tf_op jit(solution)/shard_map/dot_general | solution.py:107
  134.6 17.7 %all_to_all.15 = f32[4,128,512]{2,1,0:T(8,128)S(1)} all-to-all(f32[4,128,512]{2,1,0:T(8,128)S(1)} %fusion.22), channel_id=1, replica_groups=mesh['node'=4,'space'=64] {'node'}, dimensions={0} | all-to-all | bytes 2097152 | tf_op jit(solution)/shard_map/all_to_all | solution.py:110
  152.3 0.1 reduce_sum.18
  152.4 0.1 copy.3
  152.6 24.7 %all_to_all.16 = f32[64,128,8]{1,2,0:T(8,128)S(1)} all-to-all(f32[64,128,8]{1,2,0:T(8,128)S(1)} %bitcast.34), channel_id=1, replica_groups=mesh['node'=4,'space'=64] {'space'}, dimensions={0} | all-to-all | bytes 524288 | tf_op jit(solution)/shard_map/all_to_all | solution.py:112
  177.2 0.1 reduce_sum.19
  177.3 0.6 broadcast_multiply_fusion
  (10 shorter events, 0.2 us)
Async XLA Ops:
  19.9 5.0 %copy-start.1 = (bf16[2,8192]{1,0:T(2,128)(2,1)S(1)}, bf16[2,8192]{1,0:T(2,128)(2,1)}, u32[]{:S(2)}) copy-start(bf16[2,8192]{1,0:T(2,128)(2,1)} %param.3) | copy-start | bytes 98308
  19.9 57.0 %all-to-all-start = ((bf16[4,128,4352]{2,1,0:T(8,128)(2,1)}), bf16[4,128,4352]{2,1,0:T(8,128)(2,1)}, u32[]{:S(2)}, u32[]{:S(2)}) async-start(bf16[4,128,4352]{2,1,0:T(8,128)(2,1)} %pad_maximum_fusion), calls=%async_computation | async-start | bytes 8912896 | tf_op jit(solution)/shard_map/all_to_all | solution.py:102
  25.1 61.0 %collective-permute-start.3 = (bf16[2176]{0:T(1024)(128)(2,1)S(1)}, bf16[2176]{0:T(1024)(128)(2,1)S(1)}, u32[]{:S(2)}, u32[]{:S(2)}) collective-permute-start(bf16[2176]{0:T(1024)(128)(2,1)S(1)} %get-tuple-element.5), channel_id=1, source_target_pairs={{1,0},{2,1},{3,2},{4,3},{5,4},{6,5},{7,6},{8,7},{9,8},{10,9},{11,1... | collective-permute-start | bytes 13064 | tf_op jit(solution)/shard_map/ppermute | solution.py:96
  27.0 59.1 %collective-permute-start.2 = (bf16[2176]{0:T(1024)(128)(2,1)S(1)}, bf16[2176]{0:T(1024)(128)(2,1)S(1)}, u32[]{:S(2)}, u32[]{:S(2)}) collective-permute-start(bf16[2176]{0:T(1024)(128)(2,1)S(1)} %get-tuple-element.6), channel_id=1, source_target_pairs={{0,1},{1,2},{2,3},{3,4},{4,5},{5,6},{6,7},{7,8},{8,9},{9,10},{10,1... | collective-permute-start | bytes 13064 | tf_op jit(solution)/shard_map/ppermute | solution.py:95
  81.6 27.2 %collective-permute-start.1 = (bf16[512,2176]{1,0:T(8,128)(2,1)}, bf16[512,2176]{1,0:T(8,128)(2,1)S(1)}, u32[]{:S(2)}, u32[]{:S(2)}) collective-permute-start(bf16[512,2176]{1,0:T(8,128)(2,1)} %get-tuple-element.7), channel_id=1, source_target_pairs={{1,0},{2,1},{3,2},{4,3},{5,4},{6,5},{7,6},{8,7},{9,8},{10,9},{11,1... | collective-permute-start | bytes 6684680 | tf_op jit(solution)/shard_map/ppermute | solution.py:105
  83.5 29.1 %collective-permute-start = (bf16[512,2176]{1,0:T(8,128)(2,1)}, bf16[512,2176]{1,0:T(8,128)(2,1)}, u32[]{:S(2)}, u32[]{:S(2)}) collective-permute-start(bf16[512,2176]{1,0:T(8,128)(2,1)} %get-tuple-element.8), channel_id=1, source_target_pairs={{0,1},{1,2},{2,3},{3,4},{4,5},{5,6},{6,7},{7,8},{8,9},{9,10},{10,1... | collective-permute-start | bytes 6684680 | tf_op jit(solution)/shard_map/ppermute | solution.py:104
  108.7 3.8 %copy-start = (bf16[512,2176]{1,0:T(8,128)(2,1)}, bf16[512,2176]{1,0:T(8,128)(2,1)S(1)}, u32[]{:S(2)}) copy-start(bf16[512,2176]{1,0:T(8,128)(2,1)S(1)} %collective-permute-done.1.above_ref) | copy-start | bytes 6684676

commit v3 on v2

--- a/solution.py
+++ b/solution.py
@@ -10,6 +10,7 @@
 NY = 128
 NZ = 64
 ROWS = 32
+GROUPS = 2
 
 
 def ahead(values, offset):
@@ -28,7 +29,7 @@
     zpos = lane % NZ
     up_ok = zpos != NZ - 1
     down_ok = zpos != 0
-    inner = (lane >= NZ) & (lane < span - NZ)
+    inner = lane < span - 2 * NZ
     planes = [x_ref[:, p * span:(p + 1) * span].astype(jnp.float32) for p in range(2)]
     below = below_ref[...].astype(jnp.float32)
     above = above_ref[...].astype(jnp.float32)
@@ -70,12 +71,22 @@
     span = kap_chunk.shape[-1]
     kc = kap_chunk.astype(jnp.float32)
     zpos = jnp.arange(span, dtype=jnp.int32) % NZ
-    k_zp = jnp.where(zpos != NZ - 1, ahead(kc, 1), 0.0)
-    k_zm = jnp.where(zpos != 0, behind(kc, 1), 0.0)
+    k_zp = jnp.where(zpos != NZ - 1, jnp.roll(kc, -1, axis=-1), 0.0)
+    k_zm = jnp.where(zpos != 0, jnp.roll(kc, 1, axis=-1), 0.0)
     k_xm = jnp.stack([kap_below.astype(jnp.float32), kc[0]])
     k_xp = jnp.stack([kc[1], kap_above.astype(jnp.float32)])
-    near = [k_zp, k_zm, ahead(kc, NZ), behind(kc, NZ), k_xm, k_xp]
+    near = [k_zp, k_zm, jnp.roll(kc, -NZ, axis=-1), jnp.roll(kc, NZ, axis=-1), k_xm, k_xp]
     return jnp.stack([0.5 * (kc + k) for k in near]).reshape(6, 2 * span)
+
+
+def chunked(values, nodes):
+    lead = values.shape[:-1]
+    cut = values.reshape(lead + (nodes, values.shape[-1] // nodes))
+    pad = jnp.zeros(lead + (1, NZ), values.dtype)
+    after = jnp.concatenate([cut[..., 1:, :NZ], pad], axis=-2)
+    before = jnp.concatenate([pad, cut[..., :-1, -NZ:]], axis=-2)
+    pieces = jnp.concatenate([cut, after, before], axis=-1)
+    return jnp.moveaxis(pieces, -2, 0)
 
 
 def per_device(snapshots, kappa):
@@ -90,21 +101,28 @@
     up = [(i, i + 1) for i in range(spaces - 1)]
     down = [(j, i) for i, j in up]
 
-    kpad = jnp.pad(kappa, ((0, 0), (NZ, NZ)))
-    kap_chunk = lax.dynamic_slice_in_dim(kpad, me * chunk, span, axis=1)
+    kap_chunk = jnp.take(chunked(kappa, nodes), me, axis=0)
     kap_below = lax.ppermute(kap_chunk[1], "space", up)
     kap_above = lax.ppermute(kap_chunk[0], "space", down)
     coef = weights(kap_chunk, kap_below, kap_above)
 
-    spad = jnp.pad(snapshots, ((0, 0), (0, 0), (NZ, NZ)))
-    pieces = jnp.stack([spad[:, :, q * chunk:q * chunk + span] for q in range(nodes)])
-    pieces = pieces.reshape(nodes, rows, planes * span)
-    field = lax.all_to_all(pieces, "node", 0, 0, tiled=True).reshape(snaps, planes * span)
-
-    below = lax.ppermute(field[:, span:], "space", up)
-    above = lax.ppermute(field[:, :span], "space", down)
-    image = stencil(field, below, above, coef)
-    part = lax.dot_general(image, field, (((1,), (1,)), ((), ())), preferred_element_type=jnp.float32)
+    pieces = chunked(snapshots, nodes).reshape(nodes, rows, planes * span)
+    step = rows // GROUPS
+    images, fields = [], []
+    for g in range(GROUPS):
+        field = lax.all_to_all(pieces[:, g * step:(g + 1) * step], "node", 0, 0, tiled=True)
+        field = field.reshape(nodes * step, planes * span)
+        below = lax.ppermute(field[:, span:], "space", up)
+        above = lax.ppermute(field[:, :span], "space", down)
+        images.append(stencil(field, below, above, coef))
+        fields.append(field)
+    part = jnp.concatenate([
+        jnp.concatenate([
+            lax.dot_general(im, fd, (((1,), (1,)), ((), ())), preferred_element_type=jnp.float32)
+            for fd in fields], axis=1)
+        for im in images], axis=0)
+    order = (GROUPS, nodes, step)
+    part = part.reshape(order + order).transpose(1, 0, 2, 4, 3, 5).reshape(snaps, snaps)
 
     part = part.reshape(nodes, rows, snaps)
     part = lax.all_to_all(part, "node", 0, 0, tiled=True).sum(axis=0)

time: 181 us -> 206 us (1.14)
  local copies, waits for them, and re-layouts: 22.5 us -> 58.7 us
  waiting for transfers between devices: 72.6 us -> 50.6 us
  starting transfers between devices: 13.7 us -> 21.9 us
  matrix products: 6.11 us -> 10.6 us
  other arithmetic: 4.49 us -> 1.27 us
    ppermute x1 -> x2, waiting for transfers between devices: 21.4 us -> 0.01 us  [per_device(): above = lax.ppermute(field[:, :span], 'space', down)]
    reshape x0 -> x4, local copies, waits for them, and re-layouts: none -> 19.2 us  [the longest x1 7.8 us: per_device(): pieces = chunked(snapshots, nodes).reshape(nodes, rows, planes * span)]
    concatenate x0 -> x10, local copies, waits for them, and re-layouts: none -> 14.7 us  [the longest x2 14 us: chunked(): pieces = jnp.concatenate([cut, after, before], axis=-1)]
    transpose x0 -> x1, local copies, waits for them, and re-layouts: none -> 7.8 us  [chunked(): return jnp.moveaxis(pieces, -2, 0)]
    dot_general x1 -> x4, matrix products: 6.11 us -> 10.6 us  [per_device(): lax.dot_general(im, fd, (((1,), (1,)), ((), ())), preferred_element_type=...]
    slice x3, local copies, waits for them, and re-layouts: 10.7 us -> 6.81 us  [the longest x1 4.69 us: per_device(): pieces[:, g * step:(g + 1) * step]]
    ppermute x1 -> x2, waiting for transfers between devices: 3.82 us -> 0.01 us  [per_device(): below = lax.ppermute(field[:, span:], 'space', up)]
    all_to_all x1 -> x2, starting transfers between devices: 5.02 us -> 8.77 us  [per_device(): lax.all_to_all(pieces[:, g * step:(g + 1) * step], 'node', 0, 0, tiled=True)]
  transfers between devices with their start and end apart: 5 -> 8, of which waited for: 3 -> 2; matrix products, arithmetic and copies ran while one was open for 3% -> 27% of each run, Pallas kernels for 0% -> 4%
where the time goes in v3:
time: 206 us; the launch traced here: 203 us
  local copies, waits for them, and re-layouts  58.7 us (28%)
  waiting for transfers between devices  50.6 us (25%)
  blocking collectives  42.1 us (20%)
  starting transfers between devices  21.9 us (11%)
  Pallas kernels  16.9 us (8%)
  matrix products  10.6 us (5%)
    all_to_all x2, waiting for transfers between devices, per_device(): lax.all_to_all(pieces[:, g * step:(g + 1) * step], 'node', 0, 0, tiled=True)  50.6 us
    all_to_all x1, blocking collectives, per_device(): out = lax.all_to_all(part, 'space', 0, 0, tiled=True).sum(axis=0)  23.2 us
    all_to_all x1, blocking collectives, per_device(): part = lax.all_to_all(part, 'node', 0, 0, tiled=True).sum(axis=0)  18.9 us
    pallas_call x2, Pallas kernels, stencil(): pl.pallas_call(stencil_kernel, grid=(snaps // ROWS,), in_specs=[pl.BlockS...  16.9 us
    concatenate x2, local copies, waits for them, and re-layouts, chunked(): pieces = jnp.concatenate([cut, after, before], axis=-1)  14 us
    dot_general x4, matrix products, per_device(): lax.dot_general(im, fd, (((1,), (1,)), ((), ())), preferred_element_type=...  10.6 us
    all_to_all x2, starting transfers between devices, per_device(): lax.all_to_all(pieces[:, g * step:(g + 1) * step], 'node', 0, 0, tiled=True)  8.77 us
    transpose x1, local copies, waits for them, and re-layouts, chunked(): return jnp.moveaxis(pieces, -2, 0)  7.8 us
  transfers between devices with their start and end apart: 8, of which 2 were waited for; matrix products, arithmetic and copies ran while one was open for 27% of the time, Pallas kernels for 4%

profile of v3, /device:TPU:8, one launch (start us, length us, event | category | flops | bytes accessed | tf_op | source)
XLA Modules:
  0.0 202.6 jit_solution(5419213872589219896)
XLA Ops:
  0.0 0.8 fusion.11
  0.8 0.9 concatenate.79
  1.7 0.1 slice_reduce_fusion
  1.7 1.9 collective-permute-start.3
  3.7 2.4 %collective-permute-start.2 = (bf16[2176]{0:T(1024)(128)(2,1)S(1)}, bf16[2176]{0:T(1024)(128)(2,1)S(1)}, u32[]{:S(2)}, u32[]{:S(2)}) collective-permute-start(bf16[2176]{0:T(1024)(128)(2,1)S(1)} %get-tuple-element.17), channel_id=1, source_target_pairs={{0,1},{1,2},{2,3},{3,4},{4,5},{5,6},{6,7},{7,8},{8,9},{9,10},{10,1... | collective-permute-start | bytes 13064 | tf_op jit(solution)/shard_map/ppermute | solution.py:105
  6.1 7.7 %reshape.195 = bf16[128,2,4,2048]{3,2,1,0:T(4,128)(2,1)} reshape(bf16[128,2,8192]{2,1,0:T(2,128)(2,1)} %param.2) | data formatting | bytes 8388608 | tf_op jit(solution)/shard_map/reshape | solution.py:84
  13.7 1.4 fusion.8
  15.1 0.2 concatenate.75
  15.3 0.1 concatenate.74
  15.5 13.2 %concatenate.76 = bf16[128,2,4,2176]{3,2,1,0:T(4,128)(2,1)} concatenate(bf16[128,2,4,2048]{3,2,1,0:T(4,128)(2,1)} %reshape.195, bf16[128,2,4,64]{3,2,1,0:T(4,128)(2,1)S(1)} %concatenate.74, bf16[128,2,4,64]{3,2,1,0:T(4,128)(2,1)S(1)} %concatenate.75), dimensions={3} | concatenate | bytes 8912896 | tf_op jit(solution)/shard_map/concatenate | solution.py:88
  28.6 7.8 %copy.16 = bf16[4,128,2,2176]{3,2,1,0:T(2,128)(2,1)} copy(bf16[4,128,2,2176]{3,0,2,1:T(4,128)(2,1)} %bitcast.74) | data formatting | bytes 8912896 | tf_op jit(solution)/shard_map/transpose | solution.py:89
  36.4 7.8 %reshape.196 = bf16[4,128,4352]{2,1,0:T(8,128)(2,1)} reshape(bf16[4,128,2,2176]{3,2,1,0:T(2,128)(2,1)} %copy.16) | data formatting | bytes 8912896 | tf_op jit(solution)/shard_map/reshape | solution.py:109
  44.2 4.7 %fusion.7 = (bf16[4,64,4352]{2,1,0:T(8,128)(2,1)}, bf16[4,64,4352]{2,1,0:T(8,128)(2,1)}) fusion(bf16[4,128,4352]{2,1,0:T(8,128)(2,1)} %reshape.196), kind=kLoop, calls=%fused_computation.37 | loop fusion | bytes 8912896 | tf_op jit(solution)/shard_map/slice | solution.py:113
  48.9 4.3 %all-to-all-start.1 = ((bf16[4,64,4352]{2,1,0:T(8,128)(2,1)}), bf16[4,64,4352]{2,1,0:T(8,128)(2,1)S(1)}, u32[]{:S(2)}, u32[]{:S(2)}) async-start(bf16[4,64,4352]{2,1,0:T(8,128)(2,1)} %get-tuple-element.21), calls=%async_computation.1 | async-start | bytes 4456448 | tf_op jit(solution)/shard_map/all_to_all | solution.py:113
  53.2 0.1 slice_bitcast_fusion.6
  53.3 0.1 slice_bitcast_fusion.2
  53.4 0.1 maximum_bitcast_fusion
  53.6 0.1 slice_bitcast_fusion
  53.6 28.7 %all-to-all-done.1 = bf16[4,64,4352]{2,1,0:T(8,128)(2,1)S(1)} async-done(((bf16[4,64,4352]{2,1,0:T(8,128)(2,1)}), bf16[4,64,4352]{2,1,0:T(8,128)(2,1)S(1)}, u32[]{:S(2)}, u32[]{:S(2)}) %all-to-all-start.1) | async-done | bytes 2228256 | tf_op jit(solution)/shard_map/all_to_all | solution.py:113
  82.3 0.0 copy-start
  82.3 4.5 %all-to-all-start = ((bf16[4,64,4352]{2,1,0:T(8,128)(2,1)}), bf16[4,64,4352]{2,1,0:T(8,128)(2,1)}, u32[]{:S(2)}, u32[]{:S(2)}) async-start(bf16[4,64,4352]{2,1,0:T(8,128)(2,1)} %get-tuple-element.20), calls=%async_computation | async-start | bytes 4456448 | tf_op jit(solution)/shard_map/all_to_all | solution.py:113
  86.8 0.1 slice_bitcast_fusion.4
  86.9 0.1 maximum_bitcast_fusion.2
  87.1 0.0 collective-permute-done.3
  87.2 0.0 collective-permute-done.2
  87.3 0.0 copy-done
  87.3 1.5 fusion.10
  88.8 1.9 collective-permute-start.5
  90.7 2.4 %collective-permute-start.4 = (bf16[256,2176]{1,0:T(8,128)(2,1)}, bf16[256,2176]{1,0:T(8,128)(2,1)}, u32[]{:S(2)}, u32[]{:S(2)}) collective-permute-start(bf16[256,2176]{1,0:T(8,128)(2,1)} %get-tuple-element.27), channel_id=1, source_target_pairs={{0,1},{1,2},{2,3},{3,4},{4,5},{5,6},{6,7},{7,8},{8,9},{9,10},{10,1... | collective-permute-start | bytes 3342344 | tf_op jit(solution)/shard_map/ppermute | solution.py:115
  93.1 21.9 %all-to-all-done = bf16[4,64,4352]{2,1,0:T(8,128)(2,1)} async-done(((bf16[4,64,4352]{2,1,0:T(8,128)(2,1)}), bf16[4,64,4352]{2,1,0:T(8,128)(2,1)}, u32[]{:S(2)}, u32[]{:S(2)}) %all-to-all-start) | async-done | bytes 2228256 | tf_op jit(solution)/shard_map/all_to_all | solution.py:113
  115.1 3.2 %fusion.9 = (bf16[256,2176]{1,0:T(8,128)(2,1)}, bf16[256,2176]{1,0:T(8,128)(2,1)}) fusion(bf16[256,4352]{1,0:T(8,128)(2,1)} %bitcast.1.x_ref), kind=kLoop, calls=%fused_computation.39 | loop fusion | bytes 4456448 | tf_op jit(solution)/shard_map/slice | solution.py:116
  118.2 1.9 collective-permute-start.1
  120.2 2.6 %collective-permute-start = (bf16[256,2176]{1,0:T(8,128)(2,1)}, bf16[256,2176]{1,0:T(8,128)(2,1)}, u32[]{:S(2)}, u32[]{:S(2)}) collective-permute-start(bf16[256,2176]{1,0:T(8,128)(2,1)} %get-tuple-element.25), channel_id=1, source_target_pairs={{0,1},{1,2},{2,3},{3,4},{4,5},{5,6},{6,7},{7,8},{8,9},{9,10},{10,1... | collective-permute-start | bytes 3342344 | tf_op jit(solution)/shard_map/ppermute | solution.py:115
  122.8 0.1 add_multiply_fusion
  122.9 0.8 stack.43.coef_ref
  123.7 0.0 copy-start.1
  123.7 0.0 collective-permute-done.5.above_ref
  123.7 0.0 copy-start.4
  123.7 0.0 collective-permute-done.4.below_ref
  123.7 1.1 copy-done.4
  124.8 8.4 %shard_map.29 = bf16[256,4352]{1,0:T(8,128)(2,1)} custom-call(bf16[256,4352]{1,0:T(8,128)(2,1)} %bitcast.71, bf16[256,2176]{1,0:T(8,128)(2,1)} %collective-permute-done.4.below_ref, bf16[256,2176]{1,0:T(8,128)(2,1)} %copy-done.4, f32[6,4352]{1,0:T(8,128)} %stack.43.coef_ref), custom_call_target="tpu_custom_call" | custom-call | tf_op jit(solution)/shard_map/pallas_call | solution.py:56
  133.2 0.0 copy-done.1
  133.2 0.0 copy-start.3
  133.2 2.5 %fusion.16 = f32[256,256]{0,1:T(8,128)S(1)} fusion(bf16[256,4352]{1,0:T(8,128)(2,1)} %shard_map.29, bf16[256,4352]{1,0:T(8,128)(2,1)S(1)} %bitcast.72), kind=kOutput, calls=%fused_computation.46 | convolution fusion | flops 570425344 | bytes 4718592 | tf_op jit(solution)/shard_map/dot_general | solution.py:121
  135.8 0.0 copy-done.3
  135.8 3.1 %fusion.15 = f32[256,256]{0,1:T(8,128)} fusion(bf16[256,4352]{1,0:T(8,128)(2,1)S(1)} %copy-done.3, bf16[256,4352]{1,0:T(8,128)(2,1)} %bitcast.1.x_ref), kind=kOutput, calls=%fused_computation.45 | convolution fusion | flops 570425344 | bytes 4718592 | tf_op jit(solution)/shard_map/dot_general | solution.py:121
  138.9 0.0 collective-permute-done.1.above_ref
  138.9 0.0 collective-permute-done.below_ref
  138.9 8.5 %shard_map.28 = bf16[256,4352]{1,0:T(8,128)(2,1)} custom-call(bf16[256,4352]{1,0:T(8,128)(2,1)} %bitcast.1.x_ref, bf16[256,2176]{1,0:T(8,128)(2,1)} %collective-permute-done.below_ref, bf16[256,2176]{1,0:T(8,128)(2,1)} %collective-permute-done.1.above_ref, f32[6,4352]{1,0:T(8,128)} %stack.43.coef_ref), custom_call_target="tpu_custom_call" | custom-call | tf_op jit(solution)/shard_map/pallas_call | solution.py:56
  147.4 2.5 %fusion.14 = f32[256,256]{0,1:T(8,128)S(1)} fusion(bf16[256,4352]{1,0:T(8,128)(2,1)} %shard_map.28, bf16[256,4352]{1,0:T(8,128)(2,1)S(1)} %bitcast.73), kind=kOutput, calls=%fused_computation.44 | convolution fusion | flops 570425344 | bytes 4718592 | tf_op jit(solution)/shard_map/dot_general | solution.py:121
  149.9 0.0 copy-done.2
  149.9 0.0 copy-start.5
  149.9 2.4 %fusion.13 = f32[256,256]{0,1:T(8,128)S(1)} fusion(bf16[256,4352]{1,0:T(8,128)(2,1)S(1)} %copy-done.2, bf16[256,4352]{1,0:T(8,128)(2,1)} %bitcast.1.x_ref), kind=kOutput, calls=%fused_computation.43 | convolution fusion | flops 570425344 | bytes 4718592 | tf_op jit(solution)/shard_map/dot_general | solution.py:121
  152.4 0.0 copy-done.5
  152.4 0.1 maximum_maximum_fusion
  152.5 1.1 reshape.200
  153.6 2.6 %copy.22 = f32[2,4,64,2,4,64]{5,3,4,2,0,1:T(2,128)} copy(f32[2,4,64,2,4,64]{2,1,0,5,4,3:T(4,128)S(1)} %reshape.200) | data formatting | bytes 2097152 | tf_op jit(solution)/shard_map/reshape | solution.py:125
  156.2 3.3 %reshape_reshape.3 = f32[4,128,512]{2,1,0:T(8,128)S(1)} reshape(f32[4,2,64,4,2,64]{5,4,3,2,1,0:T(2,128)} %bitcast.75) | data formatting | bytes 2097152 | tf_op jit(solution)/shard_map/reshape;reshape | solution.py:127
  159.6 18.9 %all_to_all.20 = f32[4,128,512]{2,1,0:T(8,128)S(1)} all-to-all(f32[4,128,512]{2,1,0:T(8,128)S(1)} %reshape_reshape.3), channel_id=1, replica_groups=mesh['node'=4,'space'=64] {'node'}, dimensions={0} | all-to-all | bytes 2097152 | tf_op jit(solution)/shard_map/all_to_all | solution.py:128
  178.5 0.1 reduce_sum.18
  178.5 0.1 copy.23
  178.7 23.2 %all_to_all.21 = f32[64,128,8]{1,2,0:T(8,128)S(1)} all-to-all(f32[64,128,8]{1,2,0:T(8,128)S(1)} %bitcast.76), channel_id=1, replica_groups=mesh['node'=4,'space'=64] {'space'}, dimensions={0} | all-to-all | bytes 524288 | tf_op jit(solution)/shard_map/all_to_all | solution.py:130
  201.9 0.1 reduce_sum.19
  202.0 0.6 broadcast_multiply_fusion
  (22 shorter events, 0.3 us)
Async XLA Ops:
  1.7 85.4 %collective-permute-start.3 = (bf16[2176]{0:T(1024)(128)(2,1)S(1)}, bf16[2176]{0:T(1024)(128)(2,1)S(1)}, u32[]{:S(2)}, u32[]{:S(2)}) collective-permute-start(bf16[2176]{0:T(1024)(128)(2,1)S(1)} %get-tuple-element.16), channel_id=1, source_target_pairs={{1,0},{2,1},{3,2},{4,3},{5,4},{6,5},{7,6},{8,7},{9,8},{10,9},{11,1... | collective-permute-start | bytes 13064 | tf_op jit(solution)/shard_map/ppermute | solution.py:106
  3.7 83.5 %collective-permute-start.2 = (bf16[2176]{0:T(1024)(128)(2,1)S(1)}, bf16[2176]{0:T(1024)(128)(2,1)S(1)}, u32[]{:S(2)}, u32[]{:S(2)}) collective-permute-start(bf16[2176]{0:T(1024)(128)(2,1)S(1)} %get-tuple-element.17), channel_id=1, source_target_pairs={{0,1},{1,2},{2,3},{3,4},{4,5},{5,6},{6,7},{7,8},{8,9},{9,10},{10,1... | collective-permute-start | bytes 13064 | tf_op jit(solution)/shard_map/ppermute | solution.py:105
  48.9 33.4 %all-to-all-start.1 = ((bf16[4,64,4352]{2,1,0:T(8,128)(2,1)}), bf16[4,64,4352]{2,1,0:T(8,128)(2,1)S(1)}, u32[]{:S(2)}, u32[]{:S(2)}) async-start(bf16[4,64,4352]{2,1,0:T(8,128)(2,1)} %get-tuple-element.21), calls=%async_computation.1 | async-start | bytes 4456448 | tf_op jit(solution)/shard_map/all_to_all | solution.py:113
  82.3 5.0 %copy-start = (bf16[4,64,4352]{2,1,0:T(8,128)(2,1)}, bf16[4,64,4352]{2,1,0:T(8,128)(2,1)S(1)}, u32[]{:S(2)}) copy-start(bf16[4,64,4352]{2,1,0:T(8,128)(2,1)S(1)} %all-to-all-done.1) | copy-start | bytes 6684676
  82.3 32.8 %all-to-all-start = ((bf16[4,64,4352]{2,1,0:T(8,128)(2,1)}), bf16[4,64,4352]{2,1,0:T(8,128)(2,1)}, u32[]{:S(2)}, u32[]{:S(2)}) async-start(bf16[4,64,4352]{2,1,0:T(8,128)(2,1)} %get-tuple-element.20), calls=%async_computation | async-start | bytes 4456448 | tf_op jit(solution)/shard_map/all_to_all | solution.py:113
  88.8 34.9 %collective-permute-start.5 = (bf16[256,2176]{1,0:T(8,128)(2,1)}, bf16[256,2176]{1,0:T(8,128)(2,1)S(1)}, u32[]{:S(2)}, u32[]{:S(2)}) collective-permute-start(bf16[256,2176]{1,0:T(8,128)(2,1)} %get-tuple-element.26), channel_id=1, source_target_pairs={{1,0},{2,1},{3,2},{4,3},{5,4},{6,5},{7,6},{8,7},{9,8},{10,9},{11,1... | collective-permute-start | bytes 3342344 | tf_op jit(solution)/shard_map/ppermute | solution.py:116
  90.7 33.0 %collective-permute-start.4 = (bf16[256,2176]{1,0:T(8,128)(2,1)}, bf16[256,2176]{1,0:T(8,128)(2,1)}, u32[]{:S(2)}, u32[]{:S(2)}) collective-permute-start(bf16[256,2176]{1,0:T(8,128)(2,1)} %get-tuple-element.27), channel_id=1, source_target_pairs={{0,1},{1,2},{2,3},{3,4},{4,5},{5,6},{6,7},{7,8},{8,9},{9,10},{10,1... | collective-permute-start | bytes 3342344 | tf_op jit(solution)/shard_map/ppermute | solution.py:115
  118.2 20.7 %collective-permute-start.1 = (bf16[256,2176]{1,0:T(8,128)(2,1)}, bf16[256,2176]{1,0:T(8,128)(2,1)}, u32[]{:S(2)}, u32[]{:S(2)}) collective-permute-start(bf16[256,2176]{1,0:T(8,128)(2,1)} %get-tuple-element.24), channel_id=1, source_target_pairs={{1,0},{2,1},{3,2},{4,3},{5,4},{6,5},{7,6},{8,7},{9,8},{10,9},{11,1... | collective-permute-start | bytes 3342344 | tf_op jit(solution)/shard_map/ppermute | solution.py:116
  120.2 18.7 %collective-permute-start = (bf16[256,2176]{1,0:T(8,128)(2,1)}, bf16[256,2176]{1,0:T(8,128)(2,1)}, u32[]{:S(2)}, u32[]{:S(2)}) collective-permute-start(bf16[256,2176]{1,0:T(8,128)(2,1)} %get-tuple-element.25), channel_id=1, source_target_pairs={{0,1},{1,2},{2,3},{3,4},{4,5},{5,6},{6,7},{7,8},{8,9},{9,10},{10,1... | collective-permute-start | bytes 3342344 | tf_op jit(solution)/shard_map/ppermute | solution.py:115
  123.7 9.5 %copy-start.1 = (bf16[4,64,4352]{2,1,0:T(8,128)(2,1)S(1)}, bf16[4,64,4352]{2,1,0:T(8,128)(2,1)}, u32[]{:S(2)}) copy-start(bf16[4,64,4352]{2,1,0:T(8,128)(2,1)} %copy-done) | copy-start | bytes 6684676
  123.7 1.1 copy-start.4
  133.2 2.6 %copy-start.3 = (bf16[256,4352]{1,0:T(8,128)(2,1)S(1)}, bf16[256,4352]{1,0:T(8,128)(2,1)}, u32[]{:S(2)}) copy-start(bf16[256,4352]{1,0:T(8,128)(2,1)} %shard_map.29) | copy-start | bytes 6684676
  147.4 2.6 %copy-start.2 = (bf16[256,4352]{1,0:T(8,128)(2,1)S(1)}, bf16[256,4352]{1,0:T(8,128)(2,1)}, u32[]{:S(2)}) copy-start(bf16[256,4352]{1,0:T(8,128)(2,1)} %shard_map.28) | copy-start | bytes 6684676
  149.9 2.5 %copy-start.5 = (f32[256,256]{0,1:T(8,128)S(1)}, f32[256,256]{0,1:T(8,128)}, u32[]{:S(2)}) copy-start(f32[256,256]{0,1:T(8,128)} %fusion.15) | copy-start | bytes 786436

commit v4 on v3

--- a/solution.py
+++ b/solution.py
@@ -30,14 +30,14 @@
     up_ok = zpos != NZ - 1
     down_ok = zpos != 0
     inner = lane < span - 2 * NZ
-    planes = [x_ref[:, p * span:(p + 1) * span].astype(jnp.float32) for p in range(2)]
+    planes = [x_ref[p].astype(jnp.float32) for p in range(2)]
     below = below_ref[...].astype(jnp.float32)
     above = above_ref[...].astype(jnp.float32)
     for p in range(2):
         v = planes[p]
 
         def coef(t):
-            return coef_ref[t:t + 1, p * span:(p + 1) * span]
+            return coef_ref[t, p:p + 1, :]
 
         near = jnp.where(up_ok, pltpu.roll(v, span - 1, 1), 0.0)
         total = coef(0) * (v - near)
@@ -47,22 +47,21 @@
         total = total + coef(3) * (v - pltpu.roll(v, NZ, 1))
         total = total + coef(4) * (v - (below if p == 0 else planes[0]))
         total = total + coef(5) * (v - (planes[1] if p == 0 else above))
-        out_ref[:, p * span:(p + 1) * span] = jnp.where(inner, total, 0.0).astype(out_ref.dtype)
+        out_ref[p] = jnp.where(inner, total, 0.0).astype(out_ref.dtype)
 
 
 def stencil(field, below, above, coef):
-    snaps, width = field.shape
-    span = below.shape[1]
+    planes, snaps, span = field.shape
     return pl.pallas_call(
         stencil_kernel,
         grid=(snaps // ROWS,),
         in_specs=[
-            pl.BlockSpec((ROWS, width), lambda i: (i, 0)),
+            pl.BlockSpec((planes, ROWS, span), lambda i: (0, i, 0)),
             pl.BlockSpec((ROWS, span), lambda i: (i, 0)),
             pl.BlockSpec((ROWS, span), lambda i: (i, 0)),
-            pl.BlockSpec(coef.shape, lambda i: (0, 0)),
+            pl.BlockSpec(coef.shape, lambda i: (0, 0, 0)),
         ],
-        out_specs=pl.BlockSpec((ROWS, width), lambda i: (i, 0)),
+        out_specs=pl.BlockSpec((planes, ROWS, span), lambda i: (0, i, 0)),
         out_shape=jax.ShapeDtypeStruct(field.shape, jnp.bfloat16),
     )(field, below, above, coef)
 
@@ -76,17 +75,18 @@
     k_xm = jnp.stack([kap_below.astype(jnp.float32), kc[0]])
     k_xp = jnp.stack([kc[1], kap_above.astype(jnp.float32)])
     near = [k_zp, k_zm, jnp.roll(kc, -NZ, axis=-1), jnp.roll(kc, NZ, axis=-1), k_xm, k_xp]
-    return jnp.stack([0.5 * (kc + k) for k in near]).reshape(6, 2 * span)
+    return jnp.stack([0.5 * (kc + k) for k in near])
 
 
 def chunked(values, nodes):
-    lead = values.shape[:-1]
-    cut = values.reshape(lead + (nodes, values.shape[-1] // nodes))
-    pad = jnp.zeros(lead + (1, NZ), values.dtype)
-    after = jnp.concatenate([cut[..., 1:, :NZ], pad], axis=-2)
-    before = jnp.concatenate([pad, cut[..., :-1, -NZ:]], axis=-2)
-    pieces = jnp.concatenate([cut, after, before], axis=-1)
-    return jnp.moveaxis(pieces, -2, 0)
+    chunk = values.shape[-1] // nodes
+    zero = jnp.zeros(values.shape[:-1] + (NZ,), values.dtype)
+    pieces = []
+    for q in range(nodes):
+        after = values[..., (q + 1) * chunk:(q + 1) * chunk + NZ] if q + 1 < nodes else zero
+        before = values[..., q * chunk - NZ:q * chunk] if q > 0 else zero
+        pieces.append(jnp.concatenate([values[..., q * chunk:(q + 1) * chunk], after, before], axis=-1))
+    return jnp.stack(pieces, axis=-3)
 
 
 def per_device(snapshots, kappa):
@@ -101,24 +101,25 @@
     up = [(i, i + 1) for i in range(spaces - 1)]
     down = [(j, i) for i, j in up]
 
-    kap_chunk = jnp.take(chunked(kappa, nodes), me, axis=0)
+    kap_chunk = jnp.take(chunked(kappa[:, None], nodes)[:, :, 0], me, axis=1)
     kap_below = lax.ppermute(kap_chunk[1], "space", up)
     kap_above = lax.ppermute(kap_chunk[0], "space", down)
     coef = weights(kap_chunk, kap_below, kap_above)
 
-    pieces = chunked(snapshots, nodes).reshape(nodes, rows, planes * span)
+    major = jnp.transpose(snapshots, (1, 0, 2))
     step = rows // GROUPS
     images, fields = [], []
     for g in range(GROUPS):
-        field = lax.all_to_all(pieces[:, g * step:(g + 1) * step], "node", 0, 0, tiled=True)
-        field = field.reshape(nodes * step, planes * span)
-        below = lax.ppermute(field[:, span:], "space", up)
-        above = lax.ppermute(field[:, :span], "space", down)
+        pieces = chunked(major[:, g * step:(g + 1) * step], nodes)
+        field = lax.all_to_all(pieces, "node", 1, 1, tiled=True).reshape(planes, nodes * step, span)
+        below = lax.ppermute(field[1], "space", up)
+        above = lax.ppermute(field[0], "space", down)
         images.append(stencil(field, below, above, coef))
         fields.append(field)
+    dims = (((0, 2), (0, 2)), ((), ()))
     part = jnp.concatenate([
         jnp.concatenate([
-            lax.dot_general(im, fd, (((1,), (1,)), ((), ())), preferred_element_type=jnp.float32)
+            lax.dot_general(im, fd, dims, preferred_element_type=jnp.float32)
             for fd in fields], axis=1)
         for im in images], axis=0)
     order = (GROUPS, nodes, step)

time: 206 us -> 177 us (0.86)
  local copies, waits for them, and re-layouts: 58.7 us -> 38 us
  waiting for transfers between devices: 50.6 us -> 37.8 us
  other arithmetic: 1.27 us -> 8.16 us
  matrix products: 10.6 us -> 8.04 us
  starting transfers between devices: 21.9 us -> 24.4 us
    reshape x2 -> x0, local copies, waits for them, and re-layouts: 15.5 us -> none  [the longest x1 7.8 us: per_device(): pieces = chunked(snapshots, nodes).reshape(nodes, rows, planes * span)]
    all_to_all x2, waiting for transfers between devices: 50.6 us -> 37.8 us  [per_device(): lax.all_to_all(pieces, 'node', 1, 1, tiled=True)]
    concatenate x6 -> x3, local copies, waits for them, and re-layouts: 14.4 us -> 3.12 us  [chunked(): jnp.concatenate([values[..., q * chunk:(q + 1) * chunk], after, before],...]
    transpose x1 -> x0, local copies, waits for them, and re-layouts: 7.8 us -> none  [chunked(): return jnp.moveaxis(pieces, -2, 0)]
    another operation x0 -> x7, other arithmetic: none -> 5.26 us  [the longest x6 5.23 us: chunked(): return jnp.stack(pieces, axis=-3)]
    unnamed x23 -> x27, local copies, waits for them, and re-layouts: 1.3 us -> 6.43 us
    all_to_all x0 -> x2, local copies, waits for them, and re-layouts: none -> 4.74 us  [per_device(): lax.all_to_all(pieces, 'node', 1, 1, tiled=True)]
    dot_general x4, matrix products: 10.6 us -> 8.04 us  [per_device(): lax.dot_general(im, fd, dims, preferred_element_type=jnp.float32)]
  transfers between devices with their start and end apart: 8 -> 8, of which waited for: 2 -> 2; matrix products, arithmetic and copies ran while one was open for 27% -> 21% of each run, Pallas kernels for 4% -> 5%
where the time goes in v4:
time: 177 us; the launch traced here: 174 us
  blocking collectives  40.6 us (23%)
  local copies, waits for them, and re-layouts  38 us (21%)
  waiting for transfers between devices  37.8 us (21%)
  starting transfers between devices  24.4 us (14%)
  Pallas kernels  16.7 us (9%)
  other arithmetic  8.16 us (5%)
  matrix products  8.04 us (5%)
    all_to_all x2, waiting for transfers between devices, per_device(): lax.all_to_all(pieces, 'node', 1, 1, tiled=True)  37.8 us
    all_to_all x1, blocking collectives, per_device(): out = lax.all_to_all(part, 'space', 0, 0, tiled=True).sum(axis=0)  22.9 us
    all_to_all x1, blocking collectives, per_device(): part = lax.all_to_all(part, 'node', 0, 0, tiled=True).sum(axis=0)  17.7 us
    pallas_call x2, Pallas kernels, stencil(): pl.pallas_call(stencil_kernel, grid=(snaps // ROWS,), in_specs=[pl.BlockS...  16.7 us
    all_to_all x2, starting transfers between devices, per_device(): lax.all_to_all(pieces, 'node', 1, 1, tiled=True)  8.8 us
    dot_general x4, matrix products, per_device(): lax.dot_general(im, fd, dims, preferred_element_type=jnp.float32)  8.04 us
    ppermute x2, starting transfers between devices, per_device(): above = lax.ppermute(field[0], 'space', down)  7.42 us
    unnamed x27, local copies, waits for them, and re-layouts  6.43 us
  transfers between devices with their start and end apart: 8, of which 2 were waited for; matrix products, arithmetic and copies ran while one was open for 21% of the time, Pallas kernels for 5%

profile of v4, /device:TPU:8, one launch (start us, length us, event | category | flops | bytes accessed | tf_op | source)
XLA Modules:
  0.0 174.1 jit_solution(11110725778925516057)
XLA Ops:
  0.0 0.8 fusion.29
  0.8 0.7 slice.228
  1.5 0.8 fusion.28
  2.3 0.7 fusion.20
  3.0 0.1 concatenate.135
  3.1 0.1 maximum_bitcast_fusion.4
  3.2 0.1 convert_bitcast_fusion
  3.3 0.7 slice_reduce_fusion
  3.9 1.9 %collective-permute-start.3 = (bf16[2176]{0:T(1024)(128)(2,1)}, bf16[2176]{0:T(1024)(128)(2,1)}, u32[]{:S(2)}, u32[]{:S(2)}) collective-permute-start(bf16[2176]{0:T(1024)(128)(2,1)} %get-tuple-element.16), channel_id=1, source_target_pairs={{1,0},{2,1},{3,2},{4,3},{5,4},{6,5},{7,6},{8,7},{9,8},{10,9},{11,1... | collective-permute-start | bytes 13064 | tf_op jit(solution)/shard_map/ppermute | solution.py:106
  5.8 2.4 %collective-permute-start.2 = (bf16[2176]{0:T(1024)(128)(2,1)}, bf16[2176]{0:T(1024)(128)(2,1)}, u32[]{:S(2)}, u32[]{:S(2)}) collective-permute-start(bf16[2176]{0:T(1024)(128)(2,1)} %get-tuple-element.17), channel_id=1, source_target_pairs={{0,1},{1,2},{2,3},{3,4},{4,5},{5,6},{6,7},{7,8},{8,9},{9,10},{10,1... | collective-permute-start | bytes 13064 | tf_op jit(solution)/shard_map/ppermute | solution.py:105
  8.2 4.9 %copy.42 = bf16[128,2,8192]{2,0,1:T(8,128)(2,1)S(1)} copy(bf16[128,2,8192]{2,1,0:T(2,128)(2,1)} %param.2) | data formatting | bytes 8388608 | tf_op args[0]
  13.1 0.8 fusion.24
  13.9 1.0 fusion.25
  14.9 1.3 fusion.23
  16.2 1.2 concatenate.131
  17.4 0.1 maximum_bitcast_fusion
  17.5 1.7 pad_maximum_fusion
  19.2 4.3 %all-to-all-start = ((bf16[2,4,64,2176]{3,2,0,1:T(8,128)(2,1)}), bf16[2,4,64,2176]{3,2,0,1:T(8,128)(2,1)S(1)}, u32[]{:S(2)}, u32[]{:S(2)}) async-start(bf16[2,4,64,2176]{3,2,0,1:T(8,128)(2,1)} %pad_maximum_fusion), calls=%async_computation | async-start | bytes 4456448 | tf_op jit(solution)/shard_map/all_to_all | solution.py:114
  23.6 0.6 slice_bitcast_fusion.6
  24.2 0.7 slice_bitcast_fusion.4
  24.9 0.6 fusion.30
  25.5 0.7 slice_bitcast_fusion.2
  26.1 1.9 %pad_bitcast_fusion = bf16[2,1,64,2176]{3,2,0,1:T(8,128)(2,1)} fusion(bf16[2,64,2112]{2,1,0:T(8,128)(2,1)} %get-tuple-element.23), kind=kLoop, calls=%fused_computation.12 | loop fusion | bytes 1097728 | tf_op jit(solution)/shard_map/stack | solution.py:89
  28.1 1.9 %concatenate.151 = bf16[2,64,2176]{2,1,0:T(8,128)(2,1)} concatenate(bf16[2,64,2048]{2,1,0:T(8,128)(2,1)} %get-tuple-element.33, bf16[2,64,64]{2,1,0:T(8,128)(2,1)S(1)} %broadcast.181, bf16[2,64,64]{2,1,0:T(8,128)(2,1)S(1)} %get-tuple-element.27), dimensions={2} | concatenate | bytes 1114112 | tf_op jit(solution)/shard_map/concatenate | solution.py:88
  29.9 0.9 fusion.3
  30.8 0.8 fusion.5
  31.6 0.9 maximum_bitcast_fusion.2
  32.6 1.7 pad_maximum_fusion.1
  34.3 0.1 slice_bitcast_fusion
  34.3 0.1 fusion.7
  34.4 18.2 %all-to-all-done = bf16[2,4,64,2176]{3,2,0,1:T(8,128)(2,1)S(1)} async-done(((bf16[2,4,64,2176]{3,2,0,1:T(8,128)(2,1)}), bf16[2,4,64,2176]{3,2,0,1:T(8,128)(2,1)S(1)}, u32[]{:S(2)}, u32[]{:S(2)}) %all-to-all-start) | async-done | bytes 2228256 | tf_op jit(solution)/shard_map/all_to_all | solution.py:114
  52.6 4.5 %all-to-all-start.1 = ((bf16[2,4,64,2176]{3,2,0,1:T(8,128)(2,1)}), bf16[2,4,64,2176]{3,2,0,1:T(8,128)(2,1)}, u32[]{:S(2)}, u32[]{:S(2)}) async-start(bf16[2,4,64,2176]{3,2,0,1:T(8,128)(2,1)} %pad_maximum_fusion.1), calls=%async_computation.1 | async-start | bytes 4456448 | tf_op jit(solution)/shard_map/all_to_all | solution.py:114
  57.2 0.1 fusion.9
  57.3 0.0 collective-permute-done.3
  57.3 0.7 reshape.334
  58.0 0.7 reshape.333
  58.7 1.6 fusion.26
  60.3 2.0 %collective-permute-start = (bf16[256,2176]{1,0:T(8,128)(2,1)}, bf16[256,2176]{1,0:T(8,128)(2,1)S(1)}, u32[]{:S(2)}, u32[]{:S(2)}) collective-permute-start(bf16[256,2176]{1,0:T(8,128)(2,1)} %bitcast.6), channel_id=1, source_target_pairs={{0,1},{1,2},{2,3},{3,4},{4,5},{5,6},{6,7},{7,8},{8,9},{9,10},{10,1... | collective-permute-start | bytes 3342344 | tf_op jit(solution)/shard_map/ppermute | solution.py:115
  62.2 3.6 %collective-permute-start.1 = (bf16[256,2176]{1,0:T(8,128)(2,1)}, bf16[256,2176]{1,0:T(8,128)(2,1)}, u32[]{:S(2)}, u32[]{:S(2)}) collective-permute-start(bf16[256,2176]{1,0:T(8,128)(2,1)} %bitcast.7), channel_id=1, source_target_pairs={{1,0},{2,1},{3,2},{4,3},{5,4},{6,5},{7,6},{8,7},{9,8},{10,9},{11,1... | collective-permute-start | bytes 3342344 | tf_op jit(solution)/shard_map/ppermute | solution.py:116
  65.9 19.6 %all-to-all-done.1 = bf16[2,4,64,2176]{3,2,0,1:T(8,128)(2,1)} async-done(((bf16[2,4,64,2176]{3,2,0,1:T(8,128)(2,1)}), bf16[2,4,64,2176]{3,2,0,1:T(8,128)(2,1)}, u32[]{:S(2)}, u32[]{:S(2)}) %all-to-all-start.1) | async-done | bytes 2228256 | tf_op jit(solution)/shard_map/all_to_all | solution.py:114
  85.4 3.1 %fusion.27 = (bf16[1,4,64,2176]{3,2,1,0:T(8,128)(2,1)}, bf16[1,4,64,2176]{3,2,1,0:T(8,128)(2,1)}) fusion(bf16[2,4,64,2176]{3,2,0,1:T(8,128)(2,1)} %all-to-all-done.1), kind=kLoop, calls=%fused_computation.70 | loop fusion | bytes 4456448 | tf_op jit(solution)/shard_map/slice | solution.py:116
  88.5 1.9 %collective-permute-start.4 = (bf16[256,2176]{1,0:T(8,128)(2,1)}, bf16[256,2176]{1,0:T(8,128)(2,1)}, u32[]{:S(2)}, u32[]{:S(2)}) collective-permute-start(bf16[256,2176]{1,0:T(8,128)(2,1)} %bitcast.30), channel_id=1, source_target_pairs={{0,1},{1,2},{2,3},{3,4},{4,5},{5,6},{6,7},{7,8},{8,9},{9,10},{10,1... | collective-permute-start | bytes 3342344 | tf_op jit(solution)/shard_map/ppermute | solution.py:115
  90.5 3.8 %collective-permute-start.5 = (bf16[256,2176]{1,0:T(8,128)(2,1)}, bf16[256,2176]{1,0:T(8,128)(2,1)}, u32[]{:S(2)}, u32[]{:S(2)}) collective-permute-start(bf16[256,2176]{1,0:T(8,128)(2,1)} %bitcast.31), channel_id=1, source_target_pairs={{1,0},{2,1},{3,2},{4,3},{5,4},{6,5},{7,6},{8,7},{9,8},{10,9},{11,1... | collective-permute-start | bytes 3342344 | tf_op jit(solution)/shard_map/ppermute | solution.py:116
  94.3 1.6 copy.27
  95.9 3.2 %copy.32 = bf16[2,4,64,2176]{3,2,1,0:T(8,128)(2,1)} copy(bf16[2,4,64,2176]{3,2,0,1:T(8,128)(2,1)} %all-to-all-done.1) | data formatting | bytes 4456448 | tf_op jit(solution)/shard_map/all_to_all | solution.py:114
  99.1 1.0 copy-done.6
  100.1 8.4 %shard_map.28 = bf16[2,256,2176]{2,1,0:T(8,128)(2,1)} custom-call(bf16[2,256,2176]{2,1,0:T(8,128)(2,1)} %bitcast.74, bf16[256,2176]{1,0:T(8,128)(2,1)} %copy-done.6, bf16[256,2176]{1,0:T(8,128)(2,1)} %collective-permute-done.1.above_ref, f32[6,2,2176]{2,1,0:T(2,128)} %copy-done.8), custom_call_target="tpu_custom_call" | custom-call | tf_op jit(solution)/shard_map/pallas_call | solution.py:55
  108.5 2.5 %convolution_bitcast_fusion.3 = f32[256,256]{0,1:T(8,128)S(1)} fusion(bf16[2,256,2176]{2,1,0:T(8,128)(2,1)} %shard_map.28, bf16[2,256,2176]{2,1,0:T(8,128)(2,1)S(1)} %bitcast.75), kind=kOutput, calls=%fused_computation.6 | convolution fusion | flops 570425344 | bytes 4718592 | tf_op jit(solution)/shard_map/dot_general | solution.py:122
  111.1 0.4 copy-done.3
  111.5 1.5 convolution_bitcast_fusion.2
  113.0 8.3 %shard_map.29 = bf16[2,256,2176]{2,1,0:T(8,128)(2,1)} custom-call(bf16[2,256,2176]{2,1,0:T(8,128)(2,1)} %bitcast.77, bf16[256,2176]{1,0:T(8,128)(2,1)} %collective-permute-done.4.below_ref, bf16[256,2176]{1,0:T(8,128)(2,1)} %collective-permute-done.5.above_ref, f32[6,2,2176]{2,1,0:T(2,128)} %copy-done.8), custom_call_target="tpu_custom_call" | custom-call | tf_op jit(solution)/shard_map/pallas_call | solution.py:55
  121.2 3.2 %convolution_bitcast_fusion = f32[256,256]{0,1:T(8,128)S(1)} fusion(bf16[2,256,2176]{2,1,0:T(8,128)(2,1)} %shard_map.29, bf16[2,256,2176]{2,1,0:T(8,128)(2,1)} %bitcast.78), kind=kOutput, calls=%fused_computation.3 | convolution fusion | flops 570425344 | bytes 4718592 | tf_op jit(solution)/shard_map/dot_general | solution.py:122
  124.5 0.8 convolution_bitcast_fusion.1
  125.3 0.2 copy-done.7
  125.4 0.1 maximum_maximum_fusion
  125.6 1.1 reshape.300
  126.6 2.6 %copy.35 = f32[2,4,64,2,4,64]{5,3,4,2,0,1:T(2,128)} copy(f32[2,4,64,2,4,64]{2,1,0,5,4,3:T(4,128)S(1)} %reshape.300) | data formatting | bytes 2097152 | tf_op jit(solution)/shard_map/reshape | solution.py:126
  129.2 3.3 %reshape_reshape.3 = f32[4,128,512]{2,1,0:T(8,128)S(1)} reshape(f32[4,2,64,4,2,64]{5,4,3,2,1,0:T(2,128)} %bitcast.83) | data formatting | bytes 2097152 | tf_op jit(solution)/shard_map/reshape;reshape | solution.py:128
  132.6 17.7 %all_to_all.20 = f32[4,128,512]{2,1,0:T(8,128)S(1)} all-to-all(f32[4,128,512]{2,1,0:T(8,128)S(1)} %reshape_reshape.3), channel_id=1, replica_groups=mesh['node'=4,'space'=64] {'node'}, dimensions={0} | all-to-all | bytes 2097152 | tf_op jit(solution)/shard_map/all_to_all | solution.py:129
  150.2 0.1 reduce_sum.18
  150.3 0.1 copy.36
  150.4 22.9 %all_to_all.21 = f32[64,128,8]{1,2,0:T(8,128)S(1)} all-to-all(f32[64,128,8]{1,2,0:T(8,128)S(1)} %bitcast.86), channel_id=1, replica_groups=mesh['node'=4,'space'=64] {'space'}, dimensions={0} | all-to-all | bytes 524288 | tf_op jit(solution)/shard_map/all_to_all | solution.py:131
  173.4 0.1 reduce_sum.19
  173.5 0.6 broadcast_multiply_fusion
  (35 shorter events, 0.2 us)
Async XLA Ops:
  3.9 53.3 %collective-permute-start.3 = (bf16[2176]{0:T(1024)(128)(2,1)}, bf16[2176]{0:T(1024)(128)(2,1)}, u32[]{:S(2)}, u32[]{:S(2)}) collective-permute-start(bf16[2176]{0:T(1024)(128)(2,1)} %get-tuple-element.16), channel_id=1, source_target_pairs={{1,0},{2,1},{3,2},{4,3},{5,4},{6,5},{7,6},{8,7},{9,8},{10,9},{11,1... | collective-permute-start | bytes 13064 | tf_op jit(solution)/shard_map/ppermute | solution.py:106
  5.8 52.1 %collective-permute-start.2 = (bf16[2176]{0:T(1024)(128)(2,1)}, bf16[2176]{0:T(1024)(128)(2,1)}, u32[]{:S(2)}, u32[]{:S(2)}) collective-permute-start(bf16[2176]{0:T(1024)(128)(2,1)} %get-tuple-element.17), channel_id=1, source_target_pairs={{0,1},{1,2},{2,3},{3,4},{4,5},{5,6},{6,7},{7,8},{8,9},{9,10},{10,1... | collective-permute-start | bytes 13064 | tf_op jit(solution)/shard_map/ppermute | solution.py:105
  19.2 33.4 %all-to-all-start = ((bf16[2,4,64,2176]{3,2,0,1:T(8,128)(2,1)}), bf16[2,4,64,2176]{3,2,0,1:T(8,128)(2,1)S(1)}, u32[]{:S(2)}, u32[]{:S(2)}) async-start(bf16[2,4,64,2176]{3,2,0,1:T(8,128)(2,1)} %pad_maximum_fusion), calls=%async_computation | async-start | bytes 4456448 | tf_op jit(solution)/shard_map/all_to_all | solution.py:114
  29.9 2.6 %copy-start.4 = (bf16[2,1,64,2176]{3,2,0,1:T(8,128)(2,1)S(1)}, bf16[2,1,64,2176]{3,2,0,1:T(8,128)(2,1)}, u32[]{:S(2)}) copy-start(bf16[2,1,64,2176]{3,2,0,1:T(8,128)(2,1)} %pad_bitcast_fusion) | copy-start | bytes 1671172
  29.9 2.6 %copy-start.5 = (bf16[2,64,2176]{2,1,0:T(8,128)(2,1)S(1)}, bf16[2,64,2176]{2,1,0:T(8,128)(2,1)}, u32[]{:S(2)}) copy-start(bf16[2,64,2176]{2,1,0:T(8,128)(2,1)} %concatenate.151) | copy-start | bytes 1671172
  32.6 1.8 %copy-start.12 = (f32[1,2,64]{2,1,0:T(2,128)S(1)}, f32[1,2,64]{2,1,0:T(2,128)}, u32[]{:S(2)}) copy-start(f32[1,2,64]{2,1,0:T(2,128)} %get-tuple-element.44) | copy-start | bytes 1540
  34.4 22.7 %copy-start.11 = (f32[1,2,64]{2,1,0:T(2,128)S(1)}, f32[1,2,64]{2,1,0:T(2,128)}, u32[]{:S(2)}) copy-start(f32[1,2,64]{2,1,0:T(2,128)} %get-tuple-element.43) | copy-start | bytes 1540
  34.4 24.2 %copy-start.10 = (f32[1,1,2176]{2,1,0:T(1,128)S(1)}, f32[1,1,2176]{2,1,0:T(1,128)}, u32[]{:S(2)}) copy-start(f32[1,1,2176]{2,1,0:T(1,128)} %get-tuple-element.52) | copy-start | bytes 26116
  52.6 32.8 %all-to-all-start.1 = ((bf16[2,4,64,2176]{3,2,0,1:T(8,128)(2,1)}), bf16[2,4,64,2176]{3,2,0,1:T(8,128)(2,1)}, u32[]{:S(2)}, u32[]{:S(2)}) async-start(bf16[2,4,64,2176]{3,2,0,1:T(8,128)(2,1)} %pad_maximum_fusion.1), calls=%async_computation.1 | async-start | bytes 4456448 | tf_op jit(solution)/shard_map/all_to_all | solution.py:114
  60.3 38.8 %collective-permute-start = (bf16[256,2176]{1,0:T(8,128)(2,1)}, bf16[256,2176]{1,0:T(8,128)(2,1)S(1)}, u32[]{:S(2)}, u32[]{:S(2)}) collective-permute-start(bf16[256,2176]{1,0:T(8,128)(2,1)} %bitcast.6), channel_id=1, source_target_pairs={{0,1},{1,2},{2,3},{3,4},{4,5},{5,6},{6,7},{7,8},{8,9},{9,10},{10,1... | collective-permute-start | bytes 3342344 | tf_op jit(solution)/shard_map/ppermute | solution.py:115
  62.2 32.0 %copy-start.9 = (f32[1,1,2176]{2,1,0:T(1,128)S(1)}, f32[1,1,2176]{2,1,0:T(1,128)}, u32[]{:S(2)}) copy-start(f32[1,1,2176]{2,1,0:T(1,128)} %get-tuple-element.51) | copy-start | bytes 26116
  62.2 36.8 %collective-permute-start.1 = (bf16[256,2176]{1,0:T(8,128)(2,1)}, bf16[256,2176]{1,0:T(8,128)(2,1)}, u32[]{:S(2)}, u32[]{:S(2)}) collective-permute-start(bf16[256,2176]{1,0:T(8,128)(2,1)} %bitcast.7), channel_id=1, source_target_pairs={{1,0},{2,1},{3,2},{4,3},{5,4},{6,5},{7,6},{8,7},{9,8},{10,9},{11,1... | collective-permute-start | bytes 3342344 | tf_op jit(solution)/shard_map/ppermute | solution.py:116
  88.5 24.4 %collective-permute-start.4 = (bf16[256,2176]{1,0:T(8,128)(2,1)}, bf16[256,2176]{1,0:T(8,128)(2,1)}, u32[]{:S(2)}, u32[]{:S(2)}) collective-permute-start(bf16[256,2176]{1,0:T(8,128)(2,1)} %bitcast.30), channel_id=1, source_target_pairs={{0,1},{1,2},{2,3},{3,4},{4,5},{5,6},{6,7},{7,8},{8,9},{9,10},{10,1... | collective-permute-start | bytes 3342344 | tf_op jit(solution)/shard_map/ppermute | solution.py:115
  90.5 22.5 %collective-permute-start.5 = (bf16[256,2176]{1,0:T(8,128)(2,1)}, bf16[256,2176]{1,0:T(8,128)(2,1)}, u32[]{:S(2)}, u32[]{:S(2)}) collective-permute-start(bf16[256,2176]{1,0:T(8,128)(2,1)} %bitcast.31), channel_id=1, source_target_pairs={{1,0},{2,1},{3,2},{4,3},{5,4},{6,5},{7,6},{8,7},{9,8},{10,9},{11,1... | collective-permute-start | bytes 3342344 | tf_op jit(solution)/shard_map/ppermute | solution.py:116
  94.3 4.8 %copy-start.8 = (f32[6,2,2176]{2,1,0:T(2,128)}, f32[6,2,2176]{2,1,0:T(2,128)S(1)}, u32[]{:S(2)}) copy-start(f32[6,2,2176]{2,1,0:T(2,128)S(1)} %fusion.1.coef_ref) | copy-start | bytes 313348
  99.1 1.0 copy-start.6
  100.1 8.4 %copy-start = (bf16[2,4,64,2176]{3,2,1,0:T(8,128)(2,1)S(1)}, bf16[2,4,64,2176]{3,2,1,0:T(8,128)(2,1)}, u32[]{:S(2)}) copy-start(bf16[2,4,64,2176]{3,2,1,0:T(8,128)(2,1)} %copy.27) | copy-start | bytes 6684676
  108.5 2.6 %copy-start.1 = (bf16[2,4,64,2176]{3,2,1,0:T(8,128)(2,1)S(1)}, bf16[2,4,64,2176]{3,2,1,0:T(8,128)(2,1)}, u32[]{:S(2)}) copy-start(bf16[2,4,64,2176]{3,2,1,0:T(8,128)(2,1)} %copy.32) | copy-start | bytes 6684676
  108.5 3.0 %copy-start.3 = (bf16[2,256,2176]{2,1,0:T(8,128)(2,1)S(1)}, bf16[2,256,2176]{2,1,0:T(8,128)(2,1)}, u32[]{:S(2)}) copy-start(bf16[2,256,2176]{2,1,0:T(8,128)(2,1)} %shard_map.28) | copy-start | bytes 6684676
  121.2 3.2 %copy-start.2 = (bf16[2,256,2176]{2,1,0:T(8,128)(2,1)S(1)}, bf16[2,256,2176]{2,1,0:T(8,128)(2,1)}, u32[]{:S(2)}) copy-start(bf16[2,256,2176]{2,1,0:T(8,128)(2,1)} %shard_map.29) | copy-start | bytes 6684676
  124.5 1.0 copy-start.7

commit v5 on v4

--- a/solution.py
+++ b/solution.py
@@ -5,12 +5,13 @@
 from jax import lax
 from jax.experimental import pallas as pl
 from jax.experimental.pallas import tpu as pltpu
-from jax.sharding import PartitionSpec as P
+from jax.sharding import Mesh, PartitionSpec as P
 
 NY = 128
 NZ = 64
 ROWS = 32
 GROUPS = 2
+SPACE = ("z", "y", "core")
 
 
 def ahead(values, offset):
@@ -92,7 +93,8 @@
 def per_device(snapshots, kappa):
     rows, planes, width = snapshots.shape
     nodes = lax.axis_size("node")
-    spaces = lax.axis_size("space")
+    sizes = [lax.axis_size(a) for a in SPACE]
+    spaces = math.prod(sizes)
     me = lax.axis_index("node")
     chunk = width // nodes
     span = chunk + 2 * NZ
@@ -102,8 +104,8 @@
     down = [(j, i) for i, j in up]
 
     kap_chunk = jnp.take(chunked(kappa[:, None], nodes)[:, :, 0], me, axis=1)
-    kap_below = lax.ppermute(kap_chunk[1], "space", up)
-    kap_above = lax.ppermute(kap_chunk[0], "space", down)
+    kap_below = lax.ppermute(kap_chunk[1], SPACE, up)
+    kap_above = lax.ppermute(kap_chunk[0], SPACE, down)
     coef = weights(kap_chunk, kap_below, kap_above)
 
     major = jnp.transpose(snapshots, (1, 0, 2))
@@ -112,8 +114,8 @@
     for g in range(GROUPS):
         pieces = chunked(major[:, g * step:(g + 1) * step], nodes)
         field = lax.all_to_all(pieces, "node", 1, 1, tiled=True).reshape(planes, nodes * step, span)
-        below = lax.ppermute(field[1], "space", up)
-        above = lax.ppermute(field[0], "space", down)
+        below = lax.ppermute(field[1], SPACE, up)
+        above = lax.ppermute(field[0], SPACE, down)
         images.append(stencil(field, below, above, coef))
         fields.append(field)
     dims = (((0, 2), (0, 2)), ((), ()))
@@ -122,20 +124,27 @@
             lax.dot_general(im, fd, dims, preferred_element_type=jnp.float32)
             for fd in fields], axis=1)
         for im in images], axis=0)
-    order = (GROUPS, nodes, step)
-    part = part.reshape(order + order).transpose(1, 0, 2, 4, 3, 5).reshape(snaps, snaps)
-
-    part = part.reshape(nodes, rows, snaps)
-    part = lax.all_to_all(part, "node", 0, 0, tiled=True).sum(axis=0)
-    part = part.reshape(rows, spaces, snaps // spaces).transpose(1, 0, 2)
-    out = lax.all_to_all(part, "space", 0, 0, tiled=True).sum(axis=0)
+    part = part.reshape(GROUPS, nodes, step, snaps)
+    total = jnp.take(part, me, axis=1)
+    for d in range(1, nodes):
+        blk = jnp.take(part, (me + d) % nodes, axis=1)
+        total = total + lax.ppermute(blk, "node", [(i, (i + d) % nodes) for i in range(nodes)])
+    total = total.reshape(rows, GROUPS, nodes, step).transpose(0, 2, 1, 3)
+    total = total.reshape((rows,) + tuple(sizes) + (snaps // spaces,))
+    for axis in reversed(range(len(SPACE))):
+        total = jnp.moveaxis(total, axis + 1, 0)
+        total = lax.all_to_all(total, SPACE[axis], 0, 0, tiled=True).sum(axis=0)
+    out = total
 
     scale = jnp.float32(1.0 / math.sqrt(planes * spaces * NY * NZ))
     return out * scale
 
 
 def solution(mesh):
-    placed = (P("node", "space", None), P("space", None))
+    node, space = mesh.devices.shape
+    cores = 2
+    fine = Mesh(mesh.devices.reshape(node, space // (4 * cores), 4, cores), ("node",) + SPACE)
+    placed = (P("node", SPACE, None), P(SPACE, None))
     return jax.shard_map(
-        per_device, mesh=mesh, in_specs=placed, out_specs=P("node", "space"), check_vma=False
+        per_device, mesh=fine, in_specs=placed, out_specs=P("node", SPACE), check_vma=False
     )

time: 177 us -> 171 us (0.966)
  blocking collectives: 40.6 us -> 28.6 us
  waiting for transfers between devices: 37.8 us -> 47.5 us
  local copies, waits for them, and re-layouts: 38 us -> 32.1 us
  starting transfers between devices: 24.4 us -> 29.1 us
    all_to_all x2 -> x3, blocking collectives: 40.6 us -> 28.6 us  [per_device(): total = lax.all_to_all(total, SPACE[axis], 0, 0, tiled=True).sum(axis=0)]
    ppermute x6 -> x9, waiting for transfers between devices: 0.02 us -> 11.6 us  [the longest x3 11.6 us: per_device(): lax.ppermute(blk, 'node', [(i, (i + d) % nodes) for i in range(nodes)])]
    ppermute x6 -> x9, starting transfers between devices: 15.6 us -> 20.1 us  [the longest x2 7.29 us: per_device(): above = lax.ppermute(field[0], SPACE, down)]
    reshape x2 -> x1, local copies, waits for them, and re-layouts: 3.68 us -> 0.28 us  [per_device(): total = total.reshape(rows, GROUPS, nodes, step).transpose(0, 2, 1, 3)]
    another operation x2 -> x1, local copies, waits for them, and re-layouts: 3.34 us -> 0.01 us  [the longest x1 3.33 us: per_device(): part = part.reshape(nodes, rows, snaps)]
    all_to_all x2, waiting for transfers between devices: 37.8 us -> 36 us  [per_device(): lax.all_to_all(pieces, 'node', 1, 1, tiled=True)]
    unnamed x27 -> x29, local copies, waits for them, and re-layouts: 6.43 us -> 6.68 us
  transfers between devices with their start and end apart: 8 -> 11, of which waited for: 2 -> 4; matrix products, arithmetic and copies ran while one was open for 21% -> 21% of each run, Pallas kernels for 5% -> 5%
where the time goes in v5:
time: 171 us; the launch traced here: 168 us
  waiting for transfers between devices  47.5 us (28%)
  local copies, waits for them, and re-layouts  32.1 us (19%)
  starting transfers between devices  29.1 us (17%)
  blocking collectives  28.6 us (17%)
  Pallas kernels  16.6 us (10%)
  other arithmetic  7.5 us (4%)
  matrix products  6.63 us (4%)
    all_to_all x2, waiting for transfers between devices, per_device(): lax.all_to_all(pieces, 'node', 1, 1, tiled=True)  36 us
    all_to_all x3, blocking collectives, per_device(): total = lax.all_to_all(total, SPACE[axis], 0, 0, tiled=True).sum(axis=0)  28.6 us
    pallas_call x2, Pallas kernels, stencil(): pl.pallas_call(stencil_kernel, grid=(snaps // ROWS,), in_specs=[pl.BlockS...  16.6 us
    ppermute x3, waiting for transfers between devices, per_device(): lax.ppermute(blk, 'node', [(i, (i + d) % nodes) for i in range(nodes)])  11.6 us
    all_to_all x2, starting transfers between devices, per_device(): lax.all_to_all(pieces, 'node', 1, 1, tiled=True)  8.91 us
    ppermute x2, starting transfers between devices, per_device(): above = lax.ppermute(field[0], SPACE, down)  7.29 us
    unnamed x29, local copies, waits for them, and re-layouts  6.68 us
    dot_general x4, matrix products, per_device(): lax.dot_general(im, fd, dims, preferred_element_type=jnp.float32)  6.63 us
  transfers between devices with their start and end apart: 11, of which 4 were waited for; matrix products, arithmetic and copies ran while one was open for 21% of the time, Pallas kernels for 5%

profile of v5, /device:TPU:8, one launch (start us, length us, event | category | flops | bytes accessed | tf_op | source)
XLA Modules:
  0.0 168.5 jit_solution(14735000968838036542)
XLA Ops:
  0.0 0.8 fusion.35
  0.8 0.8 fusion.34
  1.6 0.7 slice.239
  2.3 0.7 fusion.26
  3.0 0.1 concatenate.135
  3.3 0.7 slice_reduce_fusion
  3.9 1.9 %collective-permute-start.2 = (bf16[2176]{0:T(1024)(128)(2,1)}, bf16[2176]{0:T(1024)(128)(2,1)}, u32[]{:S(2)}, u32[]{:S(2)}) collective-permute-start(bf16[2176]{0:T(1024)(128)(2,1)} %get-tuple-element.29), channel_id=1, source_target_pairs={{0,1},{1,2},{2,3},{3,4},{4,5},{5,6},{6,7},{7,8},{8,9},{9,10},{10,1... | collective-permute-start | bytes 13064 | tf_op jit(solution)/shard_map/ppermute | solution.py:107
  5.8 3.6 %collective-permute-start.3 = (bf16[2176]{0:T(1024)(128)(2,1)}, bf16[2176]{0:T(1024)(128)(2,1)}, u32[]{:S(2)}, u32[]{:S(2)}) collective-permute-start(bf16[2176]{0:T(1024)(128)(2,1)} %get-tuple-element.28), channel_id=1, source_target_pairs={{1,0},{2,1},{3,2},{4,3},{5,4},{6,5},{7,6},{8,7},{9,8},{10,9},{11,1... | collective-permute-start | bytes 13064 | tf_op jit(solution)/shard_map/ppermute | solution.py:108
  9.5 4.9 %copy.65 = bf16[128,2,8192]{2,0,1:T(8,128)(2,1)S(1)} copy(bf16[128,2,8192]{2,1,0:T(2,128)(2,1)} %param.4) | data formatting | bytes 8388608 | tf_op args[0]
  14.4 1.3 fusion.29
  15.6 0.7 fusion.30
  16.4 1.1 fusion.31
  17.5 1.2 concatenate.131
  18.6 0.1 maximum_bitcast_fusion
  18.8 1.7 %pad_maximum_fusion = bf16[2,4,64,2176]{3,2,0,1:T(8,128)(2,1)} fusion(bf16[2,1,64,2176]{3,2,0,1:T(8,128)(2,1)S(1)} %bitcast.120, bf16[2,1,64,2176]{3,2,0,1:T(8,128)(2,1)S(1)} %get-tuple-element.68, bf16[2,1,64,2176]{3,2,0,1:T(8,128)(2,1)S(1)} %get-tuple-element.67, bf16[2,1,64,2176]{3,2,0,1:T(8,128)(2,1)S(1)} %pad_bitcast_fusion.1), kind=kLoop, calls=%fused_computation.1 | loop fusion | flops 3342336 | bytes 4456448 | tf_op jit(solution)/shard_map/stack | solution.py:90
  20.5 4.4 %all-to-all-start = ((bf16[2,4,64,2176]{3,2,0,1:T(8,128)(2,1)}), bf16[2,4,64,2176]{3,2,0,1:T(8,128)(2,1)S(1)}, u32[]{:S(2)}, u32[]{:S(2)}) async-start(bf16[2,4,64,2176]{3,2,0,1:T(8,128)(2,1)} %pad_maximum_fusion), calls=%async_computation | async-start | bytes 4456448 | tf_op jit(solution)/shard_map/all_to_all | solution.py:116
  24.9 0.7 slice_bitcast_fusion.2
  25.6 0.6 slice_bitcast_fusion.6
  26.3 0.7 slice_bitcast_fusion.4
  26.9 0.6 fusion.36
  27.6 1.9 %pad_bitcast_fusion = bf16[2,1,64,2176]{3,2,0,1:T(8,128)(2,1)} fusion(bf16[2,64,2112]{2,1,0:T(8,128)(2,1)} %get-tuple-element.35), kind=kLoop, calls=%fused_computation.12 | loop fusion | bytes 1097728 | tf_op jit(solution)/shard_map/stack | solution.py:90
  29.5 1.8 %concatenate.151 = bf16[2,64,2176]{2,1,0:T(8,128)(2,1)} concatenate(bf16[2,64,2048]{2,1,0:T(8,128)(2,1)} %get-tuple-element.45, bf16[2,64,64]{2,1,0:T(8,128)(2,1)S(1)} %broadcast.184, bf16[2,64,64]{2,1,0:T(8,128)(2,1)S(1)} %copy-done.9), dimensions={2} | concatenate | bytes 1114112 | tf_op jit(solution)/shard_map/concatenate | solution.py:89
  31.3 0.9 fusion.9
  32.2 0.8 fusion.11
  33.1 0.1 maximum_bitcast_fusion.2
  33.2 1.7 %pad_maximum_fusion.1 = bf16[2,4,64,2176]{3,2,0,1:T(8,128)(2,1)} fusion(bf16[2,1,64,2176]{3,2,0,1:T(8,128)(2,1)S(1)} %bitcast.119, bf16[2,1,64,2176]{3,2,0,1:T(8,128)(2,1)S(1)} %get-tuple-element.70, bf16[2,1,64,2176]{3,2,0,1:T(8,128)(2,1)S(1)} %get-tuple-element.69, bf16[2,1,64,2176]{3,2,0,1:T(8,128)(2,1)S(1)} %copy-done.5), kind=kLoop, calls=%fused_computation.2 | loop fusion | flops 3342336 | bytes 4456448 | tf_op jit(solution)/shard_map/stack | solution.py:90
  35.0 0.1 fusion.13
  35.1 17.7 %all-to-all-done = bf16[2,4,64,2176]{3,2,0,1:T(8,128)(2,1)S(1)} async-done(((bf16[2,4,64,2176]{3,2,0,1:T(8,128)(2,1)}), bf16[2,4,64,2176]{3,2,0,1:T(8,128)(2,1)S(1)}, u32[]{:S(2)}, u32[]{:S(2)}) %all-to-all-start) | async-done | bytes 2228256 | tf_op jit(solution)/shard_map/all_to_all | solution.py:116
  52.8 4.5 %all-to-all-start.1 = ((bf16[2,4,64,2176]{3,2,0,1:T(8,128)(2,1)}), bf16[2,4,64,2176]{3,2,0,1:T(8,128)(2,1)}, u32[]{:S(2)}, u32[]{:S(2)}) async-start(bf16[2,4,64,2176]{3,2,0,1:T(8,128)(2,1)} %pad_maximum_fusion.1), calls=%async_computation.1 | async-start | bytes 4456448 | tf_op jit(solution)/shard_map/all_to_all | solution.py:116
  57.3 0.1 fusion.15
  57.5 0.7 reshape.403
  58.2 0.7 reshape.404
  58.9 1.5 fusion.32
  60.5 1.9 %collective-permute-start = (bf16[256,2176]{1,0:T(8,128)(2,1)}, bf16[256,2176]{1,0:T(8,128)(2,1)S(1)}, u32[]{:S(2)}, u32[]{:S(2)}) collective-permute-start(bf16[256,2176]{1,0:T(8,128)(2,1)} %bitcast.6), channel_id=1, source_target_pairs={{0,1},{1,2},{2,3},{3,4},{4,5},{5,6},{6,7},{7,8},{8,9},{9,10},{10,1... | collective-permute-start | bytes 3342344 | tf_op jit(solution)/shard_map/ppermute | solution.py:117
  62.4 3.6 %collective-permute-start.1 = (bf16[256,2176]{1,0:T(8,128)(2,1)}, bf16[256,2176]{1,0:T(8,128)(2,1)}, u32[]{:S(2)}, u32[]{:S(2)}) collective-permute-start(bf16[256,2176]{1,0:T(8,128)(2,1)} %bitcast.7), channel_id=1, source_target_pairs={{1,0},{2,1},{3,2},{4,3},{5,4},{6,5},{7,6},{8,7},{9,8},{10,9},{11,1... | collective-permute-start | bytes 3342344 | tf_op jit(solution)/shard_map/ppermute | solution.py:118
  66.0 18.3 %all-to-all-done.1 = bf16[2,4,64,2176]{3,2,0,1:T(8,128)(2,1)} async-done(((bf16[2,4,64,2176]{3,2,0,1:T(8,128)(2,1)}), bf16[2,4,64,2176]{3,2,0,1:T(8,128)(2,1)}, u32[]{:S(2)}, u32[]{:S(2)}) %all-to-all-start.1) | async-done | bytes 2228256 | tf_op jit(solution)/shard_map/all_to_all | solution.py:116
  84.3 3.1 %fusion.33 = (bf16[1,4,64,2176]{3,2,1,0:T(8,128)(2,1)}, bf16[1,4,64,2176]{3,2,1,0:T(8,128)(2,1)}) fusion(bf16[2,4,64,2176]{3,2,0,1:T(8,128)(2,1)} %all-to-all-done.1), kind=kLoop, calls=%fused_computation.80 | loop fusion | bytes 4456448 | tf_op jit(solution)/shard_map/slice | solution.py:118
  87.4 1.9 %collective-permute-start.4 = (bf16[256,2176]{1,0:T(8,128)(2,1)}, bf16[256,2176]{1,0:T(8,128)(2,1)}, u32[]{:S(2)}, u32[]{:S(2)}) collective-permute-start(bf16[256,2176]{1,0:T(8,128)(2,1)} %bitcast.30), channel_id=1, source_target_pairs={{0,1},{1,2},{2,3},{3,4},{4,5},{5,6},{6,7},{7,8},{8,9},{9,10},{10,1... | collective-permute-start | bytes 3342344 | tf_op jit(solution)/shard_map/ppermute | solution.py:117
  89.3 3.6 %collective-permute-start.5 = (bf16[256,2176]{1,0:T(8,128)(2,1)}, bf16[256,2176]{1,0:T(8,128)(2,1)}, u32[]{:S(2)}, u32[]{:S(2)}) collective-permute-start(bf16[256,2176]{1,0:T(8,128)(2,1)} %bitcast.31), channel_id=1, source_target_pairs={{1,0},{2,1},{3,2},{4,3},{5,4},{6,5},{7,6},{8,7},{9,8},{10,9},{11,1... | collective-permute-start | bytes 3342344 | tf_op jit(solution)/shard_map/ppermute | solution.py:118
  93.0 1.6 copy.40
  94.6 3.2 %copy.45 = bf16[2,4,64,2176]{3,2,1,0:T(8,128)(2,1)} copy(bf16[2,4,64,2176]{3,2,0,1:T(8,128)(2,1)} %all-to-all-done.1) | data formatting | bytes 4456448 | tf_op jit(solution)/shard_map/all_to_all | solution.py:116
  97.8 1.0 copy-done.7
  98.8 8.4 %shard_map.28 = bf16[2,256,2176]{2,1,0:T(8,128)(2,1)} custom-call(bf16[2,256,2176]{2,1,0:T(8,128)(2,1)} %bitcast.107, bf16[256,2176]{1,0:T(8,128)(2,1)} %copy-done.7, bf16[256,2176]{1,0:T(8,128)(2,1)} %collective-permute-done.1.above_ref, f32[6,2,2176]{2,1,0:T(2,128)} %copy-done.8), custom_call_target="tpu_custom_call" | custom-call | tf_op jit(solution)/shard_map/pallas_call | solution.py:56
  107.2 2.5 %convolution_bitcast_fusion.3 = f32[256,256]{0,1:T(8,128)S(1)} fusion(bf16[2,256,2176]{2,1,0:T(8,128)(2,1)} %shard_map.28, bf16[2,256,2176]{2,1,0:T(8,128)(2,1)S(1)} %bitcast.108), kind=kOutput, calls=%fused_computation.6 | convolution fusion | flops 570425344 | bytes 4718592 | tf_op jit(solution)/shard_map/dot_general | solution.py:124
  109.7 0.4 copy-done.4
  110.1 0.8 convolution_bitcast_fusion.2
  110.9 8.3 %shard_map.29 = bf16[2,256,2176]{2,1,0:T(8,128)(2,1)} custom-call(bf16[2,256,2176]{2,1,0:T(8,128)(2,1)} %bitcast.110, bf16[256,2176]{1,0:T(8,128)(2,1)} %collective-permute-done.4.below_ref, bf16[256,2176]{1,0:T(8,128)(2,1)} %collective-permute-done.5.above_ref, f32[6,2,2176]{2,1,0:T(2,128)} %copy-done.8), custom_call_target="tpu_custom_call" | custom-call | tf_op jit(solution)/shard_map/pallas_call | solution.py:56
  119.2 2.5 %convolution_bitcast_fusion.1 = f32[256,256]{0,1:T(8,128)S(1)} fusion(bf16[2,256,2176]{2,1,0:T(8,128)(2,1)} %shard_map.29, bf16[2,256,2176]{2,1,0:T(8,128)(2,1)S(1)} %bitcast.109), kind=kOutput, calls=%fused_computation.4 | convolution fusion | flops 570425344 | bytes 4718592 | tf_op jit(solution)/shard_map/dot_general | solution.py:124
  121.8 0.4 copy-done.3
  122.2 0.8 convolution_bitcast_fusion
  122.9 0.1 maximum_maximum_fusion
  123.1 0.3 copy.48
  123.5 0.6 collective-permute-start.6
  124.1 2.1 %collective-permute-start.7 = (f32[2,64,512]{2,1,0:T(8,128)S(1)}, f32[2,64,512]{2,1,0:T(8,128)S(1)}, u32[]{:S(2)}, u32[]{:S(2)}) collective-permute-start(f32[2,64,512]{2,1,0:T(8,128)S(1)} %get-tuple-element.51), channel_id=1, source_target_pairs={{0,128},{64,192},{128,0},{192,64},{1,129},{65,193},{129,1},{193,65... | collective-permute-start | bytes 786440 | tf_op jit(solution)/shard_map/ppermute | solution.py:131
  126.2 0.8 collective-permute-start.8
  127.0 10.9 %collective-permute-done.6 = f32[2,64,512]{2,1,0:T(8,128)S(1)} collective-permute-done((f32[2,64,512]{2,1,0:T(8,128)S(1)}, f32[2,64,512]{2,1,0:T(8,128)S(1)}, u32[]{:S(2)}, u32[]{:S(2)}) %collective-permute-start.6) | collective-permute-done | bytes 262176 | tf_op jit(solution)/shard_map/ppermute | solution.py:131
  137.9 0.6 collective-permute-done.8
  138.6 0.1 fusion.5
  138.7 0.3 reshape.305
  138.9 0.2 copy.52
  139.2 3.9 %all_to_all.25 = f32[2,128,8,4,8]{1,4,3,2,0:T(8,128)S(1)} all-to-all(f32[2,128,8,4,8]{1,4,3,2,0:T(8,128)S(1)} %copy.53), channel_id=1, replica_groups=mesh['node'=4,'z'=8,'y'=4,'core'=2] {'core'}, dimensions={0} | all-to-all | bytes 524288 | tf_op jit(solution)/shard_map/all_to_all | solution.py:136
  143.2 9.6 %all_to_all.26 = f32[4,128,8,8]{1,3,2,0:T(8,128)S(1)} all-to-all(f32[4,128,8,8]{1,3,2,0:T(8,128)S(1)} %copy.55), channel_id=1, replica_groups=mesh['node'=4,'z'=8,'y'=4,'core'=2] {'y'}, dimensions={0} | all-to-all | bytes 262144 | tf_op jit(solution)/shard_map/all_to_all | solution.py:136
  152.7 15.1 %all_to_all.27 = f32[8,128,8]{1,2,0:T(8,128)S(1)} all-to-all(f32[8,128,8]{1,2,0:T(8,128)S(1)} %bitcast.124), channel_id=1, replica_groups=mesh['node'=4,'z'=8,'y'=4,'core'=2] {'z'}, dimensions={0} | all-to-all | bytes 65536 | tf_op jit(solution)/shard_map/all_to_all | solution.py:136
  167.9 0.6 broadcast_multiply_fusion
  (49 shorter events, 0.6 us)
Async XLA Ops:
  3.9 53.5 %collective-permute-start.2 = (bf16[2176]{0:T(1024)(128)(2,1)}, bf16[2176]{0:T(1024)(128)(2,1)}, u32[]{:S(2)}, u32[]{:S(2)}) collective-permute-start(bf16[2176]{0:T(1024)(128)(2,1)} %get-tuple-element.29), channel_id=1, source_target_pairs={{0,1},{1,2},{2,3},{3,4},{4,5},{5,6},{6,7},{7,8},{8,9},{9,10},{10,1... | collective-permute-start | bytes 13064 | tf_op jit(solution)/shard_map/ppermute | solution.py:107
  5.8 52.3 %collective-permute-start.3 = (bf16[2176]{0:T(1024)(128)(2,1)}, bf16[2176]{0:T(1024)(128)(2,1)}, u32[]{:S(2)}, u32[]{:S(2)}) collective-permute-start(bf16[2176]{0:T(1024)(128)(2,1)} %get-tuple-element.28), channel_id=1, source_target_pairs={{1,0},{2,1},{3,2},{4,3},{5,4},{6,5},{7,6},{8,7},{9,8},{10,9},{11,1... | collective-permute-start | bytes 13064 | tf_op jit(solution)/shard_map/ppermute | solution.py:108
  20.5 9.0 %copy-start.9 = (bf16[2,64,64]{2,1,0:T(8,128)(2,1)S(1)}, bf16[2,64,64]{2,1,0:T(8,128)(2,1)}, u32[]{:S(2)}) copy-start(bf16[2,64,64]{2,1,0:T(8,128)(2,1)} %get-tuple-element.39) | copy-start | bytes 49156
  20.5 32.3 %all-to-all-start = ((bf16[2,4,64,2176]{3,2,0,1:T(8,128)(2,1)}), bf16[2,4,64,2176]{3,2,0,1:T(8,128)(2,1)S(1)}, u32[]{:S(2)}, u32[]{:S(2)}) async-start(bf16[2,4,64,2176]{3,2,0,1:T(8,128)(2,1)} %pad_maximum_fusion), calls=%async_computation | async-start | bytes 4456448 | tf_op jit(solution)/shard_map/all_to_all | solution.py:116
  31.3 1.9 %copy-start.5 = (bf16[2,1,64,2176]{3,2,0,1:T(8,128)(2,1)S(1)}, bf16[2,1,64,2176]{3,2,0,1:T(8,128)(2,1)}, u32[]{:S(2)}) copy-start(bf16[2,1,64,2176]{3,2,0,1:T(8,128)(2,1)} %pad_bitcast_fusion) | copy-start | bytes 1671172
  31.3 1.9 %copy-start.6 = (bf16[2,64,2176]{2,1,0:T(8,128)(2,1)S(1)}, bf16[2,64,2176]{2,1,0:T(8,128)(2,1)}, u32[]{:S(2)}) copy-start(bf16[2,64,2176]{2,1,0:T(8,128)(2,1)} %concatenate.151) | copy-start | bytes 1671172
  33.2 1.8 %copy-start.13 = (f32[1,2,64]{2,1,0:T(2,128)S(1)}, f32[1,2,64]{2,1,0:T(2,128)}, u32[]{:S(2)}) copy-start(f32[1,2,64]{2,1,0:T(2,128)} %get-tuple-element.58) | copy-start | bytes 1540
  35.1 22.2 %copy-start.12 = (f32[1,2,64]{2,1,0:T(2,128)S(1)}, f32[1,2,64]{2,1,0:T(2,128)}, u32[]{:S(2)}) copy-start(f32[1,2,64]{2,1,0:T(2,128)} %get-tuple-element.57) | copy-start | bytes 1540
  35.1 23.8 %copy-start.11 = (f32[1,1,2176]{2,1,0:T(1,128)S(1)}, f32[1,1,2176]{2,1,0:T(1,128)}, u32[]{:S(2)}) copy-start(f32[1,1,2176]{2,1,0:T(1,128)} %get-tuple-element.66) | copy-start | bytes 26116
  52.8 31.5 %all-to-all-start.1 = ((bf16[2,4,64,2176]{3,2,0,1:T(8,128)(2,1)}), bf16[2,4,64,2176]{3,2,0,1:T(8,128)(2,1)}, u32[]{:S(2)}, u32[]{:S(2)}) async-start(bf16[2,4,64,2176]{3,2,0,1:T(8,128)(2,1)} %pad_maximum_fusion.1), calls=%async_computation.1 | async-start | bytes 4456448 | tf_op jit(solution)/shard_map/all_to_all | solution.py:116
  60.5 37.3 %collective-permute-start = (bf16[256,2176]{1,0:T(8,128)(2,1)}, bf16[256,2176]{1,0:T(8,128)(2,1)S(1)}, u32[]{:S(2)}, u32[]{:S(2)}) collective-permute-start(bf16[256,2176]{1,0:T(8,128)(2,1)} %bitcast.6), channel_id=1, source_target_pairs={{0,1},{1,2},{2,3},{3,4},{4,5},{5,6},{6,7},{7,8},{8,9},{9,10},{10,1... | collective-permute-start | bytes 3342344 | tf_op jit(solution)/shard_map/ppermute | solution.py:117
  62.4 30.6 %copy-start.10 = (f32[1,1,2176]{2,1,0:T(1,128)S(1)}, f32[1,1,2176]{2,1,0:T(1,128)}, u32[]{:S(2)}) copy-start(f32[1,1,2176]{2,1,0:T(1,128)} %get-tuple-element.65) | copy-start | bytes 26116
  62.4 35.4 %collective-permute-start.1 = (bf16[256,2176]{1,0:T(8,128)(2,1)}, bf16[256,2176]{1,0:T(8,128)(2,1)}, u32[]{:S(2)}, u32[]{:S(2)}) collective-permute-start(bf16[256,2176]{1,0:T(8,128)(2,1)} %bitcast.7), channel_id=1, source_target_pairs={{1,0},{2,1},{3,2},{4,3},{5,4},{6,5},{7,6},{8,7},{9,8},{10,9},{11,1... | collective-permute-start | bytes 3342344 | tf_op jit(solution)/shard_map/ppermute | solution.py:118
  87.4 23.5 %collective-permute-start.4 = (bf16[256,2176]{1,0:T(8,128)(2,1)}, bf16[256,2176]{1,0:T(8,128)(2,1)}, u32[]{:S(2)}, u32[]{:S(2)}) collective-permute-start(bf16[256,2176]{1,0:T(8,128)(2,1)} %bitcast.30), channel_id=1, source_target_pairs={{0,1},{1,2},{2,3},{3,4},{4,5},{5,6},{6,7},{7,8},{8,9},{9,10},{10,1... | collective-permute-start | bytes 3342344 | tf_op jit(solution)/shard_map/ppermute | solution.py:117
  89.3 21.6 %collective-permute-start.5 = (bf16[256,2176]{1,0:T(8,128)(2,1)}, bf16[256,2176]{1,0:T(8,128)(2,1)}, u32[]{:S(2)}, u32[]{:S(2)}) collective-permute-start(bf16[256,2176]{1,0:T(8,128)(2,1)} %bitcast.31), channel_id=1, source_target_pairs={{1,0},{2,1},{3,2},{4,3},{5,4},{6,5},{7,6},{8,7},{9,8},{10,9},{11,1... | collective-permute-start | bytes 3342344 | tf_op jit(solution)/shard_map/ppermute | solution.py:118
  93.0 4.7 %copy-start.8 = (f32[6,2,2176]{2,1,0:T(2,128)}, f32[6,2,2176]{2,1,0:T(2,128)S(1)}, u32[]{:S(2)}) copy-start(f32[6,2,2176]{2,1,0:T(2,128)S(1)} %fusion.7.coef_ref) | copy-start | bytes 313348
  97.8 1.0 copy-start.7
  98.8 8.4 %copy-start = (bf16[2,4,64,2176]{3,2,1,0:T(8,128)(2,1)S(1)}, bf16[2,4,64,2176]{3,2,1,0:T(8,128)(2,1)}, u32[]{:S(2)}) copy-start(bf16[2,4,64,2176]{3,2,1,0:T(8,128)(2,1)} %copy.40) | copy-start | bytes 6684676
  107.2 2.6 %copy-start.1 = (bf16[2,4,64,2176]{3,2,1,0:T(8,128)(2,1)S(1)}, bf16[2,4,64,2176]{3,2,1,0:T(8,128)(2,1)}, u32[]{:S(2)}) copy-start(bf16[2,4,64,2176]{3,2,1,0:T(8,128)(2,1)} %copy.45) | copy-start | bytes 6684676
  107.2 3.0 %copy-start.4 = (bf16[2,256,2176]{2,1,0:T(8,128)(2,1)S(1)}, bf16[2,256,2176]{2,1,0:T(8,128)(2,1)}, u32[]{:S(2)}) copy-start(bf16[2,256,2176]{2,1,0:T(8,128)(2,1)} %shard_map.28) | copy-start | bytes 6684676
  119.2 2.6 %copy-start.2 = (bf16[2,4,64,2176]{3,2,1,0:T(8,128)(2,1)S(1)}, bf16[2,4,64,2176]{3,2,1,0:T(8,128)(2,1)}, u32[]{:S(2)}) copy-start(bf16[2,4,64,2176]{3,2,1,0:T(8,128)(2,1)} %copy.45) | copy-start | bytes 6684676
  119.2 3.0 %copy-start.3 = (bf16[2,256,2176]{2,1,0:T(8,128)(2,1)S(1)}, bf16[2,256,2176]{2,1,0:T(8,128)(2,1)}, u32[]{:S(2)}) copy-start(bf16[2,256,2176]{2,1,0:T(8,128)(2,1)} %shard_map.29) | copy-start | bytes 6684676
  123.5 14.5 %collective-permute-start.6 = (f32[2,64,512]{2,1,0:T(8,128)S(1)}, f32[2,64,512]{2,1,0:T(8,128)S(1)}, u32[]{:S(2)}, u32[]{:S(2)}) collective-permute-start(f32[2,64,512]{2,1,0:T(8,128)S(1)} %get-tuple-element.50), channel_id=1, source_target_pairs={{0,64},{64,128},{128,192},{192,0},{1,65},{65,129},{129,193},{193,1... | collective-permute-start | bytes 786440 | tf_op jit(solution)/shard_map/ppermute | solution.py:131
  124.1 13.8 %collective-permute-start.7 = (f32[2,64,512]{2,1,0:T(8,128)S(1)}, f32[2,64,512]{2,1,0:T(8,128)S(1)}, u32[]{:S(2)}, u32[]{:S(2)}) collective-permute-start(f32[2,64,512]{2,1,0:T(8,128)S(1)} %get-tuple-element.51), channel_id=1, source_target_pairs={{0,128},{64,192},{128,0},{192,64},{1,129},{65,193},{129,1},{193,65... | collective-permute-start | bytes 786440 | tf_op jit(solution)/shard_map/ppermute | solution.py:131
  126.2 12.3 %collective-permute-start.8 = (f32[2,64,512]{2,1,0:T(8,128)S(1)}, f32[2,64,512]{2,1,0:T(8,128)S(1)}, u32[]{:S(2)}, u32[]{:S(2)}) collective-permute-start(f32[2,64,512]{2,1,0:T(8,128)S(1)} %select_bitcast_fusion), channel_id=1, source_target_pairs={{0,192},{64,0},{128,64},{192,128},{1,193},{65,1},{129,65},{193,129... | collective-permute-start | bytes 786440 | tf_op jit(solution)/shard_map/ppermute | solution.py:131

commit v6 on v5

--- a/solution.py
+++ b/solution.py
@@ -124,14 +124,19 @@
             lax.dot_general(im, fd, dims, preferred_element_type=jnp.float32)
             for fd in fields], axis=1)
         for im in images], axis=0)
-    part = part.reshape(GROUPS, nodes, step, snaps)
+    cols = (GROUPS, nodes, sizes[0] // (GROUPS * nodes), sizes[1], sizes[2], snaps // spaces)
+    part = part.reshape((snaps,) + cols)
+    part = jnp.moveaxis(part, 5, 0)
+    part = lax.all_to_all(part, SPACE[2], 0, 0, tiled=True).sum(axis=0)
+    part = part.reshape(GROUPS, nodes, step, -1)
     total = jnp.take(part, me, axis=1)
     for d in range(1, nodes):
         blk = jnp.take(part, (me + d) % nodes, axis=1)
         total = total + lax.ppermute(blk, "node", [(i, (i + d) % nodes) for i in range(nodes)])
-    total = total.reshape(rows, GROUPS, nodes, step).transpose(0, 2, 1, 3)
-    total = total.reshape((rows,) + tuple(sizes) + (snaps // spaces,))
-    for axis in reversed(range(len(SPACE))):
+    total = total.reshape((rows,) + cols[:4] + cols[5:])
+    total = total.transpose(0, 2, 1, 3, 4, 5)
+    total = total.reshape((rows,) + tuple(sizes[:2]) + (snaps // spaces,))
+    for axis in (1, 0):
         total = jnp.moveaxis(total, axis + 1, 0)
         total = lax.all_to_all(total, SPACE[axis], 0, 0, tiled=True).sum(axis=0)
     out = total

time: 171 us -> 175 us (1.023)
    all_to_all x0 -> x1, blocking collectives: none -> 4.58 us  [per_device(): part = lax.all_to_all(part, SPACE[2], 0, 0, tiled=True).sum(axis=0)]
    all_to_all x3 -> x2, blocking collectives: 28.6 us -> 25.7 us  [per_device(): total = lax.all_to_all(total, SPACE[axis], 0, 0, tiled=True).sum(axis=0)]
where the time goes in v6:
time: 175 us; the launch traced here: 173 us
  waiting for transfers between devices  48.5 us (28%)
  local copies, waits for them, and re-layouts  32 us (18%)
  blocking collectives  30.3 us (17%)
  starting transfers between devices  29.1 us (17%)
  Pallas kernels  16.6 us (9%)
  other arithmetic  8.9 us (5%)
  matrix products  6.63 us (4%)
    all_to_all x2, waiting for transfers between devices, per_device(): lax.all_to_all(pieces, 'node', 1, 1, tiled=True)  36 us
    all_to_all x2, blocking collectives, per_device(): total = lax.all_to_all(total, SPACE[axis], 0, 0, tiled=True).sum(axis=0)  25.7 us
    pallas_call x2, Pallas kernels, stencil(): pl.pallas_call(stencil_kernel, grid=(snaps // ROWS,), in_specs=[pl.BlockS...  16.6 us
    ppermute x3, waiting for transfers between devices, per_device(): lax.ppermute(blk, 'node', [(i, (i + d) % nodes) for i in range(nodes)])  12.5 us
    all_to_all x2, starting transfers between devices, per_device(): lax.all_to_all(pieces, 'node', 1, 1, tiled=True)  8.91 us
    ppermute x2, starting transfers between devices, per_device(): above = lax.ppermute(field[0], SPACE, down)  7.29 us
    unnamed x29, local copies, waits for them, and re-layouts  6.68 us
    dot_general x4, matrix products, per_device(): lax.dot_general(im, fd, dims, preferred_element_type=jnp.float32)  6.63 us
  transfers between devices with their start and end apart: 11, of which 4 were waited for; matrix products, arithmetic and copies ran while one was open for 21% of the time, Pallas kernels for 5%

profile of v6, /device:TPU:8, one launch (start us, length us, event | category | flops | bytes accessed | tf_op | source)
XLA Modules:
  0.0 172.5 jit_solution(2040293028138949581)
XLA Ops:
  0.0 0.8 fusion.31
  0.8 0.8 fusion.30
  1.6 0.7 slice.239
  2.3 0.7 fusion.22
  3.3 0.7 slice_reduce_fusion
  3.9 1.9 %collective-permute-start.2 = (bf16[2176]{0:T(1024)(128)(2,1)}, bf16[2176]{0:T(1024)(128)(2,1)}, u32[]{:S(2)}, u32[]{:S(2)}) collective-permute-start(bf16[2176]{0:T(1024)(128)(2,1)} %get-tuple-element.29), channel_id=1, source_target_pairs={{0,1},{1,2},{2,3},{3,4},{4,5},{5,6},{6,7},{7,8},{8,9},{9,10},{10,1... | collective-permute-start | bytes 13064 | tf_op jit(solution)/shard_map/ppermute | solution.py:107
  5.8 3.6 %collective-permute-start.3 = (bf16[2176]{0:T(1024)(128)(2,1)}, bf16[2176]{0:T(1024)(128)(2,1)}, u32[]{:S(2)}, u32[]{:S(2)}) collective-permute-start(bf16[2176]{0:T(1024)(128)(2,1)} %get-tuple-element.28), channel_id=1, source_target_pairs={{1,0},{2,1},{3,2},{4,3},{5,4},{6,5},{7,6},{8,7},{9,8},{10,9},{11,1... | collective-permute-start | bytes 13064 | tf_op jit(solution)/shard_map/ppermute | solution.py:108
  9.5 4.9 %copy.61 = bf16[128,2,8192]{2,0,1:T(8,128)(2,1)S(1)} copy(bf16[128,2,8192]{2,1,0:T(2,128)(2,1)} %param.4) | data formatting | bytes 8388608 | tf_op args[0]
  14.4 1.3 fusion.25
  15.6 0.7 fusion.26
  16.4 1.1 fusion.27
  17.5 1.2 concatenate.131
  18.6 0.1 maximum_bitcast_fusion
  18.8 1.7 %pad_maximum_fusion = bf16[2,4,64,2176]{3,2,0,1:T(8,128)(2,1)} fusion(bf16[2,1,64,2176]{3,2,0,1:T(8,128)(2,1)S(1)} %bitcast.109, bf16[2,1,64,2176]{3,2,0,1:T(8,128)(2,1)S(1)} %get-tuple-element.70, bf16[2,1,64,2176]{3,2,0,1:T(8,128)(2,1)S(1)} %get-tuple-element.69, bf16[2,1,64,2176]{3,2,0,1:T(8,128)(2,1)S(1)} %pad_bitcast_fusion.1), kind=kLoop, calls=%fused_computation.1 | loop fusion | flops 3342336 | bytes 4456448 | tf_op jit(solution)/shard_map/stack | solution.py:90
  20.5 4.4 %all-to-all-start = ((bf16[2,4,64,2176]{3,2,0,1:T(8,128)(2,1)}), bf16[2,4,64,2176]{3,2,0,1:T(8,128)(2,1)S(1)}, u32[]{:S(2)}, u32[]{:S(2)}) async-start(bf16[2,4,64,2176]{3,2,0,1:T(8,128)(2,1)} %pad_maximum_fusion), calls=%async_computation | async-start | bytes 4456448 | tf_op jit(solution)/shard_map/all_to_all | solution.py:116
  24.9 0.7 slice_bitcast_fusion.2
  25.6 0.6 slice_bitcast_fusion.6
  26.3 0.7 slice_bitcast_fusion.4
  26.9 0.6 fusion.32
  27.6 1.9 %pad_bitcast_fusion = bf16[2,1,64,2176]{3,2,0,1:T(8,128)(2,1)} fusion(bf16[2,64,2112]{2,1,0:T(8,128)(2,1)} %get-tuple-element.35), kind=kLoop, calls=%fused_computation.13 | loop fusion | bytes 1097728 | tf_op jit(solution)/shard_map/stack | solution.py:90
  29.5 1.8 %concatenate.151 = bf16[2,64,2176]{2,1,0:T(8,128)(2,1)} concatenate(bf16[2,64,2048]{2,1,0:T(8,128)(2,1)} %get-tuple-element.45, bf16[2,64,64]{2,1,0:T(8,128)(2,1)S(1)} %broadcast.184, bf16[2,64,64]{2,1,0:T(8,128)(2,1)S(1)} %copy-done.9), dimensions={2} | concatenate | bytes 1114112 | tf_op jit(solution)/shard_map/concatenate | solution.py:89
  31.3 0.9 fusion.5
  32.2 0.8 fusion.7
  33.1 0.1 maximum_bitcast_fusion.2
  33.2 1.7 pad_maximum_fusion.1
  35.1 17.7 %all-to-all-done = bf16[2,4,64,2176]{3,2,0,1:T(8,128)(2,1)S(1)} async-done(((bf16[2,4,64,2176]{3,2,0,1:T(8,128)(2,1)}), bf16[2,4,64,2176]{3,2,0,1:T(8,128)(2,1)S(1)}, u32[]{:S(2)}, u32[]{:S(2)}) %all-to-all-start) | async-done | bytes 2228256 | tf_op jit(solution)/shard_map/all_to_all | solution.py:116
  52.8 4.5 %all-to-all-start.1 = ((bf16[2,4,64,2176]{3,2,0,1:T(8,128)(2,1)}), bf16[2,4,64,2176]{3,2,0,1:T(8,128)(2,1)}, u32[]{:S(2)}, u32[]{:S(2)}) async-start(bf16[2,4,64,2176]{3,2,0,1:T(8,128)(2,1)} %pad_maximum_fusion.1), calls=%async_computation.1 | async-start | bytes 4456448 | tf_op jit(solution)/shard_map/all_to_all | solution.py:116
  57.5 0.7 reshape.409
  58.2 0.7 reshape.410
  58.9 1.5 fusion.28
  60.5 1.9 %collective-permute-start = (bf16[256,2176]{1,0:T(8,128)(2,1)}, bf16[256,2176]{1,0:T(8,128)(2,1)S(1)}, u32[]{:S(2)}, u32[]{:S(2)}) collective-permute-start(bf16[256,2176]{1,0:T(8,128)(2,1)} %bitcast.6), channel_id=1, source_target_pairs={{0,1},{1,2},{2,3},{3,4},{4,5},{5,6},{6,7},{7,8},{8,9},{9,10},{10,1... | collective-permute-start | bytes 3342344 | tf_op jit(solution)/shard_map/ppermute | solution.py:117
  62.4 3.6 %collective-permute-start.1 = (bf16[256,2176]{1,0:T(8,128)(2,1)}, bf16[256,2176]{1,0:T(8,128)(2,1)}, u32[]{:S(2)}, u32[]{:S(2)}) collective-permute-start(bf16[256,2176]{1,0:T(8,128)(2,1)} %bitcast.7), channel_id=1, source_target_pairs={{1,0},{2,1},{3,2},{4,3},{5,4},{6,5},{7,6},{8,7},{9,8},{10,9},{11,1... | collective-permute-start | bytes 3342344 | tf_op jit(solution)/shard_map/ppermute | solution.py:118
  66.0 18.3 %all-to-all-done.1 = bf16[2,4,64,2176]{3,2,0,1:T(8,128)(2,1)} async-done(((bf16[2,4,64,2176]{3,2,0,1:T(8,128)(2,1)}), bf16[2,4,64,2176]{3,2,0,1:T(8,128)(2,1)}, u32[]{:S(2)}, u32[]{:S(2)}) %all-to-all-start.1) | async-done | bytes 2228256 | tf_op jit(solution)/shard_map/all_to_all | solution.py:116
  84.3 3.1 %fusion.29 = (bf16[1,4,64,2176]{3,2,1,0:T(8,128)(2,1)}, bf16[1,4,64,2176]{3,2,1,0:T(8,128)(2,1)}) fusion(bf16[2,4,64,2176]{3,2,0,1:T(8,128)(2,1)} %all-to-all-done.1), kind=kLoop, calls=%fused_computation.80 | loop fusion | bytes 4456448 | tf_op jit(solution)/shard_map/slice | solution.py:118
  87.4 1.9 %collective-permute-start.4 = (bf16[256,2176]{1,0:T(8,128)(2,1)}, bf16[256,2176]{1,0:T(8,128)(2,1)}, u32[]{:S(2)}, u32[]{:S(2)}) collective-permute-start(bf16[256,2176]{1,0:T(8,128)(2,1)} %bitcast.30), channel_id=1, source_target_pairs={{0,1},{1,2},{2,3},{3,4},{4,5},{5,6},{6,7},{7,8},{8,9},{9,10},{10,1... | collective-permute-start | bytes 3342344 | tf_op jit(solution)/shard_map/ppermute | solution.py:117
  89.3 3.6 %collective-permute-start.5 = (bf16[256,2176]{1,0:T(8,128)(2,1)}, bf16[256,2176]{1,0:T(8,128)(2,1)}, u32[]{:S(2)}, u32[]{:S(2)}) collective-permute-start(bf16[256,2176]{1,0:T(8,128)(2,1)} %bitcast.31), channel_id=1, source_target_pairs={{1,0},{2,1},{3,2},{4,3},{5,4},{6,5},{7,6},{8,7},{9,8},{10,9},{11,1... | collective-permute-start | bytes 3342344 | tf_op jit(solution)/shard_map/ppermute | solution.py:118
  93.0 1.6 copy.36
  94.6 3.2 %copy.41 = bf16[2,4,64,2176]{3,2,1,0:T(8,128)(2,1)} copy(bf16[2,4,64,2176]{3,2,0,1:T(8,128)(2,1)} %all-to-all-done.1) | data formatting | bytes 4456448 | tf_op jit(solution)/shard_map/all_to_all | solution.py:116
  97.8 1.0 copy-done.7
  98.8 8.4 %shard_map.28 = bf16[2,256,2176]{2,1,0:T(8,128)(2,1)} custom-call(bf16[2,256,2176]{2,1,0:T(8,128)(2,1)} %bitcast.97, bf16[256,2176]{1,0:T(8,128)(2,1)} %copy-done.7, bf16[256,2176]{1,0:T(8,128)(2,1)} %collective-permute-done.1.above_ref, f32[6,2,2176]{2,1,0:T(2,128)} %copy-done.8), custom_call_target="tpu_custom_call" | custom-call | tf_op jit(solution)/shard_map/pallas_call | solution.py:56
  107.2 2.5 %convolution_bitcast_fusion.3 = f32[256,256]{0,1:T(8,128)S(1)} fusion(bf16[2,256,2176]{2,1,0:T(8,128)(2,1)} %shard_map.28, bf16[2,256,2176]{2,1,0:T(8,128)(2,1)S(1)} %bitcast.98), kind=kOutput, calls=%fused_computation.6 | convolution fusion | flops 570425344 | bytes 4718592 | tf_op jit(solution)/shard_map/dot_general | solution.py:124
  109.7 0.4 copy-done.4
  110.1 0.8 convolution_bitcast_fusion.2
  110.9 8.3 %shard_map.29 = bf16[2,256,2176]{2,1,0:T(8,128)(2,1)} custom-call(bf16[2,256,2176]{2,1,0:T(8,128)(2,1)} %bitcast.100, bf16[256,2176]{1,0:T(8,128)(2,1)} %collective-permute-done.4.below_ref, bf16[256,2176]{1,0:T(8,128)(2,1)} %collective-permute-done.5.above_ref, f32[6,2,2176]{2,1,0:T(2,128)} %copy-done.8), custom_call_target="tpu_custom_call" | custom-call | tf_op jit(solution)/shard_map/pallas_call | solution.py:56
  119.2 2.5 %convolution_bitcast_fusion.1 = f32[256,256]{0,1:T(8,128)S(1)} fusion(bf16[2,256,2176]{2,1,0:T(8,128)(2,1)} %shard_map.29, bf16[2,256,2176]{2,1,0:T(8,128)(2,1)S(1)} %bitcast.99), kind=kOutput, calls=%fused_computation.4 | convolution fusion | flops 570425344 | bytes 4718592 | tf_op jit(solution)/shard_map/dot_general | solution.py:124
  121.8 0.4 copy-done.3
  122.2 0.8 convolution_bitcast_fusion
  122.9 0.1 maximum_maximum_fusion
  123.2 4.6 %all_to_all.25 = f32[2,512,2,4,1,4,8]{1,6,5,3,2,4,0:T(8,128)S(1)} all-to-all(f32[2,512,2,4,1,4,8]{1,6,5,3,2,4,0:T(8,128)S(1)} %bitcast.107), channel_id=1, replica_groups=mesh['node'=4,'z'=8,'y'=4,'core'=2] {'core'}, dimensions={0} | all-to-all | bytes 2097152 | tf_op jit(solution)/shard_map/all_to_all | solution.py:130
  127.7 0.1 reduce_sum.27
  127.9 0.5 reshape.310
  128.4 1.0 constant_dynamic-slice_fusion.2
  129.4 0.1 select_bitcast_fusion.1
  129.5 0.6 collective-permute-start.6
  130.2 0.1 select_bitcast_fusion
  130.3 2.2 %collective-permute-start.7 = (f32[2,64,256]{1,0,2:T(2,128)S(1)}, f32[2,64,256]{1,0,2:T(2,128)S(1)}, u32[]{:S(2)}, u32[]{:S(2)}) collective-permute-start(f32[2,64,256]{1,0,2:T(2,128)S(1)} %select_bitcast_fusion), channel_id=1, source_target_pairs={{0,128},{64,192},{128,0},{192,64},{1,129},{65,193},{129,1},{193,65... | collective-permute-start | bytes 393224 | tf_op jit(solution)/shard_map/ppermute | solution.py:135
  132.4 0.7 collective-permute-start.8
  133.1 11.7 %collective-permute-done.6 = f32[2,64,256]{1,0,2:T(2,128)S(1)} collective-permute-done((f32[2,64,256]{1,0,2:T(2,128)S(1)}, f32[2,64,256]{1,0,2:T(2,128)S(1)}, u32[]{:S(2)}, u32[]{:S(2)}) %collective-permute-start.6) | collective-permute-done | bytes 131104 | tf_op jit(solution)/shard_map/ppermute | solution.py:135
  144.8 0.8 collective-permute-done.8
  145.7 0.3 fusion.1
  145.9 0.2 reshape.311
  146.2 9.0 %all_to_all.26 = f32[4,128,8,8]{1,3,2,0:T(8,128)S(1)} all-to-all(f32[4,128,8,8]{1,3,2,0:T(8,128)S(1)} %copy.49), channel_id=1, replica_groups=mesh['node'=4,'z'=8,'y'=4,'core'=2] {'y'}, dimensions={0} | all-to-all | bytes 262144 | tf_op jit(solution)/shard_map/all_to_all | solution.py:141
  155.2 16.7 %all_to_all.27 = f32[8,128,8]{1,2,0:T(8,128)S(1)} all-to-all(f32[8,128,8]{1,2,0:T(8,128)S(1)} %bitcast.116), channel_id=1, replica_groups=mesh['node'=4,'z'=8,'y'=4,'core'=2] {'z'}, dimensions={0} | all-to-all | bytes 65536 | tf_op jit(solution)/shard_map/all_to_all | solution.py:141
  171.9 0.6 broadcast_multiply_fusion
  (50 shorter events, 0.8 us)
Async XLA Ops:
  3.9 53.5 %collective-permute-start.2 = (bf16[2176]{0:T(1024)(128)(2,1)}, bf16[2176]{0:T(1024)(128)(2,1)}, u32[]{:S(2)}, u32[]{:S(2)}) collective-permute-start(bf16[2176]{0:T(1024)(128)(2,1)} %get-tuple-element.29), channel_id=1, source_target_pairs={{0,1},{1,2},{2,3},{3,4},{4,5},{5,6},{6,7},{7,8},{8,9},{9,10},{10,1... | collective-permute-start | bytes 13064 | tf_op jit(solution)/shard_map/ppermute | solution.py:107
  5.8 52.3 %collective-permute-start.3 = (bf16[2176]{0:T(1024)(128)(2,1)}, bf16[2176]{0:T(1024)(128)(2,1)}, u32[]{:S(2)}, u32[]{:S(2)}) collective-permute-start(bf16[2176]{0:T(1024)(128)(2,1)} %get-tuple-element.28), channel_id=1, source_target_pairs={{1,0},{2,1},{3,2},{4,3},{5,4},{6,5},{7,6},{8,7},{9,8},{10,9},{11,1... | collective-permute-start | bytes 13064 | tf_op jit(solution)/shard_map/ppermute | solution.py:108
  20.5 9.0 %copy-start.9 = (bf16[2,64,64]{2,1,0:T(8,128)(2,1)S(1)}, bf16[2,64,64]{2,1,0:T(8,128)(2,1)}, u32[]{:S(2)}) copy-start(bf16[2,64,64]{2,1,0:T(8,128)(2,1)} %get-tuple-element.39) | copy-start | bytes 49156
  20.5 32.3 %all-to-all-start = ((bf16[2,4,64,2176]{3,2,0,1:T(8,128)(2,1)}), bf16[2,4,64,2176]{3,2,0,1:T(8,128)(2,1)S(1)}, u32[]{:S(2)}, u32[]{:S(2)}) async-start(bf16[2,4,64,2176]{3,2,0,1:T(8,128)(2,1)} %pad_maximum_fusion), calls=%async_computation | async-start | bytes 4456448 | tf_op jit(solution)/shard_map/all_to_all | solution.py:116
  31.3 1.9 %copy-start.5 = (bf16[2,1,64,2176]{3,2,0,1:T(8,128)(2,1)S(1)}, bf16[2,1,64,2176]{3,2,0,1:T(8,128)(2,1)}, u32[]{:S(2)}) copy-start(bf16[2,1,64,2176]{3,2,0,1:T(8,128)(2,1)} %pad_bitcast_fusion) | copy-start | bytes 1671172
  31.3 1.9 %copy-start.6 = (bf16[2,64,2176]{2,1,0:T(8,128)(2,1)S(1)}, bf16[2,64,2176]{2,1,0:T(8,128)(2,1)}, u32[]{:S(2)}) copy-start(bf16[2,64,2176]{2,1,0:T(8,128)(2,1)} %concatenate.151) | copy-start | bytes 1671172
  33.2 1.8 %copy-start.13 = (f32[1,2,64]{2,1,0:T(2,128)S(1)}, f32[1,2,64]{2,1,0:T(2,128)}, u32[]{:S(2)}) copy-start(f32[1,2,64]{2,1,0:T(2,128)} %get-tuple-element.60) | copy-start | bytes 1540
  35.1 22.2 %copy-start.12 = (f32[1,2,64]{2,1,0:T(2,128)S(1)}, f32[1,2,64]{2,1,0:T(2,128)}, u32[]{:S(2)}) copy-start(f32[1,2,64]{2,1,0:T(2,128)} %get-tuple-element.59) | copy-start | bytes 1540
  35.1 23.8 %copy-start.11 = (f32[1,1,2176]{2,1,0:T(1,128)S(1)}, f32[1,1,2176]{2,1,0:T(1,128)}, u32[]{:S(2)}) copy-start(f32[1,1,2176]{2,1,0:T(1,128)} %get-tuple-element.68) | copy-start | bytes 26116
  52.8 31.5 %all-to-all-start.1 = ((bf16[2,4,64,2176]{3,2,0,1:T(8,128)(2,1)}), bf16[2,4,64,2176]{3,2,0,1:T(8,128)(2,1)}, u32[]{:S(2)}, u32[]{:S(2)}) async-start(bf16[2,4,64,2176]{3,2,0,1:T(8,128)(2,1)} %pad_maximum_fusion.1), calls=%async_computation.1 | async-start | bytes 4456448 | tf_op jit(solution)/shard_map/all_to_all | solution.py:116
  60.5 37.3 %collective-permute-start = (bf16[256,2176]{1,0:T(8,128)(2,1)}, bf16[256,2176]{1,0:T(8,128)(2,1)S(1)}, u32[]{:S(2)}, u32[]{:S(2)}) collective-permute-start(bf16[256,2176]{1,0:T(8,128)(2,1)} %bitcast.6), channel_id=1, source_target_pairs={{0,1},{1,2},{2,3},{3,4},{4,5},{5,6},{6,7},{7,8},{8,9},{9,10},{10,1... | collective-permute-start | bytes 3342344 | tf_op jit(solution)/shard_map/ppermute | solution.py:117
  62.4 30.6 %copy-start.10 = (f32[1,1,2176]{2,1,0:T(1,128)S(1)}, f32[1,1,2176]{2,1,0:T(1,128)}, u32[]{:S(2)}) copy-start(f32[1,1,2176]{2,1,0:T(1,128)} %get-tuple-element.67) | copy-start | bytes 26116
  62.4 35.4 %collective-permute-start.1 = (bf16[256,2176]{1,0:T(8,128)(2,1)}, bf16[256,2176]{1,0:T(8,128)(2,1)}, u32[]{:S(2)}, u32[]{:S(2)}) collective-permute-start(bf16[256,2176]{1,0:T(8,128)(2,1)} %bitcast.7), channel_id=1, source_target_pairs={{1,0},{2,1},{3,2},{4,3},{5,4},{6,5},{7,6},{8,7},{9,8},{10,9},{11,1... | collective-permute-start | bytes 3342344 | tf_op jit(solution)/shard_map/ppermute | solution.py:118
  87.4 23.5 %collective-permute-start.4 = (bf16[256,2176]{1,0:T(8,128)(2,1)}, bf16[256,2176]{1,0:T(8,128)(2,1)}, u32[]{:S(2)}, u32[]{:S(2)}) collective-permute-start(bf16[256,2176]{1,0:T(8,128)(2,1)} %bitcast.30), channel_id=1, source_target_pairs={{0,1},{1,2},{2,3},{3,4},{4,5},{5,6},{6,7},{7,8},{8,9},{9,10},{10,1... | collective-permute-start | bytes 3342344 | tf_op jit(solution)/shard_map/ppermute | solution.py:117
  89.3 21.6 %collective-permute-start.5 = (bf16[256,2176]{1,0:T(8,128)(2,1)}, bf16[256,2176]{1,0:T(8,128)(2,1)}, u32[]{:S(2)}, u32[]{:S(2)}) collective-permute-start(bf16[256,2176]{1,0:T(8,128)(2,1)} %bitcast.31), channel_id=1, source_target_pairs={{1,0},{2,1},{3,2},{4,3},{5,4},{6,5},{7,6},{8,7},{9,8},{10,9},{11,1... | collective-permute-start | bytes 3342344 | tf_op jit(solution)/shard_map/ppermute | solution.py:118
  93.0 4.7 %copy-start.8 = (f32[6,2,2176]{2,1,0:T(2,128)}, f32[6,2,2176]{2,1,0:T(2,128)S(1)}, u32[]{:S(2)}) copy-start(f32[6,2,2176]{2,1,0:T(2,128)S(1)} %fusion.3.coef_ref) | copy-start | bytes 313348
  97.8 1.0 copy-start.7
  98.8 8.4 %copy-start = (bf16[2,4,64,2176]{3,2,1,0:T(8,128)(2,1)S(1)}, bf16[2,4,64,2176]{3,2,1,0:T(8,128)(2,1)}, u32[]{:S(2)}) copy-start(bf16[2,4,64,2176]{3,2,1,0:T(8,128)(2,1)} %copy.36) | copy-start | bytes 6684676
  107.2 2.6 %copy-start.1 = (bf16[2,4,64,2176]{3,2,1,0:T(8,128)(2,1)S(1)}, bf16[2,4,64,2176]{3,2,1,0:T(8,128)(2,1)}, u32[]{:S(2)}) copy-start(bf16[2,4,64,2176]{3,2,1,0:T(8,128)(2,1)} %copy.41) | copy-start | bytes 6684676
  107.2 3.0 %copy-start.4 = (bf16[2,256,2176]{2,1,0:T(8,128)(2,1)S(1)}, bf16[2,256,2176]{2,1,0:T(8,128)(2,1)}, u32[]{:S(2)}) copy-start(bf16[2,256,2176]{2,1,0:T(8,128)(2,1)} %shard_map.28) | copy-start | bytes 6684676
  119.2 2.6 %copy-start.2 = (bf16[2,4,64,2176]{3,2,1,0:T(8,128)(2,1)S(1)}, bf16[2,4,64,2176]{3,2,1,0:T(8,128)(2,1)}, u32[]{:S(2)}) copy-start(bf16[2,4,64,2176]{3,2,1,0:T(8,128)(2,1)} %copy.41) | copy-start | bytes 6684676
  119.2 3.0 %copy-start.3 = (bf16[2,256,2176]{2,1,0:T(8,128)(2,1)S(1)}, bf16[2,256,2176]{2,1,0:T(8,128)(2,1)}, u32[]{:S(2)}) copy-start(bf16[2,256,2176]{2,1,0:T(8,128)(2,1)} %shard_map.29) | copy-start | bytes 6684676
  129.5 15.3 %collective-permute-start.6 = (f32[2,64,256]{1,0,2:T(2,128)S(1)}, f32[2,64,256]{1,0,2:T(2,128)S(1)}, u32[]{:S(2)}, u32[]{:S(2)}) collective-permute-start(f32[2,64,256]{1,0,2:T(2,128)S(1)} %select_bitcast_fusion.1), channel_id=1, source_target_pairs={{0,64},{64,128},{128,192},{192,0},{1,65},{65,129},{129,193},{193,1... | collective-permute-start | bytes 393224 | tf_op jit(solution)/shard_map/ppermute | solution.py:135
  130.3 14.6 %collective-permute-start.7 = (f32[2,64,256]{1,0,2:T(2,128)S(1)}, f32[2,64,256]{1,0,2:T(2,128)S(1)}, u32[]{:S(2)}, u32[]{:S(2)}) collective-permute-start(f32[2,64,256]{1,0,2:T(2,128)S(1)} %select_bitcast_fusion), channel_id=1, source_target_pairs={{0,128},{64,192},{128,0},{192,64},{1,129},{65,193},{129,1},{193,65... | collective-permute-start | bytes 393224 | tf_op jit(solution)/shard_map/ppermute | solution.py:135
  132.4 13.2 %collective-permute-start.8 = (f32[2,64,256]{1,0,2:T(2,128)S(1)}, f32[2,64,256]{1,0,2:T(2,128)S(1)}, u32[]{:S(2)}, u32[]{:S(2)}) collective-permute-start(f32[2,64,256]{1,0,2:T(2,128)S(1)} %bitcast.115), channel_id=1, source_target_pairs={{0,192},{64,0},{128,64},{192,128},{1,193},{65,1},{129,65},{193,129... | collective-permute-start | bytes 393224 | tf_op jit(solution)/shard_map/ppermute | solution.py:135

commit v7 on v5

--- a/solution.py
+++ b/solution.py
@@ -124,16 +124,10 @@
             lax.dot_general(im, fd, dims, preferred_element_type=jnp.float32)
             for fd in fields], axis=1)
         for im in images], axis=0)
-    part = part.reshape(GROUPS, nodes, step, snaps)
-    total = jnp.take(part, me, axis=1)
-    for d in range(1, nodes):
-        blk = jnp.take(part, (me + d) % nodes, axis=1)
-        total = total + lax.ppermute(blk, "node", [(i, (i + d) % nodes) for i in range(nodes)])
-    total = total.reshape(rows, GROUPS, nodes, step).transpose(0, 2, 1, 3)
-    total = total.reshape((rows,) + tuple(sizes) + (snaps // spaces,))
-    for axis in reversed(range(len(SPACE))):
-        total = jnp.moveaxis(total, axis + 1, 0)
-        total = lax.all_to_all(total, SPACE[axis], 0, 0, tiled=True).sum(axis=0)
+    width = snaps // spaces
+    part = part.reshape(GROUPS, nodes, step, GROUPS, nodes, step // width, width)
+    part = part.transpose(1, 4, 3, 5, 0, 2, 6).reshape(nodes * spaces, rows, width)
+    total = lax.all_to_all(part, ("node",) + SPACE, 0, 0, tiled=True).sum(axis=0)
     out = total
 
     scale = jnp.float32(1.0 / math.sqrt(planes * spaces * NY * NZ))

time: 171 us -> 178 us (1.041)
  blocking collectives: 28.6 us -> 43.5 us
  waiting for transfers between devices: 47.5 us -> 37.8 us
  local copies, waits for them, and re-layouts: 32.1 us -> 37.1 us
  starting transfers between devices: 29.1 us -> 24.4 us
    all_to_all x3 -> x1, blocking collectives: 28.6 us -> 43.5 us  [per_device(): lax.all_to_all(part, ('node',) + SPACE, 0, 0, tiled=True).sum(axis=0)]
    ppermute x3 -> x0, waiting for transfers between devices: 11.6 us -> none  [per_device(): lax.ppermute(blk, 'node', [(i, (i + d) % nodes) for i in range(nodes)])]
    reshape x1 -> x3, local copies, waits for them, and re-layouts: 0.28 us -> 6.11 us  [the longest x2 3.52 us: per_device(): part.reshape(GROUPS, nodes, step, GROUPS, nodes, step // width, width)]
    ppermute x3 -> x0, starting transfers between devices: 3.49 us -> none  [per_device(): lax.ppermute(blk, 'node', [(i, (i + d) % nodes) for i in range(nodes)])]
    all_to_all x2, waiting for transfers between devices: 36 us -> 37.8 us  [per_device(): lax.all_to_all(pieces, 'node', 1, 1, tiled=True)]
    unnamed x29 -> x27, local copies, waits for them, and re-layouts: 6.68 us -> 6.42 us
  transfers between devices with their start and end apart: 11 -> 8, of which waited for: 4 -> 2; matrix products, arithmetic and copies ran while one was open for 21% -> 21% of each run, Pallas kernels for 5% -> 5%
where the time goes in v7:
time: 178 us; the launch traced here: 176 us
  blocking collectives  43.5 us (24%)
  waiting for transfers between devices  37.8 us (21%)
  local copies, waits for them, and re-layouts  37.1 us (21%)
  starting transfers between devices  24.4 us (14%)
  Pallas kernels  16.6 us (9%)
  other arithmetic  8.32 us (5%)
  matrix products  8.04 us (5%)
    all_to_all x1, blocking collectives, per_device(): lax.all_to_all(part, ('node',) + SPACE, 0, 0, tiled=True).sum(axis=0)  43.5 us
    all_to_all x2, waiting for transfers between devices, per_device(): lax.all_to_all(pieces, 'node', 1, 1, tiled=True)  37.8 us
    pallas_call x2, Pallas kernels, stencil(): pl.pallas_call(stencil_kernel, grid=(snaps // ROWS,), in_specs=[pl.BlockS...  16.6 us
    all_to_all x2, starting transfers between devices, per_device(): lax.all_to_all(pieces, 'node', 1, 1, tiled=True)  8.77 us
    dot_general x4, matrix products, per_device(): lax.dot_general(im, fd, dims, preferred_element_type=jnp.float32)  8.04 us
    ppermute x2, starting transfers between devices, per_device(): above = lax.ppermute(field[0], SPACE, down)  7.42 us
    unnamed x27, local copies, waits for them, and re-layouts  6.42 us
    another operation x6, other arithmetic, chunked(): return jnp.stack(pieces, axis=-3)  5.27 us
  transfers between devices with their start and end apart: 8, of which 2 were waited for; matrix products, arithmetic and copies ran while one was open for 21% of the time, Pallas kernels for 5%

profile of v7, /device:TPU:8, one launch (start us, length us, event | category | flops | bytes accessed | tf_op | source)
XLA Modules:
  0.0 176.0 jit_solution(13044024623475990322)
XLA Ops:
  0.0 0.8 fusion.29
  0.8 0.7 slice.228
  1.5 0.8 fusion.28
  2.3 0.7 fusion.20
  3.0 0.1 concatenate.135
  3.1 0.1 maximum_bitcast_fusion.4
  3.2 0.1 convert_bitcast_fusion
  3.3 0.7 slice_reduce_fusion
  3.9 1.9 %collective-permute-start.3 = (bf16[2176]{0:T(1024)(128)(2,1)}, bf16[2176]{0:T(1024)(128)(2,1)}, u32[]{:S(2)}, u32[]{:S(2)}) collective-permute-start(bf16[2176]{0:T(1024)(128)(2,1)} %get-tuple-element.16), channel_id=1, source_target_pairs={{1,0},{2,1},{3,2},{4,3},{5,4},{6,5},{7,6},{8,7},{9,8},{10,9},{11,1... | collective-permute-start | bytes 13064 | tf_op jit(solution)/shard_map/ppermute | solution.py:108
  5.8 2.4 %collective-permute-start.2 = (bf16[2176]{0:T(1024)(128)(2,1)}, bf16[2176]{0:T(1024)(128)(2,1)}, u32[]{:S(2)}, u32[]{:S(2)}) collective-permute-start(bf16[2176]{0:T(1024)(128)(2,1)} %get-tuple-element.17), channel_id=1, source_target_pairs={{0,1},{1,2},{2,3},{3,4},{4,5},{5,6},{6,7},{7,8},{8,9},{9,10},{10,1... | collective-permute-start | bytes 13064 | tf_op jit(solution)/shard_map/ppermute | solution.py:107
  8.3 4.9 %copy.41 = bf16[128,2,8192]{2,0,1:T(8,128)(2,1)S(1)} copy(bf16[128,2,8192]{2,1,0:T(2,128)(2,1)} %param.2) | data formatting | bytes 8388608 | tf_op args[0]
  13.1 0.7 fusion.24
  13.9 1.0 fusion.25
  14.9 1.3 fusion.23
  16.2 1.2 concatenate.131
  17.4 0.1 maximum_bitcast_fusion
  17.5 1.7 pad_maximum_fusion
  19.3 4.3 %all-to-all-start = ((bf16[2,4,64,2176]{3,2,0,1:T(8,128)(2,1)}), bf16[2,4,64,2176]{3,2,0,1:T(8,128)(2,1)S(1)}, u32[]{:S(2)}, u32[]{:S(2)}) async-start(bf16[2,4,64,2176]{3,2,0,1:T(8,128)(2,1)} %pad_maximum_fusion), calls=%async_computation | async-start | bytes 4456448 | tf_op jit(solution)/shard_map/all_to_all | solution.py:116
  23.6 0.6 slice_bitcast_fusion.6
  24.2 0.6 slice_bitcast_fusion.4
  24.9 0.6 fusion.30
  25.5 0.7 slice_bitcast_fusion.2
  26.2 1.9 %pad_bitcast_fusion = bf16[2,1,64,2176]{3,2,0,1:T(8,128)(2,1)} fusion(bf16[2,64,2112]{2,1,0:T(8,128)(2,1)} %get-tuple-element.23), kind=kLoop, calls=%fused_computation.13 | loop fusion | bytes 1097728 | tf_op jit(solution)/shard_map/stack | solution.py:90
  28.1 1.8 %concatenate.151 = bf16[2,64,2176]{2,1,0:T(8,128)(2,1)} concatenate(bf16[2,64,2048]{2,1,0:T(8,128)(2,1)} %get-tuple-element.33, bf16[2,64,64]{2,1,0:T(8,128)(2,1)S(1)} %broadcast.181, bf16[2,64,64]{2,1,0:T(8,128)(2,1)S(1)} %get-tuple-element.27), dimensions={2} | concatenate | bytes 1114112 | tf_op jit(solution)/shard_map/concatenate | solution.py:89
  29.9 0.9 fusion.3
  30.8 0.8 fusion.5
  31.7 0.9 maximum_bitcast_fusion.2
  32.6 1.7 pad_maximum_fusion.1
  34.3 0.1 slice_bitcast_fusion
  34.4 0.1 fusion.7
  34.5 18.2 %all-to-all-done = bf16[2,4,64,2176]{3,2,0,1:T(8,128)(2,1)S(1)} async-done(((bf16[2,4,64,2176]{3,2,0,1:T(8,128)(2,1)}), bf16[2,4,64,2176]{3,2,0,1:T(8,128)(2,1)S(1)}, u32[]{:S(2)}, u32[]{:S(2)}) %all-to-all-start) | async-done | bytes 2228256 | tf_op jit(solution)/shard_map/all_to_all | solution.py:116
  52.7 4.5 %all-to-all-start.1 = ((bf16[2,4,64,2176]{3,2,0,1:T(8,128)(2,1)}), bf16[2,4,64,2176]{3,2,0,1:T(8,128)(2,1)}, u32[]{:S(2)}, u32[]{:S(2)}) async-start(bf16[2,4,64,2176]{3,2,0,1:T(8,128)(2,1)} %pad_maximum_fusion.1), calls=%async_computation.1 | async-start | bytes 4456448 | tf_op jit(solution)/shard_map/all_to_all | solution.py:116
  57.1 0.1 fusion.9
  57.2 0.0 collective-permute-done.3
  57.3 0.7 reshape.334
  58.0 0.0 collective-permute-done.2
  58.0 0.7 reshape.333
  58.7 1.6 fusion.26
  60.3 2.0 %collective-permute-start = (bf16[256,2176]{1,0:T(8,128)(2,1)}, bf16[256,2176]{1,0:T(8,128)(2,1)S(1)}, u32[]{:S(2)}, u32[]{:S(2)}) collective-permute-start(bf16[256,2176]{1,0:T(8,128)(2,1)} %bitcast.6), channel_id=1, source_target_pairs={{0,1},{1,2},{2,3},{3,4},{4,5},{5,6},{6,7},{7,8},{8,9},{9,10},{10,1... | collective-permute-start | bytes 3342344 | tf_op jit(solution)/shard_map/ppermute | solution.py:117
  62.2 3.6 %collective-permute-start.1 = (bf16[256,2176]{1,0:T(8,128)(2,1)}, bf16[256,2176]{1,0:T(8,128)(2,1)}, u32[]{:S(2)}, u32[]{:S(2)}) collective-permute-start(bf16[256,2176]{1,0:T(8,128)(2,1)} %bitcast.7), channel_id=1, source_target_pairs={{1,0},{2,1},{3,2},{4,3},{5,4},{6,5},{7,6},{8,7},{9,8},{10,9},{11,1... | collective-permute-start | bytes 3342344 | tf_op jit(solution)/shard_map/ppermute | solution.py:118
  65.8 19.6 %all-to-all-done.1 = bf16[2,4,64,2176]{3,2,0,1:T(8,128)(2,1)} async-done(((bf16[2,4,64,2176]{3,2,0,1:T(8,128)(2,1)}), bf16[2,4,64,2176]{3,2,0,1:T(8,128)(2,1)}, u32[]{:S(2)}, u32[]{:S(2)}) %all-to-all-start.1) | async-done | bytes 2228256 | tf_op jit(solution)/shard_map/all_to_all | solution.py:116
  85.4 3.1 %fusion.27 = (bf16[1,4,64,2176]{3,2,1,0:T(8,128)(2,1)}, bf16[1,4,64,2176]{3,2,1,0:T(8,128)(2,1)}) fusion(bf16[2,4,64,2176]{3,2,0,1:T(8,128)(2,1)} %all-to-all-done.1), kind=kLoop, calls=%fused_computation.71 | loop fusion | bytes 4456448 | tf_op jit(solution)/shard_map/slice | solution.py:118
  88.5 1.9 %collective-permute-start.4 = (bf16[256,2176]{1,0:T(8,128)(2,1)}, bf16[256,2176]{1,0:T(8,128)(2,1)}, u32[]{:S(2)}, u32[]{:S(2)}) collective-permute-start(bf16[256,2176]{1,0:T(8,128)(2,1)} %bitcast.30), channel_id=1, source_target_pairs={{0,1},{1,2},{2,3},{3,4},{4,5},{5,6},{6,7},{7,8},{8,9},{9,10},{10,1... | collective-permute-start | bytes 3342344 | tf_op jit(solution)/shard_map/ppermute | solution.py:117
  90.4 3.8 %collective-permute-start.5 = (bf16[256,2176]{1,0:T(8,128)(2,1)}, bf16[256,2176]{1,0:T(8,128)(2,1)}, u32[]{:S(2)}, u32[]{:S(2)}) collective-permute-start(bf16[256,2176]{1,0:T(8,128)(2,1)} %bitcast.31), channel_id=1, source_target_pairs={{1,0},{2,1},{3,2},{4,3},{5,4},{6,5},{7,6},{8,7},{9,8},{10,9},{11,1... | collective-permute-start | bytes 3342344 | tf_op jit(solution)/shard_map/ppermute | solution.py:118
  94.3 1.6 copy.26
  95.9 3.2 %copy.31 = bf16[2,4,64,2176]{3,2,1,0:T(8,128)(2,1)} copy(bf16[2,4,64,2176]{3,2,0,1:T(8,128)(2,1)} %all-to-all-done.1) | data formatting | bytes 4456448 | tf_op jit(solution)/shard_map/all_to_all | solution.py:116
  99.1 0.0 collective-permute-done.below_ref
  99.1 0.0 collective-permute-done.1.above_ref
  99.1 1.0 copy-done.6
  100.1 8.4 %shard_map.28 = bf16[2,256,2176]{2,1,0:T(8,128)(2,1)} custom-call(bf16[2,256,2176]{2,1,0:T(8,128)(2,1)} %bitcast.75, bf16[256,2176]{1,0:T(8,128)(2,1)} %copy-done.6, bf16[256,2176]{1,0:T(8,128)(2,1)} %collective-permute-done.1.above_ref, f32[6,2,2176]{2,1,0:T(2,128)} %copy-done.8), custom_call_target="tpu_custom_call" | custom-call | tf_op jit(solution)/shard_map/pallas_call | solution.py:56
  108.5 2.5 %convolution_bitcast_fusion.3 = f32[256,256]{0,1:T(8,128)S(1)} fusion(bf16[2,256,2176]{2,1,0:T(8,128)(2,1)} %shard_map.28, bf16[2,256,2176]{2,1,0:T(8,128)(2,1)S(1)} %bitcast.76), kind=kOutput, calls=%fused_computation.7 | convolution fusion | flops 570425344 | bytes 4718592 | tf_op jit(solution)/shard_map/dot_general | solution.py:124
  111.1 0.4 copy-done.3
  111.5 1.5 convolution_bitcast_fusion.2
  113.0 8.3 %shard_map.29 = bf16[2,256,2176]{2,1,0:T(8,128)(2,1)} custom-call(bf16[2,256,2176]{2,1,0:T(8,128)(2,1)} %bitcast.78, bf16[256,2176]{1,0:T(8,128)(2,1)} %collective-permute-done.4.below_ref, bf16[256,2176]{1,0:T(8,128)(2,1)} %collective-permute-done.5.above_ref, f32[6,2,2176]{2,1,0:T(2,128)} %copy-done.8), custom_call_target="tpu_custom_call" | custom-call | tf_op jit(solution)/shard_map/pallas_call | solution.py:56
  121.2 3.2 %convolution_bitcast_fusion = f32[256,256]{0,1:T(8,128)S(1)} fusion(bf16[2,256,2176]{2,1,0:T(8,128)(2,1)} %shard_map.29, bf16[2,256,2176]{2,1,0:T(8,128)(2,1)} %bitcast.79), kind=kOutput, calls=%fused_computation.4 | convolution fusion | flops 570425344 | bytes 4718592 | tf_op jit(solution)/shard_map/dot_general | solution.py:124
  124.5 0.8 convolution_bitcast_fusion.1
  125.2 0.2 copy-done.7
  125.4 0.1 maximum_maximum_fusion
  125.5 1.1 reshape.300
  126.6 2.4 %copy.42 = f32[2,4,64,2,4,8,8]{2,0,6,5,3,4,1:T(2,128)} copy(f32[2,4,64,2,4,8,8]{2,1,0,6,5,4,3:T(4,128)S(1)} %reshape.300) | data formatting | bytes 2097152 | tf_op jit(solution)/shard_map/reshape | solution.py:128
  129.1 2.6 %reshape.301 = f32[256,128,8]{1,2,0:T(8,128)S(1)} reshape(f32[4,4,2,8,2,64,8]{5,4,6,3,2,1,0:T(2,128)} %bitcast.84) | data formatting | bytes 2097152 | tf_op jit(solution)/shard_map/reshape | solution.py:129
  131.7 43.5 %all_to_all.15 = f32[256,128,8]{1,2,0:T(8,128)S(1)} all-to-all(f32[256,128,8]{1,2,0:T(8,128)S(1)} %reshape.301), channel_id=1, replica_groups=mesh['node'=4,'z'=8,'y'=4,'core'=2] {'node','z','y','core'}, dimensions={0} | all-to-all | bytes 2097152 | tf_op jit(solution)/shard_map/all_to_all | solution.py:130
  175.1 0.3 reduce_sum.9
  175.4 0.6 broadcast_multiply_fusion
  (32 shorter events, 0.2 us)
Async XLA Ops:
  3.9 53.3 %collective-permute-start.3 = (bf16[2176]{0:T(1024)(128)(2,1)}, bf16[2176]{0:T(1024)(128)(2,1)}, u32[]{:S(2)}, u32[]{:S(2)}) collective-permute-start(bf16[2176]{0:T(1024)(128)(2,1)} %get-tuple-element.16), channel_id=1, source_target_pairs={{1,0},{2,1},{3,2},{4,3},{5,4},{6,5},{7,6},{8,7},{9,8},{10,9},{11,1... | collective-permute-start | bytes 13064 | tf_op jit(solution)/shard_map/ppermute | solution.py:108
  5.8 52.1 %collective-permute-start.2 = (bf16[2176]{0:T(1024)(128)(2,1)}, bf16[2176]{0:T(1024)(128)(2,1)}, u32[]{:S(2)}, u32[]{:S(2)}) collective-permute-start(bf16[2176]{0:T(1024)(128)(2,1)} %get-tuple-element.17), channel_id=1, source_target_pairs={{0,1},{1,2},{2,3},{3,4},{4,5},{5,6},{6,7},{7,8},{8,9},{9,10},{10,1... | collective-permute-start | bytes 13064 | tf_op jit(solution)/shard_map/ppermute | solution.py:107
  19.3 33.4 %all-to-all-start = ((bf16[2,4,64,2176]{3,2,0,1:T(8,128)(2,1)}), bf16[2,4,64,2176]{3,2,0,1:T(8,128)(2,1)S(1)}, u32[]{:S(2)}, u32[]{:S(2)}) async-start(bf16[2,4,64,2176]{3,2,0,1:T(8,128)(2,1)} %pad_maximum_fusion), calls=%async_computation | async-start | bytes 4456448 | tf_op jit(solution)/shard_map/all_to_all | solution.py:116
  29.9 2.6 %copy-start.4 = (bf16[2,1,64,2176]{3,2,0,1:T(8,128)(2,1)S(1)}, bf16[2,1,64,2176]{3,2,0,1:T(8,128)(2,1)}, u32[]{:S(2)}) copy-start(bf16[2,1,64,2176]{3,2,0,1:T(8,128)(2,1)} %pad_bitcast_fusion) | copy-start | bytes 1671172
  29.9 2.6 %copy-start.5 = (bf16[2,64,2176]{2,1,0:T(8,128)(2,1)S(1)}, bf16[2,64,2176]{2,1,0:T(8,128)(2,1)}, u32[]{:S(2)}) copy-start(bf16[2,64,2176]{2,1,0:T(8,128)(2,1)} %concatenate.151) | copy-start | bytes 1671172
  32.6 1.8 %copy-start.12 = (f32[1,2,64]{2,1,0:T(2,128)S(1)}, f32[1,2,64]{2,1,0:T(2,128)}, u32[]{:S(2)}) copy-start(f32[1,2,64]{2,1,0:T(2,128)} %get-tuple-element.44) | copy-start | bytes 1540
  34.5 22.7 %copy-start.11 = (f32[1,2,64]{2,1,0:T(2,128)S(1)}, f32[1,2,64]{2,1,0:T(2,128)}, u32[]{:S(2)}) copy-start(f32[1,2,64]{2,1,0:T(2,128)} %get-tuple-element.43) | copy-start | bytes 1540
  34.5 24.2 %copy-start.10 = (f32[1,1,2176]{2,1,0:T(1,128)S(1)}, f32[1,1,2176]{2,1,0:T(1,128)}, u32[]{:S(2)}) copy-start(f32[1,1,2176]{2,1,0:T(1,128)} %get-tuple-element.52) | copy-start | bytes 26116
  52.7 32.8 %all-to-all-start.1 = ((bf16[2,4,64,2176]{3,2,0,1:T(8,128)(2,1)}), bf16[2,4,64,2176]{3,2,0,1:T(8,128)(2,1)}, u32[]{:S(2)}, u32[]{:S(2)}) async-start(bf16[2,4,64,2176]{3,2,0,1:T(8,128)(2,1)} %pad_maximum_fusion.1), calls=%async_computation.1 | async-start | bytes 4456448 | tf_op jit(solution)/shard_map/all_to_all | solution.py:116
  60.3 38.8 %collective-permute-start = (bf16[256,2176]{1,0:T(8,128)(2,1)}, bf16[256,2176]{1,0:T(8,128)(2,1)S(1)}, u32[]{:S(2)}, u32[]{:S(2)}) collective-permute-start(bf16[256,2176]{1,0:T(8,128)(2,1)} %bitcast.6), channel_id=1, source_target_pairs={{0,1},{1,2},{2,3},{3,4},{4,5},{5,6},{6,7},{7,8},{8,9},{9,10},{10,1... | collective-permute-start | bytes 3342344 | tf_op jit(solution)/shard_map/ppermute | solution.py:117
  62.2 32.1 %copy-start.9 = (f32[1,1,2176]{2,1,0:T(1,128)S(1)}, f32[1,1,2176]{2,1,0:T(1,128)}, u32[]{:S(2)}) copy-start(f32[1,1,2176]{2,1,0:T(1,128)} %get-tuple-element.51) | copy-start | bytes 26116
  62.2 36.9 %collective-permute-start.1 = (bf16[256,2176]{1,0:T(8,128)(2,1)}, bf16[256,2176]{1,0:T(8,128)(2,1)}, u32[]{:S(2)}, u32[]{:S(2)}) collective-permute-start(bf16[256,2176]{1,0:T(8,128)(2,1)} %bitcast.7), channel_id=1, source_target_pairs={{1,0},{2,1},{3,2},{4,3},{5,4},{6,5},{7,6},{8,7},{9,8},{10,9},{11,1... | collective-permute-start | bytes 3342344 | tf_op jit(solution)/shard_map/ppermute | solution.py:118
  88.5 24.4 %collective-permute-start.4 = (bf16[256,2176]{1,0:T(8,128)(2,1)}, bf16[256,2176]{1,0:T(8,128)(2,1)}, u32[]{:S(2)}, u32[]{:S(2)}) collective-permute-start(bf16[256,2176]{1,0:T(8,128)(2,1)} %bitcast.30), channel_id=1, source_target_pairs={{0,1},{1,2},{2,3},{3,4},{4,5},{5,6},{6,7},{7,8},{8,9},{9,10},{10,1... | collective-permute-start | bytes 3342344 | tf_op jit(solution)/shard_map/ppermute | solution.py:117
  90.4 22.5 %collective-permute-start.5 = (bf16[256,2176]{1,0:T(8,128)(2,1)}, bf16[256,2176]{1,0:T(8,128)(2,1)}, u32[]{:S(2)}, u32[]{:S(2)}) collective-permute-start(bf16[256,2176]{1,0:T(8,128)(2,1)} %bitcast.31), channel_id=1, source_target_pairs={{1,0},{2,1},{3,2},{4,3},{5,4},{6,5},{7,6},{8,7},{9,8},{10,9},{11,1... | collective-permute-start | bytes 3342344 | tf_op jit(solution)/shard_map/ppermute | solution.py:118
  94.3 4.8 %copy-start.8 = (f32[6,2,2176]{2,1,0:T(2,128)}, f32[6,2,2176]{2,1,0:T(2,128)S(1)}, u32[]{:S(2)}) copy-start(f32[6,2,2176]{2,1,0:T(2,128)S(1)} %fusion.1.coef_ref) | copy-start | bytes 313348
  99.1 1.0 copy-start.6
  100.1 8.4 %copy-start = (bf16[2,4,64,2176]{3,2,1,0:T(8,128)(2,1)S(1)}, bf16[2,4,64,2176]{3,2,1,0:T(8,128)(2,1)}, u32[]{:S(2)}) copy-start(bf16[2,4,64,2176]{3,2,1,0:T(8,128)(2,1)} %copy.26) | copy-start | bytes 6684676
  108.5 2.6 %copy-start.1 = (bf16[2,4,64,2176]{3,2,1,0:T(8,128)(2,1)S(1)}, bf16[2,4,64,2176]{3,2,1,0:T(8,128)(2,1)}, u32[]{:S(2)}) copy-start(bf16[2,4,64,2176]{3,2,1,0:T(8,128)(2,1)} %copy.31) | copy-start | bytes 6684676
  108.5 3.0 %copy-start.3 = (bf16[2,256,2176]{2,1,0:T(8,128)(2,1)S(1)}, bf16[2,256,2176]{2,1,0:T(8,128)(2,1)}, u32[]{:S(2)}) copy-start(bf16[2,256,2176]{2,1,0:T(8,128)(2,1)} %shard_map.28) | copy-start | bytes 6684676
  121.2 3.2 %copy-start.2 = (bf16[2,256,2176]{2,1,0:T(8,128)(2,1)S(1)}, bf16[2,256,2176]{2,1,0:T(8,128)(2,1)}, u32[]{:S(2)}) copy-start(bf16[2,256,2176]{2,1,0:T(8,128)(2,1)} %shard_map.29) | copy-start | bytes 6684676
  124.4 1.0 copy-start.7

commit v8 on v5

--- a/solution.py
+++ b/solution.py
@@ -90,6 +90,20 @@
     return jnp.stack(pieces, axis=-3)
 
 
+def exchanged(pieces, me, nodes):
+    def shift(value, by):
+        return lax.ppermute(value, "node", [(i, (i + by) % nodes) for i in range(nodes)])
+
+    half = pieces.shape[2] // 2
+    far = jnp.take(pieces, (me + 2) % nodes, axis=1)
+    leg_up = shift(far[:, :half], 1)
+    leg_down = shift(far[:, half:], -1)
+    from_below = shift(jnp.take(pieces, (me + 1) % nodes, axis=1), 1)
+    from_above = shift(jnp.take(pieces, (me - 1) % nodes, axis=1), -1)
+    far = jnp.concatenate([shift(leg_up, 1), shift(leg_down, -1)], axis=1)
+    return jnp.stack([jnp.take(pieces, me, axis=1), from_below, far, from_above], axis=1)
+
+
 def per_device(snapshots, kappa):
     rows, planes, width = snapshots.shape
     nodes = lax.axis_size("node")
@@ -113,7 +127,7 @@
     images, fields = [], []
     for g in range(GROUPS):
         pieces = chunked(major[:, g * step:(g + 1) * step], nodes)
-        field = lax.all_to_all(pieces, "node", 1, 1, tiled=True).reshape(planes, nodes * step, span)
+        field = exchanged(pieces, me, nodes).reshape(planes, nodes * step, span)
         below = lax.ppermute(field[1], SPACE, up)
         above = lax.ppermute(field[0], SPACE, down)
         images.append(stencil(field, below, above, coef))
@@ -124,10 +138,11 @@
             lax.dot_general(im, fd, dims, preferred_element_type=jnp.float32)
             for fd in fields], axis=1)
         for im in images], axis=0)
-    part = part.reshape(GROUPS, nodes, step, snaps)
-    total = jnp.take(part, me, axis=1)
+    part = part.reshape(GROUPS, nodes, step, GROUPS, nodes, step)
+    part = jnp.take(part, (me - jnp.arange(nodes)) % nodes, axis=4).reshape(GROUPS, nodes, step, snaps)
+    total = part[:, 0]
     for d in range(1, nodes):
-        blk = jnp.take(part, (me + d) % nodes, axis=1)
+        blk = part[:, (nodes - d) % nodes]
         total = total + lax.ppermute(blk, "node", [(i, (i + d) % nodes) for i in range(nodes)])
     total = total.reshape(rows, GROUPS, nodes, step).transpose(0, 2, 1, 3)
     total = total.reshape((rows,) + tuple(sizes) + (snaps // spaces,))

time: 171 us -> 179 us (1.047); the launches traced: 168 us -> 178 us
  starting transfers between devices: 29.1 us -> 38.3 us
  waiting for transfers between devices: 47.5 us -> 41.8 us
  local copies, waits for them, and re-layouts: 32.1 us -> 36.5 us
  matrix products: 6.63 us -> 8.73 us
    all_to_all x2 -> x0, waiting for transfers between devices: 36 us -> none  [per_device(): lax.all_to_all(pieces, 'node', 1, 1, tiled=True)]
    ppermute x0 -> x12, waiting for transfers between devices: none -> 28 us  [shift(): lax.ppermute(value, 'node', [(i, (i + by) % nodes) for i in range(nodes)])]
    ppermute x0 -> x12, starting transfers between devices: none -> 19.1 us  [shift(): lax.ppermute(value, 'node', [(i, (i + by) % nodes) for i in range(nodes)])]
    all_to_all x2 -> x0, starting transfers between devices: 8.91 us -> none  [per_device(): lax.all_to_all(pieces, 'node', 1, 1, tiled=True)]
    gather x0 -> x3, local copies, waits for them, and re-layouts: none -> 6.3 us  [per_device(): jnp.take(part, (me - jnp.arange(nodes)) % nodes, axis=4)]
    all_to_all x2 -> x0, local copies, waits for them, and re-layouts: 4.74 us -> none  [per_device(): lax.all_to_all(pieces, 'node', 1, 1, tiled=True)]
    reshape x0 -> x2, local copies, waits for them, and re-layouts: none -> 4.34 us  [per_device(): part = part.reshape(GROUPS, nodes, step, GROUPS, nodes, step)]
    another operation x6, other arithmetic: 4.5 us -> 1 us  [chunked(): return jnp.stack(pieces, axis=-3)]
  transfers between devices with their start and end apart: 11 -> 21, of which waited for: 4 -> 7; matrix products, arithmetic and copies ran while one was open for 21% -> 11% of each run, Pallas kernels for 5% -> 5%
where the time goes in v8:
time: 179 us; the launch traced here: 178 us
  waiting for transfers between devices  41.8 us (23%)
  starting transfers between devices  38.3 us (21%)
  local copies, waits for them, and re-layouts  36.5 us (20%)
  blocking collectives  29.2 us (16%)
  Pallas kernels  16.6 us (9%)
  matrix products  8.73 us (5%)
  other arithmetic  6.63 us (4%)
    all_to_all x3, blocking collectives, per_device(): total = lax.all_to_all(total, SPACE[axis], 0, 0, tiled=True).sum(axis=0)  29.2 us
    ppermute x12, waiting for transfers between devices, shift(): lax.ppermute(value, 'node', [(i, (i + by) % nodes) for i in range(nodes)])  28 us
    ppermute x12, starting transfers between devices, shift(): lax.ppermute(value, 'node', [(i, (i + by) % nodes) for i in range(nodes)])  19.1 us
    pallas_call x2, Pallas kernels, stencil(): pl.pallas_call(stencil_kernel, grid=(snaps // ROWS,), in_specs=[pl.BlockS...  16.6 us
    ppermute x3, waiting for transfers between devices, per_device(): lax.ppermute(blk, 'node', [(i, (i + d) % nodes) for i in range(nodes)])  13.8 us
    unnamed x49, local copies, waits for them, and re-layouts  8.85 us
    dot_general x4, matrix products, per_device(): lax.dot_general(im, fd, dims, preferred_element_type=jnp.float32)  8.73 us
    ppermute x2, starting transfers between devices, per_device(): above = lax.ppermute(field[0], SPACE, down)  7.08 us
  transfers between devices with their start and end apart: 21, of which 7 were waited for; matrix products, arithmetic and copies ran while one was open for 11% of the time, Pallas kernels for 5%

profile of v8, /device:TPU:8, one launch (start us, length us, event | category | flops | bytes accessed | tf_op | source)
XLA Modules:
  0.0 178.3 jit_solution(18106294135995536510)
XLA Ops:
  0.0 4.9 %copy.55 = bf16[128,2,8192]{2,0,1:T(8,128)(2,1)S(1)} copy(bf16[128,2,8192]{2,1,0:T(2,128)(2,1)} %param.4) | data formatting | bytes 8388608 | tf_op args[0]
  4.9 1.0 fusion.31
  5.9 0.7 fusion.30
  6.6 1.3 fusion.29
  7.9 1.9 %pad_bitcast_fusion = (bf16[2,1,64,2176]{3,2,0,1:T(8,128)(2,1)}, bf16[2,1,64,2176]{3,2,0,1:T(8,128)(2,1)S(1)}) fusion(bf16[2,64,2112]{2,1,0:T(8,128)(2,1)} %get-tuple-element.35, bf16[2,64,2112]{2,1,0:T(8,128)(2,1)S(1)} %get-tuple-element.32), kind=kLoop, calls=%fused_computation.25 | loop fusion | bytes 2195456 | tf_op jit(solution)/shard_map/stack | solution.py:90
  9.8 1.9 %concatenate.158 = bf16[2,64,2176]{2,1,0:T(8,128)(2,1)} concatenate(bf16[2,64,2048]{2,1,0:T(8,128)(2,1)} %get-tuple-element.45, bf16[2,64,64]{2,1,0:T(8,128)(2,1)S(1)} %broadcast.281, bf16[2,64,64]{2,1,0:T(8,128)(2,1)} %get-tuple-element.39), dimensions={2} | concatenate | bytes 1114112 | tf_op jit(solution)/shard_map/concatenate | solution.py:89
  11.9 0.9 copy-done.6
  12.8 0.3 pad_maximum_fusion.2
  13.2 1.3 dynamic-slice_select_fusion
  14.5 2.8 %collective-permute-start.15 = (bf16[2,64,2176]{2,1,0:T(8,128)(2,1)}, bf16[2,64,2176]{2,1,0:T(8,128)(2,1)}, u32[]{:S(2)}, u32[]{:S(2)}) collective-permute-start(bf16[2,64,2176]{2,1,0:T(8,128)(2,1)} %get-tuple-element.55), channel_id=1, source_target_pairs={{0,192},{64,0},{128,64},{192,128},{1,193},{65,1},{129,65},{193,129... | collective-permute-start | bytes 1671176 | tf_op jit(solution)/shard_map/ppermute | solution.py:95
  17.2 0.8 fusion.35
  18.1 0.8 collective-permute-start.13
  18.9 1.2 collective-permute-start.11
  20.5 0.7 slice_reduce_fusion
  21.2 1.9 %collective-permute-start.8 = (bf16[2176]{0:T(1024)(128)(2,1)}, bf16[2176]{0:T(1024)(128)(2,1)}, u32[]{:S(2)}, u32[]{:S(2)}) collective-permute-start(bf16[2176]{0:T(1024)(128)(2,1)} %get-tuple-element.29), channel_id=1, source_target_pairs={{0,1},{1,2},{2,3},{3,4},{4,5},{5,6},{6,7},{7,8},{8,9},{9,10},{10,1... | collective-permute-start | bytes 13064 | tf_op jit(solution)/shard_map/ppermute | solution.py:121
  23.1 0.6 slice_bitcast_fusion.10
  23.8 0.7 slice_bitcast_fusion.6
  24.4 0.6 fusion.18
  25.0 0.6 slice_bitcast_fusion.8
  25.7 0.7 slice_bitcast_fusion.4
  26.4 0.6 fusion.38
  27.4 0.3 pad_maximum_fusion
  28.1 0.3 copy-done.14
  29.1 3.6 %collective-permute-start.9 = (bf16[2176]{0:T(1024)(128)(2,1)S(1)}, bf16[2176]{0:T(1024)(128)(2,1)S(1)}, u32[]{:S(2)}, u32[]{:S(2)}) collective-permute-start(bf16[2176]{0:T(1024)(128)(2,1)S(1)} %copy-done.18), channel_id=1, source_target_pairs={{1,0},{2,1},{3,2},{4,3},{5,4},{6,5},{7,6},{8,7},{9,8},{10,9},{11,1... | collective-permute-start | bytes 13064 | tf_op jit(solution)/shard_map/ppermute | solution.py:122
  32.7 0.7 reshape.504
  33.4 2.0 %collective-permute-done.13 = bf16[2,32,2176]{2,1,0:T(8,128)(2,1)} collective-permute-done((bf16[2,32,2176]{2,1,0:T(8,128)(2,1)}, bf16[2,32,2176]{2,1,0:T(8,128)(2,1)}, u32[]{:S(2)}, u32[]{:S(2)}) %collective-permute-start.13) | collective-permute-done | bytes 278560 | tf_op jit(solution)/shard_map/ppermute | solution.py:95
  35.4 3.7 %collective-permute-start.14 = (bf16[2,32,2176]{2,1,0:T(8,128)(2,1)}, bf16[2,32,2176]{2,1,0:T(8,128)(2,1)S(1)}, u32[]{:S(2)}, u32[]{:S(2)}) collective-permute-start(bf16[2,32,2176]{2,1,0:T(8,128)(2,1)} %collective-permute-done.13), channel_id=1, source_target_pairs={{0,192},{64,0},{128,64},{192,128},{1,193},{65,1},{129,65},{193,129... | collective-permute-start | bytes 835592 | tf_op jit(solution)/shard_map/ppermute | solution.py:95
  39.1 3.3 %collective-permute-start.5 = (bf16[2,64,2176]{2,1,0:T(8,128)(2,1)S(1)}, bf16[2,64,2176]{2,1,0:T(8,128)(2,1)S(1)}, u32[]{:S(2)}, u32[]{:S(2)}) collective-permute-start(bf16[2,64,2176]{2,1,0:T(8,128)(2,1)S(1)} %get-tuple-element.49), channel_id=1, source_target_pairs={{0,192},{64,0},{128,64},{192,128},{1,193},{65,1},{129,65},{193,129... | collective-permute-start | bytes 1671176 | tf_op jit(solution)/shard_map/ppermute | solution.py:95
  42.5 4.1 %collective-permute-done.14 = bf16[2,32,2176]{2,1,0:T(8,128)(2,1)S(1)} collective-permute-done((bf16[2,32,2176]{2,1,0:T(8,128)(2,1)}, bf16[2,32,2176]{2,1,0:T(8,128)(2,1)S(1)}, u32[]{:S(2)}, u32[]{:S(2)}) %collective-permute-start.14) | collective-permute-done | bytes 278560 | tf_op jit(solution)/shard_map/ppermute | solution.py:95
  46.5 3.6 %collective-permute-start.3 = (bf16[2,32,2176]{2,1,0:T(8,128)(2,1)S(1)}, bf16[2,32,2176]{2,1,0:T(8,128)(2,1)S(1)}, u32[]{:S(2)}, u32[]{:S(2)}) collective-permute-start(bf16[2,32,2176]{2,1,0:T(8,128)(2,1)S(1)} %get-tuple-element.62), channel_id=1, source_target_pairs={{0,192},{64,0},{128,64},{192,128},{1,193},{65,1},{129,65},{193,129... | collective-permute-start | bytes 835592 | tf_op jit(solution)/shard_map/ppermute | solution.py:95
  50.2 12.1 %collective-permute-done.3 = bf16[2,32,2176]{2,1,0:T(8,128)(2,1)S(1)} collective-permute-done((bf16[2,32,2176]{2,1,0:T(8,128)(2,1)S(1)}, bf16[2,32,2176]{2,1,0:T(8,128)(2,1)S(1)}, u32[]{:S(2)}, u32[]{:S(2)}) %collective-permute-start.3) | collective-permute-done | bytes 278560 | tf_op jit(solution)/shard_map/ppermute | solution.py:95
  62.2 3.7 %collective-permute-start.4 = (bf16[2,32,2176]{2,1,0:T(8,128)(2,1)S(1)}, bf16[2,32,2176]{2,1,0:T(8,128)(2,1)S(1)}, u32[]{:S(2)}, u32[]{:S(2)}) collective-permute-start(bf16[2,32,2176]{2,1,0:T(8,128)(2,1)S(1)} %collective-permute-done.3), channel_id=1, source_target_pairs={{0,192},{64,0},{128,64},{192,128},{1,193},{65,1},{129,65},{193,129... | collective-permute-start | bytes 835592 | tf_op jit(solution)/shard_map/ppermute | solution.py:95
  66.0 1.6 pad_maximum_fusion.3
  67.7 1.9 %collective-permute-start.16 = (bf16[256,2176]{1,0:T(8,128)(2,1)S(1)}, bf16[256,2176]{1,0:T(8,128)(2,1)}, u32[]{:S(2)}, u32[]{:S(2)}) collective-permute-start(bf16[256,2176]{1,0:T(8,128)(2,1)S(1)} %bitcast.141), channel_id=1, source_target_pairs={{0,1},{1,2},{2,3},{3,4},{4,5},{5,6},{6,7},{7,8},{8,9},{9,10},{10,1... | collective-permute-start | bytes 3342344 | tf_op jit(solution)/shard_map/ppermute | solution.py:131
  69.6 0.4 collective-permute-done.4
  70.1 3.2 %collective-permute-start.17 = (bf16[256,2176]{1,0:T(8,128)(2,1)S(1)}, bf16[256,2176]{1,0:T(8,128)(2,1)S(1)}, u32[]{:S(2)}, u32[]{:S(2)}) collective-permute-start(bf16[256,2176]{1,0:T(8,128)(2,1)S(1)} %bitcast.140), channel_id=1, source_target_pairs={{1,0},{2,1},{3,2},{4,3},{5,4},{6,5},{7,6},{8,7},{9,8},{10,9},{11,1... | collective-permute-start | bytes 3342344 | tf_op jit(solution)/shard_map/ppermute | solution.py:132
  73.3 9.4 %collective-permute-done.2 = bf16[2,32,2176]{2,1,0:T(8,128)(2,1)S(1)} collective-permute-done((bf16[2,32,2176]{2,1,0:T(8,128)(2,1)S(1)}, bf16[2,32,2176]{2,1,0:T(8,128)(2,1)S(1)}, u32[]{:S(2)}, u32[]{:S(2)}) %collective-permute-start.2) | collective-permute-done | bytes 278560 | tf_op jit(solution)/shard_map/ppermute | solution.py:95
  82.8 0.3 pad_maximum_fusion.1
  83.1 1.7 fusion.32
  84.9 1.9 %collective-permute-start.6 = (bf16[256,2176]{1,0:T(8,128)(2,1)}, bf16[256,2176]{1,0:T(8,128)(2,1)S(1)}, u32[]{:S(2)}, u32[]{:S(2)}) collective-permute-start(bf16[256,2176]{1,0:T(8,128)(2,1)} %bitcast.16), channel_id=1, source_target_pairs={{0,1},{1,2},{2,3},{3,4},{4,5},{5,6},{6,7},{7,8},{8,9},{9,10},{10,1... | collective-permute-start | bytes 3342344 | tf_op jit(solution)/shard_map/ppermute | solution.py:131
  86.8 3.9 %collective-permute-start.7 = (bf16[256,2176]{1,0:T(8,128)(2,1)}, bf16[256,2176]{1,0:T(8,128)(2,1)}, u32[]{:S(2)}, u32[]{:S(2)}) collective-permute-start(bf16[256,2176]{1,0:T(8,128)(2,1)} %bitcast.17), channel_id=1, source_target_pairs={{1,0},{2,1},{3,2},{4,3},{5,4},{6,5},{7,6},{8,7},{9,8},{10,9},{11,1... | collective-permute-start | bytes 3342344 | tf_op jit(solution)/shard_map/ppermute | solution.py:132
  90.7 1.6 copy.40
  92.3 1.0 copy-done.8
  93.3 8.3 %shard_map.29 = bf16[2,256,2176]{2,1,0:T(8,128)(2,1)} custom-call(bf16[2,256,2176]{2,1,0:T(8,128)(2,1)} %bitcast.130, bf16[256,2176]{1,0:T(8,128)(2,1)} %collective-permute-done.16.below_ref, bf16[256,2176]{1,0:T(8,128)(2,1)} %copy-done.8, f32[6,2,2176]{2,1,0:T(2,128)} %copy-done.12), custom_call_target="tpu_custom_call" | custom-call | tf_op jit(solution)/shard_map/pallas_call | solution.py:56
  101.6 3.9 %convolution_bitcast_fusion = f32[256,256]{0,1:T(8,128)} fusion(bf16[2,256,2176]{2,1,0:T(8,128)(2,1)} %shard_map.29, bf16[2,256,2176]{2,1,0:T(8,128)(2,1)} %bitcast.131), kind=kOutput, calls=%fused_computation.6 | convolution fusion | flops 570425344 | bytes 4718592 | tf_op jit(solution)/shard_map/dot_general | solution.py:138
  105.5 1.5 convolution_bitcast_fusion.1
  107.0 1.0 copy-done.9
  108.0 8.3 %shard_map.28 = bf16[2,256,2176]{2,1,0:T(8,128)(2,1)} custom-call(bf16[2,256,2176]{2,1,0:T(8,128)(2,1)} %bitcast.128, bf16[256,2176]{1,0:T(8,128)(2,1)} %copy-done.9, bf16[256,2176]{1,0:T(8,128)(2,1)} %collective-permute-done.7.above_ref, f32[6,2,2176]{2,1,0:T(2,128)} %copy-done.12), custom_call_target="tpu_custom_call" | custom-call | tf_op jit(solution)/shard_map/pallas_call | solution.py:56
  116.3 2.5 %convolution_bitcast_fusion.2 = f32[256,256]{0,1:T(8,128)S(1)} fusion(bf16[2,256,2176]{2,1,0:T(8,128)(2,1)} %shard_map.28, bf16[2,256,2176]{2,1,0:T(8,128)(2,1)S(1)} %bitcast.132), kind=kOutput, calls=%fused_computation.8 | convolution fusion | flops 570425344 | bytes 4718592 | tf_op jit(solution)/shard_map/dot_general | solution.py:138
  118.9 0.4 copy-done.3
  119.3 0.8 convolution_bitcast_fusion.3
  120.5 2.4 %reshape.361 = f32[2,4,64,2,4,64]{2,1,0,5,4,3:T(4,128)} reshape(f32[512,512]{0,1:T(8,128)S(1)} %maximum_maximum_fusion) | data formatting | bytes 2097152 | tf_op jit(solution)/shard_map/reshape | solution.py:141
  122.9 1.9 %copy.41 = f32[2,4,64,2,4,64]{5,2,4,3,1,0:T(8,128)S(1)} copy(f32[2,4,64,2,4,64]{2,1,0,5,4,3:T(4,128)} %reshape.361) | data formatting | bytes 2097152 | tf_op jit(solution)/shard_map/reshape | solution.py:141
  124.8 2.0 %gather_fusion = f32[4,2,4,64,2,64]{5,3,4,2,1,0:T(8,128)} fusion(f32[2,4,64,2,4,64]{5,2,4,3,1,0:T(8,128)S(1)} %copy.41, s32[1024]{0:T(1024)S(1)} %pad_clamp_fusion), kind=kCustom, calls=%fused_computation | custom fusion | bytes 2097168 | tf_op jit(solution)/shard_map/jit(_take)/gather | solution.py:142
  126.8 2.9 %copy.42 = f32[2,4,64,2,4,64]{5,4,3,2,1,0:T(4,128)S(1)} copy(f32[2,4,64,2,4,64]{5,2,3,1,0,4:T(8,128)} %bitcast.136) | data formatting | bytes 2097152 | tf_op jit(solution)/shard_map/jit(_take)/gather | solution.py:142
  129.8 1.3 gather.15
  131.3 1.8 %collective-permute-start.20 = (f32[2,64,512]{2,1,0:T(8,128)S(1)}, f32[2,64,512]{2,1,0:T(8,128)S(1)}, u32[]{:S(2)}, u32[]{:S(2)}) collective-permute-start(f32[2,64,512]{2,1,0:T(8,128)S(1)} %get-tuple-element.59), channel_id=1, source_target_pairs={{0,192},{64,0},{128,64},{192,128},{1,193},{65,1},{129,65},{193,129... | collective-permute-start | bytes 786440 | tf_op jit(solution)/shard_map/ppermute | solution.py:146
  133.1 1.0 collective-permute-start.18
  134.1 10.4 %collective-permute-done.20 = f32[2,64,512]{2,1,0:T(8,128)S(1)} collective-permute-done((f32[2,64,512]{2,1,0:T(8,128)S(1)}, f32[2,64,512]{2,1,0:T(8,128)S(1)}, u32[]{:S(2)}, u32[]{:S(2)}) %collective-permute-start.20) | collective-permute-done | bytes 262176 | tf_op jit(solution)/shard_map/ppermute | solution.py:146
  144.5 3.4 %collective-permute-done.18 = f32[2,64,512]{2,1,0:T(8,128)S(1)} collective-permute-done((f32[2,64,512]{2,1,0:T(8,128)S(1)}, f32[2,64,512]{2,1,0:T(8,128)S(1)}, u32[]{:S(2)}, u32[]{:S(2)}) %collective-permute-start.18) | collective-permute-done | bytes 262176 | tf_op jit(solution)/shard_map/ppermute | solution.py:146
  148.5 3.9 %all_to_all.15 = f32[2,128,8,4,8]{1,4,3,2,0:T(8,128)S(1)} all-to-all(f32[2,128,8,4,8]{1,4,3,2,0:T(8,128)S(1)} %copy.47), channel_id=1, replica_groups=mesh['node'=4,'z'=8,'y'=4,'core'=2] {'core'}, dimensions={0} | all-to-all | bytes 524288 | tf_op jit(solution)/shard_map/all_to_all | solution.py:151
  152.5 9.1 %all_to_all.16 = f32[4,128,8,8]{1,3,2,0:T(8,128)S(1)} all-to-all(f32[4,128,8,8]{1,3,2,0:T(8,128)S(1)} %copy.49), channel_id=1, replica_groups=mesh['node'=4,'z'=8,'y'=4,'core'=2] {'y'}, dimensions={0} | all-to-all | bytes 262144 | tf_op jit(solution)/shard_map/all_to_all | solution.py:151
  161.5 16.2 %all_to_all.17 = f32[8,128,8]{1,2,0:T(8,128)S(1)} all-to-all(f32[8,128,8]{1,2,0:T(8,128)S(1)} %bitcast.146), channel_id=1, replica_groups=mesh['node'=4,'z'=8,'y'=4,'core'=2] {'z'}, dimensions={0} | all-to-all | bytes 65536 | tf_op jit(solution)/shard_map/all_to_all | solution.py:151
  177.7 0.6 broadcast_multiply_fusion
  (104 shorter events, 3.5 us)
Async XLA Ops:
  9.8 2.1 %copy-start.5 = (bf16[2,1,64,2176]{3,2,0,1:T(8,128)(2,1)S(1)}, bf16[2,1,64,2176]{3,2,0,1:T(8,128)(2,1)}, u32[]{:S(2)}) copy-start(bf16[2,1,64,2176]{3,2,0,1:T(8,128)(2,1)} %get-tuple-element.84) | copy-start | bytes 1671172
  11.8 1.1 copy-start.6
  13.1 7.0 %copy-start.15 = (bf16[2,8192]{1,0:T(2,128)(2,1)S(1)}, bf16[2,8192]{1,0:T(2,128)(2,1)}, u32[]{:S(2)}) copy-start(bf16[2,8192]{1,0:T(2,128)(2,1)} %param.5) | copy-start | bytes 98308
  13.1 7.1 %copy-start.23 = (pred[2176]{0:T(1024)(128)(4,1)S(1)}, pred[2176]{0:T(1024)(128)(4,1)}, u32[]{:S(2)}) copy-start(pred[2176]{0:T(1024)(128)(4,1)} %constant.108.clone.1) | copy-start | bytes 6532
  13.2 13.8 %copy-start.7 = (bf16[2,64,2048]{2,1,0:T(8,128)(2,1)S(1)}, bf16[2,64,2048]{2,1,0:T(8,128)(2,1)}, u32[]{:S(2)}) copy-start(bf16[2,64,2048]{2,1,0:T(8,128)(2,1)} %get-tuple-element.44) | copy-start | bytes 1572868
  14.5 51.5 %collective-permute-start.15 = (bf16[2,64,2176]{2,1,0:T(8,128)(2,1)}, bf16[2,64,2176]{2,1,0:T(8,128)(2,1)}, u32[]{:S(2)}, u32[]{:S(2)}) collective-permute-start(bf16[2,64,2176]{2,1,0:T(8,128)(2,1)} %get-tuple-element.55), channel_id=1, source_target_pairs={{0,192},{64,0},{128,64},{192,128},{1,193},{65,1},{129,65},{193,129... | collective-permute-start | bytes 1671176 | tf_op jit(solution)/shard_map/ppermute | solution.py:95
  18.1 17.3 %collective-permute-start.13 = (bf16[2,32,2176]{2,1,0:T(8,128)(2,1)}, bf16[2,32,2176]{2,1,0:T(8,128)(2,1)}, u32[]{:S(2)}, u32[]{:S(2)}) collective-permute-start(bf16[2,32,2176]{2,1,0:T(8,128)(2,1)} %get-tuple-element.64), channel_id=1, source_target_pairs={{0,192},{64,0},{128,64},{192,128},{1,193},{65,1},{129,65},{193,129... | collective-permute-start | bytes 835592 | tf_op jit(solution)/shard_map/ppermute | solution.py:95
  18.9 20.2 %collective-permute-start.11 = (bf16[2,32,2176]{2,1,0:T(8,128)(2,1)}, bf16[2,32,2176]{2,1,0:T(8,128)(2,1)}, u32[]{:S(2)}, u32[]{:S(2)}) collective-permute-start(bf16[2,32,2176]{2,1,0:T(8,128)(2,1)} %get-tuple-element.63), channel_id=1, source_target_pairs={{0,64},{64,128},{128,192},{192,0},{1,65},{65,129},{129,193},{193,1... | collective-permute-start | bytes 835592 | tf_op jit(solution)/shard_map/ppermute | solution.py:95
  20.1 45.9 %collective-permute-start.10 = (bf16[2,64,2176]{2,1,0:T(8,128)(2,1)}, bf16[2,64,2176]{2,1,0:T(8,128)(2,1)}, u32[]{:S(2)}, u32[]{:S(2)}) collective-permute-start(bf16[2,64,2176]{2,1,0:T(8,128)(2,1)} %get-tuple-element.57), channel_id=1, source_target_pairs={{0,64},{64,128},{128,192},{192,0},{1,65},{65,129},{129,193},{193,1... | collective-permute-start | bytes 1671176 | tf_op jit(solution)/shard_map/ppermute | solution.py:95
  21.2 7.9 %collective-permute-start.8 = (bf16[2176]{0:T(1024)(128)(2,1)}, bf16[2176]{0:T(1024)(128)(2,1)}, u32[]{:S(2)}, u32[]{:S(2)}) collective-permute-start(bf16[2176]{0:T(1024)(128)(2,1)} %get-tuple-element.29), channel_id=1, source_target_pairs={{0,1},{1,2},{2,3},{3,4},{4,5},{5,6},{6,7},{7,8},{8,9},{9,10},{10,1... | collective-permute-start | bytes 13064 | tf_op jit(solution)/shard_map/ppermute | solution.py:121
  27.7 0.7 copy-start.14
  27.7 0.7 copy-start.17
  27.7 0.7 copy-start.22
  27.7 0.8 copy-start.20
  27.7 0.9 copy-start.13
  27.8 0.9 copy-start.21
  27.8 1.0 copy-start.19
  27.8 1.3 copy-start.18
  27.8 11.3 %copy-start.16 = (f32[1,1,2176]{2,1,0:T(1,128)S(1)}, f32[1,1,2176]{2,1,0:T(1,128)}, u32[]{:S(2)}) copy-start(f32[1,1,2176]{2,1,0:T(1,128)} %get-tuple-element.79) | copy-start | bytes 26116
  29.1 10.1 %collective-permute-start.9 = (bf16[2176]{0:T(1024)(128)(2,1)S(1)}, bf16[2176]{0:T(1024)(128)(2,1)S(1)}, u32[]{:S(2)}, u32[]{:S(2)}) collective-permute-start(bf16[2176]{0:T(1024)(128)(2,1)S(1)} %copy-done.18), channel_id=1, source_target_pairs={{1,0},{2,1},{3,2},{4,3},{5,4},{6,5},{7,6},{8,7},{9,8},{10,9},{11,1... | collective-permute-start | bytes 13064 | tf_op jit(solution)/shard_map/ppermute | solution.py:122
  35.4 11.1 %collective-permute-start.14 = (bf16[2,32,2176]{2,1,0:T(8,128)(2,1)}, bf16[2,32,2176]{2,1,0:T(8,128)(2,1)S(1)}, u32[]{:S(2)}, u32[]{:S(2)}) collective-permute-start(bf16[2,32,2176]{2,1,0:T(8,128)(2,1)} %collective-permute-done.13), channel_id=1, source_target_pairs={{0,192},{64,0},{128,64},{192,128},{1,193},{65,1},{129,65},{193,129... | collective-permute-start | bytes 835592 | tf_op jit(solution)/shard_map/ppermute | solution.py:95
  39.1 11.0 %collective-permute-start.12 = (bf16[2,32,2176]{2,1,0:T(8,128)(2,1)}, bf16[2,32,2176]{2,1,0:T(8,128)(2,1)S(1)}, u32[]{:S(2)}, u32[]{:S(2)}) collective-permute-start(bf16[2,32,2176]{2,1,0:T(8,128)(2,1)} %collective-permute-done.11), channel_id=1, source_target_pairs={{0,64},{64,128},{128,192},{192,0},{1,65},{65,129},{129,193},{193,1... | collective-permute-start | bytes 835592 | tf_op jit(solution)/shard_map/ppermute | solution.py:95
  39.1 43.6 %collective-permute-start.5 = (bf16[2,64,2176]{2,1,0:T(8,128)(2,1)S(1)}, bf16[2,64,2176]{2,1,0:T(8,128)(2,1)S(1)}, u32[]{:S(2)}, u32[]{:S(2)}) collective-permute-start(bf16[2,64,2176]{2,1,0:T(8,128)(2,1)S(1)} %get-tuple-element.49), channel_id=1, source_target_pairs={{0,192},{64,0},{128,64},{192,128},{1,193},{65,1},{129,65},{193,129... | collective-permute-start | bytes 1671176 | tf_op jit(solution)/shard_map/ppermute | solution.py:95
  46.5 15.7 %collective-permute-start.3 = (bf16[2,32,2176]{2,1,0:T(8,128)(2,1)S(1)}, bf16[2,32,2176]{2,1,0:T(8,128)(2,1)S(1)}, u32[]{:S(2)}, u32[]{:S(2)}) collective-permute-start(bf16[2,32,2176]{2,1,0:T(8,128)(2,1)S(1)} %get-tuple-element.62), channel_id=1, source_target_pairs={{0,192},{64,0},{128,64},{192,128},{1,193},{65,1},{129,65},{193,129... | collective-permute-start | bytes 835592 | tf_op jit(solution)/shard_map/ppermute | solution.py:95
  50.1 12.1 %collective-permute-start.1 = (bf16[2,32,2176]{2,1,0:T(8,128)(2,1)S(1)}, bf16[2,32,2176]{2,1,0:T(8,128)(2,1)S(1)}, u32[]{:S(2)}, u32[]{:S(2)}) collective-permute-start(bf16[2,32,2176]{2,1,0:T(8,128)(2,1)S(1)} %get-tuple-element.61), channel_id=1, source_target_pairs={{0,64},{64,128},{128,192},{192,0},{1,65},{65,129},{129,193},{193,1... | collective-permute-start | bytes 835592 | tf_op jit(solution)/shard_map/ppermute | solution.py:95
  62.2 20.6 %collective-permute-start = (bf16[2,64,2176]{2,1,0:T(8,128)(2,1)S(1)}, bf16[2,64,2176]{2,1,0:T(8,128)(2,1)S(1)}, u32[]{:S(2)}, u32[]{:S(2)}) collective-permute-start(bf16[2,64,2176]{2,1,0:T(8,128)(2,1)S(1)} %get-tuple-element.51), channel_id=1, source_target_pairs={{0,64},{64,128},{128,192},{192,0},{1,65},{65,129},{129,193},{193,1... | collective-permute-start | bytes 1671176 | tf_op jit(solution)/shard_map/ppermute | solution.py:95
  62.2 7.8 %collective-permute-start.4 = (bf16[2,32,2176]{2,1,0:T(8,128)(2,1)S(1)}, bf16[2,32,2176]{2,1,0:T(8,128)(2,1)S(1)}, u32[]{:S(2)}, u32[]{:S(2)}) collective-permute-start(bf16[2,32,2176]{2,1,0:T(8,128)(2,1)S(1)} %collective-permute-done.3), channel_id=1, source_target_pairs={{0,192},{64,0},{128,64},{192,128},{1,193},{65,1},{129,65},{193,129... | collective-permute-start | bytes 835592 | tf_op jit(solution)/shard_map/ppermute | solution.py:95
  65.9 16.8 %collective-permute-start.2 = (bf16[2,32,2176]{2,1,0:T(8,128)(2,1)S(1)}, bf16[2,32,2176]{2,1,0:T(8,128)(2,1)S(1)}, u32[]{:S(2)}, u32[]{:S(2)}) collective-permute-start(bf16[2,32,2176]{2,1,0:T(8,128)(2,1)S(1)} %collective-permute-done.1), channel_id=1, source_target_pairs={{0,64},{64,128},{128,192},{192,0},{1,65},{65,129},{129,193},{193,1... | collective-permute-start | bytes 835592 | tf_op jit(solution)/shard_map/ppermute | solution.py:95
  67.7 24.6 %collective-permute-start.16 = (bf16[256,2176]{1,0:T(8,128)(2,1)S(1)}, bf16[256,2176]{1,0:T(8,128)(2,1)}, u32[]{:S(2)}, u32[]{:S(2)}) collective-permute-start(bf16[256,2176]{1,0:T(8,128)(2,1)S(1)} %bitcast.141), channel_id=1, source_target_pairs={{0,1},{1,2},{2,3},{3,4},{4,5},{5,6},{6,7},{7,8},{8,9},{9,10},{10,1... | collective-permute-start | bytes 3342344 | tf_op jit(solution)/shard_map/ppermute | solution.py:131
  70.1 22.2 %collective-permute-start.17 = (bf16[256,2176]{1,0:T(8,128)(2,1)S(1)}, bf16[256,2176]{1,0:T(8,128)(2,1)S(1)}, u32[]{:S(2)}, u32[]{:S(2)}) collective-permute-start(bf16[256,2176]{1,0:T(8,128)(2,1)S(1)} %bitcast.140), channel_id=1, source_target_pairs={{1,0},{2,1},{3,2},{4,3},{5,4},{6,5},{7,6},{8,7},{9,8},{10,9},{11,1... | collective-permute-start | bytes 3342344 | tf_op jit(solution)/shard_map/ppermute | solution.py:132
  83.1 22.4 %copy-start = (bf16[2,4,64,2176]{3,2,1,0:T(8,128)(2,1)}, bf16[2,4,64,2176]{3,2,1,0:T(8,128)(2,1)S(1)}, u32[]{:S(2)}) copy-start(bf16[2,4,64,2176]{3,2,1,0:T(8,128)(2,1)S(1)} %pad_maximum_fusion.1) | copy-start | bytes 6684676
  84.9 22.1 %collective-permute-start.6 = (bf16[256,2176]{1,0:T(8,128)(2,1)}, bf16[256,2176]{1,0:T(8,128)(2,1)S(1)}, u32[]{:S(2)}, u32[]{:S(2)}) collective-permute-start(bf16[256,2176]{1,0:T(8,128)(2,1)} %bitcast.16), channel_id=1, source_target_pairs={{0,1},{1,2},{2,3},{3,4},{4,5},{5,6},{6,7},{7,8},{8,9},{9,10},{10,1... | collective-permute-start | bytes 3342344 | tf_op jit(solution)/shard_map/ppermute | solution.py:131
  86.8 20.2 %collective-permute-start.7 = (bf16[256,2176]{1,0:T(8,128)(2,1)}, bf16[256,2176]{1,0:T(8,128)(2,1)}, u32[]{:S(2)}, u32[]{:S(2)}) collective-permute-start(bf16[256,2176]{1,0:T(8,128)(2,1)} %bitcast.17), channel_id=1, source_target_pairs={{1,0},{2,1},{3,2},{4,3},{5,4},{6,5},{7,6},{8,7},{9,8},{10,9},{11,1... | collective-permute-start | bytes 3342344 | tf_op jit(solution)/shard_map/ppermute | solution.py:132
  90.7 1.6 copy-start.12
  92.3 1.0 copy-start.8
  101.6 3.9 %copy-start.4 = (bf16[2,256,2176]{2,1,0:T(8,128)(2,1)S(1)}, bf16[2,256,2176]{2,1,0:T(8,128)(2,1)}, u32[]{:S(2)}) copy-start(bf16[2,256,2176]{2,1,0:T(8,128)(2,1)} %shard_map.29) | copy-start | bytes 6684676
  107.0 9.3 %copy-start.2 = (bf16[2,4,64,2176]{3,2,1,0:T(8,128)(2,1)S(1)}, bf16[2,4,64,2176]{3,2,1,0:T(8,128)(2,1)}, u32[]{:S(2)}) copy-start(bf16[2,4,64,2176]{3,2,1,0:T(8,128)(2,1)} %copy.40) | copy-start | bytes 6684676
  107.0 1.0 copy-start.9
  116.3 2.6 %copy-start.1 = (bf16[2,4,64,2176]{3,2,1,0:T(8,128)(2,1)S(1)}, bf16[2,4,64,2176]{3,2,1,0:T(8,128)(2,1)}, u32[]{:S(2)}) copy-start(bf16[2,4,64,2176]{3,2,1,0:T(8,128)(2,1)} %copy-done) | copy-start | bytes 6684676
  116.3 3.0 %copy-start.3 = (bf16[2,256,2176]{2,1,0:T(8,128)(2,1)S(1)}, bf16[2,256,2176]{2,1,0:T(8,128)(2,1)}, u32[]{:S(2)}) copy-start(bf16[2,256,2176]{2,1,0:T(8,128)(2,1)} %shard_map.28) | copy-start | bytes 6684676
  119.3 0.9 copy-start.10
  119.3 1.0 copy-start.11
  131.3 13.2 %collective-permute-start.20 = (f32[2,64,512]{2,1,0:T(8,128)S(1)}, f32[2,64,512]{2,1,0:T(8,128)S(1)}, u32[]{:S(2)}, u32[]{:S(2)}) collective-permute-start(f32[2,64,512]{2,1,0:T(8,128)S(1)} %get-tuple-element.59), channel_id=1, source_target_pairs={{0,192},{64,0},{128,64},{192,128},{1,193},{65,1},{129,65},{193,129... | collective-permute-start | bytes 786440 | tf_op jit(solution)/shard_map/ppermute | solution.py:146
  133.1 11.3 %collective-permute-start.19 = (f32[2,64,512]{2,1,0:T(8,128)S(1)}, f32[2,64,512]{2,1,0:T(8,128)S(1)}, u32[]{:S(2)}, u32[]{:S(2)}) collective-permute-start(f32[2,64,512]{2,1,0:T(8,128)S(1)} %get-tuple-element.60), channel_id=1, source_target_pairs={{0,128},{64,192},{128,0},{192,64},{1,129},{65,193},{129,1},{193,65... | collective-permute-start | bytes 786440 | tf_op jit(solution)/shard_map/ppermute | solution.py:146
  133.1 14.7 %collective-permute-start.18 = (f32[2,64,512]{2,1,0:T(8,128)S(1)}, f32[2,64,512]{2,1,0:T(8,128)S(1)}, u32[]{:S(2)}, u32[]{:S(2)}) collective-permute-start(f32[2,64,512]{2,1,0:T(8,128)S(1)} %get-tuple-element.58), channel_id=1, source_target_pairs={{0,64},{64,128},{128,192},{192,0},{1,65},{65,129},{129,193},{193,1... | collective-permute-start | bytes 786440 | tf_op jit(solution)/shard_map/ppermute | solution.py:146

commit v9 on v5

--- a/solution.py
+++ b/solution.py
@@ -27,9 +27,6 @@
 def stencil_kernel(x_ref, below_ref, above_ref, coef_ref, out_ref):
     span = below_ref.shape[1]
     lane = lax.broadcasted_iota(jnp.int32, (1, span), 1)
-    zpos = lane % NZ
-    up_ok = zpos != NZ - 1
-    down_ok = zpos != 0
     inner = lane < span - 2 * NZ
     planes = [x_ref[p].astype(jnp.float32) for p in range(2)]
     below = below_ref[...].astype(jnp.float32)
@@ -40,14 +37,13 @@
         def coef(t):
             return coef_ref[t, p:p + 1, :]
 
-        near = jnp.where(up_ok, pltpu.roll(v, span - 1, 1), 0.0)
-        total = coef(0) * (v - near)
-        near = jnp.where(down_ok, pltpu.roll(v, 1, 1), 0.0)
-        total = total + coef(1) * (v - near)
-        total = total + coef(2) * (v - pltpu.roll(v, span - NZ, 1))
-        total = total + coef(3) * (v - pltpu.roll(v, NZ, 1))
-        total = total + coef(4) * (v - (below if p == 0 else planes[0]))
-        total = total + coef(5) * (v - (planes[1] if p == 0 else above))
+        near = coef(0) * pltpu.roll(v, span - 1, 1)
+        near = near + coef(1) * pltpu.roll(v, 1, 1)
+        near = near + coef(2) * pltpu.roll(v, span - NZ, 1)
+        near = near + coef(3) * pltpu.roll(v, NZ, 1)
+        near = near + coef(4) * (below if p == 0 else planes[0])
+        near = near + coef(5) * (planes[1] if p == 0 else above)
+        total = coef(6) * v - near
         out_ref[p] = jnp.where(inner, total, 0.0).astype(out_ref.dtype)
 
 
@@ -76,7 +72,10 @@
     k_xm = jnp.stack([kap_below.astype(jnp.float32), kc[0]])
     k_xp = jnp.stack([kc[1], kap_above.astype(jnp.float32)])
     near = [k_zp, k_zm, jnp.roll(kc, -NZ, axis=-1), jnp.roll(kc, NZ, axis=-1), k_xm, k_xp]
-    return jnp.stack([0.5 * (kc + k) for k in near])
+    zmask = [zpos != NZ - 1, zpos != 0, True, True, True, True]
+    w = [0.5 * (kc + k) for k in near]
+    diag = w[0] + w[1] + w[2] + w[3] + w[4] + w[5]
+    return jnp.stack([jnp.where(m, wt, 0.0) for m, wt in zip(zmask, w)] + [diag])
 
 
 def chunked(values, nodes):

time: 171 us -> 171 us (level)
  other arithmetic: 7.5 us -> 11 us
  waiting for transfers between devices: 47.5 us -> 44.5 us
    all_to_all x2, waiting for transfers between devices: 36 us -> 32.9 us  [per_device(): lax.all_to_all(pieces, 'node', 1, 1, tiled=True)]
    unnamed x29 -> x27, local copies, waits for them, and re-layouts: 6.68 us -> 7.27 us
  transfers between devices with their start and end apart: 11 -> 11, of which waited for: 4 -> 4; matrix products, arithmetic and copies ran while one was open for 21% -> 23% of each run, Pallas kernels for 5% -> 5%
where the time goes in v9:
time: 171 us; the launch traced here: 168 us
  waiting for transfers between devices  44.5 us (26%)
  local copies, waits for them, and re-layouts  32.6 us (19%)
  starting transfers between devices  29.1 us (17%)
  blocking collectives  28.6 us (17%)
  Pallas kernels  15.7 us (9%)
  other arithmetic  11 us (6%)
  matrix products  6.63 us (4%)
    all_to_all x2, waiting for transfers between devices, per_device(): lax.all_to_all(pieces, 'node', 1, 1, tiled=True)  32.9 us
    all_to_all x3, blocking collectives, per_device(): total = lax.all_to_all(total, SPACE[axis], 0, 0, tiled=True).sum(axis=0)  28.6 us
    pallas_call x2, Pallas kernels, stencil(): pl.pallas_call(stencil_kernel, grid=(snaps // ROWS,), in_specs=[pl.BlockS...  15.7 us
    ppermute x3, waiting for transfers between devices, per_device(): lax.ppermute(blk, 'node', [(i, (i + d) % nodes) for i in range(nodes)])  11.6 us
    all_to_all x2, starting transfers between devices, per_device(): lax.all_to_all(pieces, 'node', 1, 1, tiled=True)  8.91 us
    ppermute x2, starting transfers between devices, per_device(): above = lax.ppermute(field[0], SPACE, down)  7.29 us
    unnamed x27, local copies, waits for them, and re-layouts  7.27 us
    dot_general x4, matrix products, per_device(): lax.dot_general(im, fd, dims, preferred_element_type=jnp.float32)  6.63 us
  transfers between devices with their start and end apart: 11, of which 4 were waited for; matrix products, arithmetic and copies ran while one was open for 23% of the time, Pallas kernels for 5%

profile of v9, /device:TPU:8, one launch (start us, length us, event | category | flops | bytes accessed | tf_op | source)
XLA Modules:
  0.0 168.4 jit_solution(17174818310349243969)
XLA Ops:
  0.0 0.8 fusion.29
  0.8 0.8 fusion.28
  1.6 0.7 slice.239
  2.3 0.7 fusion.20
  3.3 0.7 slice_reduce_fusion
  3.9 1.9 %collective-permute-start.2 = (bf16[2176]{0:T(1024)(128)(2,1)}, bf16[2176]{0:T(1024)(128)(2,1)}, u32[]{:S(2)}, u32[]{:S(2)}) collective-permute-start(bf16[2176]{0:T(1024)(128)(2,1)} %get-tuple-element.29), channel_id=1, source_target_pairs={{0,1},{1,2},{2,3},{3,4},{4,5},{5,6},{6,7},{7,8},{8,9},{9,10},{10,1... | collective-permute-start | bytes 13064 | tf_op jit(solution)/shard_map/ppermute | solution.py:106
  5.8 3.6 %collective-permute-start.3 = (bf16[2176]{0:T(1024)(128)(2,1)}, bf16[2176]{0:T(1024)(128)(2,1)}, u32[]{:S(2)}, u32[]{:S(2)}) collective-permute-start(bf16[2176]{0:T(1024)(128)(2,1)} %get-tuple-element.28), channel_id=1, source_target_pairs={{1,0},{2,1},{3,2},{4,3},{5,4},{6,5},{7,6},{8,7},{9,8},{10,9},{11,1... | collective-permute-start | bytes 13064 | tf_op jit(solution)/shard_map/ppermute | solution.py:107
  9.5 4.9 %copy.65 = bf16[128,2,8192]{2,0,1:T(8,128)(2,1)S(1)} copy(bf16[128,2,8192]{2,1,0:T(2,128)(2,1)} %param.4) | data formatting | bytes 8388608 | tf_op args[0]
  14.4 1.3 fusion.23
  15.6 0.7 fusion.24
  16.4 1.1 fusion.25
  17.5 1.2 concatenate.155
  18.8 1.7 %pad_maximum_fusion = bf16[2,4,64,2176]{3,2,0,1:T(8,128)(2,1)} fusion(bf16[2,1,64,2176]{3,2,0,1:T(8,128)(2,1)S(1)} %bitcast.120, bf16[2,1,64,2176]{3,2,0,1:T(8,128)(2,1)S(1)} %get-tuple-element.68, bf16[2,1,64,2176]{3,2,0,1:T(8,128)(2,1)S(1)} %get-tuple-element.67, bf16[2,1,64,2176]{3,2,0,1:T(8,128)(2,1)S(1)} %pad_bitcast_fusion.1), kind=kLoop, calls=%fused_computation.1 | loop fusion | flops 3342336 | bytes 4456448 | tf_op jit(solution)/shard_map/stack | solution.py:89
  20.5 4.4 %all-to-all-start = ((bf16[2,4,64,2176]{3,2,0,1:T(8,128)(2,1)}), bf16[2,4,64,2176]{3,2,0,1:T(8,128)(2,1)S(1)}, u32[]{:S(2)}, u32[]{:S(2)}) async-start(bf16[2,4,64,2176]{3,2,0,1:T(8,128)(2,1)} %pad_maximum_fusion), calls=%async_computation | async-start | bytes 4456448 | tf_op jit(solution)/shard_map/all_to_all | solution.py:115
  25.0 0.6 slice_bitcast_fusion.6
  25.7 0.6 fusion.14
  26.2 0.7 slice_bitcast_fusion
  26.9 0.6 slice_bitcast_fusion.4
  27.5 0.6 fusion.30
  28.2 1.9 %pad_bitcast_fusion = bf16[2,1,64,2176]{3,2,0,1:T(8,128)(2,1)} fusion(bf16[2,64,2112]{2,1,0:T(8,128)(2,1)} %get-tuple-element.35), kind=kLoop, calls=%fused_computation.12 | loop fusion | bytes 1097728 | tf_op jit(solution)/shard_map/stack | solution.py:89
  30.1 1.8 %concatenate.175 = bf16[2,64,2176]{2,1,0:T(8,128)(2,1)} concatenate(bf16[2,64,2048]{2,1,0:T(8,128)(2,1)} %get-tuple-element.45, bf16[2,64,64]{2,1,0:T(8,128)(2,1)S(1)} %broadcast.326, bf16[2,64,64]{2,1,0:T(8,128)(2,1)S(1)} %copy-done.9), dimensions={2} | concatenate | bytes 1114112 | tf_op jit(solution)/shard_map/concatenate | solution.py:88
  31.9 0.9 select_dynamic-update-slice_fusion.1
  32.8 0.8 select_dynamic-update-slice_fusion
  33.5 0.9 maximum_bitcast_fusion.2
  34.5 0.8 constant_dynamic-update-slice_fusion.3
  35.3 0.7 constant_dynamic-update-slice_fusion.2
  36.0 1.7 %pad_maximum_fusion.1 = bf16[2,4,64,2176]{3,2,0,1:T(8,128)(2,1)} fusion(bf16[2,1,64,2176]{3,2,0,1:T(8,128)(2,1)S(1)} %bitcast.119, bf16[2,1,64,2176]{3,2,0,1:T(8,128)(2,1)S(1)} %get-tuple-element.70, bf16[2,1,64,2176]{3,2,0,1:T(8,128)(2,1)S(1)} %get-tuple-element.69, bf16[2,1,64,2176]{3,2,0,1:T(8,128)(2,1)S(1)} %copy-done.5), kind=kLoop, calls=%fused_computation.2 | loop fusion | flops 3342336 | bytes 4456448 | tf_op jit(solution)/shard_map/stack | solution.py:89
  37.7 0.7 reshape.564
  38.4 14.4 %all-to-all-done = bf16[2,4,64,2176]{3,2,0,1:T(8,128)(2,1)S(1)} async-done(((bf16[2,4,64,2176]{3,2,0,1:T(8,128)(2,1)}), bf16[2,4,64,2176]{3,2,0,1:T(8,128)(2,1)S(1)}, u32[]{:S(2)}, u32[]{:S(2)}) %all-to-all-start) | async-done | bytes 2228256 | tf_op jit(solution)/shard_map/all_to_all | solution.py:115
  52.8 4.5 %all-to-all-start.1 = ((bf16[2,4,64,2176]{3,2,0,1:T(8,128)(2,1)}), bf16[2,4,64,2176]{3,2,0,1:T(8,128)(2,1)}, u32[]{:S(2)}, u32[]{:S(2)}) async-start(bf16[2,4,64,2176]{3,2,0,1:T(8,128)(2,1)} %pad_maximum_fusion.1), calls=%async_computation.1 | async-start | bytes 4456448 | tf_op jit(solution)/shard_map/all_to_all | solution.py:115
  57.4 0.7 reshape.565
  58.1 0.6 copy-done.12
  58.7 1.5 fusion.26
  60.2 1.9 %collective-permute-start = (bf16[256,2176]{1,0:T(8,128)(2,1)}, bf16[256,2176]{1,0:T(8,128)(2,1)S(1)}, u32[]{:S(2)}, u32[]{:S(2)}) collective-permute-start(bf16[256,2176]{1,0:T(8,128)(2,1)} %bitcast.6), channel_id=1, source_target_pairs={{0,1},{1,2},{2,3},{3,4},{4,5},{5,6},{6,7},{7,8},{8,9},{9,10},{10,1... | collective-permute-start | bytes 3342344 | tf_op jit(solution)/shard_map/ppermute | solution.py:116
  62.2 3.6 %collective-permute-start.1 = (bf16[256,2176]{1,0:T(8,128)(2,1)}, bf16[256,2176]{1,0:T(8,128)(2,1)}, u32[]{:S(2)}, u32[]{:S(2)}) collective-permute-start(bf16[256,2176]{1,0:T(8,128)(2,1)} %bitcast.7), channel_id=1, source_target_pairs={{1,0},{2,1},{3,2},{4,3},{5,4},{6,5},{7,6},{8,7},{9,8},{10,9},{11,1... | collective-permute-start | bytes 3342344 | tf_op jit(solution)/shard_map/ppermute | solution.py:117
  65.8 18.5 %all-to-all-done.1 = bf16[2,4,64,2176]{3,2,0,1:T(8,128)(2,1)} async-done(((bf16[2,4,64,2176]{3,2,0,1:T(8,128)(2,1)}), bf16[2,4,64,2176]{3,2,0,1:T(8,128)(2,1)}, u32[]{:S(2)}, u32[]{:S(2)}) %all-to-all-start.1) | async-done | bytes 2228256 | tf_op jit(solution)/shard_map/all_to_all | solution.py:115
  84.3 3.1 %fusion.27 = (bf16[1,4,64,2176]{3,2,1,0:T(8,128)(2,1)}, bf16[1,4,64,2176]{3,2,1,0:T(8,128)(2,1)}) fusion(bf16[2,4,64,2176]{3,2,0,1:T(8,128)(2,1)} %all-to-all-done.1), kind=kLoop, calls=%fused_computation.81 | loop fusion | bytes 4456448 | tf_op jit(solution)/shard_map/slice | solution.py:117
  87.4 1.9 %collective-permute-start.4 = (bf16[256,2176]{1,0:T(8,128)(2,1)}, bf16[256,2176]{1,0:T(8,128)(2,1)}, u32[]{:S(2)}, u32[]{:S(2)}) collective-permute-start(bf16[256,2176]{1,0:T(8,128)(2,1)} %bitcast.30), channel_id=1, source_target_pairs={{0,1},{1,2},{2,3},{3,4},{4,5},{5,6},{6,7},{7,8},{8,9},{9,10},{10,1... | collective-permute-start | bytes 3342344 | tf_op jit(solution)/shard_map/ppermute | solution.py:116
  89.3 3.6 %collective-permute-start.5 = (bf16[256,2176]{1,0:T(8,128)(2,1)}, bf16[256,2176]{1,0:T(8,128)(2,1)}, u32[]{:S(2)}, u32[]{:S(2)}) collective-permute-start(bf16[256,2176]{1,0:T(8,128)(2,1)} %bitcast.31), channel_id=1, source_target_pairs={{1,0},{2,1},{3,2},{4,3},{5,4},{6,5},{7,6},{8,7},{9,8},{10,9},{11,1... | collective-permute-start | bytes 3342344 | tf_op jit(solution)/shard_map/ppermute | solution.py:117
  93.0 0.9 add_dynamic-update-slice_fusion.coef_ref
  93.9 1.6 copy.40
  95.5 3.2 %copy.45 = bf16[2,4,64,2176]{3,2,1,0:T(8,128)(2,1)} copy(bf16[2,4,64,2176]{3,2,0,1:T(8,128)(2,1)} %all-to-all-done.1) | data formatting | bytes 4456448 | tf_op jit(solution)/shard_map/all_to_all | solution.py:115
  98.6 1.0 copy-done.7
  99.6 7.9 %shard_map.28 = bf16[2,256,2176]{2,1,0:T(8,128)(2,1)} custom-call(bf16[2,256,2176]{2,1,0:T(8,128)(2,1)} %bitcast.107, bf16[256,2176]{1,0:T(8,128)(2,1)} %copy-done.7, bf16[256,2176]{1,0:T(8,128)(2,1)} %collective-permute-done.1.above_ref, f32[7,2,2176]{2,1,0:T(2,128)} %copy-done.8), custom_call_target="tpu_custom_call" | custom-call | tf_op jit(solution)/shard_map/pallas_call | solution.py:52
  107.6 2.5 %convolution_bitcast_fusion.3 = f32[256,256]{0,1:T(8,128)S(1)} fusion(bf16[2,256,2176]{2,1,0:T(8,128)(2,1)} %shard_map.28, bf16[2,256,2176]{2,1,0:T(8,128)(2,1)S(1)} %bitcast.108), kind=kOutput, calls=%fused_computation.6 | convolution fusion | flops 570425344 | bytes 4718592 | tf_op jit(solution)/shard_map/dot_general | solution.py:123
  110.1 0.4 copy-done.4
  110.5 0.8 convolution_bitcast_fusion.2
  111.3 7.8 %shard_map.29 = bf16[2,256,2176]{2,1,0:T(8,128)(2,1)} custom-call(bf16[2,256,2176]{2,1,0:T(8,128)(2,1)} %bitcast.110, bf16[256,2176]{1,0:T(8,128)(2,1)} %collective-permute-done.4.below_ref, bf16[256,2176]{1,0:T(8,128)(2,1)} %collective-permute-done.5.above_ref, f32[7,2,2176]{2,1,0:T(2,128)} %copy-done.8), custom_call_target="tpu_custom_call" | custom-call | tf_op jit(solution)/shard_map/pallas_call | solution.py:52
  119.1 2.5 %convolution_bitcast_fusion.1 = f32[256,256]{0,1:T(8,128)S(1)} fusion(bf16[2,256,2176]{2,1,0:T(8,128)(2,1)} %shard_map.29, bf16[2,256,2176]{2,1,0:T(8,128)(2,1)S(1)} %bitcast.109), kind=kOutput, calls=%fused_computation.4 | convolution fusion | flops 570425344 | bytes 4718592 | tf_op jit(solution)/shard_map/dot_general | solution.py:123
  121.7 0.4 copy-done.3
  122.1 0.8 convolution_bitcast_fusion
  122.9 0.1 maximum_maximum_fusion
  123.0 0.3 copy.48
  123.4 0.6 collective-permute-start.6
  124.0 2.1 %collective-permute-start.7 = (f32[2,64,512]{2,1,0:T(8,128)S(1)}, f32[2,64,512]{2,1,0:T(8,128)S(1)}, u32[]{:S(2)}, u32[]{:S(2)}) collective-permute-start(f32[2,64,512]{2,1,0:T(8,128)S(1)} %get-tuple-element.51), channel_id=1, source_target_pairs={{0,128},{64,192},{128,0},{192,64},{1,129},{65,193},{129,1},{193,65... | collective-permute-start | bytes 786440 | tf_op jit(solution)/shard_map/ppermute | solution.py:130
  126.1 0.8 collective-permute-start.8
  126.9 10.9 %collective-permute-done.6 = f32[2,64,512]{2,1,0:T(8,128)S(1)} collective-permute-done((f32[2,64,512]{2,1,0:T(8,128)S(1)}, f32[2,64,512]{2,1,0:T(8,128)S(1)}, u32[]{:S(2)}, u32[]{:S(2)}) %collective-permute-start.6) | collective-permute-done | bytes 262176 | tf_op jit(solution)/shard_map/ppermute | solution.py:130
  137.9 0.6 collective-permute-done.8
  138.6 0.3 reshape.466
  138.9 0.2 copy.52
  139.1 3.9 %all_to_all.25 = f32[2,128,8,4,8]{1,4,3,2,0:T(8,128)S(1)} all-to-all(f32[2,128,8,4,8]{1,4,3,2,0:T(8,128)S(1)} %copy.53), channel_id=1, replica_groups=mesh['node'=4,'z'=8,'y'=4,'core'=2] {'core'}, dimensions={0} | all-to-all | bytes 524288 | tf_op jit(solution)/shard_map/all_to_all | solution.py:135
  143.1 9.6 %all_to_all.26 = f32[4,128,8,8]{1,3,2,0:T(8,128)S(1)} all-to-all(f32[4,128,8,8]{1,3,2,0:T(8,128)S(1)} %copy.55), channel_id=1, replica_groups=mesh['node'=4,'z'=8,'y'=4,'core'=2] {'y'}, dimensions={0} | all-to-all | bytes 262144 | tf_op jit(solution)/shard_map/all_to_all | solution.py:135
  152.7 15.1 %all_to_all.27 = f32[8,128,8]{1,2,0:T(8,128)S(1)} all-to-all(f32[8,128,8]{1,2,0:T(8,128)S(1)} %bitcast.124), channel_id=1, replica_groups=mesh['node'=4,'z'=8,'y'=4,'core'=2] {'z'}, dimensions={0} | all-to-all | bytes 65536 | tf_op jit(solution)/shard_map/all_to_all | solution.py:135
  167.8 0.6 broadcast_multiply_fusion
  (47 shorter events, 0.9 us)
Async XLA Ops:
  3.9 33.8 %collective-permute-start.2 = (bf16[2176]{0:T(1024)(128)(2,1)}, bf16[2176]{0:T(1024)(128)(2,1)}, u32[]{:S(2)}, u32[]{:S(2)}) collective-permute-start(bf16[2176]{0:T(1024)(128)(2,1)} %get-tuple-element.29), channel_id=1, source_target_pairs={{0,1},{1,2},{2,3},{3,4},{4,5},{5,6},{6,7},{7,8},{8,9},{9,10},{10,1... | collective-permute-start | bytes 13064 | tf_op jit(solution)/shard_map/ppermute | solution.py:106
  5.8 51.5 %collective-permute-start.3 = (bf16[2176]{0:T(1024)(128)(2,1)}, bf16[2176]{0:T(1024)(128)(2,1)}, u32[]{:S(2)}, u32[]{:S(2)}) collective-permute-start(bf16[2176]{0:T(1024)(128)(2,1)} %get-tuple-element.28), channel_id=1, source_target_pairs={{1,0},{2,1},{3,2},{4,3},{5,4},{6,5},{7,6},{8,7},{9,8},{10,9},{11,1... | collective-permute-start | bytes 13064 | tf_op jit(solution)/shard_map/ppermute | solution.py:107
  20.5 9.6 %copy-start.9 = (bf16[2,64,64]{2,1,0:T(8,128)(2,1)S(1)}, bf16[2,64,64]{2,1,0:T(8,128)(2,1)}, u32[]{:S(2)}) copy-start(bf16[2,64,64]{2,1,0:T(8,128)(2,1)} %get-tuple-element.39) | copy-start | bytes 49156
  20.5 32.3 %all-to-all-start = ((bf16[2,4,64,2176]{3,2,0,1:T(8,128)(2,1)}), bf16[2,4,64,2176]{3,2,0,1:T(8,128)(2,1)S(1)}, u32[]{:S(2)}, u32[]{:S(2)}) async-start(bf16[2,4,64,2176]{3,2,0,1:T(8,128)(2,1)} %pad_maximum_fusion), calls=%async_computation | async-start | bytes 4456448 | tf_op jit(solution)/shard_map/all_to_all | solution.py:115
  31.9 4.1 %copy-start.5 = (bf16[2,1,64,2176]{3,2,0,1:T(8,128)(2,1)S(1)}, bf16[2,1,64,2176]{3,2,0,1:T(8,128)(2,1)}, u32[]{:S(2)}) copy-start(bf16[2,1,64,2176]{3,2,0,1:T(8,128)(2,1)} %pad_bitcast_fusion) | copy-start | bytes 1671172
  31.9 4.1 %copy-start.6 = (bf16[2,64,2176]{2,1,0:T(8,128)(2,1)S(1)}, bf16[2,64,2176]{2,1,0:T(8,128)(2,1)}, u32[]{:S(2)}) copy-start(bf16[2,64,2176]{2,1,0:T(8,128)(2,1)} %concatenate.175) | copy-start | bytes 1671172
  38.4 18.9 %copy-start.11 = (f32[1,1,2176]{2,1,0:T(1,128)}, f32[1,1,2176]{2,1,0:T(1,128)S(1)}, u32[]{:S(2)}) copy-start(f32[1,1,2176]{2,1,0:T(1,128)S(1)} %reshape.564) | copy-start | bytes 26116
  38.4 18.9 %copy-start.10 = (f32[1,1,2176]{2,1,0:T(1,128)S(1)}, f32[1,1,2176]{2,1,0:T(1,128)}, u32[]{:S(2)}) copy-start(f32[1,1,2176]{2,1,0:T(1,128)} %get-tuple-element.66) | copy-start | bytes 26116
  52.8 31.5 %all-to-all-start.1 = ((bf16[2,4,64,2176]{3,2,0,1:T(8,128)(2,1)}), bf16[2,4,64,2176]{3,2,0,1:T(8,128)(2,1)}, u32[]{:S(2)}, u32[]{:S(2)}) async-start(bf16[2,4,64,2176]{3,2,0,1:T(8,128)(2,1)} %pad_maximum_fusion.1), calls=%async_computation.1 | async-start | bytes 4456448 | tf_op jit(solution)/shard_map/all_to_all | solution.py:115
  58.1 0.6 copy-start.12
  60.2 38.4 %collective-permute-start = (bf16[256,2176]{1,0:T(8,128)(2,1)}, bf16[256,2176]{1,0:T(8,128)(2,1)S(1)}, u32[]{:S(2)}, u32[]{:S(2)}) collective-permute-start(bf16[256,2176]{1,0:T(8,128)(2,1)} %bitcast.6), channel_id=1, source_target_pairs={{0,1},{1,2},{2,3},{3,4},{4,5},{5,6},{6,7},{7,8},{8,9},{9,10},{10,1... | collective-permute-start | bytes 3342344 | tf_op jit(solution)/shard_map/ppermute | solution.py:116
  62.2 36.5 %collective-permute-start.1 = (bf16[256,2176]{1,0:T(8,128)(2,1)}, bf16[256,2176]{1,0:T(8,128)(2,1)}, u32[]{:S(2)}, u32[]{:S(2)}) collective-permute-start(bf16[256,2176]{1,0:T(8,128)(2,1)} %bitcast.7), channel_id=1, source_target_pairs={{1,0},{2,1},{3,2},{4,3},{5,4},{6,5},{7,6},{8,7},{9,8},{10,9},{11,1... | collective-permute-start | bytes 3342344 | tf_op jit(solution)/shard_map/ppermute | solution.py:117
  87.4 23.9 %collective-permute-start.4 = (bf16[256,2176]{1,0:T(8,128)(2,1)}, bf16[256,2176]{1,0:T(8,128)(2,1)}, u32[]{:S(2)}, u32[]{:S(2)}) collective-permute-start(bf16[256,2176]{1,0:T(8,128)(2,1)} %bitcast.30), channel_id=1, source_target_pairs={{0,1},{1,2},{2,3},{3,4},{4,5},{5,6},{6,7},{7,8},{8,9},{9,10},{10,1... | collective-permute-start | bytes 3342344 | tf_op jit(solution)/shard_map/ppermute | solution.py:116
  89.3 22.0 %collective-permute-start.5 = (bf16[256,2176]{1,0:T(8,128)(2,1)}, bf16[256,2176]{1,0:T(8,128)(2,1)}, u32[]{:S(2)}, u32[]{:S(2)}) collective-permute-start(bf16[256,2176]{1,0:T(8,128)(2,1)} %bitcast.31), channel_id=1, source_target_pairs={{1,0},{2,1},{3,2},{4,3},{5,4},{6,5},{7,6},{8,7},{9,8},{10,9},{11,1... | collective-permute-start | bytes 3342344 | tf_op jit(solution)/shard_map/ppermute | solution.py:117
  93.9 1.6 copy-start.8
  98.6 1.0 copy-start.7
  99.6 7.9 %copy-start = (bf16[2,4,64,2176]{3,2,1,0:T(8,128)(2,1)S(1)}, bf16[2,4,64,2176]{3,2,1,0:T(8,128)(2,1)}, u32[]{:S(2)}) copy-start(bf16[2,4,64,2176]{3,2,1,0:T(8,128)(2,1)} %copy.40) | copy-start | bytes 6684676
  107.5 2.6 %copy-start.1 = (bf16[2,4,64,2176]{3,2,1,0:T(8,128)(2,1)S(1)}, bf16[2,4,64,2176]{3,2,1,0:T(8,128)(2,1)}, u32[]{:S(2)}) copy-start(bf16[2,4,64,2176]{3,2,1,0:T(8,128)(2,1)} %copy.45) | copy-start | bytes 6684676
  107.5 3.0 %copy-start.4 = (bf16[2,256,2176]{2,1,0:T(8,128)(2,1)S(1)}, bf16[2,256,2176]{2,1,0:T(8,128)(2,1)}, u32[]{:S(2)}) copy-start(bf16[2,256,2176]{2,1,0:T(8,128)(2,1)} %shard_map.28) | copy-start | bytes 6684676
  119.1 2.6 %copy-start.2 = (bf16[2,4,64,2176]{3,2,1,0:T(8,128)(2,1)S(1)}, bf16[2,4,64,2176]{3,2,1,0:T(8,128)(2,1)}, u32[]{:S(2)}) copy-start(bf16[2,4,64,2176]{3,2,1,0:T(8,128)(2,1)} %copy.45) | copy-start | bytes 6684676
  119.1 3.0 %copy-start.3 = (bf16[2,256,2176]{2,1,0:T(8,128)(2,1)S(1)}, bf16[2,256,2176]{2,1,0:T(8,128)(2,1)}, u32[]{:S(2)}) copy-start(bf16[2,256,2176]{2,1,0:T(8,128)(2,1)} %shard_map.29) | copy-start | bytes 6684676
  123.4 14.5 %collective-permute-start.6 = (f32[2,64,512]{2,1,0:T(8,128)S(1)}, f32[2,64,512]{2,1,0:T(8,128)S(1)}, u32[]{:S(2)}, u32[]{:S(2)}) collective-permute-start(f32[2,64,512]{2,1,0:T(8,128)S(1)} %get-tuple-element.50), channel_id=1, source_target_pairs={{0,64},{64,128},{128,192},{192,0},{1,65},{65,129},{129,193},{193,1... | collective-permute-start | bytes 786440 | tf_op jit(solution)/shard_map/ppermute | solution.py:130
  124.0 13.8 %collective-permute-start.7 = (f32[2,64,512]{2,1,0:T(8,128)S(1)}, f32[2,64,512]{2,1,0:T(8,128)S(1)}, u32[]{:S(2)}, u32[]{:S(2)}) collective-permute-start(f32[2,64,512]{2,1,0:T(8,128)S(1)} %get-tuple-element.51), channel_id=1, source_target_pairs={{0,128},{64,192},{128,0},{192,64},{1,129},{65,193},{129,1},{193,65... | collective-permute-start | bytes 786440 | tf_op jit(solution)/shard_map/ppermute | solution.py:130
  126.1 12.3 %collective-permute-start.8 = (f32[2,64,512]{2,1,0:T(8,128)S(1)}, f32[2,64,512]{2,1,0:T(8,128)S(1)}, u32[]{:S(2)}, u32[]{:S(2)}) collective-permute-start(f32[2,64,512]{2,1,0:T(8,128)S(1)} %select_bitcast_fusion), channel_id=1, source_target_pairs={{0,192},{64,0},{128,64},{192,128},{1,193},{65,1},{129,65},{193,129... | collective-permute-start | bytes 786440 | tf_op jit(solution)/shard_map/ppermute | solution.py:130

commit v10 on v9

--- a/solution.py
+++ b/solution.py
@@ -48,17 +48,17 @@
 
 
 def stencil(field, below, above, coef):
-    planes, snaps, span = field.shape
+    nodes, planes, step, span = field.shape
     return pl.pallas_call(
         stencil_kernel,
-        grid=(snaps // ROWS,),
+        grid=(nodes, step // ROWS),
         in_specs=[
-            pl.BlockSpec((planes, ROWS, span), lambda i: (0, i, 0)),
-            pl.BlockSpec((ROWS, span), lambda i: (i, 0)),
-            pl.BlockSpec((ROWS, span), lambda i: (i, 0)),
-            pl.BlockSpec(coef.shape, lambda i: (0, 0, 0)),
+            pl.BlockSpec((None, planes, ROWS, span), lambda a, i: (a, 0, i, 0)),
+            pl.BlockSpec((None, ROWS, span), lambda a, i: (a, i, 0)),
+            pl.BlockSpec((None, ROWS, span), lambda a, i: (a, i, 0)),
+            pl.BlockSpec(coef.shape, lambda a, i: (0, 0, 0)),
         ],
-        out_specs=pl.BlockSpec((planes, ROWS, span), lambda i: (0, i, 0)),
+        out_specs=pl.BlockSpec((None, planes, ROWS, span), lambda a, i: (a, 0, i, 0)),
         out_shape=jax.ShapeDtypeStruct(field.shape, jnp.bfloat16),
     )(field, below, above, coef)
 
@@ -86,7 +86,7 @@
         after = values[..., (q + 1) * chunk:(q + 1) * chunk + NZ] if q + 1 < nodes else zero
         before = values[..., q * chunk - NZ:q * chunk] if q > 0 else zero
         pieces.append(jnp.concatenate([values[..., q * chunk:(q + 1) * chunk], after, before], axis=-1))
-    return jnp.stack(pieces, axis=-3)
+    return jnp.stack(pieces, axis=0)
 
 
 def per_device(snapshots, kappa):
@@ -102,7 +102,7 @@
     up = [(i, i + 1) for i in range(spaces - 1)]
     down = [(j, i) for i, j in up]
 
-    kap_chunk = jnp.take(chunked(kappa[:, None], nodes)[:, :, 0], me, axis=1)
+    kap_chunk = jnp.take(chunked(kappa[:, None], nodes), me, axis=0)[:, 0]
     kap_below = lax.ppermute(kap_chunk[1], SPACE, up)
     kap_above = lax.ppermute(kap_chunk[0], SPACE, down)
     coef = weights(kap_chunk, kap_below, kap_above)
@@ -112,17 +112,18 @@
     images, fields = [], []
     for g in range(GROUPS):
         pieces = chunked(major[:, g * step:(g + 1) * step], nodes)
-        field = lax.all_to_all(pieces, "node", 1, 1, tiled=True).reshape(planes, nodes * step, span)
-        below = lax.ppermute(field[1], SPACE, up)
-        above = lax.ppermute(field[0], SPACE, down)
+        field = lax.all_to_all(pieces, "node", 0, 0, tiled=True)
+        below = lax.ppermute(field[:, 1], SPACE, up)
+        above = lax.ppermute(field[:, 0], SPACE, down)
         images.append(stencil(field, below, above, coef))
         fields.append(field)
-    dims = (((0, 2), (0, 2)), ((), ()))
+    dims = (((1, 3), (1, 3)), ((), ()))
     part = jnp.concatenate([
         jnp.concatenate([
-            lax.dot_general(im, fd, dims, preferred_element_type=jnp.float32)
+            lax.dot_general(im, fd, dims, preferred_element_type=jnp.float32).reshape(nodes * step, nodes * step)
             for fd in fields], axis=1)
         for im in images], axis=0)
+    part = part.reshape(snaps, snaps)
     part = part.reshape(GROUPS, nodes, step, snaps)
     total = jnp.take(part, me, axis=1)
     for d in range(1, nodes):

time: 171 us -> 174 us (1.018)
  matrix products: 6.63 us -> 13.1 us
  local copies, waits for them, and re-layouts: 32.6 us -> 28.6 us
  waiting for transfers between devices: 44.5 us -> 47.1 us
  other arithmetic: 11 us -> 8.92 us
    dot_general x4, matrix products: 6.63 us -> 13.1 us  [per_device(): lax.dot_general(im, fd, dims, preferred_element_type=jnp.float32)]
    all_to_all x2 -> x0, local copies, waits for them, and re-layouts: 4.74 us -> none  [per_device(): lax.all_to_all(pieces, 'node', 1, 1, tiled=True)]
    squeeze x0 -> x2, local copies, waits for them, and re-layouts: none -> 4.74 us  [per_device(): above = lax.ppermute(field[:, 0], SPACE, down)]
    slice x2 -> x0, local copies, waits for them, and re-layouts: 4.65 us -> none  [per_device(): above = lax.ppermute(field[0], SPACE, down)]
    all_to_all x2, waiting for transfers between devices: 32.9 us -> 35.6 us  [per_device(): field = lax.all_to_all(pieces, 'node', 0, 0, tiled=True)]
    unnamed x27 -> x45, local copies, waits for them, and re-layouts: 7.27 us -> 5.96 us
  transfers between devices with their start and end apart: 11 -> 11, of which waited for: 4 -> 4; matrix products, arithmetic and copies ran while one was open for 23% -> 21% of each run, Pallas kernels for 5% -> 5%
where the time goes in v10:
time: 174 us; the launch traced here: 172 us
  waiting for transfers between devices  47.1 us (27%)
  starting transfers between devices  29.2 us (17%)
  local copies, waits for them, and re-layouts  28.6 us (16%)
  blocking collectives  28.6 us (16%)
  Pallas kernels  15.7 us (9%)
  matrix products  13.1 us (8%)
  other arithmetic  8.92 us (5%)
    all_to_all x2, waiting for transfers between devices, per_device(): field = lax.all_to_all(pieces, 'node', 0, 0, tiled=True)  35.6 us
    all_to_all x3, blocking collectives, per_device(): total = lax.all_to_all(total, SPACE[axis], 0, 0, tiled=True).sum(axis=0)  28.6 us
    pallas_call x2, Pallas kernels, stencil(): pl.pallas_call(stencil_kernel, grid=(nodes, step // ROWS), in_specs=[pl.B...  15.7 us
    dot_general x4, matrix products, per_device(): lax.dot_general(im, fd, dims, preferred_element_type=jnp.float32)  13.1 us
    ppermute x3, waiting for transfers between devices, per_device(): lax.ppermute(blk, 'node', [(i, (i + d) % nodes) for i in range(nodes)])  11.6 us
    all_to_all x2, starting transfers between devices, per_device(): field = lax.all_to_all(pieces, 'node', 0, 0, tiled=True)  8.89 us
    ppermute x2, starting transfers between devices, per_device(): above = lax.ppermute(field[:, 0], SPACE, down)  7.47 us
    unnamed x45, local copies, waits for them, and re-layouts  5.96 us
  transfers between devices with their start and end apart: 11, of which 4 were waited for; matrix products, arithmetic and copies ran while one was open for 21% of the time, Pallas kernels for 5%

profile of v10, /device:TPU:8, one launch (start us, length us, event | category | flops | bytes accessed | tf_op | source)
XLA Modules:
  0.0 171.9 jit_solution(7623107859974124292)
XLA Ops:
  0.0 0.8 fusion.60
  0.8 0.8 fusion.59
  1.6 0.7 slice.241
  2.3 0.7 fusion.54
  3.2 0.7 fusion.55
  3.8 0.7 slice_reduce_fusion
  4.5 1.9 %collective-permute-start.2 = (bf16[2176]{0:T(1024)(128)(2,1)}, bf16[2176]{0:T(1024)(128)(2,1)}, u32[]{:S(2)}, u32[]{:S(2)}) collective-permute-start(bf16[2176]{0:T(1024)(128)(2,1)} %get-tuple-element.29), channel_id=1, source_target_pairs={{0,1},{1,2},{2,3},{3,4},{4,5},{5,6},{6,7},{7,8},{8,9},{9,10},{10,1... | collective-permute-start | bytes 13064 | tf_op jit(solution)/shard_map/ppermute | solution.py:106
  6.4 3.6 %collective-permute-start.3 = (bf16[2176]{0:T(1024)(128)(2,1)}, bf16[2176]{0:T(1024)(128)(2,1)}, u32[]{:S(2)}, u32[]{:S(2)}) collective-permute-start(bf16[2176]{0:T(1024)(128)(2,1)} %get-tuple-element.28), channel_id=1, source_target_pairs={{1,0},{2,1},{3,2},{4,3},{5,4},{6,5},{7,6},{8,7},{9,8},{10,9},{11,1... | collective-permute-start | bytes 13064 | tf_op jit(solution)/shard_map/ppermute | solution.py:107
  10.1 4.9 %copy.85 = bf16[128,2,8192]{2,0,1:T(8,128)(2,1)S(1)} copy(bf16[128,2,8192]{2,1,0:T(2,128)(2,1)} %param.4) | data formatting | bytes 8388608 | tf_op args[0]
  14.9 1.2 fusion.56
  16.2 0.7 fusion.57
  16.9 1.1 fusion.58
  18.0 1.2 concatenate.155
  19.2 0.1 maximum_bitcast_fusion
  19.3 1.7 %pad_maximum_fusion = bf16[4,2,64,2176]{3,2,1,0:T(8,128)(2,1)} fusion(bf16[1,2,64,2176]{3,2,1,0:T(8,128)(2,1)S(1)} %bitcast.192, bf16[1,2,64,2176]{3,2,1,0:T(8,128)(2,1)S(1)} %get-tuple-element.68, bf16[1,2,64,2176]{3,2,1,0:T(8,128)(2,1)S(1)} %get-tuple-element.67, bf16[1,2,64,2176]{3,2,1,0:T(8,128)(2,1)S(1)} %pad_bitcast_fusion.1), kind=kLoop, calls=%fused_computation.1 | loop fusion | flops 3342336 | bytes 4456448 | tf_op jit(solution)/shard_map/stack | solution.py:89
  21.1 4.4 %all-to-all-start = ((bf16[4,2,64,2176]{3,2,1,0:T(8,128)(2,1)}), bf16[4,2,64,2176]{3,2,1,0:T(8,128)(2,1)S(1)}, u32[]{:S(2)}, u32[]{:S(2)}) async-start(bf16[4,2,64,2176]{3,2,1,0:T(8,128)(2,1)} %pad_maximum_fusion), calls=%async_computation | async-start | bytes 4456448 | tf_op jit(solution)/shard_map/all_to_all | solution.py:115
  25.7 0.7 slice_bitcast_fusion.4
  26.4 0.6 slice_bitcast_fusion.10
  27.0 1.9 %pad_bitcast_fusion = bf16[1,2,64,2176]{3,2,1,0:T(8,128)(2,1)} fusion(bf16[2,64,2112]{2,1,0:T(8,128)(2,1)} %get-tuple-element.35), kind=kLoop, calls=%fused_computation.28 | loop fusion | bytes 1097728 | tf_op jit(solution)/shard_map/stack | solution.py:89
  28.9 1.8 %concatenate.175 = bf16[2,64,2176]{2,1,0:T(8,128)(2,1)} concatenate(bf16[2,64,2048]{2,1,0:T(8,128)(2,1)} %get-tuple-element.45, bf16[2,64,64]{2,1,0:T(8,128)(2,1)S(1)} %broadcast.348, bf16[2,64,64]{2,1,0:T(8,128)(2,1)S(1)} %copy-done.7), dimensions={2} | concatenate | bytes 1114112 | tf_op jit(solution)/shard_map/concatenate | solution.py:88
  31.0 0.9 constant_dynamic-update-slice_fusion.3
  31.9 0.9 maximum_bitcast_fusion.2
  32.8 0.7 constant_dynamic-update-slice_fusion.2
  33.5 0.8 slice_bitcast_fusion.8
  34.4 1.7 %pad_maximum_fusion.1 = bf16[4,2,64,2176]{3,2,1,0:T(8,128)(2,1)} fusion(bf16[1,2,64,2176]{3,2,1,0:T(8,128)(2,1)S(1)} %bitcast.191, bf16[1,2,64,2176]{3,2,1,0:T(8,128)(2,1)S(1)} %get-tuple-element.70, bf16[1,2,64,2176]{3,2,1,0:T(8,128)(2,1)S(1)} %get-tuple-element.69, bf16[1,2,64,2176]{3,2,1,0:T(8,128)(2,1)S(1)} %copy-done.2), kind=kLoop, calls=%fused_computation.2 | loop fusion | flops 3342336 | bytes 4456448 | tf_op jit(solution)/shard_map/stack | solution.py:89
  36.1 0.7 reshape.589
  36.8 16.6 %all-to-all-done.x_ref = bf16[4,2,64,2176]{3,2,1,0:T(8,128)(2,1)S(1)} async-done(((bf16[4,2,64,2176]{3,2,1,0:T(8,128)(2,1)}), bf16[4,2,64,2176]{3,2,1,0:T(8,128)(2,1)S(1)}, u32[]{:S(2)}, u32[]{:S(2)}) %all-to-all-start) | async-done | bytes 2228256 | tf_op jit(solution)/shard_map/all_to_all | solution.py:115
  53.4 4.5 %all-to-all-start.1 = ((bf16[4,2,64,2176]{3,2,1,0:T(8,128)(2,1)}), bf16[4,2,64,2176]{3,2,1,0:T(8,128)(2,1)}, u32[]{:S(2)}, u32[]{:S(2)}) async-start(bf16[4,2,64,2176]{3,2,1,0:T(8,128)(2,1)} %pad_maximum_fusion.1), calls=%async_computation.1 | async-start | bytes 4456448 | tf_op jit(solution)/shard_map/all_to_all | solution.py:115
  57.9 0.7 reshape.590
  58.7 1.6 slice_bitcast_fusion.2
  60.2 1.9 %collective-permute-start = (bf16[4,64,2176]{2,1,0:T(8,128)(2,1)}, bf16[4,64,2176]{2,1,0:T(8,128)(2,1)S(1)}, u32[]{:S(2)}, u32[]{:S(2)}) collective-permute-start(bf16[4,64,2176]{2,1,0:T(8,128)(2,1)} %get-tuple-element.47), channel_id=1, source_target_pairs={{0,1},{1,2},{2,3},{3,4},{4,5},{5,6},{6,7},{7,8},{8,9},{9,10},{10,1... | collective-permute-start | bytes 3342344 | tf_op jit(solution)/shard_map/ppermute | solution.py:116
  62.2 3.6 %collective-permute-start.1 = (bf16[4,64,2176]{2,1,0:T(8,128)(2,1)}, bf16[4,64,2176]{2,1,0:T(8,128)(2,1)}, u32[]{:S(2)}, u32[]{:S(2)}) collective-permute-start(bf16[4,64,2176]{2,1,0:T(8,128)(2,1)} %get-tuple-element.46), channel_id=1, source_target_pairs={{1,0},{2,1},{3,2},{4,3},{5,4},{6,5},{7,6},{8,7},{9,8},{10,9},{11,1... | collective-permute-start | bytes 3342344 | tf_op jit(solution)/shard_map/ppermute | solution.py:117
  65.9 19.0 %all-to-all-done.1.x_ref = bf16[4,2,64,2176]{3,2,1,0:T(8,128)(2,1)} async-done(((bf16[4,2,64,2176]{3,2,1,0:T(8,128)(2,1)}), bf16[4,2,64,2176]{3,2,1,0:T(8,128)(2,1)}, u32[]{:S(2)}, u32[]{:S(2)}) %all-to-all-start.1) | async-done | bytes 2228256 | tf_op jit(solution)/shard_map/all_to_all | solution.py:115
  84.9 3.2 %slice_bitcast_fusion = (bf16[4,64,2176]{2,1,0:T(8,128)(2,1)}, bf16[4,64,2176]{2,1,0:T(8,128)(2,1)}) fusion(bf16[4,2,64,2176]{3,2,1,0:T(8,128)(2,1)} %all-to-all-done.1.x_ref), kind=kLoop, calls=%fused_computation.19 | loop fusion | bytes 4456448 | tf_op jit(solution)/shard_map/squeeze | solution.py:117
  88.0 1.9 %collective-permute-start.4 = (bf16[4,64,2176]{2,1,0:T(8,128)(2,1)}, bf16[4,64,2176]{2,1,0:T(8,128)(2,1)}, u32[]{:S(2)}, u32[]{:S(2)}) collective-permute-start(bf16[4,64,2176]{2,1,0:T(8,128)(2,1)} %get-tuple-element.49), channel_id=1, source_target_pairs={{0,1},{1,2},{2,3},{3,4},{4,5},{5,6},{6,7},{7,8},{8,9},{9,10},{10,1... | collective-permute-start | bytes 3342344 | tf_op jit(solution)/shard_map/ppermute | solution.py:116
  90.0 3.8 %collective-permute-start.5 = (bf16[4,64,2176]{2,1,0:T(8,128)(2,1)}, bf16[4,64,2176]{2,1,0:T(8,128)(2,1)}, u32[]{:S(2)}, u32[]{:S(2)}) collective-permute-start(bf16[4,64,2176]{2,1,0:T(8,128)(2,1)} %get-tuple-element.48), channel_id=1, source_target_pairs={{1,0},{2,1},{3,2},{4,3},{5,4},{6,5},{7,6},{8,7},{9,8},{10,9},{11,1... | collective-permute-start | bytes 3342344 | tf_op jit(solution)/shard_map/ppermute | solution.py:117
  93.9 0.1 add_dynamic-update-slice_fusion.coef_ref
  94.1 0.6 copy-done.5
  94.7 0.4 copy-done.4
  95.1 7.9 %shard_map.28 = bf16[4,2,64,2176]{3,2,1,0:T(8,128)(2,1)} custom-call(bf16[4,2,64,2176]{3,2,1,0:T(8,128)(2,1)} %copy-done, bf16[4,64,2176]{2,1,0:T(8,128)(2,1)} %copy-done.4, bf16[4,64,2176]{2,1,0:T(8,128)(2,1)} %collective-permute-done.1.above_ref, f32[7,2,2176]{2,1,0:T(2,128)} %copy-done.5), custom_call_target="tpu_custom_call" | custom-call | tf_op jit(solution)/shard_map/pallas_call | solution.py:52
  102.9 2.9 %fusion.12 = f32[4,64,4,64]{3,1,2,0:T(8,128)S(1)} fusion(bf16[4,2,64,2176]{3,2,1,0:T(8,128)(2,1)S(1)} %copy-done.1, bf16[4,2,64,2176]{3,2,1,0:T(8,128)(2,1)} %shard_map.28), kind=kOutput, calls=%fused_computation.15 | convolution fusion | flops 570425344 | bytes 4718592 | tf_op jit(solution)/shard_map/dot_general | solution.py:123
  105.9 0.3 copy.57
  106.2 0.3 reshape.485
  106.6 3.6 %fusion.17 = f32[4,64,4,64]{3,1,2,0:T(8,128)S(1)} fusion(bf16[4,2,64,2176]{3,2,1,0:T(8,128)(2,1)} %all-to-all-done.1.x_ref, bf16[4,2,64,2176]{3,2,1,0:T(8,128)(2,1)} %shard_map.28), kind=kOutput, calls=%fused_computation.16 | convolution fusion | flops 570425344 | bytes 4718592 | tf_op jit(solution)/shard_map/dot_general | solution.py:123
  110.2 0.3 copy.58
  110.5 0.3 reshape.486
  110.9 7.8 %shard_map.29 = bf16[4,2,64,2176]{3,2,1,0:T(8,128)(2,1)} custom-call(bf16[4,2,64,2176]{3,2,1,0:T(8,128)(2,1)} %all-to-all-done.1.x_ref, bf16[4,64,2176]{2,1,0:T(8,128)(2,1)} %collective-permute-done.4.below_ref, bf16[4,64,2176]{2,1,0:T(8,128)(2,1)} %collective-permute-done.5.above_ref, f32[7,2,2176]{2,1,0:T(2,128)} %copy-done.5), custom_call_target="tpu_custom_call" | custom-call | tf_op jit(solution)/shard_map/pallas_call | solution.py:52
  118.7 2.9 %fusion.22 = f32[4,64,4,64]{3,1,2,0:T(8,128)S(1)} fusion(bf16[4,2,64,2176]{3,2,1,0:T(8,128)(2,1)S(1)} %copy-done.1, bf16[4,2,64,2176]{3,2,1,0:T(8,128)(2,1)} %shard_map.29), kind=kOutput, calls=%fused_computation.17 | convolution fusion | flops 570425344 | bytes 4718592 | tf_op jit(solution)/shard_map/dot_general | solution.py:123
  121.7 0.3 copy.61
  122.0 0.3 reshape.487
  122.4 3.6 %fusion.27 = f32[4,64,4,64]{3,1,2,0:T(8,128)S(1)} fusion(bf16[4,2,64,2176]{3,2,1,0:T(8,128)(2,1)} %all-to-all-done.1.x_ref, bf16[4,2,64,2176]{3,2,1,0:T(8,128)(2,1)} %shard_map.29), kind=kOutput, calls=%fused_computation.18 | convolution fusion | flops 570425344 | bytes 4718592 | tf_op jit(solution)/shard_map/dot_general | solution.py:123
  126.0 0.3 copy.62
  126.4 0.3 reshape.488
  126.9 0.6 collective-permute-start.6
  127.5 2.1 %collective-permute-start.7 = (f32[2,64,512]{2,1,0:T(8,128)S(1)}, f32[2,64,512]{2,1,0:T(8,128)S(1)}, u32[]{:S(2)}, u32[]{:S(2)}) collective-permute-start(f32[2,64,512]{2,1,0:T(8,128)S(1)} %get-tuple-element.51), channel_id=1, source_target_pairs={{0,128},{64,192},{128,0},{192,64},{1,129},{65,193},{129,1},{193,65... | collective-permute-start | bytes 786440 | tf_op jit(solution)/shard_map/ppermute | solution.py:131
  129.6 0.8 collective-permute-start.8
  130.4 10.9 %collective-permute-done.6 = f32[2,64,512]{2,1,0:T(8,128)S(1)} collective-permute-done((f32[2,64,512]{2,1,0:T(8,128)S(1)}, f32[2,64,512]{2,1,0:T(8,128)S(1)}, u32[]{:S(2)}, u32[]{:S(2)}) %collective-permute-start.6) | collective-permute-done | bytes 262176 | tf_op jit(solution)/shard_map/ppermute | solution.py:131
  141.3 0.6 collective-permute-done.8
  142.0 0.3 reshape.490
  142.3 0.2 copy.66
  142.6 3.9 %all_to_all.25 = f32[2,128,8,4,8]{1,4,3,2,0:T(8,128)S(1)} all-to-all(f32[2,128,8,4,8]{1,4,3,2,0:T(8,128)S(1)} %copy.67), channel_id=1, replica_groups=mesh['node'=4,'z'=8,'y'=4,'core'=2] {'core'}, dimensions={0} | all-to-all | bytes 524288 | tf_op jit(solution)/shard_map/all_to_all | solution.py:136
  146.6 9.6 %all_to_all.26 = f32[4,128,8,8]{1,3,2,0:T(8,128)S(1)} all-to-all(f32[4,128,8,8]{1,3,2,0:T(8,128)S(1)} %copy.69), channel_id=1, replica_groups=mesh['node'=4,'z'=8,'y'=4,'core'=2] {'y'}, dimensions={0} | all-to-all | bytes 262144 | tf_op jit(solution)/shard_map/all_to_all | solution.py:136
  156.1 15.1 %all_to_all.27 = f32[8,128,8]{1,2,0:T(8,128)S(1)} all-to-all(f32[8,128,8]{1,2,0:T(8,128)S(1)} %bitcast.196), channel_id=1, replica_groups=mesh['node'=4,'z'=8,'y'=4,'core'=2] {'z'}, dimensions={0} | all-to-all | bytes 65536 | tf_op jit(solution)/shard_map/all_to_all | solution.py:136
  171.3 0.6 broadcast_multiply_fusion
  (71 shorter events, 1.1 us)
Async XLA Ops:
  4.5 31.6 %collective-permute-start.2 = (bf16[2176]{0:T(1024)(128)(2,1)}, bf16[2176]{0:T(1024)(128)(2,1)}, u32[]{:S(2)}, u32[]{:S(2)}) collective-permute-start(bf16[2176]{0:T(1024)(128)(2,1)} %get-tuple-element.29), channel_id=1, source_target_pairs={{0,1},{1,2},{2,3},{3,4},{4,5},{5,6},{6,7},{7,8},{8,9},{9,10},{10,1... | collective-permute-start | bytes 13064 | tf_op jit(solution)/shard_map/ppermute | solution.py:106
  6.4 51.5 %collective-permute-start.3 = (bf16[2176]{0:T(1024)(128)(2,1)}, bf16[2176]{0:T(1024)(128)(2,1)}, u32[]{:S(2)}, u32[]{:S(2)}) collective-permute-start(bf16[2176]{0:T(1024)(128)(2,1)} %get-tuple-element.28), channel_id=1, source_target_pairs={{1,0},{2,1},{3,2},{4,3},{5,4},{6,5},{7,6},{8,7},{9,8},{10,9},{11,1... | collective-permute-start | bytes 13064 | tf_op jit(solution)/shard_map/ppermute | solution.py:107
  21.1 7.8 %copy-start.7 = (bf16[2,64,64]{2,1,0:T(8,128)(2,1)S(1)}, bf16[2,64,64]{2,1,0:T(8,128)(2,1)}, u32[]{:S(2)}) copy-start(bf16[2,64,64]{2,1,0:T(8,128)(2,1)} %get-tuple-element.39) | copy-start | bytes 49156
  21.1 32.3 %all-to-all-start = ((bf16[4,2,64,2176]{3,2,1,0:T(8,128)(2,1)}), bf16[4,2,64,2176]{3,2,1,0:T(8,128)(2,1)S(1)}, u32[]{:S(2)}, u32[]{:S(2)}) async-start(bf16[4,2,64,2176]{3,2,1,0:T(8,128)(2,1)} %pad_maximum_fusion), calls=%async_computation | async-start | bytes 4456448 | tf_op jit(solution)/shard_map/all_to_all | solution.py:115
  25.7 7.1 %copy-start.16 = (f32[1,2,1]{2,1,0:T(2,128)}, f32[1,2,1]{2,1,0:T(2,128)S(1)}, u32[]{:S(2)}) copy-start(f32[1,2,1]{2,1,0:T(2,128)S(1)} %get-tuple-element.63) | copy-start | bytes 28
  25.7 7.1 %copy-start.18 = (f32[1,2,1]{2,1,0:T(2,128)}, f32[1,2,1]{2,1,0:T(2,128)S(1)}, u32[]{:S(2)}) copy-start(f32[1,2,1]{2,1,0:T(2,128)S(1)} %get-tuple-element.64) | copy-start | bytes 28
  25.7 7.1 %copy-start.14 = (pred[2176]{0:T(1024)(128)(4,1)}, pred[2176]{0:T(1024)(128)(4,1)S(1)}, u32[]{:S(2)}) copy-start(pred[2176]{0:T(1024)(128)(4,1)S(1)} %get-tuple-element.74) | copy-start | bytes 6532
  30.8 3.6 %copy-start.2 = (bf16[1,2,64,2176]{3,2,1,0:T(8,128)(2,1)S(1)}, bf16[1,2,64,2176]{3,2,1,0:T(8,128)(2,1)}, u32[]{:S(2)}) copy-start(bf16[1,2,64,2176]{3,2,1,0:T(8,128)(2,1)} %pad_bitcast_fusion) | copy-start | bytes 1671172
  30.8 3.6 %copy-start.3 = (bf16[2,64,2176]{2,1,0:T(8,128)(2,1)S(1)}, bf16[2,64,2176]{2,1,0:T(8,128)(2,1)}, u32[]{:S(2)}) copy-start(bf16[2,64,2176]{2,1,0:T(8,128)(2,1)} %concatenate.175) | copy-start | bytes 1671172
  34.3 23.5 %copy-start.8 = (f32[1,1,2176]{2,1,0:T(1,128)}, f32[1,1,2176]{2,1,0:T(1,128)S(1)}, u32[]{:S(2)}) copy-start(f32[1,1,2176]{2,1,0:T(1,128)S(1)} %get-tuple-element.58) | copy-start | bytes 26116
  36.8 21.1 %copy-start.10 = (f32[1,1,2176]{2,1,0:T(1,128)}, f32[1,1,2176]{2,1,0:T(1,128)S(1)}, u32[]{:S(2)}) copy-start(f32[1,1,2176]{2,1,0:T(1,128)S(1)} %reshape.589) | copy-start | bytes 26116
  53.4 5.3 %copy-start = (bf16[4,2,64,2176]{3,2,1,0:T(8,128)(2,1)}, bf16[4,2,64,2176]{3,2,1,0:T(8,128)(2,1)S(1)}, u32[]{:S(2)}) copy-start(bf16[4,2,64,2176]{3,2,1,0:T(8,128)(2,1)S(1)} %all-to-all-done.x_ref) | copy-start | bytes 6684676
  53.4 31.5 %all-to-all-start.1 = ((bf16[4,2,64,2176]{3,2,1,0:T(8,128)(2,1)}), bf16[4,2,64,2176]{3,2,1,0:T(8,128)(2,1)}, u32[]{:S(2)}, u32[]{:S(2)}) async-start(bf16[4,2,64,2176]{3,2,1,0:T(8,128)(2,1)} %pad_maximum_fusion.1), calls=%async_computation.1 | async-start | bytes 4456448 | tf_op jit(solution)/shard_map/all_to_all | solution.py:115
  58.6 1.6 copy-start.12
  60.2 33.8 %collective-permute-start = (bf16[4,64,2176]{2,1,0:T(8,128)(2,1)}, bf16[4,64,2176]{2,1,0:T(8,128)(2,1)S(1)}, u32[]{:S(2)}, u32[]{:S(2)}) collective-permute-start(bf16[4,64,2176]{2,1,0:T(8,128)(2,1)} %get-tuple-element.47), channel_id=1, source_target_pairs={{0,1},{1,2},{2,3},{3,4},{4,5},{5,6},{6,7},{7,8},{8,9},{9,10},{10,1... | collective-permute-start | bytes 3342344 | tf_op jit(solution)/shard_map/ppermute | solution.py:116
  62.1 31.7 %copy-start.6 = (f32[1,2,2112]{2,1,0:T(2,128)S(1)}, f32[1,2,2112]{2,1,0:T(2,128)}, u32[]{:S(2)}) copy-start(f32[1,2,2112]{2,1,0:T(2,128)} %get-tuple-element.62) | copy-start | bytes 50692
  62.1 31.7 %copy-start.9 = (f32[1,1,2176]{2,1,0:T(1,128)S(1)}, f32[1,1,2176]{2,1,0:T(1,128)}, u32[]{:S(2)}) copy-start(f32[1,1,2176]{2,1,0:T(1,128)} %copy-done.8) | copy-start | bytes 26116
  62.2 31.7 %copy-start.11 = (f32[1,1,2176]{2,1,0:T(1,128)S(1)}, f32[1,1,2176]{2,1,0:T(1,128)}, u32[]{:S(2)}) copy-start(f32[1,1,2176]{2,1,0:T(1,128)} %copy-done.10) | copy-start | bytes 26116
  62.2 31.7 %copy-start.13 = (f32[1,1,2176]{2,1,0:T(1,128)S(1)}, f32[1,1,2176]{2,1,0:T(1,128)}, u32[]{:S(2)}) copy-start(f32[1,1,2176]{2,1,0:T(1,128)} %copy-done.12) | copy-start | bytes 26116
  62.2 31.7 %copy-start.15 = (pred[2176]{0:T(1024)(128)(4,1)S(1)}, pred[2176]{0:T(1024)(128)(4,1)}, u32[]{:S(2)}) copy-start(pred[2176]{0:T(1024)(128)(4,1)} %copy-done.14) | copy-start | bytes 6532
  62.2 31.7 %copy-start.17 = (f32[1,2,1]{2,1,0:T(2,128)S(1)}, f32[1,2,1]{2,1,0:T(2,128)}, u32[]{:S(2)}) copy-start(f32[1,2,1]{2,1,0:T(2,128)} %copy-done.16) | copy-start | bytes 28
  62.2 31.7 %copy-start.19 = (f32[1,2,1]{2,1,0:T(2,128)S(1)}, f32[1,2,1]{2,1,0:T(2,128)}, u32[]{:S(2)}) copy-start(f32[1,2,1]{2,1,0:T(2,128)} %copy-done.18) | copy-start | bytes 28
  62.2 31.7 %copy-start.20 = (f32[1,2,64]{2,1,0:T(2,128)S(1)}, f32[1,2,64]{2,1,0:T(2,128)}, u32[]{:S(2)}) copy-start(f32[1,2,64]{2,1,0:T(2,128)} %get-tuple-element.59) | copy-start | bytes 1540
  62.2 31.7 %copy-start.21 = (f32[1,2,64]{2,1,0:T(2,128)S(1)}, f32[1,2,64]{2,1,0:T(2,128)}, u32[]{:S(2)}) copy-start(f32[1,2,64]{2,1,0:T(2,128)} %get-tuple-element.60) | copy-start | bytes 1540
  62.2 31.8 %collective-permute-start.1 = (bf16[4,64,2176]{2,1,0:T(8,128)(2,1)}, bf16[4,64,2176]{2,1,0:T(8,128)(2,1)}, u32[]{:S(2)}, u32[]{:S(2)}) collective-permute-start(bf16[4,64,2176]{2,1,0:T(8,128)(2,1)} %get-tuple-element.46), channel_id=1, source_target_pairs={{1,0},{2,1},{3,2},{4,3},{5,4},{6,5},{7,6},{8,7},{9,8},{10,9},{11,1... | collective-permute-start | bytes 3342344 | tf_op jit(solution)/shard_map/ppermute | solution.py:117
  88.0 22.8 %collective-permute-start.4 = (bf16[4,64,2176]{2,1,0:T(8,128)(2,1)}, bf16[4,64,2176]{2,1,0:T(8,128)(2,1)}, u32[]{:S(2)}, u32[]{:S(2)}) collective-permute-start(bf16[4,64,2176]{2,1,0:T(8,128)(2,1)} %get-tuple-element.49), channel_id=1, source_target_pairs={{0,1},{1,2},{2,3},{3,4},{4,5},{5,6},{6,7},{7,8},{8,9},{9,10},{10,1... | collective-permute-start | bytes 3342344 | tf_op jit(solution)/shard_map/ppermute | solution.py:116
  90.0 20.9 %collective-permute-start.5 = (bf16[4,64,2176]{2,1,0:T(8,128)(2,1)}, bf16[4,64,2176]{2,1,0:T(8,128)(2,1)}, u32[]{:S(2)}, u32[]{:S(2)}) collective-permute-start(bf16[4,64,2176]{2,1,0:T(8,128)(2,1)} %get-tuple-element.48), channel_id=1, source_target_pairs={{1,0},{2,1},{3,2},{4,3},{5,4},{6,5},{7,6},{8,7},{9,8},{10,9},{11,1... | collective-permute-start | bytes 3342344 | tf_op jit(solution)/shard_map/ppermute | solution.py:117
  94.0 0.7 copy-start.5
  94.0 8.9 %copy-start.1 = (bf16[4,2,64,2176]{3,2,1,0:T(8,128)(2,1)S(1)}, bf16[4,2,64,2176]{3,2,1,0:T(8,128)(2,1)}, u32[]{:S(2)}) copy-start(bf16[4,2,64,2176]{3,2,1,0:T(8,128)(2,1)} %copy-done) | copy-start | bytes 6684676
  94.0 1.0 copy-start.4
  126.9 14.5 %collective-permute-start.6 = (f32[2,64,512]{2,1,0:T(8,128)S(1)}, f32[2,64,512]{2,1,0:T(8,128)S(1)}, u32[]{:S(2)}, u32[]{:S(2)}) collective-permute-start(f32[2,64,512]{2,1,0:T(8,128)S(1)} %get-tuple-element.50), channel_id=1, source_target_pairs={{0,64},{64,128},{128,192},{192,0},{1,65},{65,129},{129,193},{193,1... | collective-permute-start | bytes 786440 | tf_op jit(solution)/shard_map/ppermute | solution.py:131
  127.5 13.8 %collective-permute-start.7 = (f32[2,64,512]{2,1,0:T(8,128)S(1)}, f32[2,64,512]{2,1,0:T(8,128)S(1)}, u32[]{:S(2)}, u32[]{:S(2)}) collective-permute-start(f32[2,64,512]{2,1,0:T(8,128)S(1)} %get-tuple-element.51), channel_id=1, source_target_pairs={{0,128},{64,192},{128,0},{192,64},{1,129},{65,193},{129,1},{193,65... | collective-permute-start | bytes 786440 | tf_op jit(solution)/shard_map/ppermute | solution.py:131
  129.6 12.4 %collective-permute-start.8 = (f32[2,64,512]{2,1,0:T(8,128)S(1)}, f32[2,64,512]{2,1,0:T(8,128)S(1)}, u32[]{:S(2)}, u32[]{:S(2)}) collective-permute-start(f32[2,64,512]{2,1,0:T(8,128)S(1)} %select_bitcast_fusion), channel_id=1, source_target_pairs={{0,192},{64,0},{128,64},{192,128},{1,193},{65,1},{129,65},{193,129... | collective-permute-start | bytes 786440 | tf_op jit(solution)/shard_map/ppermute | solution.py:131

commit v11 on v9

--- a/solution.py
+++ b/solution.py
@@ -10,7 +10,7 @@
 NY = 128
 NZ = 64
 ROWS = 32
-GROUPS = 2
+GROUPS = 4
 SPACE = ("z", "y", "core")
 
 

time: 171 us -> 206 us (1.20)
  starting transfers between devices: 29.1 us -> 48.7 us
  matrix products: 6.63 us -> 18.3 us
  waiting for transfers between devices: 44.5 us -> 35.4 us
  local copies, waits for them, and re-layouts: 32.6 us -> 37.6 us
  blocking collectives: 28.6 us -> 31.5 us
  Pallas kernels: 15.7 us -> 18.3 us
    dot_general x4 -> x16, matrix products: 6.63 us -> 18.3 us  [per_device(): lax.dot_general(im, fd, dims, preferred_element_type=jnp.float32)]
    all_to_all x2 -> x4, starting transfers between devices: 8.91 us -> 16.9 us  [per_device(): lax.all_to_all(pieces, 'node', 1, 1, tiled=True)]
    ppermute x2 -> x4, starting transfers between devices: 7.29 us -> 15.1 us  [per_device(): above = lax.ppermute(field[0], SPACE, down)]
    all_to_all x2 -> x4, waiting for transfers between devices: 32.9 us -> 25.1 us  [per_device(): lax.all_to_all(pieces, 'node', 1, 1, tiled=True)]
    ppermute x2 -> x4, starting transfers between devices: 3.82 us -> 7.65 us  [per_device(): below = lax.ppermute(field[1], SPACE, up)]
    all_to_all x3, blocking collectives: 28.6 us -> 31.5 us  [per_device(): total = lax.all_to_all(total, SPACE[axis], 0, 0, tiled=True).sum(axis=0)]
    pallas_call x2 -> x4, Pallas kernels: 15.7 us -> 18.3 us  [stencil(): pl.pallas_call(stencil_kernel, grid=(snaps // ROWS,), in_specs=[pl.BlockS...]
    concatenate x3 -> x5, local copies, waits for them, and re-layouts: 3.11 us -> 5.05 us  [chunked(): jnp.concatenate([values[..., q * chunk:(q + 1) * chunk], after, before],...]
  transfers between devices with their start and end apart: 11 -> 17, of which waited for: 4 -> 5; matrix products, arithmetic and copies ran while one was open for 23% -> 27% of each run, Pallas kernels for 5% -> 7%
where the time goes in v11:
time: 206 us; the launch traced here: 203 us
  starting transfers between devices  48.7 us (24%)
  local copies, waits for them, and re-layouts  37.6 us (18%)
  waiting for transfers between devices  35.4 us (17%)
  blocking collectives  31.5 us (15%)
  Pallas kernels  18.3 us (9%)
  matrix products  18.3 us (9%)
  other arithmetic  12.3 us (6%)
    all_to_all x3, blocking collectives, per_device(): total = lax.all_to_all(total, SPACE[axis], 0, 0, tiled=True).sum(axis=0)  31.5 us
    all_to_all x4, waiting for transfers between devices, per_device(): lax.all_to_all(pieces, 'node', 1, 1, tiled=True)  25.1 us
    dot_general x16, matrix products, per_device(): lax.dot_general(im, fd, dims, preferred_element_type=jnp.float32)  18.3 us
    pallas_call x4, Pallas kernels, stencil(): pl.pallas_call(stencil_kernel, grid=(snaps // ROWS,), in_specs=[pl.BlockS...  18.3 us
    all_to_all x4, starting transfers between devices, per_device(): lax.all_to_all(pieces, 'node', 1, 1, tiled=True)  16.9 us
    ppermute x4, starting transfers between devices, per_device(): above = lax.ppermute(field[0], SPACE, down)  15.1 us
    ppermute x3, waiting for transfers between devices, per_device(): lax.ppermute(blk, 'node', [(i, (i + d) % nodes) for i in range(nodes)])  10.2 us
    unnamed x75, local copies, waits for them, and re-layouts  8.8 us
  transfers between devices with their start and end apart: 17, of which 5 were waited for; matrix products, arithmetic and copies ran while one was open for 27% of the time, Pallas kernels for 7%

profile of v11, /device:TPU:8, one launch (start us, length us, event | category | flops | bytes accessed | tf_op | source)
XLA Modules:
  0.0 202.6 jit_solution(3568707915853271996)
XLA Ops:
  0.8 0.8 fusion.30
  3.9 1.9 collective-permute-start.2
  5.8 3.6 %collective-permute-start.3 = (bf16[2176]{0:T(1024)(128)(2,1)}, bf16[2176]{0:T(1024)(128)(2,1)}, u32[]{:S(2)}, u32[]{:S(2)}) collective-permute-start(bf16[2176]{0:T(1024)(128)(2,1)} %get-tuple-element.28), channel_id=1, source_target_pairs={{1,0},{2,1},{3,2},{4,3},{5,4},{6,5},{7,6},{8,7},{9,8},{10,9},{11,1... | collective-permute-start | bytes 13064 | tf_op jit(solution)/shard_map/ppermute | solution.py:107
  9.5 4.9 %copy.125 = bf16[128,2,8192]{2,0,1:T(8,128)(2,1)S(1)} copy(bf16[128,2,8192]{2,1,0:T(2,128)(2,1)} %param.4) | data formatting | bytes 8388608 | tf_op args[0]
  14.3 1.1 fusion.23
  16.2 1.0 fusion.25
  17.2 1.0 concatenate.191
  18.4 1.2 pad_maximum_fusion
  19.6 4.3 %all-to-all-start = ((bf16[2,4,32,2176]{3,2,0,1:T(8,128)(2,1)}), bf16[2,4,32,2176]{3,2,0,1:T(8,128)(2,1)S(1)}, u32[]{:S(2)}, u32[]{:S(2)}) async-start(bf16[2,4,32,2176]{3,2,0,1:T(8,128)(2,1)} %pad_maximum_fusion), calls=%async_computation | async-start | bytes 2228224 | tf_op jit(solution)/shard_map/all_to_all | solution.py:115
  27.2 1.7 pad_bitcast_fusion.2
  29.6 1.8 concatenate.211
  31.4 0.8 select_dynamic-update-slice_fusion.1
  32.2 0.8 select_dynamic-update-slice_fusion
  33.0 0.8 constant_dynamic-update-slice_fusion.3
  34.5 0.8 maximum_bitcast_fusion.2
  35.4 1.2 pad_maximum_fusion.1
  37.4 1.1 concatenate.215
  38.5 1.0 concatenate.219
  39.5 1.2 pad_maximum_fusion.2
  40.7 1.2 pad_maximum_fusion.3
  42.7 4.8 %all-to-all-start.1 = ((bf16[2,4,32,2176]{3,2,0,1:T(8,128)(2,1)}), bf16[2,4,32,2176]{3,2,0,1:T(8,128)(2,1)S(1)}, u32[]{:S(2)}, u32[]{:S(2)}) async-start(bf16[2,4,32,2176]{3,2,0,1:T(8,128)(2,1)} %pad_maximum_fusion.1), calls=%async_computation.1 | async-start | bytes 2228224 | tf_op jit(solution)/shard_map/all_to_all | solution.py:115
  48.3 14.6 %all-to-all-done.1 = bf16[2,4,32,2176]{3,2,0,1:T(8,128)(2,1)S(1)} async-done(((bf16[2,4,32,2176]{3,2,0,1:T(8,128)(2,1)}), bf16[2,4,32,2176]{3,2,0,1:T(8,128)(2,1)S(1)}, u32[]{:S(2)}, u32[]{:S(2)}) %all-to-all-start.1) | async-done | bytes 1114144 | tf_op jit(solution)/shard_map/all_to_all | solution.py:115
  62.9 3.5 %all-to-all-start.2 = ((bf16[2,4,32,2176]{3,2,0,1:T(8,128)(2,1)}), bf16[2,4,32,2176]{3,2,0,1:T(8,128)(2,1)S(1)}, u32[]{:S(2)}, u32[]{:S(2)}) async-start(bf16[2,4,32,2176]{3,2,0,1:T(8,128)(2,1)} %pad_maximum_fusion.2), calls=%async_computation.2 | async-start | bytes 2228224 | tf_op jit(solution)/shard_map/all_to_all | solution.py:115
  66.4 0.9 add_dynamic-update-slice_fusion.coef_ref
  67.3 1.1 fusion.26
  68.4 1.9 collective-permute-start
  70.3 3.6 %collective-permute-start.1 = (bf16[128,2176]{1,0:T(8,128)(2,1)}, bf16[128,2176]{1,0:T(8,128)(2,1)}, u32[]{:S(2)}, u32[]{:S(2)}) collective-permute-start(bf16[128,2176]{1,0:T(8,128)(2,1)} %bitcast.7), channel_id=1, source_target_pairs={{1,0},{2,1},{3,2},{4,3},{5,4},{6,5},{7,6},{8,7},{9,8},{10,9},{11,1... | collective-permute-start | bytes 1671176 | tf_op jit(solution)/shard_map/ppermute | solution.py:117
  74.0 6.8 %all-to-all-done.2 = bf16[2,4,32,2176]{3,2,0,1:T(8,128)(2,1)S(1)} async-done(((bf16[2,4,32,2176]{3,2,0,1:T(8,128)(2,1)}), bf16[2,4,32,2176]{3,2,0,1:T(8,128)(2,1)S(1)}, u32[]{:S(2)}, u32[]{:S(2)}) %all-to-all-start.2) | async-done | bytes 1114144 | tf_op jit(solution)/shard_map/all_to_all | solution.py:115
  80.8 4.3 %all-to-all-start.3 = ((bf16[2,4,32,2176]{3,2,0,1:T(8,128)(2,1)}), bf16[2,4,32,2176]{3,2,0,1:T(8,128)(2,1)}, u32[]{:S(2)}, u32[]{:S(2)}) async-start(bf16[2,4,32,2176]{3,2,0,1:T(8,128)(2,1)} %pad_maximum_fusion.3), calls=%async_computation.3 | async-start | bytes 2228224 | tf_op jit(solution)/shard_map/all_to_all | solution.py:115
  85.1 1.1 fusion.27
  86.2 1.9 collective-permute-start.4
  88.1 3.6 %collective-permute-start.5 = (bf16[128,2176]{1,0:T(8,128)(2,1)}, bf16[128,2176]{1,0:T(8,128)(2,1)}, u32[]{:S(2)}, u32[]{:S(2)}) collective-permute-start(bf16[128,2176]{1,0:T(8,128)(2,1)} %bitcast.43), channel_id=1, source_target_pairs={{1,0},{2,1},{3,2},{4,3},{5,4},{6,5},{7,6},{8,7},{9,8},{10,9},{11,1... | collective-permute-start | bytes 1671176 | tf_op jit(solution)/shard_map/ppermute | solution.py:117
  91.8 1.2 fusion.28
  92.9 1.9 collective-permute-start.6
  94.9 3.8 %all-to-all-done.3 = bf16[2,4,32,2176]{3,2,0,1:T(8,128)(2,1)} async-done(((bf16[2,4,32,2176]{3,2,0,1:T(8,128)(2,1)}), bf16[2,4,32,2176]{3,2,0,1:T(8,128)(2,1)}, u32[]{:S(2)}, u32[]{:S(2)}) %all-to-all-start.3) | async-done | bytes 1114144 | tf_op jit(solution)/shard_map/all_to_all | solution.py:115
  98.6 2.3 %fusion.29 = (bf16[1,4,32,2176]{3,2,1,0:T(8,128)(2,1)}, bf16[1,4,32,2176]{3,2,1,0:T(8,128)(2,1)}) fusion(bf16[2,4,32,2176]{3,2,0,1:T(8,128)(2,1)} %all-to-all-done.3), kind=kLoop, calls=%fused_computation.103 | loop fusion | bytes 2228224 | tf_op jit(solution)/shard_map/slice | solution.py:117
  100.9 1.1 copy.90
  102.1 1.2 copy-done.14
  103.4 3.1 %copy.97 = bf16[2,4,32,2176]{3,2,1,0:T(8,128)(2,1)} copy(bf16[2,4,32,2176]{3,2,0,1:T(8,128)(2,1)} %all-to-all-done.3) | data formatting | bytes 2228224 | tf_op jit(solution)/shard_map/all_to_all | solution.py:115
  106.5 3.3 %collective-permute-start.7 = (bf16[128,2176]{1,0:T(8,128)(2,1)}, bf16[128,2176]{1,0:T(8,128)(2,1)}, u32[]{:S(2)}, u32[]{:S(2)}) collective-permute-start(bf16[128,2176]{1,0:T(8,128)(2,1)} %bitcast.49), channel_id=1, source_target_pairs={{1,0},{2,1},{3,2},{4,3},{5,4},{6,5},{7,6},{8,7},{9,8},{10,9},{11,1... | collective-permute-start | bytes 1671176 | tf_op jit(solution)/shard_map/ppermute | solution.py:117
  109.8 1.9 collective-permute-start.8
  111.7 4.6 %shard_map.28 = bf16[2,128,2176]{2,1,0:T(8,128)(2,1)} custom-call(bf16[2,128,2176]{2,1,0:T(8,128)(2,1)} %bitcast.175, bf16[128,2176]{1,0:T(8,128)(2,1)} %collective-permute-done.below_ref, bf16[128,2176]{1,0:T(8,128)(2,1)} %collective-permute-done.1.above_ref, f32[7,2,2176]{2,1,0:T(2,128)} %copy-done.15), custom_call_target="tpu_custom_call" | custom-call | tf_op jit(solution)/shard_map/pallas_call | solution.py:52
  116.3 1.8 convolution_bitcast_fusion.15
  118.6 4.6 %collective-permute-start.9 = (bf16[128,2176]{1,0:T(8,128)(2,1)}, bf16[128,2176]{1,0:T(8,128)(2,1)}, u32[]{:S(2)}, u32[]{:S(2)}) collective-permute-start(bf16[128,2176]{1,0:T(8,128)(2,1)} %bitcast.55), channel_id=1, source_target_pairs={{1,0},{2,1},{3,2},{4,3},{5,4},{6,5},{7,6},{8,7},{9,8},{10,9},{11,1... | collective-permute-start | bytes 1671176 | tf_op jit(solution)/shard_map/ppermute | solution.py:117
  123.2 4.6 %shard_map.29 = bf16[2,128,2176]{2,1,0:T(8,128)(2,1)} custom-call(bf16[2,128,2176]{2,1,0:T(8,128)(2,1)} %bitcast.181, bf16[128,2176]{1,0:T(8,128)(2,1)} %collective-permute-done.4.below_ref, bf16[128,2176]{1,0:T(8,128)(2,1)} %collective-permute-done.5.above_ref, f32[7,2,2176]{2,1,0:T(2,128)} %copy-done.15), custom_call_target="tpu_custom_call" | custom-call | tf_op jit(solution)/shard_map/pallas_call | solution.py:52
  127.8 1.8 convolution_bitcast_fusion.11
  129.7 1.1 convolution_bitcast_fusion.10
  131.0 1.1 convolution_bitcast_fusion.13
  132.1 1.1 convolution_bitcast_fusion.9
  133.3 1.1 convolution_bitcast_fusion.12
  134.4 1.1 convolution_bitcast_fusion.8
  135.5 4.5 %shard_map.30 = bf16[2,128,2176]{2,1,0:T(8,128)(2,1)} custom-call(bf16[2,128,2176]{2,1,0:T(8,128)(2,1)} %bitcast.187, bf16[128,2176]{1,0:T(8,128)(2,1)} %collective-permute-done.6.below_ref, bf16[128,2176]{1,0:T(8,128)(2,1)} %collective-permute-done.7.above_ref, f32[7,2,2176]{2,1,0:T(2,128)} %copy-done.15), custom_call_target="tpu_custom_call" | custom-call | tf_op jit(solution)/shard_map/pallas_call | solution.py:52
  140.0 2.4 %convolution_bitcast_fusion.7 = f32[128,128]{0,1:T(8,128)} fusion(bf16[2,128,2176]{2,1,0:T(8,128)(2,1)} %shard_map.30, bf16[2,128,2176]{2,1,0:T(8,128)(2,1)S(1)} %bitcast.178), kind=kOutput, calls=%fused_computation.8 | convolution fusion | flops 142606336 | bytes 2293760 | tf_op jit(solution)/shard_map/dot_general | solution.py:123
  142.4 1.1 convolution_bitcast_fusion.6
  143.7 1.1 convolution_bitcast_fusion.5
  144.9 1.1 convolution_bitcast_fusion.4
  146.0 4.5 %shard_map.31 = bf16[2,128,2176]{2,1,0:T(8,128)(2,1)} custom-call(bf16[2,128,2176]{2,1,0:T(8,128)(2,1)} %bitcast.190, bf16[128,2176]{1,0:T(8,128)(2,1)} %collective-permute-done.8.below_ref, bf16[128,2176]{1,0:T(8,128)(2,1)} %collective-permute-done.9.above_ref, f32[7,2,2176]{2,1,0:T(2,128)} %copy-done.15), custom_call_target="tpu_custom_call" | custom-call | tf_op jit(solution)/shard_map/pallas_call | solution.py:52
  150.5 1.8 convolution_bitcast_fusion.3
  156.2 2.1 %collective-permute-start.11 = (f32[4,32,512]{2,1,0:T(8,128)S(1)}, f32[4,32,512]{2,1,0:T(8,128)S(1)}, u32[]{:S(2)}, u32[]{:S(2)}) collective-permute-start(f32[4,32,512]{2,1,0:T(8,128)S(1)} %get-tuple-element.69), channel_id=1, source_target_pairs={{0,128},{64,192},{128,0},{192,64},{1,129},{65,193},{129,1},{193,65... | collective-permute-start | bytes 786440 | tf_op jit(solution)/shard_map/ppermute | solution.py:130
  158.3 0.8 collective-permute-start.12
  159.1 9.6 %collective-permute-done.10 = f32[4,32,512]{2,1,0:T(8,128)S(1)} collective-permute-done((f32[4,32,512]{2,1,0:T(8,128)S(1)}, f32[4,32,512]{2,1,0:T(8,128)S(1)}, u32[]{:S(2)}, u32[]{:S(2)}) %collective-permute-start.10) | collective-permute-done | bytes 262176 | tf_op jit(solution)/shard_map/ppermute | solution.py:130
  170.5 3.9 %all_to_all.35 = f32[2,128,8,4,8]{1,4,3,2,0:T(8,128)S(1)} all-to-all(f32[2,128,8,4,8]{1,4,3,2,0:T(8,128)S(1)} %copy.109), channel_id=1, replica_groups=mesh['node'=4,'z'=8,'y'=4,'core'=2] {'core'}, dimensions={0} | all-to-all | bytes 524288 | tf_op jit(solution)/shard_map/all_to_all | solution.py:135
  174.5 10.6 %all_to_all.36 = f32[4,128,8,8]{1,3,2,0:T(8,128)S(1)} all-to-all(f32[4,128,8,8]{1,3,2,0:T(8,128)S(1)} %copy.111), channel_id=1, replica_groups=mesh['node'=4,'z'=8,'y'=4,'core'=2] {'y'}, dimensions={0} | all-to-all | bytes 262144 | tf_op jit(solution)/shard_map/all_to_all | solution.py:135
  185.1 16.9 %all_to_all.37 = f32[8,128,8]{1,2,0:T(8,128)S(1)} all-to-all(f32[8,128,8]{1,2,0:T(8,128)S(1)} %bitcast.208), channel_id=1, replica_groups=mesh['node'=4,'z'=8,'y'=4,'core'=2] {'z'}, dimensions={0} | all-to-all | bytes 65536 | tf_op jit(solution)/shard_map/all_to_all | solution.py:135
  (133 shorter events, 18.6 us)
Async XLA Ops:
  3.9 38.1 %collective-permute-start.2 = (bf16[2176]{0:T(1024)(128)(2,1)}, bf16[2176]{0:T(1024)(128)(2,1)}, u32[]{:S(2)}, u32[]{:S(2)}) collective-permute-start(bf16[2176]{0:T(1024)(128)(2,1)} %get-tuple-element.29), channel_id=1, source_target_pairs={{0,1},{1,2},{2,3},{3,4},{4,5},{5,6},{6,7},{7,8},{8,9},{9,10},{10,1... | collective-permute-start | bytes 13064 | tf_op jit(solution)/shard_map/ppermute | solution.py:106
  5.8 41.7 %collective-permute-start.3 = (bf16[2176]{0:T(1024)(128)(2,1)}, bf16[2176]{0:T(1024)(128)(2,1)}, u32[]{:S(2)}, u32[]{:S(2)}) collective-permute-start(bf16[2176]{0:T(1024)(128)(2,1)} %get-tuple-element.28), channel_id=1, source_target_pairs={{1,0},{2,1},{3,2},{4,3},{5,4},{6,5},{7,6},{8,7},{9,8},{10,9},{11,1... | collective-permute-start | bytes 13064 | tf_op jit(solution)/shard_map/ppermute | solution.py:107
  19.6 23.1 %all-to-all-start = ((bf16[2,4,32,2176]{3,2,0,1:T(8,128)(2,1)}), bf16[2,4,32,2176]{3,2,0,1:T(8,128)(2,1)S(1)}, u32[]{:S(2)}, u32[]{:S(2)}) async-start(bf16[2,4,32,2176]{3,2,0,1:T(8,128)(2,1)} %pad_maximum_fusion), calls=%async_computation | async-start | bytes 2228224 | tf_op jit(solution)/shard_map/all_to_all | solution.py:115
  29.6 5.8 %copy-start.17 = (bf16[2,1,32,2176]{3,2,0,1:T(8,128)(2,1)S(1)}, bf16[2,1,32,2176]{3,2,0,1:T(8,128)(2,1)}, u32[]{:S(2)}) copy-start(bf16[2,1,32,2176]{3,2,0,1:T(8,128)(2,1)} %pad_bitcast_fusion.2) | copy-start | bytes 835588
  31.4 4.0 %copy-start.18 = (bf16[2,32,2176]{2,1,0:T(8,128)(2,1)S(1)}, bf16[2,32,2176]{2,1,0:T(8,128)(2,1)}, u32[]{:S(2)}) copy-start(bf16[2,32,2176]{2,1,0:T(8,128)(2,1)} %concatenate.211) | copy-start | bytes 835588
  35.4 1.2 copy-start.34
  35.4 1.2 copy-start.35
  36.6 0.7 copy-start.32
  36.6 0.7 copy-start.33
  37.4 2.2 %copy-start.16 = (bf16[2,1,32,2176]{3,2,0,1:T(8,128)(2,1)S(1)}, bf16[2,1,32,2176]{3,2,0,1:T(8,128)(2,1)}, u32[]{:S(2)}) copy-start(bf16[2,1,32,2176]{3,2,0,1:T(8,128)(2,1)} %pad_bitcast_fusion.1) | copy-start | bytes 835588
  42.6 4.8 %copy-start.30 = (f32[1,1,2176]{2,1,0:T(1,128)}, f32[1,1,2176]{2,1,0:T(1,128)S(1)}, u32[]{:S(2)}) copy-start(f32[1,1,2176]{2,1,0:T(1,128)S(1)} %reshape.580) | copy-start | bytes 26116
  42.7 4.8 %copy-start.29 = (f32[1,1,2176]{2,1,0:T(1,128)S(1)}, f32[1,1,2176]{2,1,0:T(1,128)}, u32[]{:S(2)}) copy-start(f32[1,1,2176]{2,1,0:T(1,128)} %get-tuple-element.84) | copy-start | bytes 26116
  42.7 5.6 %copy-start.28 = (f32[1,1,2176]{2,1,0:T(1,128)S(1)}, f32[1,1,2176]{2,1,0:T(1,128)}, u32[]{:S(2)}) copy-start(f32[1,1,2176]{2,1,0:T(1,128)} %get-tuple-element.83) | copy-start | bytes 26116
  42.7 20.2 %all-to-all-start.1 = ((bf16[2,4,32,2176]{3,2,0,1:T(8,128)(2,1)}), bf16[2,4,32,2176]{3,2,0,1:T(8,128)(2,1)S(1)}, u32[]{:S(2)}, u32[]{:S(2)}) async-start(bf16[2,4,32,2176]{3,2,0,1:T(8,128)(2,1)} %pad_maximum_fusion.1), calls=%async_computation.1 | async-start | bytes 2228224 | tf_op jit(solution)/shard_map/all_to_all | solution.py:115
  48.2 14.6 %copy-start.31 = (f32[1,1,2176]{2,1,0:T(1,128)}, f32[1,1,2176]{2,1,0:T(1,128)S(1)}, u32[]{:S(2)}) copy-start(f32[1,1,2176]{2,1,0:T(1,128)S(1)} %reshape.581) | copy-start | bytes 26116
  48.3 18.1 %copy-start.36 = (pred[2176]{0:T(1024)(128)(4,1)S(1)}, pred[2176]{0:T(1024)(128)(4,1)}, u32[]{:S(2)}) copy-start(pred[2176]{0:T(1024)(128)(4,1)} %get-tuple-element.95) | copy-start | bytes 6532
  62.9 17.9 %all-to-all-start.2 = ((bf16[2,4,32,2176]{3,2,0,1:T(8,128)(2,1)}), bf16[2,4,32,2176]{3,2,0,1:T(8,128)(2,1)S(1)}, u32[]{:S(2)}, u32[]{:S(2)}) async-start(bf16[2,4,32,2176]{3,2,0,1:T(8,128)(2,1)} %pad_maximum_fusion.2), calls=%async_computation.2 | async-start | bytes 2228224 | tf_op jit(solution)/shard_map/all_to_all | solution.py:115
  67.3 1.1 copy-start.15
  68.4 38.1 %collective-permute-start = (bf16[128,2176]{1,0:T(8,128)(2,1)}, bf16[128,2176]{1,0:T(8,128)(2,1)}, u32[]{:S(2)}, u32[]{:S(2)}) collective-permute-start(bf16[128,2176]{1,0:T(8,128)(2,1)} %bitcast.6), channel_id=1, source_target_pairs={{0,1},{1,2},{2,3},{3,4},{4,5},{5,6},{6,7},{7,8},{8,9},{9,10},{10,1... | collective-permute-start | bytes 1671176 | tf_op jit(solution)/shard_map/ppermute | solution.py:116
  70.3 39.4 %collective-permute-start.1 = (bf16[128,2176]{1,0:T(8,128)(2,1)}, bf16[128,2176]{1,0:T(8,128)(2,1)}, u32[]{:S(2)}, u32[]{:S(2)}) collective-permute-start(bf16[128,2176]{1,0:T(8,128)(2,1)} %bitcast.7), channel_id=1, source_target_pairs={{1,0},{2,1},{3,2},{4,3},{5,4},{6,5},{7,6},{8,7},{9,8},{10,9},{11,1... | collective-permute-start | bytes 1671176 | tf_op jit(solution)/shard_map/ppermute | solution.py:117
  80.8 11.0 %copy-start.13 = (bf16[2,4,32,2176]{3,2,0,1:T(8,128)(2,1)}, bf16[2,4,32,2176]{3,2,0,1:T(8,128)(2,1)S(1)}, u32[]{:S(2)}) copy-start(bf16[2,4,32,2176]{3,2,0,1:T(8,128)(2,1)S(1)} %all-to-all-done.2) | copy-start | bytes 3342340
  80.8 17.8 %all-to-all-start.3 = ((bf16[2,4,32,2176]{3,2,0,1:T(8,128)(2,1)}), bf16[2,4,32,2176]{3,2,0,1:T(8,128)(2,1)}, u32[]{:S(2)}, u32[]{:S(2)}) async-start(bf16[2,4,32,2176]{3,2,0,1:T(8,128)(2,1)} %pad_maximum_fusion.3), calls=%async_computation.3 | async-start | bytes 2228224 | tf_op jit(solution)/shard_map/all_to_all | solution.py:115
  86.2 32.4 %collective-permute-start.4 = (bf16[128,2176]{1,0:T(8,128)(2,1)}, bf16[128,2176]{1,0:T(8,128)(2,1)}, u32[]{:S(2)}, u32[]{:S(2)}) collective-permute-start(bf16[128,2176]{1,0:T(8,128)(2,1)} %bitcast.42), channel_id=1, source_target_pairs={{0,1},{1,2},{2,3},{3,4},{4,5},{5,6},{6,7},{7,8},{8,9},{9,10},{10,1... | collective-permute-start | bytes 1671176 | tf_op jit(solution)/shard_map/ppermute | solution.py:116
  88.1 35.1 %collective-permute-start.5 = (bf16[128,2176]{1,0:T(8,128)(2,1)}, bf16[128,2176]{1,0:T(8,128)(2,1)}, u32[]{:S(2)}, u32[]{:S(2)}) collective-permute-start(bf16[128,2176]{1,0:T(8,128)(2,1)} %bitcast.43), channel_id=1, source_target_pairs={{1,0},{2,1},{3,2},{4,3},{5,4},{6,5},{7,6},{8,7},{9,8},{10,9},{11,1... | collective-permute-start | bytes 1671176 | tf_op jit(solution)/shard_map/ppermute | solution.py:117
  92.9 42.5 %collective-permute-start.6 = (bf16[128,2176]{1,0:T(8,128)(2,1)}, bf16[128,2176]{1,0:T(8,128)(2,1)}, u32[]{:S(2)}, u32[]{:S(2)}) collective-permute-start(bf16[128,2176]{1,0:T(8,128)(2,1)} %bitcast.48), channel_id=1, source_target_pairs={{0,1},{1,2},{2,3},{3,4},{4,5},{5,6},{6,7},{7,8},{8,9},{9,10},{10,1... | collective-permute-start | bytes 1671176 | tf_op jit(solution)/shard_map/ppermute | solution.py:116
  102.0 1.2 copy-start.14
  103.3 14.9 %copy-start.1 = (bf16[2,4,32,2176]{3,2,1,0:T(8,128)(2,1)}, bf16[2,4,32,2176]{3,2,1,0:T(8,128)(2,1)S(1)}, u32[]{:S(2)}) copy-start(bf16[2,4,32,2176]{3,2,1,0:T(8,128)(2,1)S(1)} %copy.95) | copy-start | bytes 3342340
  103.4 28.7 %copy-start.3 = (bf16[2,4,32,2176]{3,2,1,0:T(8,128)(2,1)}, bf16[2,4,32,2176]{3,2,1,0:T(8,128)(2,1)S(1)}, u32[]{:S(2)}) copy-start(bf16[2,4,32,2176]{3,2,1,0:T(8,128)(2,1)S(1)} %copy.96) | copy-start | bytes 3342340
  106.5 29.0 %collective-permute-start.7 = (bf16[128,2176]{1,0:T(8,128)(2,1)}, bf16[128,2176]{1,0:T(8,128)(2,1)}, u32[]{:S(2)}, u32[]{:S(2)}) collective-permute-start(bf16[128,2176]{1,0:T(8,128)(2,1)} %bitcast.49), channel_id=1, source_target_pairs={{1,0},{2,1},{3,2},{4,3},{5,4},{6,5},{7,6},{8,7},{9,8},{10,9},{11,1... | collective-permute-start | bytes 1671176 | tf_op jit(solution)/shard_map/ppermute | solution.py:117
  109.8 36.2 %collective-permute-start.8 = (bf16[128,2176]{1,0:T(8,128)(2,1)}, bf16[128,2176]{1,0:T(8,128)(2,1)}, u32[]{:S(2)}, u32[]{:S(2)}) collective-permute-start(bf16[128,2176]{1,0:T(8,128)(2,1)} %bitcast.54), channel_id=1, source_target_pairs={{0,1},{1,2},{2,3},{3,4},{4,5},{5,6},{6,7},{7,8},{8,9},{9,10},{10,1... | collective-permute-start | bytes 1671176 | tf_op jit(solution)/shard_map/ppermute | solution.py:116
  111.7 4.6 %copy-start = (bf16[2,4,32,2176]{3,2,1,0:T(8,128)(2,1)S(1)}, bf16[2,4,32,2176]{3,2,1,0:T(8,128)(2,1)}, u32[]{:S(2)}) copy-start(bf16[2,4,32,2176]{3,2,1,0:T(8,128)(2,1)} %copy.90) | copy-start | bytes 3342340
  116.3 1.8 copy-start.8
  118.6 27.4 %collective-permute-start.9 = (bf16[128,2176]{1,0:T(8,128)(2,1)}, bf16[128,2176]{1,0:T(8,128)(2,1)}, u32[]{:S(2)}, u32[]{:S(2)}) collective-permute-start(bf16[128,2176]{1,0:T(8,128)(2,1)} %bitcast.55), channel_id=1, source_target_pairs={{1,0},{2,1},{3,2},{4,3},{5,4},{6,5},{7,6},{8,7},{9,8},{10,9},{11,1... | collective-permute-start | bytes 1671176 | tf_op jit(solution)/shard_map/ppermute | solution.py:117
  127.8 1.9 copy-start.2
  127.8 1.9 copy-start.11
  129.7 1.2 copy-start.9
  132.1 1.2 copy-start.5
  140.0 2.4 %copy-start.12 = (bf16[2,128,2176]{2,1,0:T(8,128)(2,1)S(1)}, bf16[2,128,2176]{2,1,0:T(8,128)(2,1)}, u32[]{:S(2)}) copy-start(bf16[2,128,2176]{2,1,0:T(8,128)(2,1)} %shard_map.30) | copy-start | bytes 3342340
  142.4 1.2 copy-start.4
  143.7 1.2 copy-start.6
  150.5 1.8 copy-start.10
  152.8 1.2 copy-start.7
  154.0 0.8 copy-start.19
  154.0 0.9 copy-start.20
  154.0 0.9 copy-start.21
  154.0 0.9 copy-start.22
  154.0 1.0 copy-start.23
  154.1 1.0 copy-start.24
  154.1 1.0 copy-start.25
  154.1 1.0 copy-start.26
  154.1 1.1 copy-start.27
  155.6 13.1 %collective-permute-start.10 = (f32[4,32,512]{2,1,0:T(8,128)S(1)}, f32[4,32,512]{2,1,0:T(8,128)S(1)}, u32[]{:S(2)}, u32[]{:S(2)}) collective-permute-start(f32[4,32,512]{2,1,0:T(8,128)S(1)} %get-tuple-element.68), channel_id=1, source_target_pairs={{0,64},{64,128},{128,192},{192,0},{1,65},{65,129},{129,193},{193,1... | collective-permute-start | bytes 786440 | tf_op jit(solution)/shard_map/ppermute | solution.py:130
  156.2 12.5 %collective-permute-start.11 = (f32[4,32,512]{2,1,0:T(8,128)S(1)}, f32[4,32,512]{2,1,0:T(8,128)S(1)}, u32[]{:S(2)}, u32[]{:S(2)}) collective-permute-start(f32[4,32,512]{2,1,0:T(8,128)S(1)} %get-tuple-element.69), channel_id=1, source_target_pairs={{0,128},{64,192},{128,0},{192,64},{1,129},{65,193},{129,1},{193,65... | collective-permute-start | bytes 786440 | tf_op jit(solution)/shard_map/ppermute | solution.py:130
  158.3 11.0 %collective-permute-start.12 = (f32[4,32,512]{2,1,0:T(8,128)S(1)}, f32[4,32,512]{2,1,0:T(8,128)S(1)}, u32[]{:S(2)}, u32[]{:S(2)}) collective-permute-start(f32[4,32,512]{2,1,0:T(8,128)S(1)} %select_bitcast_fusion), channel_id=1, source_target_pairs={{0,192},{64,0},{128,64},{192,128},{1,193},{65,1},{129,65},{193,129... | collective-permute-start | bytes 786440 | tf_op jit(solution)/shard_map/ppermute | solution.py:130

commit v12 on v9

--- a/solution.py
+++ b/solution.py
@@ -102,21 +102,23 @@
     up = [(i, i + 1) for i in range(spaces - 1)]
     down = [(j, i) for i, j in up]
 
-    kap_chunk = jnp.take(chunked(kappa[:, None], nodes)[:, :, 0], me, axis=1)
-    kap_below = lax.ppermute(kap_chunk[1], SPACE, up)
-    kap_above = lax.ppermute(kap_chunk[0], SPACE, down)
-    coef = weights(kap_chunk, kap_below, kap_above)
-
-    major = jnp.transpose(snapshots, (1, 0, 2))
     step = rows // GROUPS
-    images, fields = [], []
+    images, fields, fronts = [], [], []
     for g in range(GROUPS):
-        pieces = chunked(major[:, g * step:(g + 1) * step], nodes)
-        field = lax.all_to_all(pieces, "node", 1, 1, tiled=True).reshape(planes, nodes * step, span)
+        major = jnp.transpose(snapshots[g * step:(g + 1) * step], (1, 0, 2))
+        field = lax.all_to_all(chunked(major, nodes), "node", 1, 1, tiled=True).reshape(planes, nodes * step, span)
         below = lax.ppermute(field[1], SPACE, up)
         above = lax.ppermute(field[0], SPACE, down)
+        fields.append(field)
+        fronts.append((below, above))
+        if g == 0:
+            late, _ = lax.optimization_barrier((kappa, field))
+            kap_chunk = jnp.take(chunked(late[:, None], nodes)[:, :, 0], me, axis=1)
+            kap_below = lax.ppermute(kap_chunk[1], SPACE, up)
+            kap_above = lax.ppermute(kap_chunk[0], SPACE, down)
+            coef = weights(kap_chunk, kap_below, kap_above)
+    for field, (below, above) in zip(fields, fronts):
         images.append(stencil(field, below, above, coef))
-        fields.append(field)
     dims = (((0, 2), (0, 2)), ((), ()))
     part = jnp.concatenate([
         jnp.concatenate([

time: 171 us -> 162 us (0.947)
  local copies, waits for them, and re-layouts: 32.6 us -> 26.3 us
  other arithmetic: 11 us -> 5.66 us
  waiting for transfers between devices: 44.5 us -> 46.4 us
    slice x0 -> x1, local copies, waits for them, and re-layouts: none -> 5.04 us  [per_device(): major = jnp.transpose(snapshots[g * step:(g + 1) * step], (1, 0, 2))]
    unnamed x27 -> x18, local copies, waits for them, and re-layouts: 7.27 us -> 2.32 us
    unnamed x6, other arithmetic: 3.22 us -> 0.46 us
    transpose x0 -> x1, local copies, waits for them, and re-layouts: none -> 2.68 us  [per_device(): major = jnp.transpose(snapshots[g * step:(g + 1) * step], (1, 0, 2))]
    another operation x3 -> x1, local copies, waits for them, and re-layouts: 1.96 us -> 0.01 us  [the longest x2 1.95 us: chunked(): return jnp.stack(pieces, axis=-3)]
    another operation x6 -> x10, other arithmetic: 5.27 us -> 4.05 us  [chunked(): return jnp.stack(pieces, axis=-3)]
    slice x4 -> x6, local copies, waits for them, and re-layouts: 3.8 us -> 3.34 us  [chunked(): values[..., q * chunk:(q + 1) * chunk]]
  transfers between devices with their start and end apart: 11 -> 11, of which waited for: 4 -> 6; matrix products, arithmetic and copies ran while one was open for 23% -> 13% of each run, Pallas kernels for 5% -> 5%
where the time goes in v12:
time: 162 us; the launch traced here: 160 us
  waiting for transfers between devices  46.4 us (29%)
  blocking collectives  29.7 us (18%)
  starting transfers between devices  28.9 us (18%)
  local copies, waits for them, and re-layouts  26.3 us (16%)
  Pallas kernels  15.6 us (10%)
  matrix products  6.63 us (4%)
  other arithmetic  5.66 us (3%)
    all_to_all x2, waiting for transfers between devices, per_device(): lax.all_to_all(chunked(major, nodes), 'node', 1, 1, tiled=True)  32.7 us
    all_to_all x3, blocking collectives, per_device(): total = lax.all_to_all(total, SPACE[axis], 0, 0, tiled=True).sum(axis=0)  29.7 us
    pallas_call x2, Pallas kernels, stencil(): pl.pallas_call(stencil_kernel, grid=(snaps // ROWS,), in_specs=[pl.BlockS...  15.6 us
    ppermute x3, waiting for transfers between devices, per_device(): lax.ppermute(blk, 'node', [(i, (i + d) % nodes) for i in range(nodes)])  12.9 us
    all_to_all x2, starting transfers between devices, per_device(): lax.all_to_all(chunked(major, nodes), 'node', 1, 1, tiled=True)  8.76 us
    ppermute x2, starting transfers between devices, per_device(): above = lax.ppermute(field[0], SPACE, down)  7.28 us
    dot_general x4, matrix products, per_device(): lax.dot_general(im, fd, dims, preferred_element_type=jnp.float32)  6.63 us
    slice x1, local copies, waits for them, and re-layouts, per_device(): major = jnp.transpose(snapshots[g * step:(g + 1) * step], (1, 0, 2))  5.04 us
  transfers between devices with their start and end apart: 11, of which 6 were waited for; matrix products, arithmetic and copies ran while one was open for 13% of the time, Pallas kernels for 5%

profile of v12, /device:TPU:8, one launch (start us, length us, event | category | flops | bytes accessed | tf_op | source)
XLA Modules:
  0.0 159.7 jit_solution(18393908634675148318)
XLA Ops:
  0.0 5.0 %fusion.25 = (bf16[64,2,8192]{2,1,0:T(2,128)(2,1)S(1)}, bf16[64,2,8192]{2,1,0:T(2,128)(2,1)S(1)}) fusion(bf16[128,2,8192]{2,1,0:T(2,128)(2,1)} %param.4), kind=kLoop, calls=%fused_computation.80 | loop fusion | bytes 8388608 | tf_op jit(solution)/shard_map/slice | solution.py:108
  5.1 2.7 %copy_bitcast_fusion = (bf16[2,64,8192]{2,1,0:T(8,128)(2,1)S(1)}, bf16[2,64,8192]{2,1,0:T(8,128)(2,1)S(1)}) fusion(bf16[64,2,8192]{2,1,0:T(2,128)(2,1)S(1)} %get-tuple-element.35, bf16[64,2,8192]{2,1,0:T(2,128)(2,1)S(1)} %get-tuple-element.34), kind=kLoop, calls=%fused_computation.2 | loop fusion | bytes 8388608 | tf_op jit(solution)/shard_map/transpose | solution.py:108
  7.7 0.1 fusion.29
  7.8 0.1 fusion.28
  8.0 0.1 maximum_bitcast_fusion
  8.1 0.1 maximum_bitcast_fusion.1
  8.2 0.9 copy-done.5
  9.1 0.1 fusion.1
  9.2 0.3 concatenate.155
  9.5 1.7 %pad_maximum_fusion = bf16[2,4,64,2176]{3,2,0,1:T(8,128)(2,1)} fusion(bf16[2,1,64,2176]{3,2,0,1:T(8,128)(2,1)S(1)} %bitcast.118, bf16[2,1,64,2176]{3,2,0,1:T(8,128)(2,1)S(1)} %maximum_bitcast_fusion.1, bf16[2,1,64,2176]{3,2,0,1:T(8,128)(2,1)S(1)} %maximum_bitcast_fusion, bf16[2,1,64,2176]{3,2,0,1:T(8,128)(2,1)S(1)} %get-tuple-element.67), kind=kLoop, calls=%fused_computation | loop fusion | flops 3342336 | bytes 4456448 | tf_op jit(solution)/shard_map/stack | solution.py:89
  11.2 4.3 %all-to-all-start = ((bf16[2,4,64,2176]{3,2,0,1:T(8,128)(2,1)}), bf16[2,4,64,2176]{3,2,0,1:T(8,128)(2,1)S(1)}, u32[]{:S(2)}, u32[]{:S(2)}) async-start(bf16[2,4,64,2176]{3,2,0,1:T(8,128)(2,1)} %pad_maximum_fusion), calls=%async_computation | async-start | bytes 4456448 | tf_op jit(solution)/shard_map/all_to_all | solution.py:109
  15.5 0.9 fusion.31
  16.4 1.9 %slice.246 = bf16[2,64,2048]{2,1,0:T(8,128)(2,1)} slice(bf16[2,64,8192]{2,1,0:T(8,128)(2,1)} %copy-done.5), slice={[0:2], [0:64], [6144:8192]} | slice | bytes 1048576 | tf_op jit(solution)/shard_map/slice | solution.py:88
  18.3 1.2 concatenate.175
  19.4 1.3 fusion.30
  20.7 0.1 maximum_bitcast_fusion.2
  20.8 0.1 maximum_bitcast_fusion.3
  20.9 1.7 %pad_maximum_fusion.1 = bf16[2,4,64,2176]{3,2,0,1:T(8,128)(2,1)} fusion(bf16[2,1,64,2176]{3,2,0,1:T(8,128)(2,1)S(1)} %bitcast.117, bf16[2,1,64,2176]{3,2,0,1:T(8,128)(2,1)S(1)} %maximum_bitcast_fusion.3, bf16[2,1,64,2176]{3,2,0,1:T(8,128)(2,1)S(1)} %maximum_bitcast_fusion.2, bf16[2,1,64,2176]{3,2,0,1:T(8,128)(2,1)S(1)} %get-tuple-element.68), kind=kLoop, calls=%fused_computation.1 | loop fusion | flops 3342336 | bytes 4456448 | tf_op jit(solution)/shard_map/stack | solution.py:89
  22.6 20.6 %all-to-all-done = bf16[2,4,64,2176]{3,2,0,1:T(8,128)(2,1)S(1)} async-done(((bf16[2,4,64,2176]{3,2,0,1:T(8,128)(2,1)}), bf16[2,4,64,2176]{3,2,0,1:T(8,128)(2,1)S(1)}, u32[]{:S(2)}, u32[]{:S(2)}) %all-to-all-start) | async-done | bytes 2228256 | tf_op jit(solution)/shard_map/all_to_all | solution.py:109
  43.2 4.5 %all-to-all-start.1 = ((bf16[2,4,64,2176]{3,2,0,1:T(8,128)(2,1)}), bf16[2,4,64,2176]{3,2,0,1:T(8,128)(2,1)}, u32[]{:S(2)}, u32[]{:S(2)}) async-start(bf16[2,4,64,2176]{3,2,0,1:T(8,128)(2,1)} %pad_maximum_fusion.1), calls=%async_computation.1 | async-start | bytes 4456448 | tf_op jit(solution)/shard_map/all_to_all | solution.py:109
  47.7 1.5 copy.42
  49.4 0.1 maximum_bitcast_fusion.4
  49.5 0.1 concatenate.159
  49.9 1.9 %collective-permute-start.2 = (bf16[2176]{0:T(1024)(128)(2,1)S(1)}, bf16[2176]{0:T(1024)(128)(2,1)S(1)}, u32[]{:S(2)}, u32[]{:S(2)}) collective-permute-start(bf16[2176]{0:T(1024)(128)(2,1)S(1)} %get-tuple-element.31), channel_id=1, source_target_pairs={{0,1},{1,2},{2,3},{3,4},{4,5},{5,6},{6,7},{7,8},{8,9},{9,10},{10,1... | collective-permute-start | bytes 13064 | tf_op jit(solution)/shard_map/ppermute | solution.py:117
  51.8 3.6 %collective-permute-start.3 = (bf16[2176]{0:T(1024)(128)(2,1)S(1)}, bf16[2176]{0:T(1024)(128)(2,1)S(1)}, u32[]{:S(2)}, u32[]{:S(2)}) collective-permute-start(bf16[2176]{0:T(1024)(128)(2,1)S(1)} %get-tuple-element.30), channel_id=1, source_target_pairs={{1,0},{2,1},{3,2},{4,3},{5,4},{6,5},{7,6},{8,7},{9,8},{10,9},{11,1... | collective-permute-start | bytes 13064 | tf_op jit(solution)/shard_map/ppermute | solution.py:118
  55.4 1.2 fusion.26
  56.6 1.9 %collective-permute-start = (bf16[256,2176]{1,0:T(8,128)(2,1)}, bf16[256,2176]{1,0:T(8,128)(2,1)}, u32[]{:S(2)}, u32[]{:S(2)}) collective-permute-start(bf16[256,2176]{1,0:T(8,128)(2,1)} %bitcast.6), channel_id=1, source_target_pairs={{0,1},{1,2},{2,3},{3,4},{4,5},{5,6},{6,7},{7,8},{8,9},{9,10},{10,1... | collective-permute-start | bytes 3342344 | tf_op jit(solution)/shard_map/ppermute | solution.py:110
  58.5 3.6 %collective-permute-start.1 = (bf16[256,2176]{1,0:T(8,128)(2,1)S(1)}, bf16[256,2176]{1,0:T(8,128)(2,1)}, u32[]{:S(2)}, u32[]{:S(2)}) collective-permute-start(bf16[256,2176]{1,0:T(8,128)(2,1)S(1)} %bitcast.120), channel_id=1, source_target_pairs={{1,0},{2,1},{3,2},{4,3},{5,4},{6,5},{7,6},{8,7},{9,8},{10,9},{11,1... | collective-permute-start | bytes 3342344 | tf_op jit(solution)/shard_map/ppermute | solution.py:111
  62.3 0.1 slice_bitcast_fusion
  62.4 12.1 %all-to-all-done.1 = bf16[2,4,64,2176]{3,2,0,1:T(8,128)(2,1)} async-done(((bf16[2,4,64,2176]{3,2,0,1:T(8,128)(2,1)}), bf16[2,4,64,2176]{3,2,0,1:T(8,128)(2,1)}, u32[]{:S(2)}, u32[]{:S(2)}) %all-to-all-start.1) | async-done | bytes 2228256 | tf_op jit(solution)/shard_map/all_to_all | solution.py:109
  74.6 3.2 %fusion.27 = (bf16[1,4,64,2176]{3,2,1,0:T(8,128)(2,1)}, bf16[1,4,64,2176]{3,2,1,0:T(8,128)(2,1)}) fusion(bf16[2,4,64,2176]{3,2,0,1:T(8,128)(2,1)} %all-to-all-done.1), kind=kLoop, calls=%fused_computation.82 | loop fusion | bytes 4456448 | tf_op jit(solution)/shard_map/slice | solution.py:111
  77.7 1.9 %collective-permute-start.4 = (bf16[256,2176]{1,0:T(8,128)(2,1)}, bf16[256,2176]{1,0:T(8,128)(2,1)}, u32[]{:S(2)}, u32[]{:S(2)}) collective-permute-start(bf16[256,2176]{1,0:T(8,128)(2,1)} %bitcast.31), channel_id=1, source_target_pairs={{0,1},{1,2},{2,3},{3,4},{4,5},{5,6},{6,7},{7,8},{8,9},{9,10},{10,1... | collective-permute-start | bytes 3342344 | tf_op jit(solution)/shard_map/ppermute | solution.py:110
  79.7 0.1 select_dynamic-update-slice_fusion.1
  79.8 0.1 select_dynamic-update-slice_fusion
  79.9 0.1 constant_dynamic-update-slice_fusion.3
  80.0 0.1 constant_dynamic-update-slice_fusion.2
  80.1 3.2 %copy.48 = bf16[2,4,64,2176]{3,2,1,0:T(8,128)(2,1)} copy(bf16[2,4,64,2176]{3,2,0,1:T(8,128)(2,1)} %all-to-all-done.1) | data formatting | bytes 4456448 | tf_op jit(solution)/shard_map/all_to_all | solution.py:109
  83.2 3.6 %collective-permute-start.5 = (bf16[256,2176]{1,0:T(8,128)(2,1)}, bf16[256,2176]{1,0:T(8,128)(2,1)}, u32[]{:S(2)}, u32[]{:S(2)}) collective-permute-start(bf16[256,2176]{1,0:T(8,128)(2,1)} %bitcast.32), channel_id=1, source_target_pairs={{1,0},{2,1},{3,2},{4,3},{5,4},{6,5},{7,6},{8,7},{9,8},{10,9},{11,1... | collective-permute-start | bytes 3342344 | tf_op jit(solution)/shard_map/ppermute | solution.py:111
  87.0 0.1 add_dynamic-update-slice_fusion.coef_ref
  87.2 0.6 copy-done.6
  87.8 7.8 %shard_map.28 = bf16[2,256,2176]{2,1,0:T(8,128)(2,1)} custom-call(bf16[2,256,2176]{2,1,0:T(8,128)(2,1)} %bitcast.108, bf16[256,2176]{1,0:T(8,128)(2,1)} %collective-permute-done.below_ref, bf16[256,2176]{1,0:T(8,128)(2,1)} %collective-permute-done.1.above_ref, f32[7,2,2176]{2,1,0:T(2,128)} %copy-done.6), custom_call_target="tpu_custom_call" | custom-call | tf_op jit(solution)/shard_map/pallas_call | solution.py:52
  95.6 2.5 %convolution_bitcast_fusion.3 = f32[256,256]{0,1:T(8,128)S(1)} fusion(bf16[2,256,2176]{2,1,0:T(8,128)(2,1)} %shard_map.28, bf16[2,256,2176]{2,1,0:T(8,128)(2,1)S(1)} %bitcast.109), kind=kOutput, calls=%fused_computation.7 | convolution fusion | flops 570425344 | bytes 4718592 | tf_op jit(solution)/shard_map/dot_general | solution.py:125
  98.2 0.4 copy-done.4
  98.6 0.8 convolution_bitcast_fusion.2
  99.4 0.8 collective-permute-done.5.above_ref
  100.2 7.8 %shard_map.29 = bf16[2,256,2176]{2,1,0:T(8,128)(2,1)} custom-call(bf16[2,256,2176]{2,1,0:T(8,128)(2,1)} %bitcast.111, bf16[256,2176]{1,0:T(8,128)(2,1)} %collective-permute-done.4.below_ref, bf16[256,2176]{1,0:T(8,128)(2,1)} %collective-permute-done.5.above_ref, f32[7,2,2176]{2,1,0:T(2,128)} %copy-done.6), custom_call_target="tpu_custom_call" | custom-call | tf_op jit(solution)/shard_map/pallas_call | solution.py:52
  108.0 2.5 %convolution_bitcast_fusion.1 = f32[256,256]{0,1:T(8,128)S(1)} fusion(bf16[2,256,2176]{2,1,0:T(8,128)(2,1)} %shard_map.29, bf16[2,256,2176]{2,1,0:T(8,128)(2,1)S(1)} %bitcast.110), kind=kOutput, calls=%fused_computation.5 | convolution fusion | flops 570425344 | bytes 4718592 | tf_op jit(solution)/shard_map/dot_general | solution.py:125
  110.5 0.4 copy-done.3
  110.9 0.8 convolution_bitcast_fusion
  111.7 0.1 maximum_maximum_fusion
  111.8 0.3 copy.51
  112.2 0.6 collective-permute-start.6
  112.9 2.1 %collective-permute-start.7 = (f32[2,64,512]{2,1,0:T(8,128)S(1)}, f32[2,64,512]{2,1,0:T(8,128)S(1)}, u32[]{:S(2)}, u32[]{:S(2)}) collective-permute-start(f32[2,64,512]{2,1,0:T(8,128)S(1)} %get-tuple-element.51), channel_id=1, source_target_pairs={{0,128},{64,192},{128,0},{192,64},{1,129},{65,193},{129,1},{193,65... | collective-permute-start | bytes 786440 | tf_op jit(solution)/shard_map/ppermute | solution.py:132
  115.0 0.8 collective-permute-start.8
  115.8 6.7 %collective-permute-done.6 = f32[2,64,512]{2,1,0:T(8,128)S(1)} collective-permute-done((f32[2,64,512]{2,1,0:T(8,128)S(1)}, f32[2,64,512]{2,1,0:T(8,128)S(1)}, u32[]{:S(2)}, u32[]{:S(2)}) %collective-permute-start.6) | collective-permute-done | bytes 262176 | tf_op jit(solution)/shard_map/ppermute | solution.py:132
  122.4 4.5 %collective-permute-done.7 = f32[2,64,512]{2,1,0:T(8,128)S(1)} collective-permute-done((f32[2,64,512]{2,1,0:T(8,128)S(1)}, f32[2,64,512]{2,1,0:T(8,128)S(1)}, u32[]{:S(2)}, u32[]{:S(2)}) %collective-permute-start.7) | collective-permute-done | bytes 262176 | tf_op jit(solution)/shard_map/ppermute | solution.py:132
  127.0 1.7 %collective-permute-done.8 = f32[2,64,512]{2,1,0:T(8,128)S(1)} collective-permute-done((f32[2,64,512]{2,1,0:T(8,128)S(1)}, f32[2,64,512]{2,1,0:T(8,128)S(1)}, u32[]{:S(2)}, u32[]{:S(2)}) %collective-permute-start.8) | collective-permute-done | bytes 262176 | tf_op jit(solution)/shard_map/ppermute | solution.py:132
  128.7 0.1 fusion.7
  128.8 0.3 reshape.466
  129.1 0.2 copy.55
  129.3 3.9 %all_to_all.25 = f32[2,128,8,4,8]{1,4,3,2,0:T(8,128)S(1)} all-to-all(f32[2,128,8,4,8]{1,4,3,2,0:T(8,128)S(1)} %copy.56), channel_id=1, replica_groups=mesh['node'=4,'z'=8,'y'=4,'core'=2] {'core'}, dimensions={0} | all-to-all | bytes 524288 | tf_op jit(solution)/shard_map/all_to_all | solution.py:137
  133.3 9.5 %all_to_all.26 = f32[4,128,8,8]{1,3,2,0:T(8,128)S(1)} all-to-all(f32[4,128,8,8]{1,3,2,0:T(8,128)S(1)} %copy.58), channel_id=1, replica_groups=mesh['node'=4,'z'=8,'y'=4,'core'=2] {'y'}, dimensions={0} | all-to-all | bytes 262144 | tf_op jit(solution)/shard_map/all_to_all | solution.py:137
  142.8 16.3 %all_to_all.27 = f32[8,128,8]{1,2,0:T(8,128)S(1)} all-to-all(f32[8,128,8]{1,2,0:T(8,128)S(1)} %bitcast.123), channel_id=1, replica_groups=mesh['node'=4,'z'=8,'y'=4,'core'=2] {'z'}, dimensions={0} | all-to-all | bytes 65536 | tf_op jit(solution)/shard_map/all_to_all | solution.py:137
  159.1 0.6 broadcast_multiply_fusion
  (45 shorter events, 0.9 us)
Async XLA Ops:
  7.7 1.3 copy-start.5
  7.9 1.1 copy-start.8
  11.2 32.0 %all-to-all-start = ((bf16[2,4,64,2176]{3,2,0,1:T(8,128)(2,1)}), bf16[2,4,64,2176]{3,2,0,1:T(8,128)(2,1)S(1)}, u32[]{:S(2)}, u32[]{:S(2)}) async-start(bf16[2,4,64,2176]{3,2,0,1:T(8,128)(2,1)} %pad_maximum_fusion), calls=%async_computation | async-start | bytes 4456448 | tf_op jit(solution)/shard_map/all_to_all | solution.py:109
  43.2 31.4 %all-to-all-start.1 = ((bf16[2,4,64,2176]{3,2,0,1:T(8,128)(2,1)}), bf16[2,4,64,2176]{3,2,0,1:T(8,128)(2,1)}, u32[]{:S(2)}, u32[]{:S(2)}) async-start(bf16[2,4,64,2176]{3,2,0,1:T(8,128)(2,1)} %pad_maximum_fusion.1), calls=%async_computation.1 | async-start | bytes 4456448 | tf_op jit(solution)/shard_map/all_to_all | solution.py:109
  47.7 1.6 copy-start.7
  49.9 33.4 %collective-permute-start.2 = (bf16[2176]{0:T(1024)(128)(2,1)S(1)}, bf16[2176]{0:T(1024)(128)(2,1)S(1)}, u32[]{:S(2)}, u32[]{:S(2)}) collective-permute-start(bf16[2176]{0:T(1024)(128)(2,1)S(1)} %get-tuple-element.31), channel_id=1, source_target_pairs={{0,1},{1,2},{2,3},{3,4},{4,5},{5,6},{6,7},{7,8},{8,9},{9,10},{10,1... | collective-permute-start | bytes 13064 | tf_op jit(solution)/shard_map/ppermute | solution.py:117
  51.8 35.2 %collective-permute-start.3 = (bf16[2176]{0:T(1024)(128)(2,1)S(1)}, bf16[2176]{0:T(1024)(128)(2,1)S(1)}, u32[]{:S(2)}, u32[]{:S(2)}) collective-permute-start(bf16[2176]{0:T(1024)(128)(2,1)S(1)} %get-tuple-element.30), channel_id=1, source_target_pairs={{1,0},{2,1},{3,2},{4,3},{5,4},{6,5},{7,6},{8,7},{9,8},{10,9},{11,1... | collective-permute-start | bytes 13064 | tf_op jit(solution)/shard_map/ppermute | solution.py:118
  56.6 30.5 %collective-permute-start = (bf16[256,2176]{1,0:T(8,128)(2,1)}, bf16[256,2176]{1,0:T(8,128)(2,1)}, u32[]{:S(2)}, u32[]{:S(2)}) collective-permute-start(bf16[256,2176]{1,0:T(8,128)(2,1)} %bitcast.6), channel_id=1, source_target_pairs={{0,1},{1,2},{2,3},{3,4},{4,5},{5,6},{6,7},{7,8},{8,9},{9,10},{10,1... | collective-permute-start | bytes 3342344 | tf_op jit(solution)/shard_map/ppermute | solution.py:110
  58.5 28.6 %collective-permute-start.1 = (bf16[256,2176]{1,0:T(8,128)(2,1)S(1)}, bf16[256,2176]{1,0:T(8,128)(2,1)}, u32[]{:S(2)}, u32[]{:S(2)}) collective-permute-start(bf16[256,2176]{1,0:T(8,128)(2,1)S(1)} %bitcast.120), channel_id=1, source_target_pairs={{1,0},{2,1},{3,2},{4,3},{5,4},{6,5},{7,6},{8,7},{9,8},{10,9},{11,1... | collective-permute-start | bytes 3342344 | tf_op jit(solution)/shard_map/ppermute | solution.py:111
  77.7 21.6 %collective-permute-start.4 = (bf16[256,2176]{1,0:T(8,128)(2,1)}, bf16[256,2176]{1,0:T(8,128)(2,1)}, u32[]{:S(2)}, u32[]{:S(2)}) collective-permute-start(bf16[256,2176]{1,0:T(8,128)(2,1)} %bitcast.31), channel_id=1, source_target_pairs={{0,1},{1,2},{2,3},{3,4},{4,5},{5,6},{6,7},{7,8},{8,9},{9,10},{10,1... | collective-permute-start | bytes 3342344 | tf_op jit(solution)/shard_map/ppermute | solution.py:110
  83.2 17.0 %collective-permute-start.5 = (bf16[256,2176]{1,0:T(8,128)(2,1)}, bf16[256,2176]{1,0:T(8,128)(2,1)}, u32[]{:S(2)}, u32[]{:S(2)}) collective-permute-start(bf16[256,2176]{1,0:T(8,128)(2,1)} %bitcast.32), channel_id=1, source_target_pairs={{1,0},{2,1},{3,2},{4,3},{5,4},{6,5},{7,6},{8,7},{9,8},{10,9},{11,1... | collective-permute-start | bytes 3342344 | tf_op jit(solution)/shard_map/ppermute | solution.py:111
  87.1 0.7 copy-start.6
  87.1 8.5 %copy-start = (bf16[2,4,64,2176]{3,2,1,0:T(8,128)(2,1)S(1)}, bf16[2,4,64,2176]{3,2,1,0:T(8,128)(2,1)}, u32[]{:S(2)}) copy-start(bf16[2,4,64,2176]{3,2,1,0:T(8,128)(2,1)} %copy.42) | copy-start | bytes 6684676
  95.6 2.6 %copy-start.1 = (bf16[2,4,64,2176]{3,2,1,0:T(8,128)(2,1)S(1)}, bf16[2,4,64,2176]{3,2,1,0:T(8,128)(2,1)}, u32[]{:S(2)}) copy-start(bf16[2,4,64,2176]{3,2,1,0:T(8,128)(2,1)} %copy.48) | copy-start | bytes 6684676
  95.6 3.0 %copy-start.4 = (bf16[2,256,2176]{2,1,0:T(8,128)(2,1)S(1)}, bf16[2,256,2176]{2,1,0:T(8,128)(2,1)}, u32[]{:S(2)}) copy-start(bf16[2,256,2176]{2,1,0:T(8,128)(2,1)} %shard_map.28) | copy-start | bytes 6684676
  108.0 2.6 %copy-start.2 = (bf16[2,4,64,2176]{3,2,1,0:T(8,128)(2,1)S(1)}, bf16[2,4,64,2176]{3,2,1,0:T(8,128)(2,1)}, u32[]{:S(2)}) copy-start(bf16[2,4,64,2176]{3,2,1,0:T(8,128)(2,1)} %copy.48) | copy-start | bytes 6684676
  108.0 3.0 %copy-start.3 = (bf16[2,256,2176]{2,1,0:T(8,128)(2,1)S(1)}, bf16[2,256,2176]{2,1,0:T(8,128)(2,1)}, u32[]{:S(2)}) copy-start(bf16[2,256,2176]{2,1,0:T(8,128)(2,1)} %shard_map.29) | copy-start | bytes 6684676
  112.2 10.2 %collective-permute-start.6 = (f32[2,64,512]{2,1,0:T(8,128)S(1)}, f32[2,64,512]{2,1,0:T(8,128)S(1)}, u32[]{:S(2)}, u32[]{:S(2)}) collective-permute-start(f32[2,64,512]{2,1,0:T(8,128)S(1)} %get-tuple-element.50), channel_id=1, source_target_pairs={{0,64},{64,128},{128,192},{192,0},{1,65},{65,129},{129,193},{193,1... | collective-permute-start | bytes 786440 | tf_op jit(solution)/shard_map/ppermute | solution.py:132
  112.9 14.1 %collective-permute-start.7 = (f32[2,64,512]{2,1,0:T(8,128)S(1)}, f32[2,64,512]{2,1,0:T(8,128)S(1)}, u32[]{:S(2)}, u32[]{:S(2)}) collective-permute-start(f32[2,64,512]{2,1,0:T(8,128)S(1)} %get-tuple-element.51), channel_id=1, source_target_pairs={{0,128},{64,192},{128,0},{192,64},{1,129},{65,193},{129,1},{193,65... | collective-permute-start | bytes 786440 | tf_op jit(solution)/shard_map/ppermute | solution.py:132
  115.0 13.7 %collective-permute-start.8 = (f32[2,64,512]{2,1,0:T(8,128)S(1)}, f32[2,64,512]{2,1,0:T(8,128)S(1)}, u32[]{:S(2)}, u32[]{:S(2)}) collective-permute-start(f32[2,64,512]{2,1,0:T(8,128)S(1)} %select_bitcast_fusion), channel_id=1, source_target_pairs={{0,192},{64,0},{128,64},{192,128},{1,193},{65,1},{129,65},{193,129... | collective-permute-start | bytes 786440 | tf_op jit(solution)/shard_map/ppermute | solution.py:132

commit v13 on v12

--- a/solution.py
+++ b/solution.py
@@ -24,10 +24,11 @@
     return jnp.concatenate([head, values[..., :-offset]], axis=-1)
 
 
-def stencil_kernel(x_ref, below_ref, above_ref, coef_ref, out_ref):
+def stencil_kernel(x_ref, below_ref, above_ref, coef_ref, out_ref, copy_ref):
     span = below_ref.shape[1]
     lane = lax.broadcasted_iota(jnp.int32, (1, span), 1)
     inner = lane < span - 2 * NZ
+    copy_ref[...] = x_ref[...]
     planes = [x_ref[p].astype(jnp.float32) for p in range(2)]
     below = below_ref[...].astype(jnp.float32)
     above = above_ref[...].astype(jnp.float32)
@@ -48,18 +49,21 @@
 
 
 def stencil(field, below, above, coef):
-    planes, snaps, span = field.shape
+    nodes, planes, step, span = field.shape
+    blocks = step // ROWS
+    out_spec = pl.BlockSpec((planes, ROWS, span), lambda a, i: (0, a * blocks + i, 0))
+    flat = jax.ShapeDtypeStruct((planes, nodes * step, span), jnp.bfloat16)
     return pl.pallas_call(
         stencil_kernel,
-        grid=(snaps // ROWS,),
+        grid=(nodes, blocks),
         in_specs=[
-            pl.BlockSpec((planes, ROWS, span), lambda i: (0, i, 0)),
-            pl.BlockSpec((ROWS, span), lambda i: (i, 0)),
-            pl.BlockSpec((ROWS, span), lambda i: (i, 0)),
-            pl.BlockSpec(coef.shape, lambda i: (0, 0, 0)),
+            pl.BlockSpec((None, planes, ROWS, span), lambda a, i: (a, 0, i, 0)),
+            pl.BlockSpec((None, ROWS, span), lambda a, i: (a, i, 0)),
+            pl.BlockSpec((None, ROWS, span), lambda a, i: (a, i, 0)),
+            pl.BlockSpec(coef.shape, lambda a, i: (0, 0, 0)),
         ],
-        out_specs=pl.BlockSpec((planes, ROWS, span), lambda i: (0, i, 0)),
-        out_shape=jax.ShapeDtypeStruct(field.shape, jnp.bfloat16),
+        out_specs=[out_spec, out_spec],
+        out_shape=[flat, flat],
     )(field, below, above, coef)
 
 
@@ -86,7 +90,7 @@
         after = values[..., (q + 1) * chunk:(q + 1) * chunk + NZ] if q + 1 < nodes else zero
         before = values[..., q * chunk - NZ:q * chunk] if q > 0 else zero
         pieces.append(jnp.concatenate([values[..., q * chunk:(q + 1) * chunk], after, before], axis=-1))
-    return jnp.stack(pieces, axis=-3)
+    return jnp.stack(pieces, axis=0)
 
 
 def per_device(snapshots, kappa):
@@ -106,19 +110,20 @@
     images, fields, fronts = [], [], []
     for g in range(GROUPS):
         major = jnp.transpose(snapshots[g * step:(g + 1) * step], (1, 0, 2))
-        field = lax.all_to_all(chunked(major, nodes), "node", 1, 1, tiled=True).reshape(planes, nodes * step, span)
-        below = lax.ppermute(field[1], SPACE, up)
-        above = lax.ppermute(field[0], SPACE, down)
+        field = lax.all_to_all(chunked(major, nodes), "node", 0, 0, tiled=True)
+        below = lax.ppermute(field[:, 1], SPACE, up)
+        above = lax.ppermute(field[:, 0], SPACE, down)
         fields.append(field)
         fronts.append((below, above))
         if g == 0:
             late, _ = lax.optimization_barrier((kappa, field))
-            kap_chunk = jnp.take(chunked(late[:, None], nodes)[:, :, 0], me, axis=1)
+            kap_chunk = jnp.take(chunked(late[:, None], nodes), me, axis=0)[:, 0]
             kap_below = lax.ppermute(kap_chunk[1], SPACE, up)
             kap_above = lax.ppermute(kap_chunk[0], SPACE, down)
             coef = weights(kap_chunk, kap_below, kap_above)
-    for field, (below, above) in zip(fields, fronts):
-        images.append(stencil(field, below, above, coef))
+    for g, (below, above) in enumerate(fronts):
+        image, fields[g] = stencil(fields[g], below, above, coef)
+        images.append(image)
     dims = (((0, 2), (0, 2)), ((), ()))
     part = jnp.concatenate([
         jnp.concatenate([

time: 162 us -> 163 us (level)
  waiting for transfers between devices: 46.4 us -> 43 us
    all_to_all x2 -> x0, local copies, waits for them, and re-layouts: 4.73 us -> none  [per_device(): lax.all_to_all(chunked(major, nodes), 'node', 1, 1, tiled=True)]
    slice x2 -> x0, local copies, waits for them, and re-layouts: 4.36 us -> none  [per_device(): above = lax.ppermute(field[0], SPACE, down)]
    squeeze x0 -> x2, local copies, waits for them, and re-layouts: none -> 4.31 us  [per_device(): above = lax.ppermute(field[:, 0], SPACE, down)]
    all_to_all x2, waiting for transfers between devices: 32.7 us -> 30.6 us  [per_device(): field = lax.all_to_all(chunked(major, nodes), 'node', 0, 0, tiled=True)]
    unnamed x18 -> x36, local copies, waits for them, and re-layouts: 2.32 us -> 4.21 us
  transfers between devices with their start and end apart: 11 -> 11, of which waited for: 6 -> 4; matrix products, arithmetic and copies ran while one was open for 13% -> 13% of each run, Pallas kernels for 5% -> 5%
where the time goes in v13:
time: 163 us; the launch traced here: 161 us
  waiting for transfers between devices  43 us (26%)
  blocking collectives  30.4 us (19%)
  starting transfers between devices  28.9 us (18%)
  local copies, waits for them, and re-layouts  27.8 us (17%)
  Pallas kernels  16.7 us (10%)
  matrix products  7.15 us (4%)
  other arithmetic  6.28 us (4%)
    all_to_all x2, waiting for transfers between devices, per_device(): field = lax.all_to_all(chunked(major, nodes), 'node', 0, 0, tiled=True)  30.6 us
    all_to_all x3, blocking collectives, per_device(): total = lax.all_to_all(total, SPACE[axis], 0, 0, tiled=True).sum(axis=0)  30.4 us
    pallas_call x2, Pallas kernels, stencil(): pl.pallas_call(stencil_kernel, grid=(nodes, blocks), in_specs=[pl.BlockSp...  16.7 us
    ppermute x3, waiting for transfers between devices, per_device(): lax.ppermute(blk, 'node', [(i, (i + d) % nodes) for i in range(nodes)])  12.3 us
    all_to_all x2, starting transfers between devices, per_device(): field = lax.all_to_all(chunked(major, nodes), 'node', 0, 0, tiled=True)  8.76 us
    ppermute x2, starting transfers between devices, per_device(): above = lax.ppermute(field[:, 0], SPACE, down)  7.29 us
    dot_general x4, matrix products, per_device(): lax.dot_general(im, fd, dims, preferred_element_type=jnp.float32)  7.15 us
    slice x1, local copies, waits for them, and re-layouts, per_device(): major = jnp.transpose(snapshots[g * step:(g + 1) * step], (1, 0, 2))  5.04 us
  transfers between devices with their start and end apart: 11, of which 4 were waited for; matrix products, arithmetic and copies ran while one was open for 13% of the time, Pallas kernels for 5%

profile of v13, /device:TPU:8, one launch (start us, length us, event | category | flops | bytes accessed | tf_op | source)
XLA Modules:
  0.0 160.6 jit_solution(5654387610317503424)
XLA Ops:
  0.0 5.0 %fusion.26 = (bf16[64,2,8192]{2,1,0:T(2,128)(2,1)S(1)}, bf16[64,2,8192]{2,1,0:T(2,128)(2,1)S(1)}) fusion(bf16[128,2,8192]{2,1,0:T(2,128)(2,1)} %param.4), kind=kLoop, calls=%fused_computation.86 | loop fusion | bytes 8388608 | tf_op jit(solution)/shard_map/slice | solution.py:112
  5.1 2.7 %copy_bitcast_fusion = (bf16[2,64,8192]{2,1,0:T(8,128)(2,1)S(1)}, bf16[2,64,8192]{2,1,0:T(8,128)(2,1)S(1)}) fusion(bf16[64,2,8192]{2,1,0:T(2,128)(2,1)S(1)} %get-tuple-element.43, bf16[64,2,8192]{2,1,0:T(2,128)(2,1)S(1)} %get-tuple-element.42), kind=kLoop, calls=%fused_computation.2 | loop fusion | bytes 8388608 | tf_op jit(solution)/shard_map/transpose | solution.py:112
  7.7 0.1 fusion.28
  7.8 0.1 fusion.27
  8.2 0.9 copy-done.1
  9.1 0.1 fusion.1
  9.2 0.3 concatenate.155
  9.5 1.7 %pad_maximum_fusion = bf16[4,2,64,2176]{3,2,1,0:T(8,128)(2,1)} fusion(bf16[1,2,64,2176]{3,2,1,0:T(8,128)(2,1)S(1)} %bitcast.154, bf16[1,2,64,2176]{3,2,1,0:T(8,128)(2,1)S(1)} %maximum_bitcast_fusion.1, bf16[1,2,64,2176]{3,2,1,0:T(8,128)(2,1)S(1)} %maximum_bitcast_fusion, bf16[1,2,64,2176]{3,2,1,0:T(8,128)(2,1)S(1)} %get-tuple-element.75), kind=kLoop, calls=%fused_computation | loop fusion | flops 3342336 | bytes 4456448 | tf_op jit(solution)/shard_map/stack | solution.py:93
  11.2 4.3 %all-to-all-start = ((bf16[4,2,64,2176]{3,2,1,0:T(8,128)(2,1)}), bf16[4,2,64,2176]{3,2,1,0:T(8,128)(2,1)S(1)}, u32[]{:S(2)}, u32[]{:S(2)}) async-start(bf16[4,2,64,2176]{3,2,1,0:T(8,128)(2,1)} %pad_maximum_fusion), calls=%async_computation | async-start | bytes 4456448 | tf_op jit(solution)/shard_map/all_to_all | solution.py:113
  15.5 0.6 fusion.18
  16.1 0.9 fusion.30
  17.0 1.9 %slice.248 = bf16[2,64,2048]{2,1,0:T(8,128)(2,1)} slice(bf16[2,64,8192]{2,1,0:T(8,128)(2,1)} %copy-done.1), slice={[0:2], [0:64], [6144:8192]} | slice | bytes 1048576 | tf_op jit(solution)/shard_map/slice | solution.py:92
  18.8 1.2 concatenate.175
  20.0 1.3 fusion.29
  21.5 1.7 %pad_maximum_fusion.1 = bf16[4,2,64,2176]{3,2,1,0:T(8,128)(2,1)} fusion(bf16[1,2,64,2176]{3,2,1,0:T(8,128)(2,1)S(1)} %bitcast.153, bf16[1,2,64,2176]{3,2,1,0:T(8,128)(2,1)S(1)} %maximum_bitcast_fusion.3, bf16[1,2,64,2176]{3,2,1,0:T(8,128)(2,1)S(1)} %maximum_bitcast_fusion.2, bf16[1,2,64,2176]{3,2,1,0:T(8,128)(2,1)S(1)} %get-tuple-element.76), kind=kLoop, calls=%fused_computation.1 | loop fusion | flops 3342336 | bytes 4456448 | tf_op jit(solution)/shard_map/stack | solution.py:93
  23.2 20.0 %all-to-all-done.x_ref = bf16[4,2,64,2176]{3,2,1,0:T(8,128)(2,1)S(1)} async-done(((bf16[4,2,64,2176]{3,2,1,0:T(8,128)(2,1)}), bf16[4,2,64,2176]{3,2,1,0:T(8,128)(2,1)S(1)}, u32[]{:S(2)}, u32[]{:S(2)}) %all-to-all-start) | async-done | bytes 2228256 | tf_op jit(solution)/shard_map/all_to_all | solution.py:113
  43.2 4.5 %all-to-all-start.1 = ((bf16[4,2,64,2176]{3,2,1,0:T(8,128)(2,1)}), bf16[4,2,64,2176]{3,2,1,0:T(8,128)(2,1)}, u32[]{:S(2)}, u32[]{:S(2)}) async-start(bf16[4,2,64,2176]{3,2,1,0:T(8,128)(2,1)} %pad_maximum_fusion.1), calls=%async_computation.1 | async-start | bytes 4456448 | tf_op jit(solution)/shard_map/all_to_all | solution.py:113
  48.0 0.1 concatenate.159
  48.2 0.7 slice_reduce_fusion
  48.9 0.7 slice_bitcast_fusion.12
  49.5 1.9 %collective-permute-start.2 = (bf16[2176]{0:T(1024)(128)(2,1)}, bf16[2176]{0:T(1024)(128)(2,1)}, u32[]{:S(2)}, u32[]{:S(2)}) collective-permute-start(bf16[2176]{0:T(1024)(128)(2,1)} %get-tuple-element.39), channel_id=1, source_target_pairs={{0,1},{1,2},{2,3},{3,4},{4,5},{5,6},{6,7},{7,8},{8,9},{9,10},{10,1... | collective-permute-start | bytes 13064 | tf_op jit(solution)/shard_map/ppermute | solution.py:121
  51.4 0.6 slice_bitcast_fusion.8
  52.0 3.6 %collective-permute-start.3 = (bf16[2176]{0:T(1024)(128)(2,1)}, bf16[2176]{0:T(1024)(128)(2,1)}, u32[]{:S(2)}, u32[]{:S(2)}) collective-permute-start(bf16[2176]{0:T(1024)(128)(2,1)} %get-tuple-element.38), channel_id=1, source_target_pairs={{1,0},{2,1},{3,2},{4,3},{5,4},{6,5},{7,6},{8,7},{9,8},{10,9},{11,1... | collective-permute-start | bytes 13064 | tf_op jit(solution)/shard_map/ppermute | solution.py:122
  55.7 1.2 slice_bitcast_fusion.2
  56.9 1.9 %collective-permute-start = (bf16[4,64,2176]{2,1,0:T(8,128)(2,1)}, bf16[4,64,2176]{2,1,0:T(8,128)(2,1)S(1)}, u32[]{:S(2)}, u32[]{:S(2)}) collective-permute-start(bf16[4,64,2176]{2,1,0:T(8,128)(2,1)} %get-tuple-element.45), channel_id=1, source_target_pairs={{0,1},{1,2},{2,3},{3,4},{4,5},{5,6},{6,7},{7,8},{8,9},{9,10},{10,1... | collective-permute-start | bytes 3342344 | tf_op jit(solution)/shard_map/ppermute | solution.py:114
  58.8 3.6 %collective-permute-start.1 = (bf16[4,64,2176]{2,1,0:T(8,128)(2,1)S(1)}, bf16[4,64,2176]{2,1,0:T(8,128)(2,1)S(1)}, u32[]{:S(2)}, u32[]{:S(2)}) collective-permute-start(bf16[4,64,2176]{2,1,0:T(8,128)(2,1)S(1)} %get-tuple-element.44), channel_id=1, source_target_pairs={{1,0},{2,1},{3,2},{4,3},{5,4},{6,5},{7,6},{8,7},{9,8},{10,9},{11,1... | collective-permute-start | bytes 3342344 | tf_op jit(solution)/shard_map/ppermute | solution.py:115
  62.4 0.7 slice_bitcast_fusion.10
  63.2 0.7 slice_bitcast_fusion.4
  63.9 10.7 %all-to-all-done.1.x_ref = bf16[4,2,64,2176]{3,2,1,0:T(8,128)(2,1)} async-done(((bf16[4,2,64,2176]{3,2,1,0:T(8,128)(2,1)}), bf16[4,2,64,2176]{3,2,1,0:T(8,128)(2,1)}, u32[]{:S(2)}, u32[]{:S(2)}) %all-to-all-start.1) | async-done | bytes 2228256 | tf_op jit(solution)/shard_map/all_to_all | solution.py:113
  74.6 3.1 %slice_bitcast_fusion = (bf16[4,64,2176]{2,1,0:T(8,128)(2,1)}, bf16[4,64,2176]{2,1,0:T(8,128)(2,1)}) fusion(bf16[4,2,64,2176]{3,2,1,0:T(8,128)(2,1)} %all-to-all-done.1.x_ref), kind=kLoop, calls=%fused_computation.8 | loop fusion | bytes 4456448 | tf_op jit(solution)/shard_map/squeeze | solution.py:115
  77.7 1.9 %collective-permute-start.4 = (bf16[4,64,2176]{2,1,0:T(8,128)(2,1)}, bf16[4,64,2176]{2,1,0:T(8,128)(2,1)}, u32[]{:S(2)}, u32[]{:S(2)}) collective-permute-start(bf16[4,64,2176]{2,1,0:T(8,128)(2,1)} %get-tuple-element.47), channel_id=1, source_target_pairs={{0,1},{1,2},{2,3},{3,4},{4,5},{5,6},{6,7},{7,8},{8,9},{9,10},{10,1... | collective-permute-start | bytes 3342344 | tf_op jit(solution)/shard_map/ppermute | solution.py:114
  79.7 0.1 select_dynamic-update-slice_fusion.1
  79.8 0.1 select_dynamic-update-slice_fusion
  79.9 0.1 constant_dynamic-update-slice_fusion.3
  80.0 0.1 constant_dynamic-update-slice_fusion.2
  80.1 3.6 %collective-permute-start.5 = (bf16[4,64,2176]{2,1,0:T(8,128)(2,1)}, bf16[4,64,2176]{2,1,0:T(8,128)(2,1)}, u32[]{:S(2)}, u32[]{:S(2)}) collective-permute-start(bf16[4,64,2176]{2,1,0:T(8,128)(2,1)} %get-tuple-element.46), channel_id=1, source_target_pairs={{1,0},{2,1},{3,2},{4,3},{5,4},{6,5},{7,6},{8,7},{9,8},{10,9},{11,1... | collective-permute-start | bytes 3342344 | tf_op jit(solution)/shard_map/ppermute | solution.py:115
  83.8 0.7 reshape.573
  84.5 0.7 reshape.574
  85.2 0.1 add_dynamic-update-slice_fusion.coef_ref
  85.4 0.6 copy-done.8
  86.0 0.4 copy-done.6
  86.4 1.0 copy-done.7
  87.4 8.2 %shard_map.28 = (bf16[2,256,2176]{2,1,0:T(8,128)(2,1)}, bf16[2,256,2176]{2,1,0:T(8,128)(2,1)}) custom-call(bf16[4,2,64,2176]{3,2,1,0:T(8,128)(2,1)} %copy-done, bf16[4,64,2176]{2,1,0:T(8,128)(2,1)} %copy-done.6, bf16[4,64,2176]{2,1,0:T(8,128)(2,1)} %copy-done.7, f32[7,2,2176]{2,1,0:T(2,128)} %copy-done.8), custom_call_target="tpu_custom_call" | custom-call | tf_op jit(solution)/shard_map/pallas_call | solution.py:56
  95.7 3.1 %convolution_bitcast_fusion.3 = f32[256,256]{0,1:T(8,128)S(1)} fusion(bf16[2,256,2176]{2,1,0:T(8,128)(2,1)} %get-tuple-element.12, bf16[2,256,2176]{2,1,0:T(8,128)(2,1)} %get-tuple-element.13), kind=kOutput, calls=%fused_computation.7 | convolution fusion | flops 570425344 | bytes 4718592 | tf_op jit(solution)/shard_map/dot_general | solution.py:130
  98.8 8.4 %shard_map.29 = (bf16[2,256,2176]{2,1,0:T(8,128)(2,1)}, bf16[2,256,2176]{2,1,0:T(8,128)(2,1)}) custom-call(bf16[4,2,64,2176]{3,2,1,0:T(8,128)(2,1)} %all-to-all-done.1.x_ref, bf16[4,64,2176]{2,1,0:T(8,128)(2,1)} %collective-permute-done.4.below_ref, bf16[4,64,2176]{2,1,0:T(8,128)(2,1)} %collective-permute-done.5.above_ref, f32[7,2,2176]{2,1,0:T(2,128)} %copy-done.8), custom_call_target="tpu_custom_call" | custom-call | tf_op jit(solution)/shard_map/pallas_call | solution.py:56
  107.2 2.5 %convolution_bitcast_fusion.2 = f32[256,256]{0,1:T(8,128)S(1)} fusion(bf16[2,256,2176]{2,1,0:T(8,128)(2,1)S(1)} %copy-done.3, bf16[2,256,2176]{2,1,0:T(8,128)(2,1)} %get-tuple-element.14), kind=kOutput, calls=%fused_computation.6 | convolution fusion | flops 570425344 | bytes 4718592 | tf_op jit(solution)/shard_map/dot_general | solution.py:130
  109.8 0.4 copy-done.4
  110.2 0.8 convolution_bitcast_fusion.1
  111.0 0.8 copy-done.5
  111.8 0.8 convolution_bitcast_fusion
  112.6 0.1 maximum_maximum_fusion
  112.7 0.3 copy.53
  113.1 0.6 collective-permute-start.6
  113.8 2.1 %collective-permute-start.7 = (f32[2,64,512]{2,1,0:T(8,128)S(1)}, f32[2,64,512]{2,1,0:T(8,128)S(1)}, u32[]{:S(2)}, u32[]{:S(2)}) collective-permute-start(f32[2,64,512]{2,1,0:T(8,128)S(1)} %get-tuple-element.59), channel_id=1, source_target_pairs={{0,128},{64,192},{128,0},{192,64},{1,129},{65,193},{129,1},{193,65... | collective-permute-start | bytes 786440 | tf_op jit(solution)/shard_map/ppermute | solution.py:137
  115.9 0.8 collective-permute-start.8
  116.7 11.7 %collective-permute-done.6 = f32[2,64,512]{2,1,0:T(8,128)S(1)} collective-permute-done((f32[2,64,512]{2,1,0:T(8,128)S(1)}, f32[2,64,512]{2,1,0:T(8,128)S(1)}, u32[]{:S(2)}, u32[]{:S(2)}) %collective-permute-start.6) | collective-permute-done | bytes 262176 | tf_op jit(solution)/shard_map/ppermute | solution.py:137
  128.3 0.6 collective-permute-done.8
  129.0 0.1 fusion.7
  129.1 0.3 reshape.474
  129.4 0.2 copy.57
  129.6 3.9 %all_to_all.25 = f32[2,128,8,4,8]{1,4,3,2,0:T(8,128)S(1)} all-to-all(f32[2,128,8,4,8]{1,4,3,2,0:T(8,128)S(1)} %copy.58), channel_id=1, replica_groups=mesh['node'=4,'z'=8,'y'=4,'core'=2] {'core'}, dimensions={0} | all-to-all | bytes 524288 | tf_op jit(solution)/shard_map/all_to_all | solution.py:142
  133.6 9.5 %all_to_all.26 = f32[4,128,8,8]{1,3,2,0:T(8,128)S(1)} all-to-all(f32[4,128,8,8]{1,3,2,0:T(8,128)S(1)} %copy.60), channel_id=1, replica_groups=mesh['node'=4,'z'=8,'y'=4,'core'=2] {'y'}, dimensions={0} | all-to-all | bytes 262144 | tf_op jit(solution)/shard_map/all_to_all | solution.py:142
  143.1 16.9 %all_to_all.27 = f32[8,128,8]{1,2,0:T(8,128)S(1)} all-to-all(f32[8,128,8]{1,2,0:T(8,128)S(1)} %bitcast.158), channel_id=1, replica_groups=mesh['node'=4,'z'=8,'y'=4,'core'=2] {'z'}, dimensions={0} | all-to-all | bytes 65536 | tf_op jit(solution)/shard_map/all_to_all | solution.py:142
  160.1 0.6 broadcast_multiply_fusion
  (62 shorter events, 1.1 us)
Async XLA Ops:
  7.7 1.3 copy-start.1
  7.9 1.1 copy-start.13
  11.2 32.0 %all-to-all-start = ((bf16[4,2,64,2176]{3,2,1,0:T(8,128)(2,1)}), bf16[4,2,64,2176]{3,2,1,0:T(8,128)(2,1)S(1)}, u32[]{:S(2)}, u32[]{:S(2)}) async-start(bf16[4,2,64,2176]{3,2,1,0:T(8,128)(2,1)} %pad_maximum_fusion), calls=%async_computation | async-start | bytes 4456448 | tf_op jit(solution)/shard_map/all_to_all | solution.py:113
  23.2 24.5 %copy-start.11 = (bf16[2,8192]{1,0:T(2,128)(2,1)S(1)}, bf16[2,8192]{1,0:T(2,128)(2,1)}, u32[]{:S(2)}) copy-start(bf16[2,8192]{1,0:T(2,128)(2,1)} %param.5) | copy-start | bytes 98308
  43.2 12.5 %copy-start = (bf16[4,2,64,2176]{3,2,1,0:T(8,128)(2,1)}, bf16[4,2,64,2176]{3,2,1,0:T(8,128)(2,1)S(1)}, u32[]{:S(2)}) copy-start(bf16[4,2,64,2176]{3,2,1,0:T(8,128)(2,1)S(1)} %all-to-all-done.x_ref) | copy-start | bytes 6684676
  43.2 31.4 %all-to-all-start.1 = ((bf16[4,2,64,2176]{3,2,1,0:T(8,128)(2,1)}), bf16[4,2,64,2176]{3,2,1,0:T(8,128)(2,1)}, u32[]{:S(2)}, u32[]{:S(2)}) async-start(bf16[4,2,64,2176]{3,2,1,0:T(8,128)(2,1)} %pad_maximum_fusion.1), calls=%async_computation.1 | async-start | bytes 4456448 | tf_op jit(solution)/shard_map/all_to_all | solution.py:113
  49.5 30.6 %collective-permute-start.2 = (bf16[2176]{0:T(1024)(128)(2,1)}, bf16[2176]{0:T(1024)(128)(2,1)}, u32[]{:S(2)}, u32[]{:S(2)}) collective-permute-start(bf16[2176]{0:T(1024)(128)(2,1)} %get-tuple-element.39), channel_id=1, source_target_pairs={{0,1},{1,2},{2,3},{3,4},{4,5},{5,6},{6,7},{7,8},{8,9},{9,10},{10,1... | collective-permute-start | bytes 13064 | tf_op jit(solution)/shard_map/ppermute | solution.py:121
  52.0 32.5 %collective-permute-start.3 = (bf16[2176]{0:T(1024)(128)(2,1)}, bf16[2176]{0:T(1024)(128)(2,1)}, u32[]{:S(2)}, u32[]{:S(2)}) collective-permute-start(bf16[2176]{0:T(1024)(128)(2,1)} %get-tuple-element.38), channel_id=1, source_target_pairs={{1,0},{2,1},{3,2},{4,3},{5,4},{6,5},{7,6},{8,7},{9,8},{10,9},{11,1... | collective-permute-start | bytes 13064 | tf_op jit(solution)/shard_map/ppermute | solution.py:122
  56.9 28.5 %collective-permute-start = (bf16[4,64,2176]{2,1,0:T(8,128)(2,1)}, bf16[4,64,2176]{2,1,0:T(8,128)(2,1)S(1)}, u32[]{:S(2)}, u32[]{:S(2)}) collective-permute-start(bf16[4,64,2176]{2,1,0:T(8,128)(2,1)} %get-tuple-element.45), channel_id=1, source_target_pairs={{0,1},{1,2},{2,3},{3,4},{4,5},{5,6},{6,7},{7,8},{8,9},{9,10},{10,1... | collective-permute-start | bytes 3342344 | tf_op jit(solution)/shard_map/ppermute | solution.py:114
  58.8 26.6 %collective-permute-start.1 = (bf16[4,64,2176]{2,1,0:T(8,128)(2,1)S(1)}, bf16[4,64,2176]{2,1,0:T(8,128)(2,1)S(1)}, u32[]{:S(2)}, u32[]{:S(2)}) collective-permute-start(bf16[4,64,2176]{2,1,0:T(8,128)(2,1)S(1)} %get-tuple-element.44), channel_id=1, source_target_pairs={{1,0},{2,1},{3,2},{4,3},{5,4},{6,5},{7,6},{8,7},{9,8},{10,9},{11,1... | collective-permute-start | bytes 3342344 | tf_op jit(solution)/shard_map/ppermute | solution.py:115
  74.6 5.1 %copy-start.12 = (pred[2176]{0:T(1024)(128)(4,1)S(1)}, pred[2176]{0:T(1024)(128)(4,1)}, u32[]{:S(2)}) copy-start(pred[2176]{0:T(1024)(128)(4,1)} %get-tuple-element.80) | copy-start | bytes 6532
  74.6 5.1 %copy-start.15 = (f32[1,2,1]{2,1,0:T(2,128)S(1)}, f32[1,2,1]{2,1,0:T(2,128)}, u32[]{:S(2)}) copy-start(f32[1,2,1]{2,1,0:T(2,128)} %get-tuple-element.72) | copy-start | bytes 28
  74.6 5.2 %copy-start.14 = (f32[1,2,1]{2,1,0:T(2,128)S(1)}, f32[1,2,1]{2,1,0:T(2,128)}, u32[]{:S(2)}) copy-start(f32[1,2,1]{2,1,0:T(2,128)} %get-tuple-element.71) | copy-start | bytes 28
  74.6 5.3 %copy-start.9 = (f32[1,2,2112]{2,1,0:T(2,128)S(1)}, f32[1,2,2112]{2,1,0:T(2,128)}, u32[]{:S(2)}) copy-start(f32[1,2,2112]{2,1,0:T(2,128)} %get-tuple-element.70) | copy-start | bytes 50692
  74.6 5.3 %copy-start.17 = (f32[1,2,64]{2,1,0:T(2,128)S(1)}, f32[1,2,64]{2,1,0:T(2,128)}, u32[]{:S(2)}) copy-start(f32[1,2,64]{2,1,0:T(2,128)} %get-tuple-element.68) | copy-start | bytes 1540
  74.6 5.4 %copy-start.16 = (f32[1,2,64]{2,1,0:T(2,128)S(1)}, f32[1,2,64]{2,1,0:T(2,128)}, u32[]{:S(2)}) copy-start(f32[1,2,64]{2,1,0:T(2,128)} %get-tuple-element.67) | copy-start | bytes 1540
  74.6 9.8 %copy-start.10 = (f32[1,1,2176]{2,1,0:T(1,128)S(1)}, f32[1,1,2176]{2,1,0:T(1,128)}, u32[]{:S(2)}) copy-start(f32[1,1,2176]{2,1,0:T(1,128)} %get-tuple-element.66) | copy-start | bytes 26116
  77.7 21.0 %collective-permute-start.4 = (bf16[4,64,2176]{2,1,0:T(8,128)(2,1)}, bf16[4,64,2176]{2,1,0:T(8,128)(2,1)}, u32[]{:S(2)}, u32[]{:S(2)}) collective-permute-start(bf16[4,64,2176]{2,1,0:T(8,128)(2,1)} %get-tuple-element.47), channel_id=1, source_target_pairs={{0,1},{1,2},{2,3},{3,4},{4,5},{5,6},{6,7},{7,8},{8,9},{9,10},{10,1... | collective-permute-start | bytes 3342344 | tf_op jit(solution)/shard_map/ppermute | solution.py:114
  80.1 18.7 %collective-permute-start.5 = (bf16[4,64,2176]{2,1,0:T(8,128)(2,1)}, bf16[4,64,2176]{2,1,0:T(8,128)(2,1)}, u32[]{:S(2)}, u32[]{:S(2)}) collective-permute-start(bf16[4,64,2176]{2,1,0:T(8,128)(2,1)} %get-tuple-element.46), channel_id=1, source_target_pairs={{1,0},{2,1},{3,2},{4,3},{5,4},{6,5},{7,6},{8,7},{9,8},{10,9},{11,1... | collective-permute-start | bytes 3342344 | tf_op jit(solution)/shard_map/ppermute | solution.py:115
  85.4 0.6 copy-start.8
  85.4 1.0 copy-start.6
  86.4 1.0 copy-start.7
  98.7 8.5 %copy-start.3 = (bf16[2,256,2176]{2,1,0:T(8,128)(2,1)S(1)}, bf16[2,256,2176]{2,1,0:T(8,128)(2,1)}, u32[]{:S(2)}) copy-start(bf16[2,256,2176]{2,1,0:T(8,128)(2,1)} %get-tuple-element.12) | copy-start | bytes 6684676
  107.2 2.6 %copy-start.2 = (bf16[2,256,2176]{2,1,0:T(8,128)(2,1)S(1)}, bf16[2,256,2176]{2,1,0:T(8,128)(2,1)}, u32[]{:S(2)}) copy-start(bf16[2,256,2176]{2,1,0:T(8,128)(2,1)} %get-tuple-element.13) | copy-start | bytes 6684676
  107.2 3.0 %copy-start.4 = (bf16[2,256,2176]{2,1,0:T(8,128)(2,1)S(1)}, bf16[2,256,2176]{2,1,0:T(8,128)(2,1)}, u32[]{:S(2)}) copy-start(bf16[2,256,2176]{2,1,0:T(8,128)(2,1)} %get-tuple-element.15) | copy-start | bytes 6684676
  110.2 1.6 %copy-start.5 = (bf16[2,256,2176]{2,1,0:T(8,128)(2,1)S(1)}, bf16[2,256,2176]{2,1,0:T(8,128)(2,1)}, u32[]{:S(2)}) copy-start(bf16[2,256,2176]{2,1,0:T(8,128)(2,1)} %get-tuple-element.14) | copy-start | bytes 6684676
  113.1 15.2 %collective-permute-start.6 = (f32[2,64,512]{2,1,0:T(8,128)S(1)}, f32[2,64,512]{2,1,0:T(8,128)S(1)}, u32[]{:S(2)}, u32[]{:S(2)}) collective-permute-start(f32[2,64,512]{2,1,0:T(8,128)S(1)} %get-tuple-element.58), channel_id=1, source_target_pairs={{0,64},{64,128},{128,192},{192,0},{1,65},{65,129},{129,193},{193,1... | collective-permute-start | bytes 786440 | tf_op jit(solution)/shard_map/ppermute | solution.py:137
  113.8 14.6 %collective-permute-start.7 = (f32[2,64,512]{2,1,0:T(8,128)S(1)}, f32[2,64,512]{2,1,0:T(8,128)S(1)}, u32[]{:S(2)}, u32[]{:S(2)}) collective-permute-start(f32[2,64,512]{2,1,0:T(8,128)S(1)} %get-tuple-element.59), channel_id=1, source_target_pairs={{0,128},{64,192},{128,0},{192,64},{1,129},{65,193},{129,1},{193,65... | collective-permute-start | bytes 786440 | tf_op jit(solution)/shard_map/ppermute | solution.py:137
  115.9 13.1 %collective-permute-start.8 = (f32[2,64,512]{2,1,0:T(8,128)S(1)}, f32[2,64,512]{2,1,0:T(8,128)S(1)}, u32[]{:S(2)}, u32[]{:S(2)}) collective-permute-start(f32[2,64,512]{2,1,0:T(8,128)S(1)} %select_bitcast_fusion), channel_id=1, source_target_pairs={{0,192},{64,0},{128,64},{192,128},{1,193},{65,1},{129,65},{193,129... | collective-permute-start | bytes 786440 | tf_op jit(solution)/shard_map/ppermute | solution.py:137

commit v14 on v12

--- a/solution.py
+++ b/solution.py
@@ -9,7 +9,7 @@
 
 NY = 128
 NZ = 64
-ROWS = 32
+ROWS = 64
 GROUPS = 2
 SPACE = ("z", "y", "core")
 

time: 162 us -> 160 us (0.988)
  Pallas kernels: 15.6 us -> 12.7 us
    pallas_call x2, Pallas kernels: 15.6 us -> 12.7 us  [stencil(): pl.pallas_call(stencil_kernel, grid=(snaps // ROWS,), in_specs=[pl.BlockS...]
  transfers between devices with their start and end apart: 11 -> 11, of which waited for: 6 -> 6; matrix products, arithmetic and copies ran while one was open for 13% -> 13% of each run, Pallas kernels for 5% -> 4%
where the time goes in v14:
time: 160 us; the launch traced here: 158 us
  waiting for transfers between devices  47.7 us (30%)
  blocking collectives  29.7 us (19%)
  starting transfers between devices  29.1 us (18%)
  local copies, waits for them, and re-layouts  26.3 us (16%)
  Pallas kernels  12.7 us (8%)
  matrix products  6.63 us (4%)
  other arithmetic  5.66 us (4%)
    all_to_all x2, waiting for transfers between devices, per_device(): lax.all_to_all(chunked(major, nodes), 'node', 1, 1, tiled=True)  32.7 us
    all_to_all x3, blocking collectives, per_device(): total = lax.all_to_all(total, SPACE[axis], 0, 0, tiled=True).sum(axis=0)  29.7 us
    ppermute x3, waiting for transfers between devices, per_device(): lax.ppermute(blk, 'node', [(i, (i + d) % nodes) for i in range(nodes)])  12.9 us
    pallas_call x2, Pallas kernels, stencil(): pl.pallas_call(stencil_kernel, grid=(snaps // ROWS,), in_specs=[pl.BlockS...  12.7 us
    all_to_all x2, starting transfers between devices, per_device(): lax.all_to_all(chunked(major, nodes), 'node', 1, 1, tiled=True)  8.76 us
    ppermute x2, starting transfers between devices, per_device(): above = lax.ppermute(field[0], SPACE, down)  7.46 us
    dot_general x4, matrix products, per_device(): lax.dot_general(im, fd, dims, preferred_element_type=jnp.float32)  6.63 us
    slice x1, local copies, waits for them, and re-layouts, per_device(): major = jnp.transpose(snapshots[g * step:(g + 1) * step], (1, 0, 2))  5.04 us
  transfers between devices with their start and end apart: 11, of which 6 were waited for; matrix products, arithmetic and copies ran while one was open for 13% of the time, Pallas kernels for 4%

profile of v14, /device:TPU:8, one launch (start us, length us, event | category | flops | bytes accessed | tf_op | source)
XLA Modules:
  0.0 158.2 jit_solution(761484067211487371)
XLA Ops:
  0.0 5.0 %fusion.25 = (bf16[64,2,8192]{2,1,0:T(2,128)(2,1)S(1)}, bf16[64,2,8192]{2,1,0:T(2,128)(2,1)S(1)}) fusion(bf16[128,2,8192]{2,1,0:T(2,128)(2,1)} %param.4), kind=kLoop, calls=%fused_computation.80 | loop fusion | bytes 8388608 | tf_op jit(solution)/shard_map/slice | solution.py:108
  5.1 2.7 %copy_bitcast_fusion = (bf16[2,64,8192]{2,1,0:T(8,128)(2,1)S(1)}, bf16[2,64,8192]{2,1,0:T(8,128)(2,1)S(1)}) fusion(bf16[64,2,8192]{2,1,0:T(2,128)(2,1)S(1)} %get-tuple-element.35, bf16[64,2,8192]{2,1,0:T(2,128)(2,1)S(1)} %get-tuple-element.34), kind=kLoop, calls=%fused_computation.2 | loop fusion | bytes 8388608 | tf_op jit(solution)/shard_map/transpose | solution.py:108
  7.7 0.1 fusion.29
  7.8 0.1 fusion.28
  8.0 0.1 maximum_bitcast_fusion
  8.1 0.1 maximum_bitcast_fusion.1
  8.2 0.9 copy-done.5
  9.1 0.1 fusion.1
  9.2 0.3 concatenate.155
  9.5 1.7 %pad_maximum_fusion = bf16[2,4,64,2176]{3,2,0,1:T(8,128)(2,1)} fusion(bf16[2,1,64,2176]{3,2,0,1:T(8,128)(2,1)S(1)} %bitcast.118, bf16[2,1,64,2176]{3,2,0,1:T(8,128)(2,1)S(1)} %maximum_bitcast_fusion.1, bf16[2,1,64,2176]{3,2,0,1:T(8,128)(2,1)S(1)} %maximum_bitcast_fusion, bf16[2,1,64,2176]{3,2,0,1:T(8,128)(2,1)S(1)} %get-tuple-element.67), kind=kLoop, calls=%fused_computation | loop fusion | flops 3342336 | bytes 4456448 | tf_op jit(solution)/shard_map/stack | solution.py:89
  11.2 4.3 %all-to-all-start = ((bf16[2,4,64,2176]{3,2,0,1:T(8,128)(2,1)}), bf16[2,4,64,2176]{3,2,0,1:T(8,128)(2,1)S(1)}, u32[]{:S(2)}, u32[]{:S(2)}) async-start(bf16[2,4,64,2176]{3,2,0,1:T(8,128)(2,1)} %pad_maximum_fusion), calls=%async_computation | async-start | bytes 4456448 | tf_op jit(solution)/shard_map/all_to_all | solution.py:109
  15.5 0.9 fusion.31
  16.4 1.9 %slice.246 = bf16[2,64,2048]{2,1,0:T(8,128)(2,1)} slice(bf16[2,64,8192]{2,1,0:T(8,128)(2,1)} %copy-done.5), slice={[0:2], [0:64], [6144:8192]} | slice | bytes 1048576 | tf_op jit(solution)/shard_map/slice | solution.py:88
  18.3 1.2 concatenate.175
  19.4 1.3 fusion.30
  20.7 0.1 maximum_bitcast_fusion.2
  20.8 0.1 maximum_bitcast_fusion.3
  20.9 1.7 %pad_maximum_fusion.1 = bf16[2,4,64,2176]{3,2,0,1:T(8,128)(2,1)} fusion(bf16[2,1,64,2176]{3,2,0,1:T(8,128)(2,1)S(1)} %bitcast.117, bf16[2,1,64,2176]{3,2,0,1:T(8,128)(2,1)S(1)} %maximum_bitcast_fusion.3, bf16[2,1,64,2176]{3,2,0,1:T(8,128)(2,1)S(1)} %maximum_bitcast_fusion.2, bf16[2,1,64,2176]{3,2,0,1:T(8,128)(2,1)S(1)} %get-tuple-element.68), kind=kLoop, calls=%fused_computation.1 | loop fusion | flops 3342336 | bytes 4456448 | tf_op jit(solution)/shard_map/stack | solution.py:89
  22.6 20.6 %all-to-all-done = bf16[2,4,64,2176]{3,2,0,1:T(8,128)(2,1)S(1)} async-done(((bf16[2,4,64,2176]{3,2,0,1:T(8,128)(2,1)}), bf16[2,4,64,2176]{3,2,0,1:T(8,128)(2,1)S(1)}, u32[]{:S(2)}, u32[]{:S(2)}) %all-to-all-start) | async-done | bytes 2228256 | tf_op jit(solution)/shard_map/all_to_all | solution.py:109
  43.2 4.5 %all-to-all-start.1 = ((bf16[2,4,64,2176]{3,2,0,1:T(8,128)(2,1)}), bf16[2,4,64,2176]{3,2,0,1:T(8,128)(2,1)}, u32[]{:S(2)}, u32[]{:S(2)}) async-start(bf16[2,4,64,2176]{3,2,0,1:T(8,128)(2,1)} %pad_maximum_fusion.1), calls=%async_computation.1 | async-start | bytes 4456448 | tf_op jit(solution)/shard_map/all_to_all | solution.py:109
  47.7 1.5 copy.42
  49.4 0.1 maximum_bitcast_fusion.4
  49.5 0.1 concatenate.159
  49.9 1.9 %collective-permute-start.2 = (bf16[2176]{0:T(1024)(128)(2,1)S(1)}, bf16[2176]{0:T(1024)(128)(2,1)S(1)}, u32[]{:S(2)}, u32[]{:S(2)}) collective-permute-start(bf16[2176]{0:T(1024)(128)(2,1)S(1)} %get-tuple-element.31), channel_id=1, source_target_pairs={{0,1},{1,2},{2,3},{3,4},{4,5},{5,6},{6,7},{7,8},{8,9},{9,10},{10,1... | collective-permute-start | bytes 13064 | tf_op jit(solution)/shard_map/ppermute | solution.py:117
  51.8 3.6 %collective-permute-start.3 = (bf16[2176]{0:T(1024)(128)(2,1)S(1)}, bf16[2176]{0:T(1024)(128)(2,1)S(1)}, u32[]{:S(2)}, u32[]{:S(2)}) collective-permute-start(bf16[2176]{0:T(1024)(128)(2,1)S(1)} %get-tuple-element.30), channel_id=1, source_target_pairs={{1,0},{2,1},{3,2},{4,3},{5,4},{6,5},{7,6},{8,7},{9,8},{10,9},{11,1... | collective-permute-start | bytes 13064 | tf_op jit(solution)/shard_map/ppermute | solution.py:118
  55.4 1.2 fusion.26
  56.6 1.9 %collective-permute-start = (bf16[256,2176]{1,0:T(8,128)(2,1)}, bf16[256,2176]{1,0:T(8,128)(2,1)}, u32[]{:S(2)}, u32[]{:S(2)}) collective-permute-start(bf16[256,2176]{1,0:T(8,128)(2,1)} %bitcast.6), channel_id=1, source_target_pairs={{0,1},{1,2},{2,3},{3,4},{4,5},{5,6},{6,7},{7,8},{8,9},{9,10},{10,1... | collective-permute-start | bytes 3342344 | tf_op jit(solution)/shard_map/ppermute | solution.py:110
  58.5 3.6 %collective-permute-start.1 = (bf16[256,2176]{1,0:T(8,128)(2,1)S(1)}, bf16[256,2176]{1,0:T(8,128)(2,1)}, u32[]{:S(2)}, u32[]{:S(2)}) collective-permute-start(bf16[256,2176]{1,0:T(8,128)(2,1)S(1)} %bitcast.120), channel_id=1, source_target_pairs={{1,0},{2,1},{3,2},{4,3},{5,4},{6,5},{7,6},{8,7},{9,8},{10,9},{11,1... | collective-permute-start | bytes 3342344 | tf_op jit(solution)/shard_map/ppermute | solution.py:111
  62.3 0.1 slice_bitcast_fusion
  62.4 12.1 %all-to-all-done.1 = bf16[2,4,64,2176]{3,2,0,1:T(8,128)(2,1)} async-done(((bf16[2,4,64,2176]{3,2,0,1:T(8,128)(2,1)}), bf16[2,4,64,2176]{3,2,0,1:T(8,128)(2,1)}, u32[]{:S(2)}, u32[]{:S(2)}) %all-to-all-start.1) | async-done | bytes 2228256 | tf_op jit(solution)/shard_map/all_to_all | solution.py:109
  74.6 3.2 %fusion.27 = (bf16[1,4,64,2176]{3,2,1,0:T(8,128)(2,1)}, bf16[1,4,64,2176]{3,2,1,0:T(8,128)(2,1)}) fusion(bf16[2,4,64,2176]{3,2,0,1:T(8,128)(2,1)} %all-to-all-done.1), kind=kLoop, calls=%fused_computation.82 | loop fusion | bytes 4456448 | tf_op jit(solution)/shard_map/slice | solution.py:111
  77.7 1.9 %collective-permute-start.4 = (bf16[256,2176]{1,0:T(8,128)(2,1)}, bf16[256,2176]{1,0:T(8,128)(2,1)}, u32[]{:S(2)}, u32[]{:S(2)}) collective-permute-start(bf16[256,2176]{1,0:T(8,128)(2,1)} %bitcast.31), channel_id=1, source_target_pairs={{0,1},{1,2},{2,3},{3,4},{4,5},{5,6},{6,7},{7,8},{8,9},{9,10},{10,1... | collective-permute-start | bytes 3342344 | tf_op jit(solution)/shard_map/ppermute | solution.py:110
  79.7 0.1 select_dynamic-update-slice_fusion.1
  79.8 0.1 select_dynamic-update-slice_fusion
  79.9 0.1 constant_dynamic-update-slice_fusion.3
  80.0 0.1 constant_dynamic-update-slice_fusion.2
  80.1 3.2 %copy.48 = bf16[2,4,64,2176]{3,2,1,0:T(8,128)(2,1)} copy(bf16[2,4,64,2176]{3,2,0,1:T(8,128)(2,1)} %all-to-all-done.1) | data formatting | bytes 4456448 | tf_op jit(solution)/shard_map/all_to_all | solution.py:109
  83.2 3.8 %collective-permute-start.5 = (bf16[256,2176]{1,0:T(8,128)(2,1)}, bf16[256,2176]{1,0:T(8,128)(2,1)}, u32[]{:S(2)}, u32[]{:S(2)}) collective-permute-start(bf16[256,2176]{1,0:T(8,128)(2,1)} %bitcast.32), channel_id=1, source_target_pairs={{1,0},{2,1},{3,2},{4,3},{5,4},{6,5},{7,6},{8,7},{9,8},{10,9},{11,1... | collective-permute-start | bytes 3342344 | tf_op jit(solution)/shard_map/ppermute | solution.py:111
  87.2 0.1 add_dynamic-update-slice_fusion.coef_ref
  87.4 0.6 copy-done.6
  88.0 6.4 %shard_map.28 = bf16[2,256,2176]{2,1,0:T(8,128)(2,1)} custom-call(bf16[2,256,2176]{2,1,0:T(8,128)(2,1)} %bitcast.108, bf16[256,2176]{1,0:T(8,128)(2,1)} %collective-permute-done.below_ref, bf16[256,2176]{1,0:T(8,128)(2,1)} %collective-permute-done.1.above_ref, f32[7,2,2176]{2,1,0:T(2,128)} %copy-done.6), custom_call_target="tpu_custom_call" | custom-call | tf_op jit(solution)/shard_map/pallas_call | solution.py:52
  94.4 2.5 %convolution_bitcast_fusion.3 = f32[256,256]{0,1:T(8,128)S(1)} fusion(bf16[2,256,2176]{2,1,0:T(8,128)(2,1)} %shard_map.28, bf16[2,256,2176]{2,1,0:T(8,128)(2,1)S(1)} %bitcast.109), kind=kOutput, calls=%fused_computation.7 | convolution fusion | flops 570425344 | bytes 4718592 | tf_op jit(solution)/shard_map/dot_general | solution.py:125
  96.9 0.4 copy-done.4
  97.3 0.8 convolution_bitcast_fusion.2
  98.1 2.1 %collective-permute-done.5.above_ref = bf16[256,2176]{1,0:T(8,128)(2,1)} collective-permute-done((bf16[256,2176]{1,0:T(8,128)(2,1)}, bf16[256,2176]{1,0:T(8,128)(2,1)}, u32[]{:S(2)}, u32[]{:S(2)}) %collective-permute-start.5) | collective-permute-done | bytes 1114144 | tf_op jit(solution)/shard_map/ppermute | solution.py:111
  100.2 6.3 %shard_map.29 = bf16[2,256,2176]{2,1,0:T(8,128)(2,1)} custom-call(bf16[2,256,2176]{2,1,0:T(8,128)(2,1)} %bitcast.111, bf16[256,2176]{1,0:T(8,128)(2,1)} %collective-permute-done.4.below_ref, bf16[256,2176]{1,0:T(8,128)(2,1)} %collective-permute-done.5.above_ref, f32[7,2,2176]{2,1,0:T(2,128)} %copy-done.6), custom_call_target="tpu_custom_call" | custom-call | tf_op jit(solution)/shard_map/pallas_call | solution.py:52
  106.5 2.5 %convolution_bitcast_fusion.1 = f32[256,256]{0,1:T(8,128)S(1)} fusion(bf16[2,256,2176]{2,1,0:T(8,128)(2,1)} %shard_map.29, bf16[2,256,2176]{2,1,0:T(8,128)(2,1)S(1)} %bitcast.110), kind=kOutput, calls=%fused_computation.5 | convolution fusion | flops 570425344 | bytes 4718592 | tf_op jit(solution)/shard_map/dot_general | solution.py:125
  109.1 0.4 copy-done.3
  109.5 0.8 convolution_bitcast_fusion
  110.2 0.1 maximum_maximum_fusion
  110.4 0.3 copy.51
  110.8 0.6 collective-permute-start.6
  111.4 2.1 %collective-permute-start.7 = (f32[2,64,512]{2,1,0:T(8,128)S(1)}, f32[2,64,512]{2,1,0:T(8,128)S(1)}, u32[]{:S(2)}, u32[]{:S(2)}) collective-permute-start(f32[2,64,512]{2,1,0:T(8,128)S(1)} %get-tuple-element.51), channel_id=1, source_target_pairs={{0,128},{64,192},{128,0},{192,64},{1,129},{65,193},{129,1},{193,65... | collective-permute-start | bytes 786440 | tf_op jit(solution)/shard_map/ppermute | solution.py:132
  113.5 0.8 collective-permute-start.8
  114.3 6.7 %collective-permute-done.6 = f32[2,64,512]{2,1,0:T(8,128)S(1)} collective-permute-done((f32[2,64,512]{2,1,0:T(8,128)S(1)}, f32[2,64,512]{2,1,0:T(8,128)S(1)}, u32[]{:S(2)}, u32[]{:S(2)}) %collective-permute-start.6) | collective-permute-done | bytes 262176 | tf_op jit(solution)/shard_map/ppermute | solution.py:132
  121.0 4.5 %collective-permute-done.7 = f32[2,64,512]{2,1,0:T(8,128)S(1)} collective-permute-done((f32[2,64,512]{2,1,0:T(8,128)S(1)}, f32[2,64,512]{2,1,0:T(8,128)S(1)}, u32[]{:S(2)}, u32[]{:S(2)}) %collective-permute-start.7) | collective-permute-done | bytes 262176 | tf_op jit(solution)/shard_map/ppermute | solution.py:132
  125.5 1.7 %collective-permute-done.8 = f32[2,64,512]{2,1,0:T(8,128)S(1)} collective-permute-done((f32[2,64,512]{2,1,0:T(8,128)S(1)}, f32[2,64,512]{2,1,0:T(8,128)S(1)}, u32[]{:S(2)}, u32[]{:S(2)}) %collective-permute-start.8) | collective-permute-done | bytes 262176 | tf_op jit(solution)/shard_map/ppermute | solution.py:132
  127.2 0.1 fusion.7
  127.3 0.3 reshape.466
  127.6 0.2 copy.55
  127.9 3.9 %all_to_all.25 = f32[2,128,8,4,8]{1,4,3,2,0:T(8,128)S(1)} all-to-all(f32[2,128,8,4,8]{1,4,3,2,0:T(8,128)S(1)} %copy.56), channel_id=1, replica_groups=mesh['node'=4,'z'=8,'y'=4,'core'=2] {'core'}, dimensions={0} | all-to-all | bytes 524288 | tf_op jit(solution)/shard_map/all_to_all | solution.py:137
  131.8 9.5 %all_to_all.26 = f32[4,128,8,8]{1,3,2,0:T(8,128)S(1)} all-to-all(f32[4,128,8,8]{1,3,2,0:T(8,128)S(1)} %copy.58), channel_id=1, replica_groups=mesh['node'=4,'z'=8,'y'=4,'core'=2] {'y'}, dimensions={0} | all-to-all | bytes 262144 | tf_op jit(solution)/shard_map/all_to_all | solution.py:137
  141.3 16.3 %all_to_all.27 = f32[8,128,8]{1,2,0:T(8,128)S(1)} all-to-all(f32[8,128,8]{1,2,0:T(8,128)S(1)} %bitcast.123), channel_id=1, replica_groups=mesh['node'=4,'z'=8,'y'=4,'core'=2] {'z'}, dimensions={0} | all-to-all | bytes 65536 | tf_op jit(solution)/shard_map/all_to_all | solution.py:137
  157.6 0.6 broadcast_multiply_fusion
  (45 shorter events, 0.9 us)
Async XLA Ops:
  7.7 1.3 copy-start.5
  7.9 1.1 copy-start.8
  11.2 32.0 %all-to-all-start = ((bf16[2,4,64,2176]{3,2,0,1:T(8,128)(2,1)}), bf16[2,4,64,2176]{3,2,0,1:T(8,128)(2,1)S(1)}, u32[]{:S(2)}, u32[]{:S(2)}) async-start(bf16[2,4,64,2176]{3,2,0,1:T(8,128)(2,1)} %pad_maximum_fusion), calls=%async_computation | async-start | bytes 4456448 | tf_op jit(solution)/shard_map/all_to_all | solution.py:109
  43.2 31.4 %all-to-all-start.1 = ((bf16[2,4,64,2176]{3,2,0,1:T(8,128)(2,1)}), bf16[2,4,64,2176]{3,2,0,1:T(8,128)(2,1)}, u32[]{:S(2)}, u32[]{:S(2)}) async-start(bf16[2,4,64,2176]{3,2,0,1:T(8,128)(2,1)} %pad_maximum_fusion.1), calls=%async_computation.1 | async-start | bytes 4456448 | tf_op jit(solution)/shard_map/all_to_all | solution.py:109
  47.7 1.6 copy-start.7
  49.9 33.4 %collective-permute-start.2 = (bf16[2176]{0:T(1024)(128)(2,1)S(1)}, bf16[2176]{0:T(1024)(128)(2,1)S(1)}, u32[]{:S(2)}, u32[]{:S(2)}) collective-permute-start(bf16[2176]{0:T(1024)(128)(2,1)S(1)} %get-tuple-element.31), channel_id=1, source_target_pairs={{0,1},{1,2},{2,3},{3,4},{4,5},{5,6},{6,7},{7,8},{8,9},{9,10},{10,1... | collective-permute-start | bytes 13064 | tf_op jit(solution)/shard_map/ppermute | solution.py:117
  51.8 35.3 %collective-permute-start.3 = (bf16[2176]{0:T(1024)(128)(2,1)S(1)}, bf16[2176]{0:T(1024)(128)(2,1)S(1)}, u32[]{:S(2)}, u32[]{:S(2)}) collective-permute-start(bf16[2176]{0:T(1024)(128)(2,1)S(1)} %get-tuple-element.30), channel_id=1, source_target_pairs={{1,0},{2,1},{3,2},{4,3},{5,4},{6,5},{7,6},{8,7},{9,8},{10,9},{11,1... | collective-permute-start | bytes 13064 | tf_op jit(solution)/shard_map/ppermute | solution.py:118
  56.6 30.7 %collective-permute-start = (bf16[256,2176]{1,0:T(8,128)(2,1)}, bf16[256,2176]{1,0:T(8,128)(2,1)}, u32[]{:S(2)}, u32[]{:S(2)}) collective-permute-start(bf16[256,2176]{1,0:T(8,128)(2,1)} %bitcast.6), channel_id=1, source_target_pairs={{0,1},{1,2},{2,3},{3,4},{4,5},{5,6},{6,7},{7,8},{8,9},{9,10},{10,1... | collective-permute-start | bytes 3342344 | tf_op jit(solution)/shard_map/ppermute | solution.py:110
  58.5 28.8 %collective-permute-start.1 = (bf16[256,2176]{1,0:T(8,128)(2,1)S(1)}, bf16[256,2176]{1,0:T(8,128)(2,1)}, u32[]{:S(2)}, u32[]{:S(2)}) collective-permute-start(bf16[256,2176]{1,0:T(8,128)(2,1)S(1)} %bitcast.120), channel_id=1, source_target_pairs={{1,0},{2,1},{3,2},{4,3},{5,4},{6,5},{7,6},{8,7},{9,8},{10,9},{11,1... | collective-permute-start | bytes 3342344 | tf_op jit(solution)/shard_map/ppermute | solution.py:111
  77.7 20.4 %collective-permute-start.4 = (bf16[256,2176]{1,0:T(8,128)(2,1)}, bf16[256,2176]{1,0:T(8,128)(2,1)}, u32[]{:S(2)}, u32[]{:S(2)}) collective-permute-start(bf16[256,2176]{1,0:T(8,128)(2,1)} %bitcast.31), channel_id=1, source_target_pairs={{0,1},{1,2},{2,3},{3,4},{4,5},{5,6},{6,7},{7,8},{8,9},{9,10},{10,1... | collective-permute-start | bytes 3342344 | tf_op jit(solution)/shard_map/ppermute | solution.py:110
  83.2 17.0 %collective-permute-start.5 = (bf16[256,2176]{1,0:T(8,128)(2,1)}, bf16[256,2176]{1,0:T(8,128)(2,1)}, u32[]{:S(2)}, u32[]{:S(2)}) collective-permute-start(bf16[256,2176]{1,0:T(8,128)(2,1)} %bitcast.32), channel_id=1, source_target_pairs={{1,0},{2,1},{3,2},{4,3},{5,4},{6,5},{7,6},{8,7},{9,8},{10,9},{11,1... | collective-permute-start | bytes 3342344 | tf_op jit(solution)/shard_map/ppermute | solution.py:111
  87.3 0.7 copy-start.6
  87.3 7.0 %copy-start = (bf16[2,4,64,2176]{3,2,1,0:T(8,128)(2,1)S(1)}, bf16[2,4,64,2176]{3,2,1,0:T(8,128)(2,1)}, u32[]{:S(2)}) copy-start(bf16[2,4,64,2176]{3,2,1,0:T(8,128)(2,1)} %copy.42) | copy-start | bytes 6684676
  94.3 2.6 %copy-start.1 = (bf16[2,4,64,2176]{3,2,1,0:T(8,128)(2,1)S(1)}, bf16[2,4,64,2176]{3,2,1,0:T(8,128)(2,1)}, u32[]{:S(2)}) copy-start(bf16[2,4,64,2176]{3,2,1,0:T(8,128)(2,1)} %copy.48) | copy-start | bytes 6684676
  94.3 3.0 %copy-start.4 = (bf16[2,256,2176]{2,1,0:T(8,128)(2,1)S(1)}, bf16[2,256,2176]{2,1,0:T(8,128)(2,1)}, u32[]{:S(2)}) copy-start(bf16[2,256,2176]{2,1,0:T(8,128)(2,1)} %shard_map.28) | copy-start | bytes 6684676
  106.5 2.6 %copy-start.2 = (bf16[2,4,64,2176]{3,2,1,0:T(8,128)(2,1)S(1)}, bf16[2,4,64,2176]{3,2,1,0:T(8,128)(2,1)}, u32[]{:S(2)}) copy-start(bf16[2,4,64,2176]{3,2,1,0:T(8,128)(2,1)} %copy.48) | copy-start | bytes 6684676
  106.5 3.0 %copy-start.3 = (bf16[2,256,2176]{2,1,0:T(8,128)(2,1)S(1)}, bf16[2,256,2176]{2,1,0:T(8,128)(2,1)}, u32[]{:S(2)}) copy-start(bf16[2,256,2176]{2,1,0:T(8,128)(2,1)} %shard_map.29) | copy-start | bytes 6684676
  110.8 10.2 %collective-permute-start.6 = (f32[2,64,512]{2,1,0:T(8,128)S(1)}, f32[2,64,512]{2,1,0:T(8,128)S(1)}, u32[]{:S(2)}, u32[]{:S(2)}) collective-permute-start(f32[2,64,512]{2,1,0:T(8,128)S(1)} %get-tuple-element.50), channel_id=1, source_target_pairs={{0,64},{64,128},{128,192},{192,0},{1,65},{65,129},{129,193},{193,1... | collective-permute-start | bytes 786440 | tf_op jit(solution)/shard_map/ppermute | solution.py:132
  111.4 14.1 %collective-permute-start.7 = (f32[2,64,512]{2,1,0:T(8,128)S(1)}, f32[2,64,512]{2,1,0:T(8,128)S(1)}, u32[]{:S(2)}, u32[]{:S(2)}) collective-permute-start(f32[2,64,512]{2,1,0:T(8,128)S(1)} %get-tuple-element.51), channel_id=1, source_target_pairs={{0,128},{64,192},{128,0},{192,64},{1,129},{65,193},{129,1},{193,65... | collective-permute-start | bytes 786440 | tf_op jit(solution)/shard_map/ppermute | solution.py:132
  113.5 13.7 %collective-permute-start.8 = (f32[2,64,512]{2,1,0:T(8,128)S(1)}, f32[2,64,512]{2,1,0:T(8,128)S(1)}, u32[]{:S(2)}, u32[]{:S(2)}) collective-permute-start(f32[2,64,512]{2,1,0:T(8,128)S(1)} %select_bitcast_fusion), channel_id=1, source_target_pairs={{0,192},{64,0},{128,64},{192,128},{1,193},{65,1},{129,65},{193,129... | collective-permute-start | bytes 786440 | tf_op jit(solution)/shard_map/ppermute | solution.py:132

commit v15 on v14

--- a/solution.py
+++ b/solution.py
@@ -9,7 +9,7 @@
 
 NY = 128
 NZ = 64
-ROWS = 64
+ROWS = 128
 GROUPS = 2
 SPACE = ("z", "y", "core")
 

time: 160 us -> 160 us (level)
  no operation moved by 1% of the time
where the time goes in v15:
time: 160 us; the launch traced here: 158 us
  waiting for transfers between devices  47.7 us (30%)
  blocking collectives  29.7 us (19%)
  starting transfers between devices  29.1 us (18%)
  local copies, waits for them, and re-layouts  26.3 us (16%)
  Pallas kernels  12.8 us (8%)
  matrix products  6.63 us (4%)
  other arithmetic  5.66 us (4%)
    all_to_all x2, waiting for transfers between devices, per_device(): lax.all_to_all(chunked(major, nodes), 'node', 1, 1, tiled=True)  32.7 us
    all_to_all x3, blocking collectives, per_device(): total = lax.all_to_all(total, SPACE[axis], 0, 0, tiled=True).sum(axis=0)  29.7 us
    ppermute x3, waiting for transfers between devices, per_device(): lax.ppermute(blk, 'node', [(i, (i + d) % nodes) for i in range(nodes)])  12.9 us
    pallas_call x2, Pallas kernels, stencil(): pl.pallas_call(stencil_kernel, grid=(snaps // ROWS,), in_specs=[pl.BlockS...  12.8 us
    all_to_all x2, starting transfers between devices, per_device(): lax.all_to_all(chunked(major, nodes), 'node', 1, 1, tiled=True)  8.76 us
    ppermute x2, starting transfers between devices, per_device(): above = lax.ppermute(field[0], SPACE, down)  7.46 us
    dot_general x4, matrix products, per_device(): lax.dot_general(im, fd, dims, preferred_element_type=jnp.float32)  6.63 us
    slice x1, local copies, waits for them, and re-layouts, per_device(): major = jnp.transpose(snapshots[g * step:(g + 1) * step], (1, 0, 2))  5.04 us
  transfers between devices with their start and end apart: 11, of which 6 were waited for; matrix products, arithmetic and copies ran while one was open for 13% of the time, Pallas kernels for 4%

profile of v15, /device:TPU:8, one launch (start us, length us, event | category | flops | bytes accessed | tf_op | source)
XLA Modules:
  0.0 158.3 jit_solution(624689081520311098)
XLA Ops:
  0.0 5.0 %fusion.25 = (bf16[64,2,8192]{2,1,0:T(2,128)(2,1)S(1)}, bf16[64,2,8192]{2,1,0:T(2,128)(2,1)S(1)}) fusion(bf16[128,2,8192]{2,1,0:T(2,128)(2,1)} %param.4), kind=kLoop, calls=%fused_computation.80 | loop fusion | bytes 8388608 | tf_op jit(solution)/shard_map/slice | solution.py:108
  5.1 2.7 %copy_bitcast_fusion = (bf16[2,64,8192]{2,1,0:T(8,128)(2,1)S(1)}, bf16[2,64,8192]{2,1,0:T(8,128)(2,1)S(1)}) fusion(bf16[64,2,8192]{2,1,0:T(2,128)(2,1)S(1)} %get-tuple-element.35, bf16[64,2,8192]{2,1,0:T(2,128)(2,1)S(1)} %get-tuple-element.34), kind=kLoop, calls=%fused_computation.2 | loop fusion | bytes 8388608 | tf_op jit(solution)/shard_map/transpose | solution.py:108
  7.7 0.1 fusion.29
  7.8 0.1 fusion.28
  8.0 0.1 maximum_bitcast_fusion
  8.1 0.1 maximum_bitcast_fusion.1
  8.2 0.9 copy-done.5
  9.1 0.1 fusion.1
  9.2 0.3 concatenate.155
  9.5 1.7 %pad_maximum_fusion = bf16[2,4,64,2176]{3,2,0,1:T(8,128)(2,1)} fusion(bf16[2,1,64,2176]{3,2,0,1:T(8,128)(2,1)S(1)} %bitcast.118, bf16[2,1,64,2176]{3,2,0,1:T(8,128)(2,1)S(1)} %maximum_bitcast_fusion.1, bf16[2,1,64,2176]{3,2,0,1:T(8,128)(2,1)S(1)} %maximum_bitcast_fusion, bf16[2,1,64,2176]{3,2,0,1:T(8,128)(2,1)S(1)} %get-tuple-element.67), kind=kLoop, calls=%fused_computation | loop fusion | flops 3342336 | bytes 4456448 | tf_op jit(solution)/shard_map/stack | solution.py:89
  11.2 4.3 %all-to-all-start = ((bf16[2,4,64,2176]{3,2,0,1:T(8,128)(2,1)}), bf16[2,4,64,2176]{3,2,0,1:T(8,128)(2,1)S(1)}, u32[]{:S(2)}, u32[]{:S(2)}) async-start(bf16[2,4,64,2176]{3,2,0,1:T(8,128)(2,1)} %pad_maximum_fusion), calls=%async_computation | async-start | bytes 4456448 | tf_op jit(solution)/shard_map/all_to_all | solution.py:109
  15.5 0.9 fusion.31
  16.4 1.9 %slice.246 = bf16[2,64,2048]{2,1,0:T(8,128)(2,1)} slice(bf16[2,64,8192]{2,1,0:T(8,128)(2,1)} %copy-done.5), slice={[0:2], [0:64], [6144:8192]} | slice | bytes 1048576 | tf_op jit(solution)/shard_map/slice | solution.py:88
  18.3 1.2 concatenate.175
  19.4 1.3 fusion.30
  20.7 0.1 maximum_bitcast_fusion.2
  20.8 0.1 maximum_bitcast_fusion.3
  20.9 1.7 %pad_maximum_fusion.1 = bf16[2,4,64,2176]{3,2,0,1:T(8,128)(2,1)} fusion(bf16[2,1,64,2176]{3,2,0,1:T(8,128)(2,1)S(1)} %bitcast.117, bf16[2,1,64,2176]{3,2,0,1:T(8,128)(2,1)S(1)} %maximum_bitcast_fusion.3, bf16[2,1,64,2176]{3,2,0,1:T(8,128)(2,1)S(1)} %maximum_bitcast_fusion.2, bf16[2,1,64,2176]{3,2,0,1:T(8,128)(2,1)S(1)} %get-tuple-element.68), kind=kLoop, calls=%fused_computation.1 | loop fusion | flops 3342336 | bytes 4456448 | tf_op jit(solution)/shard_map/stack | solution.py:89
  22.6 20.6 %all-to-all-done = bf16[2,4,64,2176]{3,2,0,1:T(8,128)(2,1)S(1)} async-done(((bf16[2,4,64,2176]{3,2,0,1:T(8,128)(2,1)}), bf16[2,4,64,2176]{3,2,0,1:T(8,128)(2,1)S(1)}, u32[]{:S(2)}, u32[]{:S(2)}) %all-to-all-start) | async-done | bytes 2228256 | tf_op jit(solution)/shard_map/all_to_all | solution.py:109
  43.2 4.5 %all-to-all-start.1 = ((bf16[2,4,64,2176]{3,2,0,1:T(8,128)(2,1)}), bf16[2,4,64,2176]{3,2,0,1:T(8,128)(2,1)}, u32[]{:S(2)}, u32[]{:S(2)}) async-start(bf16[2,4,64,2176]{3,2,0,1:T(8,128)(2,1)} %pad_maximum_fusion.1), calls=%async_computation.1 | async-start | bytes 4456448 | tf_op jit(solution)/shard_map/all_to_all | solution.py:109
  47.7 1.5 copy.42
  49.4 0.1 maximum_bitcast_fusion.4
  49.5 0.1 concatenate.159
  49.9 1.9 %collective-permute-start.2 = (bf16[2176]{0:T(1024)(128)(2,1)S(1)}, bf16[2176]{0:T(1024)(128)(2,1)S(1)}, u32[]{:S(2)}, u32[]{:S(2)}) collective-permute-start(bf16[2176]{0:T(1024)(128)(2,1)S(1)} %get-tuple-element.31), channel_id=1, source_target_pairs={{0,1},{1,2},{2,3},{3,4},{4,5},{5,6},{6,7},{7,8},{8,9},{9,10},{10,1... | collective-permute-start | bytes 13064 | tf_op jit(solution)/shard_map/ppermute | solution.py:117
  51.8 3.6 %collective-permute-start.3 = (bf16[2176]{0:T(1024)(128)(2,1)S(1)}, bf16[2176]{0:T(1024)(128)(2,1)S(1)}, u32[]{:S(2)}, u32[]{:S(2)}) collective-permute-start(bf16[2176]{0:T(1024)(128)(2,1)S(1)} %get-tuple-element.30), channel_id=1, source_target_pairs={{1,0},{2,1},{3,2},{4,3},{5,4},{6,5},{7,6},{8,7},{9,8},{10,9},{11,1... | collective-permute-start | bytes 13064 | tf_op jit(solution)/shard_map/ppermute | solution.py:118
  55.4 1.2 fusion.26
  56.6 1.9 %collective-permute-start = (bf16[256,2176]{1,0:T(8,128)(2,1)}, bf16[256,2176]{1,0:T(8,128)(2,1)}, u32[]{:S(2)}, u32[]{:S(2)}) collective-permute-start(bf16[256,2176]{1,0:T(8,128)(2,1)} %bitcast.6), channel_id=1, source_target_pairs={{0,1},{1,2},{2,3},{3,4},{4,5},{5,6},{6,7},{7,8},{8,9},{9,10},{10,1... | collective-permute-start | bytes 3342344 | tf_op jit(solution)/shard_map/ppermute | solution.py:110
  58.5 3.6 %collective-permute-start.1 = (bf16[256,2176]{1,0:T(8,128)(2,1)S(1)}, bf16[256,2176]{1,0:T(8,128)(2,1)}, u32[]{:S(2)}, u32[]{:S(2)}) collective-permute-start(bf16[256,2176]{1,0:T(8,128)(2,1)S(1)} %bitcast.120), channel_id=1, source_target_pairs={{1,0},{2,1},{3,2},{4,3},{5,4},{6,5},{7,6},{8,7},{9,8},{10,9},{11,1... | collective-permute-start | bytes 3342344 | tf_op jit(solution)/shard_map/ppermute | solution.py:111
  62.3 0.1 slice_bitcast_fusion
  62.4 12.1 %all-to-all-done.1 = bf16[2,4,64,2176]{3,2,0,1:T(8,128)(2,1)} async-done(((bf16[2,4,64,2176]{3,2,0,1:T(8,128)(2,1)}), bf16[2,4,64,2176]{3,2,0,1:T(8,128)(2,1)}, u32[]{:S(2)}, u32[]{:S(2)}) %all-to-all-start.1) | async-done | bytes 2228256 | tf_op jit(solution)/shard_map/all_to_all | solution.py:109
  74.6 3.2 %fusion.27 = (bf16[1,4,64,2176]{3,2,1,0:T(8,128)(2,1)}, bf16[1,4,64,2176]{3,2,1,0:T(8,128)(2,1)}) fusion(bf16[2,4,64,2176]{3,2,0,1:T(8,128)(2,1)} %all-to-all-done.1), kind=kLoop, calls=%fused_computation.82 | loop fusion | bytes 4456448 | tf_op jit(solution)/shard_map/slice | solution.py:111
  77.7 1.9 %collective-permute-start.4 = (bf16[256,2176]{1,0:T(8,128)(2,1)}, bf16[256,2176]{1,0:T(8,128)(2,1)}, u32[]{:S(2)}, u32[]{:S(2)}) collective-permute-start(bf16[256,2176]{1,0:T(8,128)(2,1)} %bitcast.31), channel_id=1, source_target_pairs={{0,1},{1,2},{2,3},{3,4},{4,5},{5,6},{6,7},{7,8},{8,9},{9,10},{10,1... | collective-permute-start | bytes 3342344 | tf_op jit(solution)/shard_map/ppermute | solution.py:110
  79.7 0.1 select_dynamic-update-slice_fusion.1
  79.8 0.1 select_dynamic-update-slice_fusion
  79.9 0.1 constant_dynamic-update-slice_fusion.3
  80.0 0.1 constant_dynamic-update-slice_fusion.2
  80.1 3.2 %copy.48 = bf16[2,4,64,2176]{3,2,1,0:T(8,128)(2,1)} copy(bf16[2,4,64,2176]{3,2,0,1:T(8,128)(2,1)} %all-to-all-done.1) | data formatting | bytes 4456448 | tf_op jit(solution)/shard_map/all_to_all | solution.py:109
  83.2 3.8 %collective-permute-start.5 = (bf16[256,2176]{1,0:T(8,128)(2,1)}, bf16[256,2176]{1,0:T(8,128)(2,1)}, u32[]{:S(2)}, u32[]{:S(2)}) collective-permute-start(bf16[256,2176]{1,0:T(8,128)(2,1)} %bitcast.32), channel_id=1, source_target_pairs={{1,0},{2,1},{3,2},{4,3},{5,4},{6,5},{7,6},{8,7},{9,8},{10,9},{11,1... | collective-permute-start | bytes 3342344 | tf_op jit(solution)/shard_map/ppermute | solution.py:111
  87.2 0.1 add_dynamic-update-slice_fusion.coef_ref
  87.4 0.6 copy-done.6
  88.0 6.5 %shard_map.28 = bf16[2,256,2176]{2,1,0:T(8,128)(2,1)} custom-call(bf16[2,256,2176]{2,1,0:T(8,128)(2,1)} %bitcast.108, bf16[256,2176]{1,0:T(8,128)(2,1)} %collective-permute-done.below_ref, bf16[256,2176]{1,0:T(8,128)(2,1)} %collective-permute-done.1.above_ref, f32[7,2,2176]{2,1,0:T(2,128)} %copy-done.6), custom_call_target="tpu_custom_call" | custom-call | tf_op jit(solution)/shard_map/pallas_call | solution.py:52
  94.4 2.5 %convolution_bitcast_fusion.3 = f32[256,256]{0,1:T(8,128)S(1)} fusion(bf16[2,256,2176]{2,1,0:T(8,128)(2,1)} %shard_map.28, bf16[2,256,2176]{2,1,0:T(8,128)(2,1)S(1)} %bitcast.109), kind=kOutput, calls=%fused_computation.7 | convolution fusion | flops 570425344 | bytes 4718592 | tf_op jit(solution)/shard_map/dot_general | solution.py:125
  97.0 0.4 copy-done.4
  97.4 0.8 convolution_bitcast_fusion.2
  98.2 2.0 %collective-permute-done.5.above_ref = bf16[256,2176]{1,0:T(8,128)(2,1)} collective-permute-done((bf16[256,2176]{1,0:T(8,128)(2,1)}, bf16[256,2176]{1,0:T(8,128)(2,1)}, u32[]{:S(2)}, u32[]{:S(2)}) %collective-permute-start.5) | collective-permute-done | bytes 1114144 | tf_op jit(solution)/shard_map/ppermute | solution.py:111
  100.2 6.4 %shard_map.29 = bf16[2,256,2176]{2,1,0:T(8,128)(2,1)} custom-call(bf16[2,256,2176]{2,1,0:T(8,128)(2,1)} %bitcast.111, bf16[256,2176]{1,0:T(8,128)(2,1)} %collective-permute-done.4.below_ref, bf16[256,2176]{1,0:T(8,128)(2,1)} %collective-permute-done.5.above_ref, f32[7,2,2176]{2,1,0:T(2,128)} %copy-done.6), custom_call_target="tpu_custom_call" | custom-call | tf_op jit(solution)/shard_map/pallas_call | solution.py:52
  106.6 2.5 %convolution_bitcast_fusion.1 = f32[256,256]{0,1:T(8,128)S(1)} fusion(bf16[2,256,2176]{2,1,0:T(8,128)(2,1)} %shard_map.29, bf16[2,256,2176]{2,1,0:T(8,128)(2,1)S(1)} %bitcast.110), kind=kOutput, calls=%fused_computation.5 | convolution fusion | flops 570425344 | bytes 4718592 | tf_op jit(solution)/shard_map/dot_general | solution.py:125
  109.1 0.4 copy-done.3
  109.5 0.8 convolution_bitcast_fusion
  110.3 0.1 maximum_maximum_fusion
  110.5 0.3 copy.51
  110.9 0.6 collective-permute-start.6
  111.5 2.1 %collective-permute-start.7 = (f32[2,64,512]{2,1,0:T(8,128)S(1)}, f32[2,64,512]{2,1,0:T(8,128)S(1)}, u32[]{:S(2)}, u32[]{:S(2)}) collective-permute-start(f32[2,64,512]{2,1,0:T(8,128)S(1)} %get-tuple-element.51), channel_id=1, source_target_pairs={{0,128},{64,192},{128,0},{192,64},{1,129},{65,193},{129,1},{193,65... | collective-permute-start | bytes 786440 | tf_op jit(solution)/shard_map/ppermute | solution.py:132
  113.6 0.8 collective-permute-start.8
  114.4 6.7 %collective-permute-done.6 = f32[2,64,512]{2,1,0:T(8,128)S(1)} collective-permute-done((f32[2,64,512]{2,1,0:T(8,128)S(1)}, f32[2,64,512]{2,1,0:T(8,128)S(1)}, u32[]{:S(2)}, u32[]{:S(2)}) %collective-permute-start.6) | collective-permute-done | bytes 262176 | tf_op jit(solution)/shard_map/ppermute | solution.py:132
  121.1 4.5 %collective-permute-done.7 = f32[2,64,512]{2,1,0:T(8,128)S(1)} collective-permute-done((f32[2,64,512]{2,1,0:T(8,128)S(1)}, f32[2,64,512]{2,1,0:T(8,128)S(1)}, u32[]{:S(2)}, u32[]{:S(2)}) %collective-permute-start.7) | collective-permute-done | bytes 262176 | tf_op jit(solution)/shard_map/ppermute | solution.py:132
  125.6 1.7 %collective-permute-done.8 = f32[2,64,512]{2,1,0:T(8,128)S(1)} collective-permute-done((f32[2,64,512]{2,1,0:T(8,128)S(1)}, f32[2,64,512]{2,1,0:T(8,128)S(1)}, u32[]{:S(2)}, u32[]{:S(2)}) %collective-permute-start.8) | collective-permute-done | bytes 262176 | tf_op jit(solution)/shard_map/ppermute | solution.py:132
  127.3 0.1 fusion.7
  127.4 0.3 reshape.466
  127.7 0.2 copy.55
  128.0 3.9 %all_to_all.25 = f32[2,128,8,4,8]{1,4,3,2,0:T(8,128)S(1)} all-to-all(f32[2,128,8,4,8]{1,4,3,2,0:T(8,128)S(1)} %copy.56), channel_id=1, replica_groups=mesh['node'=4,'z'=8,'y'=4,'core'=2] {'core'}, dimensions={0} | all-to-all | bytes 524288 | tf_op jit(solution)/shard_map/all_to_all | solution.py:137
  131.9 9.5 %all_to_all.26 = f32[4,128,8,8]{1,3,2,0:T(8,128)S(1)} all-to-all(f32[4,128,8,8]{1,3,2,0:T(8,128)S(1)} %copy.58), channel_id=1, replica_groups=mesh['node'=4,'z'=8,'y'=4,'core'=2] {'y'}, dimensions={0} | all-to-all | bytes 262144 | tf_op jit(solution)/shard_map/all_to_all | solution.py:137
  141.4 16.3 %all_to_all.27 = f32[8,128,8]{1,2,0:T(8,128)S(1)} all-to-all(f32[8,128,8]{1,2,0:T(8,128)S(1)} %bitcast.123), channel_id=1, replica_groups=mesh['node'=4,'z'=8,'y'=4,'core'=2] {'z'}, dimensions={0} | all-to-all | bytes 65536 | tf_op jit(solution)/shard_map/all_to_all | solution.py:137
  157.7 0.6 broadcast_multiply_fusion
  (45 shorter events, 0.9 us)
Async XLA Ops:
  7.7 1.3 copy-start.5
  7.9 1.1 copy-start.8
  11.2 32.0 %all-to-all-start = ((bf16[2,4,64,2176]{3,2,0,1:T(8,128)(2,1)}), bf16[2,4,64,2176]{3,2,0,1:T(8,128)(2,1)S(1)}, u32[]{:S(2)}, u32[]{:S(2)}) async-start(bf16[2,4,64,2176]{3,2,0,1:T(8,128)(2,1)} %pad_maximum_fusion), calls=%async_computation | async-start | bytes 4456448 | tf_op jit(solution)/shard_map/all_to_all | solution.py:109
  43.2 31.4 %all-to-all-start.1 = ((bf16[2,4,64,2176]{3,2,0,1:T(8,128)(2,1)}), bf16[2,4,64,2176]{3,2,0,1:T(8,128)(2,1)}, u32[]{:S(2)}, u32[]{:S(2)}) async-start(bf16[2,4,64,2176]{3,2,0,1:T(8,128)(2,1)} %pad_maximum_fusion.1), calls=%async_computation.1 | async-start | bytes 4456448 | tf_op jit(solution)/shard_map/all_to_all | solution.py:109
  47.7 1.6 copy-start.7
  49.9 33.4 %collective-permute-start.2 = (bf16[2176]{0:T(1024)(128)(2,1)S(1)}, bf16[2176]{0:T(1024)(128)(2,1)S(1)}, u32[]{:S(2)}, u32[]{:S(2)}) collective-permute-start(bf16[2176]{0:T(1024)(128)(2,1)S(1)} %get-tuple-element.31), channel_id=1, source_target_pairs={{0,1},{1,2},{2,3},{3,4},{4,5},{5,6},{6,7},{7,8},{8,9},{9,10},{10,1... | collective-permute-start | bytes 13064 | tf_op jit(solution)/shard_map/ppermute | solution.py:117
  51.8 35.3 %collective-permute-start.3 = (bf16[2176]{0:T(1024)(128)(2,1)S(1)}, bf16[2176]{0:T(1024)(128)(2,1)S(1)}, u32[]{:S(2)}, u32[]{:S(2)}) collective-permute-start(bf16[2176]{0:T(1024)(128)(2,1)S(1)} %get-tuple-element.30), channel_id=1, source_target_pairs={{1,0},{2,1},{3,2},{4,3},{5,4},{6,5},{7,6},{8,7},{9,8},{10,9},{11,1... | collective-permute-start | bytes 13064 | tf_op jit(solution)/shard_map/ppermute | solution.py:118
  56.6 30.7 %collective-permute-start = (bf16[256,2176]{1,0:T(8,128)(2,1)}, bf16[256,2176]{1,0:T(8,128)(2,1)}, u32[]{:S(2)}, u32[]{:S(2)}) collective-permute-start(bf16[256,2176]{1,0:T(8,128)(2,1)} %bitcast.6), channel_id=1, source_target_pairs={{0,1},{1,2},{2,3},{3,4},{4,5},{5,6},{6,7},{7,8},{8,9},{9,10},{10,1... | collective-permute-start | bytes 3342344 | tf_op jit(solution)/shard_map/ppermute | solution.py:110
  58.5 28.8 %collective-permute-start.1 = (bf16[256,2176]{1,0:T(8,128)(2,1)S(1)}, bf16[256,2176]{1,0:T(8,128)(2,1)}, u32[]{:S(2)}, u32[]{:S(2)}) collective-permute-start(bf16[256,2176]{1,0:T(8,128)(2,1)S(1)} %bitcast.120), channel_id=1, source_target_pairs={{1,0},{2,1},{3,2},{4,3},{5,4},{6,5},{7,6},{8,7},{9,8},{10,9},{11,1... | collective-permute-start | bytes 3342344 | tf_op jit(solution)/shard_map/ppermute | solution.py:111
  77.7 20.4 %collective-permute-start.4 = (bf16[256,2176]{1,0:T(8,128)(2,1)}, bf16[256,2176]{1,0:T(8,128)(2,1)}, u32[]{:S(2)}, u32[]{:S(2)}) collective-permute-start(bf16[256,2176]{1,0:T(8,128)(2,1)} %bitcast.31), channel_id=1, source_target_pairs={{0,1},{1,2},{2,3},{3,4},{4,5},{5,6},{6,7},{7,8},{8,9},{9,10},{10,1... | collective-permute-start | bytes 3342344 | tf_op jit(solution)/shard_map/ppermute | solution.py:110
  83.2 17.0 %collective-permute-start.5 = (bf16[256,2176]{1,0:T(8,128)(2,1)}, bf16[256,2176]{1,0:T(8,128)(2,1)}, u32[]{:S(2)}, u32[]{:S(2)}) collective-permute-start(bf16[256,2176]{1,0:T(8,128)(2,1)} %bitcast.32), channel_id=1, source_target_pairs={{1,0},{2,1},{3,2},{4,3},{5,4},{6,5},{7,6},{8,7},{9,8},{10,9},{11,1... | collective-permute-start | bytes 3342344 | tf_op jit(solution)/shard_map/ppermute | solution.py:111
  87.3 0.7 copy-start.6
  87.3 7.1 %copy-start = (bf16[2,4,64,2176]{3,2,1,0:T(8,128)(2,1)S(1)}, bf16[2,4,64,2176]{3,2,1,0:T(8,128)(2,1)}, u32[]{:S(2)}) copy-start(bf16[2,4,64,2176]{3,2,1,0:T(8,128)(2,1)} %copy.42) | copy-start | bytes 6684676
  94.4 2.6 %copy-start.1 = (bf16[2,4,64,2176]{3,2,1,0:T(8,128)(2,1)S(1)}, bf16[2,4,64,2176]{3,2,1,0:T(8,128)(2,1)}, u32[]{:S(2)}) copy-start(bf16[2,4,64,2176]{3,2,1,0:T(8,128)(2,1)} %copy.48) | copy-start | bytes 6684676
  94.4 3.0 %copy-start.4 = (bf16[2,256,2176]{2,1,0:T(8,128)(2,1)S(1)}, bf16[2,256,2176]{2,1,0:T(8,128)(2,1)}, u32[]{:S(2)}) copy-start(bf16[2,256,2176]{2,1,0:T(8,128)(2,1)} %shard_map.28) | copy-start | bytes 6684676
  106.6 2.6 %copy-start.2 = (bf16[2,4,64,2176]{3,2,1,0:T(8,128)(2,1)S(1)}, bf16[2,4,64,2176]{3,2,1,0:T(8,128)(2,1)}, u32[]{:S(2)}) copy-start(bf16[2,4,64,2176]{3,2,1,0:T(8,128)(2,1)} %copy.48) | copy-start | bytes 6684676
  106.6 3.0 %copy-start.3 = (bf16[2,256,2176]{2,1,0:T(8,128)(2,1)S(1)}, bf16[2,256,2176]{2,1,0:T(8,128)(2,1)}, u32[]{:S(2)}) copy-start(bf16[2,256,2176]{2,1,0:T(8,128)(2,1)} %shard_map.29) | copy-start | bytes 6684676
  110.9 10.2 %collective-permute-start.6 = (f32[2,64,512]{2,1,0:T(8,128)S(1)}, f32[2,64,512]{2,1,0:T(8,128)S(1)}, u32[]{:S(2)}, u32[]{:S(2)}) collective-permute-start(f32[2,64,512]{2,1,0:T(8,128)S(1)} %get-tuple-element.50), channel_id=1, source_target_pairs={{0,64},{64,128},{128,192},{192,0},{1,65},{65,129},{129,193},{193,1... | collective-permute-start | bytes 786440 | tf_op jit(solution)/shard_map/ppermute | solution.py:132
  111.5 14.1 %collective-permute-start.7 = (f32[2,64,512]{2,1,0:T(8,128)S(1)}, f32[2,64,512]{2,1,0:T(8,128)S(1)}, u32[]{:S(2)}, u32[]{:S(2)}) collective-permute-start(f32[2,64,512]{2,1,0:T(8,128)S(1)} %get-tuple-element.51), channel_id=1, source_target_pairs={{0,128},{64,192},{128,0},{192,64},{1,129},{65,193},{129,1},{193,65... | collective-permute-start | bytes 786440 | tf_op jit(solution)/shard_map/ppermute | solution.py:132
  113.6 13.7 %collective-permute-start.8 = (f32[2,64,512]{2,1,0:T(8,128)S(1)}, f32[2,64,512]{2,1,0:T(8,128)S(1)}, u32[]{:S(2)}, u32[]{:S(2)}) collective-permute-start(f32[2,64,512]{2,1,0:T(8,128)S(1)} %select_bitcast_fusion), channel_id=1, source_target_pairs={{0,192},{64,0},{128,64},{192,128},{1,193},{65,1},{129,65},{193,129... | collective-permute-start | bytes 786440 | tf_op jit(solution)/shard_map/ppermute | solution.py:132

commit v16 on v15

--- a/solution.py
+++ b/solution.py
@@ -10,7 +10,7 @@
 NY = 128
 NZ = 64
 ROWS = 128
-GROUPS = 2
+SPLIT = (96, 32)
 SPACE = ("z", "y", "core")
 
 
@@ -102,10 +102,11 @@
     up = [(i, i + 1) for i in range(spaces - 1)]
     down = [(j, i) for i, j in up]
 
-    step = rows // GROUPS
     images, fields, fronts = [], [], []
-    for g in range(GROUPS):
-        major = jnp.transpose(snapshots[g * step:(g + 1) * step], (1, 0, 2))
+    start = 0
+    for g, step in enumerate(SPLIT):
+        major = jnp.transpose(snapshots[start:start + step], (1, 0, 2))
+        start += step
         field = lax.all_to_all(chunked(major, nodes), "node", 1, 1, tiled=True).reshape(planes, nodes * step, span)
         below = lax.ppermute(field[1], SPACE, up)
         above = lax.ppermute(field[0], SPACE, down)
@@ -125,12 +126,21 @@
             lax.dot_general(im, fd, dims, preferred_element_type=jnp.float32)
             for fd in fields], axis=1)
         for im in images], axis=0)
-    part = part.reshape(GROUPS, nodes, step, snaps)
-    total = jnp.take(part, me, axis=1)
+
+    def in_order(values, axis):
+        parts = []
+        for a in range(nodes):
+            for g, step in enumerate(SPLIT):
+                first = nodes * sum(SPLIT[:g]) + a * step
+                parts.append(lax.slice_in_dim(values, first, first + step, axis=axis))
+        return jnp.concatenate(parts, axis=axis)
+
+    part = in_order(in_order(part, 0), 1)
+    part = part.reshape(nodes, rows, snaps)
+    total = jnp.take(part, me, axis=0)
     for d in range(1, nodes):
-        blk = jnp.take(part, (me + d) % nodes, axis=1)
+        blk = jnp.take(part, (me + d) % nodes, axis=0)
         total = total + lax.ppermute(blk, "node", [(i, (i + d) % nodes) for i in range(nodes)])
-    total = total.reshape(rows, GROUPS, nodes, step).transpose(0, 2, 1, 3)
     total = total.reshape((rows,) + tuple(sizes) + (snaps // spaces,))
     for axis in reversed(range(len(SPACE))):
         total = jnp.moveaxis(total, axis + 1, 0)

time: 160 us -> 174 us (1.087)
  waiting for transfers between devices: 47.7 us -> 65.3 us
  local copies, waits for them, and re-layouts: 26.3 us -> 21.2 us
  matrix products: 6.63 us -> 10.2 us
  starting transfers between devices: 29.1 us -> 26 us
    ppermute x1, waiting for transfers between devices: 0.01 us -> 15.2 us  [per_device(): kap_below = lax.ppermute(kap_chunk[1], SPACE, up)]
    dot_general x4, matrix products: 6.63 us -> 10.2 us  [per_device(): lax.dot_general(im, fd, dims, preferred_element_type=jnp.float32)]
    transpose x2 -> x0, local copies, waits for them, and re-layouts: 2.88 us -> none  [the longest x1 2.68 us: per_device(): major = jnp.transpose(snapshots[g * step:(g + 1) * step], (1, 0, 2))]
    ppermute x2, waiting for transfers between devices: 2.01 us -> 0.01 us  [per_device(): above = lax.ppermute(field[0], SPACE, down)]
    slice x1 -> x4, local copies, waits for them, and re-layouts: 5.04 us -> 3.11 us  [per_device(): major = jnp.transpose(snapshots[start:start + step], (1, 0, 2))]
    ppermute x3, waiting for transfers between devices: 12.9 us -> 14.7 us  [per_device(): lax.ppermute(blk, 'node', [(i, (i + d) % nodes) for i in range(nodes)])]
    unnamed x18 -> x27, local copies, waits for them, and re-layouts: 2.32 us -> 4.07 us
    another operation x10 -> x9, other arithmetic: 4.05 us -> 5.14 us  [chunked(): return jnp.stack(pieces, axis=-3)]
  transfers between devices with their start and end apart: 11 -> 11, of which waited for: 6 -> 7; matrix products, arithmetic and copies ran while one was open for 13% -> 12% of each run, Pallas kernels for 4% -> 3%
where the time goes in v16:
time: 174 us; the launch traced here: 173 us
  waiting for transfers between devices  65.3 us (38%)
  blocking collectives  29.6 us (17%)
  starting transfers between devices  26 us (15%)
  local copies, waits for them, and re-layouts  21.2 us (12%)
  Pallas kernels  13.1 us (8%)
  matrix products  10.2 us (6%)
  other arithmetic  7.08 us (4%)
    all_to_all x2, waiting for transfers between devices, per_device(): lax.all_to_all(chunked(major, nodes), 'node', 1, 1, tiled=True)  34.3 us
    all_to_all x3, blocking collectives, per_device(): total = lax.all_to_all(total, SPACE[axis], 0, 0, tiled=True).sum(axis=0)  29.6 us
    ppermute x1, waiting for transfers between devices, per_device(): kap_below = lax.ppermute(kap_chunk[1], SPACE, up)  15.2 us
    ppermute x3, waiting for transfers between devices, per_device(): lax.ppermute(blk, 'node', [(i, (i + d) % nodes) for i in range(nodes)])  14.7 us
    pallas_call x2, Pallas kernels, stencil(): pl.pallas_call(stencil_kernel, grid=(snaps // ROWS,), in_specs=[pl.BlockS...  13.1 us
    dot_general x4, matrix products, per_device(): lax.dot_general(im, fd, dims, preferred_element_type=jnp.float32)  10.2 us
    all_to_all x2, starting transfers between devices, per_device(): lax.all_to_all(chunked(major, nodes), 'node', 1, 1, tiled=True)  8.01 us
    ppermute x2, starting transfers between devices, per_device(): above = lax.ppermute(field[0], SPACE, down)  7.29 us
  transfers between devices with their start and end apart: 11, of which 7 were waited for; matrix products, arithmetic and copies ran while one was open for 12% of the time, Pallas kernels for 3%

profile of v16, /device:TPU:8, one launch (start us, length us, event | category | flops | bytes accessed | tf_op | source)
XLA Modules:
  0.0 173.0 jit_solution(14445058007912388958)
XLA Ops:
  0.0 1.2 slice-done
  1.2 0.6 copy.75
  1.8 0.1 fusion.32
  2.0 0.1 concatenate.178
  2.1 0.1 maximum_bitcast_fusion.2
  2.2 1.2 pad_maximum_fusion.1
  3.4 4.3 %all-to-all-start.1 = ((bf16[2,4,32,2176]{3,2,0,1:T(8,128)(2,1)}), bf16[2,4,32,2176]{3,2,0,1:T(8,128)(2,1)S(1)}, u32[]{:S(2)}, u32[]{:S(2)}) async-start(bf16[2,4,32,2176]{3,2,0,1:T(8,128)(2,1)} %pad_maximum_fusion.1), calls=%async_computation.1 | async-start | bytes 2228224 | tf_op jit(solution)/shard_map/all_to_all | solution.py:110
  7.7 1.9 %slice-done.1 = bf16[96,2,8192]{2,1,0:T(2,128)(2,1)S(1)} async-done(((bf16[128,2,8192]{2,1,0:T(2,128)(2,1)}), bf16[96,2,8192]{2,1,0:T(2,128)(2,1)S(1)}, s32[]{:S(2)}) %slice-start.1) | async-done | bytes 3145752 | tf_op jit(solution)/shard_map/slice | solution.py:108
  9.6 1.8 %copy.74 = bf16[96,2,8192]{2,0,1:T(8,128)(2,1)S(1)} copy(bf16[96,2,8192]{2,1,0:T(2,128)(2,1)S(1)} %slice-done.1) | data formatting | bytes 6291456
  11.4 1.0 slice.280
  12.3 0.1 fusion.29
  12.4 1.4 fusion.28
  13.8 0.1 fusion
  13.9 1.2 concatenate.158
  15.2 1.6 maximum_bitcast_fusion
  16.7 2.0 %pad_maximum_fusion = bf16[2,4,96,2176]{3,2,0,1:T(8,128)(2,1)} fusion(bf16[2,1,96,2176]{3,2,0,1:T(8,128)(2,1)S(1)} %bitcast.108, bf16[2,1,96,2176]{3,2,0,1:T(8,128)(2,1)S(1)} %get-tuple-element.76, bf16[2,1,96,2176]{3,2,0,1:T(8,128)(2,1)S(1)} %get-tuple-element.75, bf16[2,1,96,2176]{3,2,0,1:T(8,128)(2,1)S(1)} %fusion), kind=kLoop, calls=%fused_computation | loop fusion | flops 5013504 | bytes 6684672 | tf_op jit(solution)/shard_map/stack | solution.py:89
  18.7 4.7 %all-to-all-done.1 = bf16[2,4,32,2176]{3,2,0,1:T(8,128)(2,1)S(1)} async-done(((bf16[2,4,32,2176]{3,2,0,1:T(8,128)(2,1)}), bf16[2,4,32,2176]{3,2,0,1:T(8,128)(2,1)S(1)}, u32[]{:S(2)}, u32[]{:S(2)}) %all-to-all-start.1) | async-done | bytes 1114144 | tf_op jit(solution)/shard_map/all_to_all | solution.py:110
  23.5 1.0 copy-done.3
  24.5 3.7 %all-to-all-start = ((bf16[2,4,96,2176]{3,2,0,1:T(8,128)(2,1)}), bf16[2,4,96,2176]{3,2,0,1:T(8,128)(2,1)S(1)}, u32[]{:S(2)}, u32[]{:S(2)}) async-start(bf16[2,4,96,2176]{3,2,0,1:T(8,128)(2,1)} %pad_maximum_fusion), calls=%async_computation | async-start | bytes 6684672 | tf_op jit(solution)/shard_map/all_to_all | solution.py:110
  28.3 2.4 %fusion.30 = (bf16[1,4,32,2176]{3,2,1,0:T(8,128)(2,1)}, bf16[1,4,32,2176]{3,2,1,0:T(8,128)(2,1)}) fusion(bf16[2,4,32,2176]{3,2,0,1:T(8,128)(2,1)} %copy-done.3), kind=kLoop, calls=%fused_computation.110 | loop fusion | bytes 2228224 | tf_op jit(solution)/shard_map/slice | solution.py:112
  30.7 1.9 %collective-permute-start.4 = (bf16[128,2176]{1,0:T(8,128)(2,1)}, bf16[128,2176]{1,0:T(8,128)(2,1)}, u32[]{:S(2)}, u32[]{:S(2)}) collective-permute-start(bf16[128,2176]{1,0:T(8,128)(2,1)} %bitcast.31), channel_id=1, source_target_pairs={{0,1},{1,2},{2,3},{3,4},{4,5},{5,6},{6,7},{7,8},{8,9},{9,10},{10,1... | collective-permute-start | bytes 1671176 | tf_op jit(solution)/shard_map/ppermute | solution.py:111
  32.6 3.6 %collective-permute-start.5 = (bf16[128,2176]{1,0:T(8,128)(2,1)}, bf16[128,2176]{1,0:T(8,128)(2,1)}, u32[]{:S(2)}, u32[]{:S(2)}) collective-permute-start(bf16[128,2176]{1,0:T(8,128)(2,1)} %bitcast.32), channel_id=1, source_target_pairs={{1,0},{2,1},{3,2},{4,3},{5,4},{6,5},{7,6},{8,7},{9,8},{10,9},{11,1... | collective-permute-start | bytes 1671176 | tf_op jit(solution)/shard_map/ppermute | solution.py:112
  36.3 1.1 copy.48
  37.4 29.6 %all-to-all-done = bf16[2,4,96,2176]{3,2,0,1:T(8,128)(2,1)S(1)} async-done(((bf16[2,4,96,2176]{3,2,0,1:T(8,128)(2,1)}), bf16[2,4,96,2176]{3,2,0,1:T(8,128)(2,1)S(1)}, u32[]{:S(2)}, u32[]{:S(2)}) %all-to-all-start) | async-done | bytes 3342368 | tf_op jit(solution)/shard_map/all_to_all | solution.py:110
  66.9 1.9 %copy.42 = bf16[2,4,96,2176]{3,2,1,0:T(8,128)(2,1)} copy(bf16[2,4,96,2176]{3,2,0,1:T(8,128)(2,1)S(1)} %all-to-all-done) | data formatting | bytes 6684672 | tf_op jit(solution)/shard_map/all_to_all | solution.py:110
  69.0 0.1 maximum_bitcast_fusion.5
  69.1 0.1 maximum_bitcast_fusion.4
  69.2 0.1 concatenate.162
  69.4 0.1 slice_bitcast_fusion.2
  69.6 0.1 slice_bitcast_fusion
  69.8 2.0 %fusion.27 = (bf16[1,4,96,2176]{3,2,1,0:T(8,128)(2,1)}, bf16[1,4,96,2176]{3,2,1,0:T(8,128)(2,1)}) fusion(bf16[2,4,96,2176]{3,2,0,1:T(8,128)(2,1)S(1)} %all-to-all-done), kind=kLoop, calls=%fused_computation.107 | loop fusion | bytes 6684672 | tf_op jit(solution)/shard_map/slice | solution.py:112
  71.7 1.9 %collective-permute-start = (bf16[384,2176]{1,0:T(8,128)(2,1)}, bf16[384,2176]{1,0:T(8,128)(2,1)}, u32[]{:S(2)}, u32[]{:S(2)}) collective-permute-start(bf16[384,2176]{1,0:T(8,128)(2,1)} %bitcast.6), channel_id=1, source_target_pairs={{0,1},{1,2},{2,3},{3,4},{4,5},{5,6},{6,7},{7,8},{8,9},{9,10},{10,1... | collective-permute-start | bytes 5013512 | tf_op jit(solution)/shard_map/ppermute | solution.py:111
  73.6 3.6 %collective-permute-start.1 = (bf16[384,2176]{1,0:T(8,128)(2,1)}, bf16[384,2176]{1,0:T(8,128)(2,1)}, u32[]{:S(2)}, u32[]{:S(2)}) collective-permute-start(bf16[384,2176]{1,0:T(8,128)(2,1)} %bitcast.7), channel_id=1, source_target_pairs={{1,0},{2,1},{3,2},{4,3},{5,4},{6,5},{7,6},{8,7},{9,8},{10,9},{11,1... | collective-permute-start | bytes 5013512 | tf_op jit(solution)/shard_map/ppermute | solution.py:112
  77.3 1.9 %collective-permute-start.2 = (bf16[2176]{0:T(1024)(128)(2,1)S(1)}, bf16[2176]{0:T(1024)(128)(2,1)S(1)}, u32[]{:S(2)}, u32[]{:S(2)}) collective-permute-start(bf16[2176]{0:T(1024)(128)(2,1)S(1)} %get-tuple-element.31), channel_id=1, source_target_pairs={{0,1},{1,2},{2,3},{3,4},{4,5},{5,6},{6,7},{7,8},{8,9},{9,10},{10,1... | collective-permute-start | bytes 13064 | tf_op jit(solution)/shard_map/ppermute | solution.py:118
  79.2 0.1 constant_dynamic-update-slice_fusion.6
  79.3 0.1 constant_dynamic-update-slice_fusion.5
  79.4 0.1 constant_dynamic-update-slice_fusion.4
  79.5 0.1 constant_dynamic-update-slice_fusion.3
  79.6 15.2 %collective-permute-done.2 = bf16[2176]{0:T(1024)(128)(2,1)S(1)} collective-permute-done((bf16[2176]{0:T(1024)(128)(2,1)S(1)}, bf16[2176]{0:T(1024)(128)(2,1)S(1)}, u32[]{:S(2)}, u32[]{:S(2)}) %collective-permute-start.2) | collective-permute-done | bytes 4384 | tf_op jit(solution)/shard_map/ppermute | solution.py:118
  94.8 2.1 %collective-permute-start.3 = (bf16[2176]{0:T(1024)(128)(2,1)S(1)}, bf16[2176]{0:T(1024)(128)(2,1)S(1)}, u32[]{:S(2)}, u32[]{:S(2)}) collective-permute-start(bf16[2176]{0:T(1024)(128)(2,1)S(1)} %get-tuple-element.30), channel_id=1, source_target_pairs={{1,0},{2,1},{3,2},{4,3},{5,4},{6,5},{7,6},{8,7},{9,8},{10,9},{11,1... | collective-permute-start | bytes 13064 | tf_op jit(solution)/shard_map/ppermute | solution.py:119
  97.0 1.1 collective-permute-done.3
  98.1 0.1 constant_dynamic-update-slice_fusion.coef_ref
  98.3 0.6 copy-done.6
  98.9 4.6 %shard_map.29 = bf16[2,128,2176]{2,1,0:T(8,128)(2,1)} custom-call(bf16[2,128,2176]{2,1,0:T(8,128)(2,1)} %bitcast.97, bf16[128,2176]{1,0:T(8,128)(2,1)} %collective-permute-done.4.below_ref, bf16[128,2176]{1,0:T(8,128)(2,1)} %collective-permute-done.5.above_ref, f32[7,2,2176]{2,1,0:T(2,128)} %copy-done.6), custom_call_target="tpu_custom_call" | custom-call | tf_op jit(solution)/shard_map/pallas_call | solution.py:52
  103.5 2.1 %convolution_bitcast_fusion.3 = f32[128,128]{0,1:T(8,128)S(1)} fusion(bf16[2,128,2176]{2,1,0:T(8,128)(2,1)} %shard_map.29, bf16[2,128,2176]{2,1,0:T(8,128)(2,1)} %bitcast.98), kind=kOutput, calls=%fused_computation.8 | convolution fusion | flops 142606336 | bytes 2293760 | tf_op jit(solution)/shard_map/dot_general | solution.py:126
  105.6 1.0 convolution_bitcast_fusion.1
  106.7 0.3 pad_maximum_fusion.2
  107.0 8.4 %shard_map.28 = bf16[2,384,2176]{2,1,0:T(8,128)(2,1)} custom-call(bf16[2,384,2176]{2,1,0:T(8,128)(2,1)} %bitcast.94, bf16[384,2176]{1,0:T(8,128)(2,1)} %collective-permute-done.below_ref, bf16[384,2176]{1,0:T(8,128)(2,1)} %collective-permute-done.1.above_ref, f32[7,2,2176]{2,1,0:T(2,128)} %copy-done.6), custom_call_target="tpu_custom_call" | custom-call | tf_op jit(solution)/shard_map/pallas_call | solution.py:52
  115.4 3.2 %convolution_bitcast_fusion.2 = f32[384,128]{0,1:T(8,128)S(1)} fusion(bf16[2,384,2176]{2,1,0:T(8,128)(2,1)} %shard_map.28, bf16[2,128,2176]{2,1,0:T(8,128)(2,1)S(1)} %bitcast.99), kind=kOutput, calls=%fused_computation.7 | convolution fusion | flops 427819008 | bytes 4653056 | tf_op jit(solution)/shard_map/dot_general | solution.py:126
  118.7 3.9 %convolution_bitcast_fusion = f32[384,384]{0,1:T(8,128)S(1)} fusion(bf16[2,384,2176]{2,1,0:T(8,128)(2,1)} %shard_map.28, bf16[2,384,2176]{2,1,0:T(8,128)(2,1)S(1)} %bitcast.96), kind=kOutput, calls=%fused_computation.5 | convolution fusion | flops 1283457024 | bytes 7274496 | tf_op jit(solution)/shard_map/dot_general | solution.py:126
  122.5 0.3 pad_maximum_fusion.3
  122.8 0.8 concatenate.181
  123.7 0.4 reshape.462
  124.1 0.9 constant_dynamic-slice_fusion.2
  125.0 1.2 collective-permute-start.8
  126.3 1.6 collective-permute-start.7
  127.9 0.1 collective-permute-start.6
  128.0 5.7 %collective-permute-done.8 = f32[128,512]{0,1:T(8,128)S(1)} collective-permute-done((f32[128,512]{0,1:T(8,128)S(1)}, f32[128,512]{0,1:T(8,128)S(1)}, u32[]{:S(2)}, u32[]{:S(2)}) %collective-permute-start.8) | collective-permute-done | bytes 262176 | tf_op jit(solution)/shard_map/ppermute | solution.py:143
  133.6 3.2 %collective-permute-done.7 = f32[128,512]{0,1:T(8,128)S(1)} collective-permute-done((f32[128,512]{0,1:T(8,128)S(1)}, f32[128,512]{0,1:T(8,128)S(1)}, u32[]{:S(2)}, u32[]{:S(2)}) %collective-permute-start.7) | collective-permute-done | bytes 262176 | tf_op jit(solution)/shard_map/ppermute | solution.py:143
  136.8 5.8 %collective-permute-done.6 = f32[128,512]{0,1:T(8,128)S(1)} collective-permute-done((f32[128,512]{0,1:T(8,128)S(1)}, f32[128,512]{0,1:T(8,128)S(1)}, u32[]{:S(2)}, u32[]{:S(2)}) %collective-permute-start.6) | collective-permute-done | bytes 262176 | tf_op jit(solution)/shard_map/ppermute | solution.py:143
  142.7 3.9 %all_to_all.25 = f32[2,128,8,4,8]{1,4,3,2,0:T(8,128)S(1)} all-to-all(f32[2,128,8,4,8]{1,4,3,2,0:T(8,128)S(1)} %copy.56), channel_id=1, replica_groups=mesh['node'=4,'z'=8,'y'=4,'core'=2] {'core'}, dimensions={0} | all-to-all | bytes 524288 | tf_op jit(solution)/shard_map/all_to_all | solution.py:147
  146.7 9.3 %all_to_all.26 = f32[4,128,8,8]{1,3,2,0:T(8,128)S(1)} all-to-all(f32[4,128,8,8]{1,3,2,0:T(8,128)S(1)} %copy.58), channel_id=1, replica_groups=mesh['node'=4,'z'=8,'y'=4,'core'=2] {'y'}, dimensions={0} | all-to-all | bytes 262144 | tf_op jit(solution)/shard_map/all_to_all | solution.py:147
  156.0 16.4 %all_to_all.27 = f32[8,128,8]{1,2,0:T(8,128)S(1)} all-to-all(f32[8,128,8]{1,2,0:T(8,128)S(1)} %bitcast.116), channel_id=1, replica_groups=mesh['node'=4,'z'=8,'y'=4,'core'=2] {'z'}, dimensions={0} | all-to-all | bytes 65536 | tf_op jit(solution)/shard_map/all_to_all | solution.py:147
  172.4 0.6 broadcast_multiply_fusion
  (59 shorter events, 0.9 us)
Async XLA Ops:
  0.0 1.2 slice-start
  1.2 0.8 copy-start.8
  3.4 20.1 %all-to-all-start.1 = ((bf16[2,4,32,2176]{3,2,0,1:T(8,128)(2,1)}), bf16[2,4,32,2176]{3,2,0,1:T(8,128)(2,1)S(1)}, u32[]{:S(2)}, u32[]{:S(2)}) async-start(bf16[2,4,32,2176]{3,2,0,1:T(8,128)(2,1)} %pad_maximum_fusion.1), calls=%async_computation.1 | async-start | bytes 2228224 | tf_op jit(solution)/shard_map/all_to_all | solution.py:110
  7.7 1.9 %slice-start.1 = ((bf16[128,2,8192]{2,1,0:T(2,128)(2,1)}), bf16[96,2,8192]{2,1,0:T(2,128)(2,1)S(1)}, s32[]{:S(2)}) async-start(bf16[128,2,8192]{2,1,0:T(2,128)(2,1)} %param.4), calls=%async_computation.6 | async-start | bytes 6291456 | tf_op jit(solution)/shard_map/slice | solution.py:108
  23.5 1.0 copy-start.3
  24.5 42.5 %all-to-all-start = ((bf16[2,4,96,2176]{3,2,0,1:T(8,128)(2,1)}), bf16[2,4,96,2176]{3,2,0,1:T(8,128)(2,1)S(1)}, u32[]{:S(2)}, u32[]{:S(2)}) async-start(bf16[2,4,96,2176]{3,2,0,1:T(8,128)(2,1)} %pad_maximum_fusion), calls=%async_computation | async-start | bytes 6684672 | tf_op jit(solution)/shard_map/all_to_all | solution.py:110
  28.3 8.0 %copy-start.4 = (bf16[2,4,32,2176]{3,2,0,1:T(8,128)(2,1)S(1)}, bf16[2,4,32,2176]{3,2,0,1:T(8,128)(2,1)}, u32[]{:S(2)}) copy-start(bf16[2,4,32,2176]{3,2,0,1:T(8,128)(2,1)} %copy-done.3) | copy-start | bytes 3342340
  30.7 67.5 %collective-permute-start.4 = (bf16[128,2176]{1,0:T(8,128)(2,1)}, bf16[128,2176]{1,0:T(8,128)(2,1)}, u32[]{:S(2)}, u32[]{:S(2)}) collective-permute-start(bf16[128,2176]{1,0:T(8,128)(2,1)} %bitcast.31), channel_id=1, source_target_pairs={{0,1},{1,2},{2,3},{3,4},{4,5},{5,6},{6,7},{7,8},{8,9},{9,10},{10,1... | collective-permute-start | bytes 1671176 | tf_op jit(solution)/shard_map/ppermute | solution.py:111
  32.6 65.6 %collective-permute-start.5 = (bf16[128,2176]{1,0:T(8,128)(2,1)}, bf16[128,2176]{1,0:T(8,128)(2,1)}, u32[]{:S(2)}, u32[]{:S(2)}) collective-permute-start(bf16[128,2176]{1,0:T(8,128)(2,1)} %bitcast.32), channel_id=1, source_target_pairs={{1,0},{2,1},{3,2},{4,3},{5,4},{6,5},{7,6},{8,7},{9,8},{10,9},{11,1... | collective-permute-start | bytes 1671176 | tf_op jit(solution)/shard_map/ppermute | solution.py:112
  37.4 31.5 %copy-start.7 = (bf16[2,8192]{1,0:T(2,128)(2,1)S(1)}, bf16[2,8192]{1,0:T(2,128)(2,1)}, u32[]{:S(2)}) copy-start(bf16[2,8192]{1,0:T(2,128)(2,1)} %param.5) | copy-start | bytes 98308
  71.7 35.2 %collective-permute-start = (bf16[384,2176]{1,0:T(8,128)(2,1)}, bf16[384,2176]{1,0:T(8,128)(2,1)}, u32[]{:S(2)}, u32[]{:S(2)}) collective-permute-start(bf16[384,2176]{1,0:T(8,128)(2,1)} %bitcast.6), channel_id=1, source_target_pairs={{0,1},{1,2},{2,3},{3,4},{4,5},{5,6},{6,7},{7,8},{8,9},{9,10},{10,1... | collective-permute-start | bytes 5013512 | tf_op jit(solution)/shard_map/ppermute | solution.py:111
  73.6 33.3 %collective-permute-start.1 = (bf16[384,2176]{1,0:T(8,128)(2,1)}, bf16[384,2176]{1,0:T(8,128)(2,1)}, u32[]{:S(2)}, u32[]{:S(2)}) collective-permute-start(bf16[384,2176]{1,0:T(8,128)(2,1)} %bitcast.7), channel_id=1, source_target_pairs={{1,0},{2,1},{3,2},{4,3},{5,4},{6,5},{7,6},{8,7},{9,8},{10,9},{11,1... | collective-permute-start | bytes 5013512 | tf_op jit(solution)/shard_map/ppermute | solution.py:112
  77.3 17.5 %collective-permute-start.2 = (bf16[2176]{0:T(1024)(128)(2,1)S(1)}, bf16[2176]{0:T(1024)(128)(2,1)S(1)}, u32[]{:S(2)}, u32[]{:S(2)}) collective-permute-start(bf16[2176]{0:T(1024)(128)(2,1)S(1)} %get-tuple-element.31), channel_id=1, source_target_pairs={{0,1},{1,2},{2,3},{3,4},{4,5},{5,6},{6,7},{7,8},{8,9},{9,10},{10,1... | collective-permute-start | bytes 13064 | tf_op jit(solution)/shard_map/ppermute | solution.py:118
  94.8 3.2 %collective-permute-start.3 = (bf16[2176]{0:T(1024)(128)(2,1)S(1)}, bf16[2176]{0:T(1024)(128)(2,1)S(1)}, u32[]{:S(2)}, u32[]{:S(2)}) collective-permute-start(bf16[2176]{0:T(1024)(128)(2,1)S(1)} %get-tuple-element.30), channel_id=1, source_target_pairs={{1,0},{2,1},{3,2},{4,3},{5,4},{6,5},{7,6},{8,7},{9,8},{10,9},{11,1... | collective-permute-start | bytes 13064 | tf_op jit(solution)/shard_map/ppermute | solution.py:119
  98.2 0.6 copy-start.6
  98.9 6.8 %copy-start = (bf16[2,4,96,2176]{3,2,1,0:T(8,128)(2,1)S(1)}, bf16[2,4,96,2176]{3,2,1,0:T(8,128)(2,1)}, u32[]{:S(2)}) copy-start(bf16[2,4,96,2176]{3,2,1,0:T(8,128)(2,1)} %copy.42) | copy-start | bytes 10027012
  103.5 2.1 %copy-start.5 = (bf16[2,128,2176]{2,1,0:T(8,128)(2,1)S(1)}, bf16[2,128,2176]{2,1,0:T(8,128)(2,1)}, u32[]{:S(2)}) copy-start(bf16[2,128,2176]{2,1,0:T(8,128)(2,1)} %shard_map.29) | copy-start | bytes 3342340
  106.9 8.5 %copy-start.2 = (bf16[2,4,32,2176]{3,2,1,0:T(8,128)(2,1)S(1)}, bf16[2,4,32,2176]{3,2,1,0:T(8,128)(2,1)}, u32[]{:S(2)}) copy-start(bf16[2,4,32,2176]{3,2,1,0:T(8,128)(2,1)} %copy.48) | copy-start | bytes 3342340
  115.4 3.2 %copy-start.1 = (bf16[2,4,96,2176]{3,2,1,0:T(8,128)(2,1)S(1)}, bf16[2,4,96,2176]{3,2,1,0:T(8,128)(2,1)}, u32[]{:S(2)}) copy-start(bf16[2,4,96,2176]{3,2,1,0:T(8,128)(2,1)} %copy.42) | copy-start | bytes 10027012
  125.0 8.6 %collective-permute-start.8 = (f32[128,512]{0,1:T(8,128)S(1)}, f32[128,512]{0,1:T(8,128)S(1)}, u32[]{:S(2)}, u32[]{:S(2)}) collective-permute-start(f32[128,512]{0,1:T(8,128)S(1)} %select_bitcast_fusion), channel_id=1, source_target_pairs={{0,192},{64,0},{128,64},{192,128},{1,193},{65,1},{129,65},{193,129... | collective-permute-start | bytes 786440 | tf_op jit(solution)/shard_map/ppermute | solution.py:143
  126.3 10.5 %collective-permute-start.7 = (f32[128,512]{0,1:T(8,128)S(1)}, f32[128,512]{0,1:T(8,128)S(1)}, u32[]{:S(2)}, u32[]{:S(2)}) collective-permute-start(f32[128,512]{0,1:T(8,128)S(1)} %select_bitcast_fusion.1), channel_id=1, source_target_pairs={{0,128},{64,192},{128,0},{192,64},{1,129},{65,193},{129,1},{193,65... | collective-permute-start | bytes 786440 | tf_op jit(solution)/shard_map/ppermute | solution.py:143
  127.9 14.8 %collective-permute-start.6 = (f32[128,512]{0,1:T(8,128)S(1)}, f32[128,512]{0,1:T(8,128)S(1)}, u32[]{:S(2)}, u32[]{:S(2)}) collective-permute-start(f32[128,512]{0,1:T(8,128)S(1)} %select_bitcast_fusion.2), channel_id=1, source_target_pairs={{0,64},{64,128},{128,192},{192,0},{1,65},{65,129},{129,193},{193,1... | collective-permute-start | bytes 786440 | tf_op jit(solution)/shard_map/ppermute | solution.py:143

commit v17 on v15

--- a/solution.py
+++ b/solution.py
@@ -132,9 +132,11 @@
         total = total + lax.ppermute(blk, "node", [(i, (i + d) % nodes) for i in range(nodes)])
     total = total.reshape(rows, GROUPS, nodes, step).transpose(0, 2, 1, 3)
     total = total.reshape((rows,) + tuple(sizes) + (snaps // spaces,))
-    for axis in reversed(range(len(SPACE))):
-        total = jnp.moveaxis(total, axis + 1, 0)
-        total = lax.all_to_all(total, SPACE[axis], 0, 0, tiled=True).sum(axis=0)
+    total = jnp.moveaxis(total, 3, 0)
+    total = lax.all_to_all(total, SPACE[2], 0, 0, tiled=True).sum(axis=0)
+    total = total.reshape(rows, sizes[0] * sizes[1], snaps // spaces)
+    total = jnp.moveaxis(total, 1, 0)
+    total = lax.all_to_all(total, SPACE[:2], 0, 0, tiled=True).sum(axis=0)
     out = total
 
     scale = jnp.float32(1.0 / math.sqrt(planes * spaces * NY * NZ))

time: 160 us -> 156 us (0.975)
  blocking collectives: 29.7 us -> 24.8 us
    all_to_all x3 -> x2, blocking collectives: 29.7 us -> 24.8 us  [the longest x1 20.8 us: per_device(): total = lax.all_to_all(total, SPACE[:2], 0, 0, tiled=True).sum(axis=0)]
  transfers between devices with their start and end apart: 11 -> 11, of which waited for: 6 -> 6; matrix products, arithmetic and copies ran while one was open for 13% -> 14% of each run, Pallas kernels for 4% -> 4%
where the time goes in v17:
time: 156 us; the launch traced here: 153 us
  waiting for transfers between devices  47.6 us (31%)
  starting transfers between devices  29.1 us (19%)
  local copies, waits for them, and re-layouts  26.4 us (17%)
  blocking collectives  24.8 us (16%)
  Pallas kernels  12.8 us (8%)
  matrix products  6.63 us (4%)
  other arithmetic  5.7 us (4%)
    all_to_all x2, waiting for transfers between devices, per_device(): lax.all_to_all(chunked(major, nodes), 'node', 1, 1, tiled=True)  32.7 us
    all_to_all x1, blocking collectives, per_device(): total = lax.all_to_all(total, SPACE[:2], 0, 0, tiled=True).sum(axis=0)  20.8 us
    ppermute x3, waiting for transfers between devices, per_device(): lax.ppermute(blk, 'node', [(i, (i + d) % nodes) for i in range(nodes)])  12.9 us
    pallas_call x2, Pallas kernels, stencil(): pl.pallas_call(stencil_kernel, grid=(snaps // ROWS,), in_specs=[pl.BlockS...  12.8 us
    all_to_all x2, starting transfers between devices, per_device(): lax.all_to_all(chunked(major, nodes), 'node', 1, 1, tiled=True)  8.77 us
    ppermute x2, starting transfers between devices, per_device(): above = lax.ppermute(field[0], SPACE, down)  7.46 us
    dot_general x4, matrix products, per_device(): lax.dot_general(im, fd, dims, preferred_element_type=jnp.float32)  6.63 us
    slice x1, local copies, waits for them, and re-layouts, per_device(): major = jnp.transpose(snapshots[g * step:(g + 1) * step], (1, 0, 2))  5.04 us
  transfers between devices with their start and end apart: 11, of which 6 were waited for; matrix products, arithmetic and copies ran while one was open for 14% of the time, Pallas kernels for 4%

profile of v17, /device:TPU:8, one launch (start us, length us, event | category | flops | bytes accessed | tf_op | source)
XLA Modules:
  0.0 153.4 jit_solution(10312666133117918976)
XLA Ops:
  0.0 5.0 %fusion.25 = (bf16[64,2,8192]{2,1,0:T(2,128)(2,1)S(1)}, bf16[64,2,8192]{2,1,0:T(2,128)(2,1)S(1)}) fusion(bf16[128,2,8192]{2,1,0:T(2,128)(2,1)} %param.4), kind=kLoop, calls=%fused_computation.80 | loop fusion | bytes 8388608 | tf_op jit(solution)/shard_map/slice | solution.py:108
  5.1 2.7 %copy_bitcast_fusion = (bf16[2,64,8192]{2,1,0:T(8,128)(2,1)S(1)}, bf16[2,64,8192]{2,1,0:T(8,128)(2,1)S(1)}) fusion(bf16[64,2,8192]{2,1,0:T(2,128)(2,1)S(1)} %get-tuple-element.35, bf16[64,2,8192]{2,1,0:T(2,128)(2,1)S(1)} %get-tuple-element.34), kind=kLoop, calls=%fused_computation.2 | loop fusion | bytes 8388608 | tf_op jit(solution)/shard_map/transpose | solution.py:108
  7.7 0.1 fusion.29
  7.8 0.1 fusion.28
  8.0 0.1 maximum_bitcast_fusion
  8.1 0.1 maximum_bitcast_fusion.1
  8.2 0.9 copy-done.5
  9.1 0.1 fusion.1
  9.2 0.3 concatenate.155
  9.5 1.7 %pad_maximum_fusion = bf16[2,4,64,2176]{3,2,0,1:T(8,128)(2,1)} fusion(bf16[2,1,64,2176]{3,2,0,1:T(8,128)(2,1)S(1)} %bitcast.119, bf16[2,1,64,2176]{3,2,0,1:T(8,128)(2,1)S(1)} %maximum_bitcast_fusion.1, bf16[2,1,64,2176]{3,2,0,1:T(8,128)(2,1)S(1)} %maximum_bitcast_fusion, bf16[2,1,64,2176]{3,2,0,1:T(8,128)(2,1)S(1)} %get-tuple-element.67), kind=kLoop, calls=%fused_computation | loop fusion | flops 3342336 | bytes 4456448 | tf_op jit(solution)/shard_map/stack | solution.py:89
  11.2 4.3 %all-to-all-start = ((bf16[2,4,64,2176]{3,2,0,1:T(8,128)(2,1)}), bf16[2,4,64,2176]{3,2,0,1:T(8,128)(2,1)S(1)}, u32[]{:S(2)}, u32[]{:S(2)}) async-start(bf16[2,4,64,2176]{3,2,0,1:T(8,128)(2,1)} %pad_maximum_fusion), calls=%async_computation | async-start | bytes 4456448 | tf_op jit(solution)/shard_map/all_to_all | solution.py:109
  15.5 0.9 fusion.31
  16.4 1.9 %slice.246 = bf16[2,64,2048]{2,1,0:T(8,128)(2,1)} slice(bf16[2,64,8192]{2,1,0:T(8,128)(2,1)} %copy-done.5), slice={[0:2], [0:64], [6144:8192]} | slice | bytes 1048576 | tf_op jit(solution)/shard_map/slice | solution.py:88
  18.3 1.2 concatenate.175
  19.5 1.3 fusion.30
  20.8 0.1 maximum_bitcast_fusion.2
  20.9 0.1 maximum_bitcast_fusion.3
  20.9 1.7 %pad_maximum_fusion.1 = bf16[2,4,64,2176]{3,2,0,1:T(8,128)(2,1)} fusion(bf16[2,1,64,2176]{3,2,0,1:T(8,128)(2,1)S(1)} %bitcast.118, bf16[2,1,64,2176]{3,2,0,1:T(8,128)(2,1)S(1)} %maximum_bitcast_fusion.3, bf16[2,1,64,2176]{3,2,0,1:T(8,128)(2,1)S(1)} %maximum_bitcast_fusion.2, bf16[2,1,64,2176]{3,2,0,1:T(8,128)(2,1)S(1)} %get-tuple-element.68), kind=kLoop, calls=%fused_computation.1 | loop fusion | flops 3342336 | bytes 4456448 | tf_op jit(solution)/shard_map/stack | solution.py:89
  22.7 20.5 %all-to-all-done = bf16[2,4,64,2176]{3,2,0,1:T(8,128)(2,1)S(1)} async-done(((bf16[2,4,64,2176]{3,2,0,1:T(8,128)(2,1)}), bf16[2,4,64,2176]{3,2,0,1:T(8,128)(2,1)S(1)}, u32[]{:S(2)}, u32[]{:S(2)}) %all-to-all-start) | async-done | bytes 2228256 | tf_op jit(solution)/shard_map/all_to_all | solution.py:109
  43.2 4.5 %all-to-all-start.1 = ((bf16[2,4,64,2176]{3,2,0,1:T(8,128)(2,1)}), bf16[2,4,64,2176]{3,2,0,1:T(8,128)(2,1)}, u32[]{:S(2)}, u32[]{:S(2)}) async-start(bf16[2,4,64,2176]{3,2,0,1:T(8,128)(2,1)} %pad_maximum_fusion.1), calls=%async_computation.1 | async-start | bytes 4456448 | tf_op jit(solution)/shard_map/all_to_all | solution.py:109
  47.7 1.6 %copy.41 = bf16[2,4,64,2176]{3,2,1,0:T(8,128)(2,1)} copy(bf16[2,4,64,2176]{3,2,0,1:T(8,128)(2,1)S(1)} %all-to-all-done) | data formatting | bytes 4456448 | tf_op jit(solution)/shard_map/all_to_all | solution.py:109
  49.4 0.1 maximum_bitcast_fusion.4
  49.5 0.1 maximum_bitcast_fusion.5
  49.6 0.1 concatenate.159
  49.9 1.9 %collective-permute-start.2 = (bf16[2176]{0:T(1024)(128)(2,1)S(1)}, bf16[2176]{0:T(1024)(128)(2,1)S(1)}, u32[]{:S(2)}, u32[]{:S(2)}) collective-permute-start(bf16[2176]{0:T(1024)(128)(2,1)S(1)} %get-tuple-element.31), channel_id=1, source_target_pairs={{0,1},{1,2},{2,3},{3,4},{4,5},{5,6},{6,7},{7,8},{8,9},{9,10},{10,1... | collective-permute-start | bytes 13064 | tf_op jit(solution)/shard_map/ppermute | solution.py:117
  51.8 3.6 %collective-permute-start.3 = (bf16[2176]{0:T(1024)(128)(2,1)S(1)}, bf16[2176]{0:T(1024)(128)(2,1)S(1)}, u32[]{:S(2)}, u32[]{:S(2)}) collective-permute-start(bf16[2176]{0:T(1024)(128)(2,1)S(1)} %get-tuple-element.30), channel_id=1, source_target_pairs={{1,0},{2,1},{3,2},{4,3},{5,4},{6,5},{7,6},{8,7},{9,8},{10,9},{11,1... | collective-permute-start | bytes 13064 | tf_op jit(solution)/shard_map/ppermute | solution.py:118
  55.5 1.2 fusion.26
  56.6 1.9 %collective-permute-start = (bf16[256,2176]{1,0:T(8,128)(2,1)}, bf16[256,2176]{1,0:T(8,128)(2,1)}, u32[]{:S(2)}, u32[]{:S(2)}) collective-permute-start(bf16[256,2176]{1,0:T(8,128)(2,1)} %bitcast.6), channel_id=1, source_target_pairs={{0,1},{1,2},{2,3},{3,4},{4,5},{5,6},{6,7},{7,8},{8,9},{9,10},{10,1... | collective-permute-start | bytes 3342344 | tf_op jit(solution)/shard_map/ppermute | solution.py:110
  58.6 3.6 %collective-permute-start.1 = (bf16[256,2176]{1,0:T(8,128)(2,1)S(1)}, bf16[256,2176]{1,0:T(8,128)(2,1)}, u32[]{:S(2)}, u32[]{:S(2)}) collective-permute-start(bf16[256,2176]{1,0:T(8,128)(2,1)S(1)} %bitcast.121), channel_id=1, source_target_pairs={{1,0},{2,1},{3,2},{4,3},{5,4},{6,5},{7,6},{8,7},{9,8},{10,9},{11,1... | collective-permute-start | bytes 3342344 | tf_op jit(solution)/shard_map/ppermute | solution.py:111
  62.4 0.1 slice_bitcast_fusion
  62.4 12.1 %all-to-all-done.1 = bf16[2,4,64,2176]{3,2,0,1:T(8,128)(2,1)} async-done(((bf16[2,4,64,2176]{3,2,0,1:T(8,128)(2,1)}), bf16[2,4,64,2176]{3,2,0,1:T(8,128)(2,1)}, u32[]{:S(2)}, u32[]{:S(2)}) %all-to-all-start.1) | async-done | bytes 2228256 | tf_op jit(solution)/shard_map/all_to_all | solution.py:109
  74.6 3.2 %fusion.27 = (bf16[1,4,64,2176]{3,2,1,0:T(8,128)(2,1)}, bf16[1,4,64,2176]{3,2,1,0:T(8,128)(2,1)}) fusion(bf16[2,4,64,2176]{3,2,0,1:T(8,128)(2,1)} %all-to-all-done.1), kind=kLoop, calls=%fused_computation.82 | loop fusion | bytes 4456448 | tf_op jit(solution)/shard_map/slice | solution.py:111
  77.8 1.9 %collective-permute-start.4 = (bf16[256,2176]{1,0:T(8,128)(2,1)}, bf16[256,2176]{1,0:T(8,128)(2,1)}, u32[]{:S(2)}, u32[]{:S(2)}) collective-permute-start(bf16[256,2176]{1,0:T(8,128)(2,1)} %bitcast.31), channel_id=1, source_target_pairs={{0,1},{1,2},{2,3},{3,4},{4,5},{5,6},{6,7},{7,8},{8,9},{9,10},{10,1... | collective-permute-start | bytes 3342344 | tf_op jit(solution)/shard_map/ppermute | solution.py:110
  79.7 0.1 select_dynamic-update-slice_fusion.1
  79.8 0.1 select_dynamic-update-slice_fusion
  79.9 0.1 constant_dynamic-update-slice_fusion.3
  80.0 0.1 constant_dynamic-update-slice_fusion.2
  80.1 3.2 %copy.47 = bf16[2,4,64,2176]{3,2,1,0:T(8,128)(2,1)} copy(bf16[2,4,64,2176]{3,2,0,1:T(8,128)(2,1)} %all-to-all-done.1) | data formatting | bytes 4456448 | tf_op jit(solution)/shard_map/all_to_all | solution.py:109
  83.3 3.8 %collective-permute-start.5 = (bf16[256,2176]{1,0:T(8,128)(2,1)}, bf16[256,2176]{1,0:T(8,128)(2,1)}, u32[]{:S(2)}, u32[]{:S(2)}) collective-permute-start(bf16[256,2176]{1,0:T(8,128)(2,1)} %bitcast.32), channel_id=1, source_target_pairs={{1,0},{2,1},{3,2},{4,3},{5,4},{6,5},{7,6},{8,7},{9,8},{10,9},{11,1... | collective-permute-start | bytes 3342344 | tf_op jit(solution)/shard_map/ppermute | solution.py:111
  87.2 0.1 add_dynamic-update-slice_fusion.coef_ref
  87.4 0.6 copy-done.6
  88.0 6.5 %shard_map.28 = bf16[2,256,2176]{2,1,0:T(8,128)(2,1)} custom-call(bf16[2,256,2176]{2,1,0:T(8,128)(2,1)} %bitcast.109, bf16[256,2176]{1,0:T(8,128)(2,1)} %collective-permute-done.below_ref, bf16[256,2176]{1,0:T(8,128)(2,1)} %collective-permute-done.1.above_ref, f32[7,2,2176]{2,1,0:T(2,128)} %copy-done.6), custom_call_target="tpu_custom_call" | custom-call | tf_op jit(solution)/shard_map/pallas_call | solution.py:52
  94.5 2.5 %convolution_bitcast_fusion.3 = f32[256,256]{0,1:T(8,128)S(1)} fusion(bf16[2,256,2176]{2,1,0:T(8,128)(2,1)} %shard_map.28, bf16[2,256,2176]{2,1,0:T(8,128)(2,1)S(1)} %bitcast.110), kind=kOutput, calls=%fused_computation.7 | convolution fusion | flops 570425344 | bytes 4718592 | tf_op jit(solution)/shard_map/dot_general | solution.py:125
  97.0 0.4 copy-done.4
  97.4 0.8 convolution_bitcast_fusion.2
  98.2 2.0 %collective-permute-done.5.above_ref = bf16[256,2176]{1,0:T(8,128)(2,1)} collective-permute-done((bf16[256,2176]{1,0:T(8,128)(2,1)}, bf16[256,2176]{1,0:T(8,128)(2,1)}, u32[]{:S(2)}, u32[]{:S(2)}) %collective-permute-start.5) | collective-permute-done | bytes 1114144 | tf_op jit(solution)/shard_map/ppermute | solution.py:111
  100.2 6.4 %shard_map.29 = bf16[2,256,2176]{2,1,0:T(8,128)(2,1)} custom-call(bf16[2,256,2176]{2,1,0:T(8,128)(2,1)} %bitcast.112, bf16[256,2176]{1,0:T(8,128)(2,1)} %collective-permute-done.4.below_ref, bf16[256,2176]{1,0:T(8,128)(2,1)} %collective-permute-done.5.above_ref, f32[7,2,2176]{2,1,0:T(2,128)} %copy-done.6), custom_call_target="tpu_custom_call" | custom-call | tf_op jit(solution)/shard_map/pallas_call | solution.py:52
  106.6 2.5 %convolution_bitcast_fusion.1 = f32[256,256]{0,1:T(8,128)S(1)} fusion(bf16[2,256,2176]{2,1,0:T(8,128)(2,1)} %shard_map.29, bf16[2,256,2176]{2,1,0:T(8,128)(2,1)S(1)} %bitcast.111), kind=kOutput, calls=%fused_computation.5 | convolution fusion | flops 570425344 | bytes 4718592 | tf_op jit(solution)/shard_map/dot_general | solution.py:125
  109.2 0.4 copy-done.3
  109.6 0.8 convolution_bitcast_fusion
  110.3 0.1 maximum_maximum_fusion
  110.5 0.3 copy.50
  110.9 0.6 collective-permute-start.6
  111.5 2.1 %collective-permute-start.7 = (f32[2,64,512]{2,1,0:T(8,128)S(1)}, f32[2,64,512]{2,1,0:T(8,128)S(1)}, u32[]{:S(2)}, u32[]{:S(2)}) collective-permute-start(f32[2,64,512]{2,1,0:T(8,128)S(1)} %get-tuple-element.51), channel_id=1, source_target_pairs={{0,128},{64,192},{128,0},{192,64},{1,129},{65,193},{129,1},{193,65... | collective-permute-start | bytes 786440 | tf_op jit(solution)/shard_map/ppermute | solution.py:132
  113.6 0.8 collective-permute-start.8
  114.4 6.7 %collective-permute-done.6 = f32[2,64,512]{2,1,0:T(8,128)S(1)} collective-permute-done((f32[2,64,512]{2,1,0:T(8,128)S(1)}, f32[2,64,512]{2,1,0:T(8,128)S(1)}, u32[]{:S(2)}, u32[]{:S(2)}) %collective-permute-start.6) | collective-permute-done | bytes 262176 | tf_op jit(solution)/shard_map/ppermute | solution.py:132
  121.1 4.5 %collective-permute-done.7 = f32[2,64,512]{2,1,0:T(8,128)S(1)} collective-permute-done((f32[2,64,512]{2,1,0:T(8,128)S(1)}, f32[2,64,512]{2,1,0:T(8,128)S(1)}, u32[]{:S(2)}, u32[]{:S(2)}) %collective-permute-start.7) | collective-permute-done | bytes 262176 | tf_op jit(solution)/shard_map/ppermute | solution.py:132
  125.6 1.7 %collective-permute-done.8 = f32[2,64,512]{2,1,0:T(8,128)S(1)} collective-permute-done((f32[2,64,512]{2,1,0:T(8,128)S(1)}, f32[2,64,512]{2,1,0:T(8,128)S(1)}, u32[]{:S(2)}, u32[]{:S(2)}) %collective-permute-start.8) | collective-permute-done | bytes 262176 | tf_op jit(solution)/shard_map/ppermute | solution.py:132
  127.3 0.1 fusion.7
  127.4 0.3 reshape.469
  127.7 0.2 copy.54
  128.0 3.9 %all_to_all.20 = f32[2,128,8,4,8]{1,4,3,2,0:T(8,128)S(1)} all-to-all(f32[2,128,8,4,8]{1,4,3,2,0:T(8,128)S(1)} %copy.55), channel_id=1, replica_groups=mesh['node'=4,'z'=8,'y'=4,'core'=2] {'core'}, dimensions={0} | all-to-all | bytes 524288 | tf_op jit(solution)/shard_map/all_to_all | solution.py:136
  131.9 20.8 %all_to_all.21 = f32[32,128,8]{1,2,0:T(8,128)S(1)} all-to-all(f32[32,128,8]{1,2,0:T(8,128)S(1)} %bitcast.123), channel_id=1, replica_groups=mesh['node'=4,'z'=8,'y'=4,'core'=2] {'z','y'}, dimensions={0} | all-to-all | bytes 262144 | tf_op jit(solution)/shard_map/all_to_all | solution.py:139
  152.8 0.6 broadcast_multiply_fusion
  (42 shorter events, 0.8 us)
Async XLA Ops:
  7.7 1.4 copy-start.5
  7.9 1.1 copy-start.8
  11.2 32.0 %all-to-all-start = ((bf16[2,4,64,2176]{3,2,0,1:T(8,128)(2,1)}), bf16[2,4,64,2176]{3,2,0,1:T(8,128)(2,1)S(1)}, u32[]{:S(2)}, u32[]{:S(2)}) async-start(bf16[2,4,64,2176]{3,2,0,1:T(8,128)(2,1)} %pad_maximum_fusion), calls=%async_computation | async-start | bytes 4456448 | tf_op jit(solution)/shard_map/all_to_all | solution.py:109
  43.2 31.4 %all-to-all-start.1 = ((bf16[2,4,64,2176]{3,2,0,1:T(8,128)(2,1)}), bf16[2,4,64,2176]{3,2,0,1:T(8,128)(2,1)}, u32[]{:S(2)}, u32[]{:S(2)}) async-start(bf16[2,4,64,2176]{3,2,0,1:T(8,128)(2,1)} %pad_maximum_fusion.1), calls=%async_computation.1 | async-start | bytes 4456448 | tf_op jit(solution)/shard_map/all_to_all | solution.py:109
  47.7 1.6 %copy-start.7 = (bf16[2,8192]{1,0:T(2,128)(2,1)S(1)}, bf16[2,8192]{1,0:T(2,128)(2,1)}, u32[]{:S(2)}) copy-start(bf16[2,8192]{1,0:T(2,128)(2,1)} %param.5) | copy-start | bytes 98308
  49.9 33.4 %collective-permute-start.2 = (bf16[2176]{0:T(1024)(128)(2,1)S(1)}, bf16[2176]{0:T(1024)(128)(2,1)S(1)}, u32[]{:S(2)}, u32[]{:S(2)}) collective-permute-start(bf16[2176]{0:T(1024)(128)(2,1)S(1)} %get-tuple-element.31), channel_id=1, source_target_pairs={{0,1},{1,2},{2,3},{3,4},{4,5},{5,6},{6,7},{7,8},{8,9},{9,10},{10,1... | collective-permute-start | bytes 13064 | tf_op jit(solution)/shard_map/ppermute | solution.py:117
  51.8 35.3 %collective-permute-start.3 = (bf16[2176]{0:T(1024)(128)(2,1)S(1)}, bf16[2176]{0:T(1024)(128)(2,1)S(1)}, u32[]{:S(2)}, u32[]{:S(2)}) collective-permute-start(bf16[2176]{0:T(1024)(128)(2,1)S(1)} %get-tuple-element.30), channel_id=1, source_target_pairs={{1,0},{2,1},{3,2},{4,3},{5,4},{6,5},{7,6},{8,7},{9,8},{10,9},{11,1... | collective-permute-start | bytes 13064 | tf_op jit(solution)/shard_map/ppermute | solution.py:118
  56.6 30.7 %collective-permute-start = (bf16[256,2176]{1,0:T(8,128)(2,1)}, bf16[256,2176]{1,0:T(8,128)(2,1)}, u32[]{:S(2)}, u32[]{:S(2)}) collective-permute-start(bf16[256,2176]{1,0:T(8,128)(2,1)} %bitcast.6), channel_id=1, source_target_pairs={{0,1},{1,2},{2,3},{3,4},{4,5},{5,6},{6,7},{7,8},{8,9},{9,10},{10,1... | collective-permute-start | bytes 3342344 | tf_op jit(solution)/shard_map/ppermute | solution.py:110
  58.6 28.8 %collective-permute-start.1 = (bf16[256,2176]{1,0:T(8,128)(2,1)S(1)}, bf16[256,2176]{1,0:T(8,128)(2,1)}, u32[]{:S(2)}, u32[]{:S(2)}) collective-permute-start(bf16[256,2176]{1,0:T(8,128)(2,1)S(1)} %bitcast.121), channel_id=1, source_target_pairs={{1,0},{2,1},{3,2},{4,3},{5,4},{6,5},{7,6},{8,7},{9,8},{10,9},{11,1... | collective-permute-start | bytes 3342344 | tf_op jit(solution)/shard_map/ppermute | solution.py:111
  77.8 20.5 %collective-permute-start.4 = (bf16[256,2176]{1,0:T(8,128)(2,1)}, bf16[256,2176]{1,0:T(8,128)(2,1)}, u32[]{:S(2)}, u32[]{:S(2)}) collective-permute-start(bf16[256,2176]{1,0:T(8,128)(2,1)} %bitcast.31), channel_id=1, source_target_pairs={{0,1},{1,2},{2,3},{3,4},{4,5},{5,6},{6,7},{7,8},{8,9},{9,10},{10,1... | collective-permute-start | bytes 3342344 | tf_op jit(solution)/shard_map/ppermute | solution.py:110
  83.3 17.0 %collective-permute-start.5 = (bf16[256,2176]{1,0:T(8,128)(2,1)}, bf16[256,2176]{1,0:T(8,128)(2,1)}, u32[]{:S(2)}, u32[]{:S(2)}) collective-permute-start(bf16[256,2176]{1,0:T(8,128)(2,1)} %bitcast.32), channel_id=1, source_target_pairs={{1,0},{2,1},{3,2},{4,3},{5,4},{6,5},{7,6},{8,7},{9,8},{10,9},{11,1... | collective-permute-start | bytes 3342344 | tf_op jit(solution)/shard_map/ppermute | solution.py:111
  87.3 0.7 copy-start.6
  87.4 7.1 %copy-start = (bf16[2,4,64,2176]{3,2,1,0:T(8,128)(2,1)S(1)}, bf16[2,4,64,2176]{3,2,1,0:T(8,128)(2,1)}, u32[]{:S(2)}) copy-start(bf16[2,4,64,2176]{3,2,1,0:T(8,128)(2,1)} %copy.41) | copy-start | bytes 6684676
  94.5 2.6 %copy-start.1 = (bf16[2,4,64,2176]{3,2,1,0:T(8,128)(2,1)S(1)}, bf16[2,4,64,2176]{3,2,1,0:T(8,128)(2,1)}, u32[]{:S(2)}) copy-start(bf16[2,4,64,2176]{3,2,1,0:T(8,128)(2,1)} %copy.47) | copy-start | bytes 6684676
  94.5 3.0 %copy-start.4 = (bf16[2,256,2176]{2,1,0:T(8,128)(2,1)S(1)}, bf16[2,256,2176]{2,1,0:T(8,128)(2,1)}, u32[]{:S(2)}) copy-start(bf16[2,256,2176]{2,1,0:T(8,128)(2,1)} %shard_map.28) | copy-start | bytes 6684676
  106.6 2.6 %copy-start.2 = (bf16[2,4,64,2176]{3,2,1,0:T(8,128)(2,1)S(1)}, bf16[2,4,64,2176]{3,2,1,0:T(8,128)(2,1)}, u32[]{:S(2)}) copy-start(bf16[2,4,64,2176]{3,2,1,0:T(8,128)(2,1)} %copy.47) | copy-start | bytes 6684676
  106.6 3.0 %copy-start.3 = (bf16[2,256,2176]{2,1,0:T(8,128)(2,1)S(1)}, bf16[2,256,2176]{2,1,0:T(8,128)(2,1)}, u32[]{:S(2)}) copy-start(bf16[2,256,2176]{2,1,0:T(8,128)(2,1)} %shard_map.29) | copy-start | bytes 6684676
  110.9 10.2 %collective-permute-start.6 = (f32[2,64,512]{2,1,0:T(8,128)S(1)}, f32[2,64,512]{2,1,0:T(8,128)S(1)}, u32[]{:S(2)}, u32[]{:S(2)}) collective-permute-start(f32[2,64,512]{2,1,0:T(8,128)S(1)} %get-tuple-element.50), channel_id=1, source_target_pairs={{0,64},{64,128},{128,192},{192,0},{1,65},{65,129},{129,193},{193,1... | collective-permute-start | bytes 786440 | tf_op jit(solution)/shard_map/ppermute | solution.py:132
  111.5 14.1 %collective-permute-start.7 = (f32[2,64,512]{2,1,0:T(8,128)S(1)}, f32[2,64,512]{2,1,0:T(8,128)S(1)}, u32[]{:S(2)}, u32[]{:S(2)}) collective-permute-start(f32[2,64,512]{2,1,0:T(8,128)S(1)} %get-tuple-element.51), channel_id=1, source_target_pairs={{0,128},{64,192},{128,0},{192,64},{1,129},{65,193},{129,1},{193,65... | collective-permute-start | bytes 786440 | tf_op jit(solution)/shard_map/ppermute | solution.py:132
  113.6 13.7 %collective-permute-start.8 = (f32[2,64,512]{2,1,0:T(8,128)S(1)}, f32[2,64,512]{2,1,0:T(8,128)S(1)}, u32[]{:S(2)}, u32[]{:S(2)}) collective-permute-start(f32[2,64,512]{2,1,0:T(8,128)S(1)} %select_bitcast_fusion), channel_id=1, source_target_pairs={{0,192},{64,0},{128,64},{192,128},{1,193},{65,1},{129,65},{193,129... | collective-permute-start | bytes 786440 | tf_op jit(solution)/shard_map/ppermute | solution.py:132

commit v18 on v17

--- a/solution.py
+++ b/solution.py
@@ -132,11 +132,9 @@
         total = total + lax.ppermute(blk, "node", [(i, (i + d) % nodes) for i in range(nodes)])
     total = total.reshape(rows, GROUPS, nodes, step).transpose(0, 2, 1, 3)
     total = total.reshape((rows,) + tuple(sizes) + (snaps // spaces,))
-    total = jnp.moveaxis(total, 3, 0)
-    total = lax.all_to_all(total, SPACE[2], 0, 0, tiled=True).sum(axis=0)
-    total = total.reshape(rows, sizes[0] * sizes[1], snaps // spaces)
+    total = total.reshape(rows, spaces, snaps // spaces)
     total = jnp.moveaxis(total, 1, 0)
-    total = lax.all_to_all(total, SPACE[:2], 0, 0, tiled=True).sum(axis=0)
+    total = lax.all_to_all(total, SPACE, 0, 0, tiled=True).sum(axis=0)
     out = total
 
     scale = jnp.float32(1.0 / math.sqrt(planes * spaces * NY * NZ))

time: 156 us -> 156 us (level)
    all_to_all x2 -> x1, blocking collectives: 24.8 us -> 24.4 us  [per_device(): total = lax.all_to_all(total, SPACE, 0, 0, tiled=True).sum(axis=0)]
where the time goes in v18:
time: 156 us; the launch traced here: 153 us
  waiting for transfers between devices  47.6 us (31%)
  starting transfers between devices  29.1 us (19%)
  local copies, waits for them, and re-layouts  26.3 us (17%)
  blocking collectives  24.4 us (16%)
  Pallas kernels  12.8 us (8%)
  matrix products  6.63 us (4%)
  other arithmetic  5.7 us (4%)
    all_to_all x2, waiting for transfers between devices, per_device(): lax.all_to_all(chunked(major, nodes), 'node', 1, 1, tiled=True)  32.7 us
    all_to_all x1, blocking collectives, per_device(): total = lax.all_to_all(total, SPACE, 0, 0, tiled=True).sum(axis=0)  24.4 us
    ppermute x3, waiting for transfers between devices, per_device(): lax.ppermute(blk, 'node', [(i, (i + d) % nodes) for i in range(nodes)])  12.9 us
    pallas_call x2, Pallas kernels, stencil(): pl.pallas_call(stencil_kernel, grid=(snaps // ROWS,), in_specs=[pl.BlockS...  12.8 us
    all_to_all x2, starting transfers between devices, per_device(): lax.all_to_all(chunked(major, nodes), 'node', 1, 1, tiled=True)  8.77 us
    ppermute x2, starting transfers between devices, per_device(): above = lax.ppermute(field[0], SPACE, down)  7.46 us
    dot_general x4, matrix products, per_device(): lax.dot_general(im, fd, dims, preferred_element_type=jnp.float32)  6.63 us
    slice x1, local copies, waits for them, and re-layouts, per_device(): major = jnp.transpose(snapshots[g * step:(g + 1) * step], (1, 0, 2))  5.04 us
  transfers between devices with their start and end apart: 11, of which 6 were waited for; matrix products, arithmetic and copies ran while one was open for 14% of the time, Pallas kernels for 4%

profile of v18, /device:TPU:8, one launch (start us, length us, event | category | flops | bytes accessed | tf_op | source)
XLA Modules:
  0.0 152.9 jit_solution(13348563817427335495)
XLA Ops:
  0.0 5.0 %fusion.25 = (bf16[64,2,8192]{2,1,0:T(2,128)(2,1)S(1)}, bf16[64,2,8192]{2,1,0:T(2,128)(2,1)S(1)}) fusion(bf16[128,2,8192]{2,1,0:T(2,128)(2,1)} %param.4), kind=kLoop, calls=%fused_computation.80 | loop fusion | bytes 8388608 | tf_op jit(solution)/shard_map/slice | solution.py:108
  5.1 2.7 %copy_bitcast_fusion = (bf16[2,64,8192]{2,1,0:T(8,128)(2,1)S(1)}, bf16[2,64,8192]{2,1,0:T(8,128)(2,1)S(1)}) fusion(bf16[64,2,8192]{2,1,0:T(2,128)(2,1)S(1)} %get-tuple-element.35, bf16[64,2,8192]{2,1,0:T(2,128)(2,1)S(1)} %get-tuple-element.34), kind=kLoop, calls=%fused_computation.2 | loop fusion | bytes 8388608 | tf_op jit(solution)/shard_map/transpose | solution.py:108
  7.7 0.1 fusion.29
  7.8 0.1 fusion.28
  8.0 0.1 maximum_bitcast_fusion
  8.1 0.1 maximum_bitcast_fusion.1
  8.2 0.9 copy-done.5
  9.1 0.1 fusion.1
  9.2 0.3 concatenate.155
  9.5 1.7 %pad_maximum_fusion = bf16[2,4,64,2176]{3,2,0,1:T(8,128)(2,1)} fusion(bf16[2,1,64,2176]{3,2,0,1:T(8,128)(2,1)S(1)} %bitcast.116, bf16[2,1,64,2176]{3,2,0,1:T(8,128)(2,1)S(1)} %maximum_bitcast_fusion.1, bf16[2,1,64,2176]{3,2,0,1:T(8,128)(2,1)S(1)} %maximum_bitcast_fusion, bf16[2,1,64,2176]{3,2,0,1:T(8,128)(2,1)S(1)} %get-tuple-element.67), kind=kLoop, calls=%fused_computation | loop fusion | flops 3342336 | bytes 4456448 | tf_op jit(solution)/shard_map/stack | solution.py:89
  11.2 4.3 %all-to-all-start = ((bf16[2,4,64,2176]{3,2,0,1:T(8,128)(2,1)}), bf16[2,4,64,2176]{3,2,0,1:T(8,128)(2,1)S(1)}, u32[]{:S(2)}, u32[]{:S(2)}) async-start(bf16[2,4,64,2176]{3,2,0,1:T(8,128)(2,1)} %pad_maximum_fusion), calls=%async_computation | async-start | bytes 4456448 | tf_op jit(solution)/shard_map/all_to_all | solution.py:109
  15.5 0.9 fusion.31
  16.4 1.9 %slice.246 = bf16[2,64,2048]{2,1,0:T(8,128)(2,1)} slice(bf16[2,64,8192]{2,1,0:T(8,128)(2,1)} %copy-done.5), slice={[0:2], [0:64], [6144:8192]} | slice | bytes 1048576 | tf_op jit(solution)/shard_map/slice | solution.py:88
  18.3 1.2 concatenate.175
  19.5 1.3 fusion.30
  20.8 0.1 maximum_bitcast_fusion.2
  20.9 0.1 maximum_bitcast_fusion.3
  21.0 1.7 %pad_maximum_fusion.1 = bf16[2,4,64,2176]{3,2,0,1:T(8,128)(2,1)} fusion(bf16[2,1,64,2176]{3,2,0,1:T(8,128)(2,1)S(1)} %bitcast.115, bf16[2,1,64,2176]{3,2,0,1:T(8,128)(2,1)S(1)} %maximum_bitcast_fusion.3, bf16[2,1,64,2176]{3,2,0,1:T(8,128)(2,1)S(1)} %maximum_bitcast_fusion.2, bf16[2,1,64,2176]{3,2,0,1:T(8,128)(2,1)S(1)} %get-tuple-element.68), kind=kLoop, calls=%fused_computation.1 | loop fusion | flops 3342336 | bytes 4456448 | tf_op jit(solution)/shard_map/stack | solution.py:89
  22.7 20.5 %all-to-all-done = bf16[2,4,64,2176]{3,2,0,1:T(8,128)(2,1)S(1)} async-done(((bf16[2,4,64,2176]{3,2,0,1:T(8,128)(2,1)}), bf16[2,4,64,2176]{3,2,0,1:T(8,128)(2,1)S(1)}, u32[]{:S(2)}, u32[]{:S(2)}) %all-to-all-start) | async-done | bytes 2228256 | tf_op jit(solution)/shard_map/all_to_all | solution.py:109
  43.2 4.5 %all-to-all-start.1 = ((bf16[2,4,64,2176]{3,2,0,1:T(8,128)(2,1)}), bf16[2,4,64,2176]{3,2,0,1:T(8,128)(2,1)}, u32[]{:S(2)}, u32[]{:S(2)}) async-start(bf16[2,4,64,2176]{3,2,0,1:T(8,128)(2,1)} %pad_maximum_fusion.1), calls=%async_computation.1 | async-start | bytes 4456448 | tf_op jit(solution)/shard_map/all_to_all | solution.py:109
  47.7 1.6 %copy.39 = bf16[2,4,64,2176]{3,2,1,0:T(8,128)(2,1)} copy(bf16[2,4,64,2176]{3,2,0,1:T(8,128)(2,1)S(1)} %all-to-all-done) | data formatting | bytes 4456448 | tf_op jit(solution)/shard_map/all_to_all | solution.py:109
  49.4 0.1 maximum_bitcast_fusion.4
  49.5 0.1 maximum_bitcast_fusion.5
  49.6 0.1 concatenate.159
  49.9 1.9 %collective-permute-start.2 = (bf16[2176]{0:T(1024)(128)(2,1)S(1)}, bf16[2176]{0:T(1024)(128)(2,1)S(1)}, u32[]{:S(2)}, u32[]{:S(2)}) collective-permute-start(bf16[2176]{0:T(1024)(128)(2,1)S(1)} %get-tuple-element.31), channel_id=1, source_target_pairs={{0,1},{1,2},{2,3},{3,4},{4,5},{5,6},{6,7},{7,8},{8,9},{9,10},{10,1... | collective-permute-start | bytes 13064 | tf_op jit(solution)/shard_map/ppermute | solution.py:117
  51.8 3.6 %collective-permute-start.3 = (bf16[2176]{0:T(1024)(128)(2,1)S(1)}, bf16[2176]{0:T(1024)(128)(2,1)S(1)}, u32[]{:S(2)}, u32[]{:S(2)}) collective-permute-start(bf16[2176]{0:T(1024)(128)(2,1)S(1)} %get-tuple-element.30), channel_id=1, source_target_pairs={{1,0},{2,1},{3,2},{4,3},{5,4},{6,5},{7,6},{8,7},{9,8},{10,9},{11,1... | collective-permute-start | bytes 13064 | tf_op jit(solution)/shard_map/ppermute | solution.py:118
  55.5 1.2 fusion.26
  56.7 1.9 %collective-permute-start = (bf16[256,2176]{1,0:T(8,128)(2,1)}, bf16[256,2176]{1,0:T(8,128)(2,1)}, u32[]{:S(2)}, u32[]{:S(2)}) collective-permute-start(bf16[256,2176]{1,0:T(8,128)(2,1)} %bitcast.6), channel_id=1, source_target_pairs={{0,1},{1,2},{2,3},{3,4},{4,5},{5,6},{6,7},{7,8},{8,9},{9,10},{10,1... | collective-permute-start | bytes 3342344 | tf_op jit(solution)/shard_map/ppermute | solution.py:110
  58.6 3.6 %collective-permute-start.1 = (bf16[256,2176]{1,0:T(8,128)(2,1)S(1)}, bf16[256,2176]{1,0:T(8,128)(2,1)}, u32[]{:S(2)}, u32[]{:S(2)}) collective-permute-start(bf16[256,2176]{1,0:T(8,128)(2,1)S(1)} %bitcast.118), channel_id=1, source_target_pairs={{1,0},{2,1},{3,2},{4,3},{5,4},{6,5},{7,6},{8,7},{9,8},{10,9},{11,1... | collective-permute-start | bytes 3342344 | tf_op jit(solution)/shard_map/ppermute | solution.py:111
  62.3 0.1 slice_bitcast_fusion.2
  62.4 0.1 slice_bitcast_fusion
  62.5 12.1 %all-to-all-done.1 = bf16[2,4,64,2176]{3,2,0,1:T(8,128)(2,1)} async-done(((bf16[2,4,64,2176]{3,2,0,1:T(8,128)(2,1)}), bf16[2,4,64,2176]{3,2,0,1:T(8,128)(2,1)}, u32[]{:S(2)}, u32[]{:S(2)}) %all-to-all-start.1) | async-done | bytes 2228256 | tf_op jit(solution)/shard_map/all_to_all | solution.py:109
  74.6 3.2 %fusion.27 = (bf16[1,4,64,2176]{3,2,1,0:T(8,128)(2,1)}, bf16[1,4,64,2176]{3,2,1,0:T(8,128)(2,1)}) fusion(bf16[2,4,64,2176]{3,2,0,1:T(8,128)(2,1)} %all-to-all-done.1), kind=kLoop, calls=%fused_computation.82 | loop fusion | bytes 4456448 | tf_op jit(solution)/shard_map/slice | solution.py:111
  77.8 1.9 %collective-permute-start.4 = (bf16[256,2176]{1,0:T(8,128)(2,1)}, bf16[256,2176]{1,0:T(8,128)(2,1)}, u32[]{:S(2)}, u32[]{:S(2)}) collective-permute-start(bf16[256,2176]{1,0:T(8,128)(2,1)} %bitcast.31), channel_id=1, source_target_pairs={{0,1},{1,2},{2,3},{3,4},{4,5},{5,6},{6,7},{7,8},{8,9},{9,10},{10,1... | collective-permute-start | bytes 3342344 | tf_op jit(solution)/shard_map/ppermute | solution.py:110
  79.7 0.1 select_dynamic-update-slice_fusion.1
  79.8 0.1 select_dynamic-update-slice_fusion
  79.9 0.1 constant_dynamic-update-slice_fusion.3
  80.0 0.1 constant_dynamic-update-slice_fusion.2
  80.1 3.2 %copy.45 = bf16[2,4,64,2176]{3,2,1,0:T(8,128)(2,1)} copy(bf16[2,4,64,2176]{3,2,0,1:T(8,128)(2,1)} %all-to-all-done.1) | data formatting | bytes 4456448 | tf_op jit(solution)/shard_map/all_to_all | solution.py:109
  83.3 3.8 %collective-permute-start.5 = (bf16[256,2176]{1,0:T(8,128)(2,1)}, bf16[256,2176]{1,0:T(8,128)(2,1)}, u32[]{:S(2)}, u32[]{:S(2)}) collective-permute-start(bf16[256,2176]{1,0:T(8,128)(2,1)} %bitcast.32), channel_id=1, source_target_pairs={{1,0},{2,1},{3,2},{4,3},{5,4},{6,5},{7,6},{8,7},{9,8},{10,9},{11,1... | collective-permute-start | bytes 3342344 | tf_op jit(solution)/shard_map/ppermute | solution.py:111
  87.2 0.1 add_dynamic-update-slice_fusion.coef_ref
  87.4 0.6 copy-done.6
  88.0 6.4 %shard_map.28 = bf16[2,256,2176]{2,1,0:T(8,128)(2,1)} custom-call(bf16[2,256,2176]{2,1,0:T(8,128)(2,1)} %bitcast.106, bf16[256,2176]{1,0:T(8,128)(2,1)} %collective-permute-done.below_ref, bf16[256,2176]{1,0:T(8,128)(2,1)} %collective-permute-done.1.above_ref, f32[7,2,2176]{2,1,0:T(2,128)} %copy-done.6), custom_call_target="tpu_custom_call" | custom-call | tf_op jit(solution)/shard_map/pallas_call | solution.py:52
  94.4 2.5 %convolution_bitcast_fusion.3 = f32[256,256]{0,1:T(8,128)S(1)} fusion(bf16[2,256,2176]{2,1,0:T(8,128)(2,1)} %shard_map.28, bf16[2,256,2176]{2,1,0:T(8,128)(2,1)S(1)} %bitcast.107), kind=kOutput, calls=%fused_computation.7 | convolution fusion | flops 570425344 | bytes 4718592 | tf_op jit(solution)/shard_map/dot_general | solution.py:125
  97.0 0.4 copy-done.4
  97.4 0.8 convolution_bitcast_fusion.2
  98.2 2.0 %collective-permute-done.5.above_ref = bf16[256,2176]{1,0:T(8,128)(2,1)} collective-permute-done((bf16[256,2176]{1,0:T(8,128)(2,1)}, bf16[256,2176]{1,0:T(8,128)(2,1)}, u32[]{:S(2)}, u32[]{:S(2)}) %collective-permute-start.5) | collective-permute-done | bytes 1114144 | tf_op jit(solution)/shard_map/ppermute | solution.py:111
  100.2 6.4 %shard_map.29 = bf16[2,256,2176]{2,1,0:T(8,128)(2,1)} custom-call(bf16[2,256,2176]{2,1,0:T(8,128)(2,1)} %bitcast.109, bf16[256,2176]{1,0:T(8,128)(2,1)} %collective-permute-done.4.below_ref, bf16[256,2176]{1,0:T(8,128)(2,1)} %collective-permute-done.5.above_ref, f32[7,2,2176]{2,1,0:T(2,128)} %copy-done.6), custom_call_target="tpu_custom_call" | custom-call | tf_op jit(solution)/shard_map/pallas_call | solution.py:52
  106.6 2.5 %convolution_bitcast_fusion.1 = f32[256,256]{0,1:T(8,128)S(1)} fusion(bf16[2,256,2176]{2,1,0:T(8,128)(2,1)} %shard_map.29, bf16[2,256,2176]{2,1,0:T(8,128)(2,1)S(1)} %bitcast.108), kind=kOutput, calls=%fused_computation.5 | convolution fusion | flops 570425344 | bytes 4718592 | tf_op jit(solution)/shard_map/dot_general | solution.py:125
  109.2 0.4 copy-done.3
  109.6 0.8 convolution_bitcast_fusion
  110.3 0.1 maximum_maximum_fusion
  110.5 0.3 copy.48
  110.9 0.6 collective-permute-start.6
  111.5 2.1 %collective-permute-start.7 = (f32[2,64,512]{2,1,0:T(8,128)S(1)}, f32[2,64,512]{2,1,0:T(8,128)S(1)}, u32[]{:S(2)}, u32[]{:S(2)}) collective-permute-start(f32[2,64,512]{2,1,0:T(8,128)S(1)} %get-tuple-element.51), channel_id=1, source_target_pairs={{0,128},{64,192},{128,0},{192,64},{1,129},{65,193},{129,1},{193,65... | collective-permute-start | bytes 786440 | tf_op jit(solution)/shard_map/ppermute | solution.py:132
  113.6 0.8 collective-permute-start.8
  114.4 6.7 %collective-permute-done.6 = f32[2,64,512]{2,1,0:T(8,128)S(1)} collective-permute-done((f32[2,64,512]{2,1,0:T(8,128)S(1)}, f32[2,64,512]{2,1,0:T(8,128)S(1)}, u32[]{:S(2)}, u32[]{:S(2)}) %collective-permute-start.6) | collective-permute-done | bytes 262176 | tf_op jit(solution)/shard_map/ppermute | solution.py:132
  121.1 4.5 %collective-permute-done.7 = f32[2,64,512]{2,1,0:T(8,128)S(1)} collective-permute-done((f32[2,64,512]{2,1,0:T(8,128)S(1)}, f32[2,64,512]{2,1,0:T(8,128)S(1)}, u32[]{:S(2)}, u32[]{:S(2)}) %collective-permute-start.7) | collective-permute-done | bytes 262176 | tf_op jit(solution)/shard_map/ppermute | solution.py:132
  125.6 1.7 %collective-permute-done.8 = f32[2,64,512]{2,1,0:T(8,128)S(1)} collective-permute-done((f32[2,64,512]{2,1,0:T(8,128)S(1)}, f32[2,64,512]{2,1,0:T(8,128)S(1)}, u32[]{:S(2)}, u32[]{:S(2)}) %collective-permute-start.8) | collective-permute-done | bytes 262176 | tf_op jit(solution)/shard_map/ppermute | solution.py:132
  127.3 0.1 fusion.7
  127.4 0.3 reshape.463
  127.7 0.2 copy.52
  127.9 24.4 %all_to_all.15 = f32[64,128,8]{1,2,0:T(8,128)S(1)} all-to-all(f32[64,128,8]{1,2,0:T(8,128)S(1)} %bitcast.119), channel_id=1, replica_groups=mesh['node'=4,'z'=8,'y'=4,'core'=2] {'z','y','core'}, dimensions={0} | all-to-all | bytes 524288 | tf_op jit(solution)/shard_map/all_to_all | solution.py:137
  152.3 0.6 broadcast_multiply_fusion
  (39 shorter events, 0.7 us)
Async XLA Ops:
  7.7 1.4 copy-start.5
  7.9 1.1 copy-start.8
  11.2 32.0 %all-to-all-start = ((bf16[2,4,64,2176]{3,2,0,1:T(8,128)(2,1)}), bf16[2,4,64,2176]{3,2,0,1:T(8,128)(2,1)S(1)}, u32[]{:S(2)}, u32[]{:S(2)}) async-start(bf16[2,4,64,2176]{3,2,0,1:T(8,128)(2,1)} %pad_maximum_fusion), calls=%async_computation | async-start | bytes 4456448 | tf_op jit(solution)/shard_map/all_to_all | solution.py:109
  43.2 31.4 %all-to-all-start.1 = ((bf16[2,4,64,2176]{3,2,0,1:T(8,128)(2,1)}), bf16[2,4,64,2176]{3,2,0,1:T(8,128)(2,1)}, u32[]{:S(2)}, u32[]{:S(2)}) async-start(bf16[2,4,64,2176]{3,2,0,1:T(8,128)(2,1)} %pad_maximum_fusion.1), calls=%async_computation.1 | async-start | bytes 4456448 | tf_op jit(solution)/shard_map/all_to_all | solution.py:109
  47.7 1.6 %copy-start.7 = (bf16[2,8192]{1,0:T(2,128)(2,1)S(1)}, bf16[2,8192]{1,0:T(2,128)(2,1)}, u32[]{:S(2)}) copy-start(bf16[2,8192]{1,0:T(2,128)(2,1)} %param.5) | copy-start | bytes 98308
  49.9 33.4 %collective-permute-start.2 = (bf16[2176]{0:T(1024)(128)(2,1)S(1)}, bf16[2176]{0:T(1024)(128)(2,1)S(1)}, u32[]{:S(2)}, u32[]{:S(2)}) collective-permute-start(bf16[2176]{0:T(1024)(128)(2,1)S(1)} %get-tuple-element.31), channel_id=1, source_target_pairs={{0,1},{1,2},{2,3},{3,4},{4,5},{5,6},{6,7},{7,8},{8,9},{9,10},{10,1... | collective-permute-start | bytes 13064 | tf_op jit(solution)/shard_map/ppermute | solution.py:117
  51.8 35.3 %collective-permute-start.3 = (bf16[2176]{0:T(1024)(128)(2,1)S(1)}, bf16[2176]{0:T(1024)(128)(2,1)S(1)}, u32[]{:S(2)}, u32[]{:S(2)}) collective-permute-start(bf16[2176]{0:T(1024)(128)(2,1)S(1)} %get-tuple-element.30), channel_id=1, source_target_pairs={{1,0},{2,1},{3,2},{4,3},{5,4},{6,5},{7,6},{8,7},{9,8},{10,9},{11,1... | collective-permute-start | bytes 13064 | tf_op jit(solution)/shard_map/ppermute | solution.py:118
  56.7 30.7 %collective-permute-start = (bf16[256,2176]{1,0:T(8,128)(2,1)}, bf16[256,2176]{1,0:T(8,128)(2,1)}, u32[]{:S(2)}, u32[]{:S(2)}) collective-permute-start(bf16[256,2176]{1,0:T(8,128)(2,1)} %bitcast.6), channel_id=1, source_target_pairs={{0,1},{1,2},{2,3},{3,4},{4,5},{5,6},{6,7},{7,8},{8,9},{9,10},{10,1... | collective-permute-start | bytes 3342344 | tf_op jit(solution)/shard_map/ppermute | solution.py:110
  58.6 28.8 %collective-permute-start.1 = (bf16[256,2176]{1,0:T(8,128)(2,1)S(1)}, bf16[256,2176]{1,0:T(8,128)(2,1)}, u32[]{:S(2)}, u32[]{:S(2)}) collective-permute-start(bf16[256,2176]{1,0:T(8,128)(2,1)S(1)} %bitcast.118), channel_id=1, source_target_pairs={{1,0},{2,1},{3,2},{4,3},{5,4},{6,5},{7,6},{8,7},{9,8},{10,9},{11,1... | collective-permute-start | bytes 3342344 | tf_op jit(solution)/shard_map/ppermute | solution.py:111
  77.8 20.4 %collective-permute-start.4 = (bf16[256,2176]{1,0:T(8,128)(2,1)}, bf16[256,2176]{1,0:T(8,128)(2,1)}, u32[]{:S(2)}, u32[]{:S(2)}) collective-permute-start(bf16[256,2176]{1,0:T(8,128)(2,1)} %bitcast.31), channel_id=1, source_target_pairs={{0,1},{1,2},{2,3},{3,4},{4,5},{5,6},{6,7},{7,8},{8,9},{9,10},{10,1... | collective-permute-start | bytes 3342344 | tf_op jit(solution)/shard_map/ppermute | solution.py:110
  83.3 17.0 %collective-permute-start.5 = (bf16[256,2176]{1,0:T(8,128)(2,1)}, bf16[256,2176]{1,0:T(8,128)(2,1)}, u32[]{:S(2)}, u32[]{:S(2)}) collective-permute-start(bf16[256,2176]{1,0:T(8,128)(2,1)} %bitcast.32), channel_id=1, source_target_pairs={{1,0},{2,1},{3,2},{4,3},{5,4},{6,5},{7,6},{8,7},{9,8},{10,9},{11,1... | collective-permute-start | bytes 3342344 | tf_op jit(solution)/shard_map/ppermute | solution.py:111
  87.3 0.7 copy-start.6
  87.3 7.1 %copy-start = (bf16[2,4,64,2176]{3,2,1,0:T(8,128)(2,1)S(1)}, bf16[2,4,64,2176]{3,2,1,0:T(8,128)(2,1)}, u32[]{:S(2)}) copy-start(bf16[2,4,64,2176]{3,2,1,0:T(8,128)(2,1)} %copy.39) | copy-start | bytes 6684676
  94.4 2.6 %copy-start.1 = (bf16[2,4,64,2176]{3,2,1,0:T(8,128)(2,1)S(1)}, bf16[2,4,64,2176]{3,2,1,0:T(8,128)(2,1)}, u32[]{:S(2)}) copy-start(bf16[2,4,64,2176]{3,2,1,0:T(8,128)(2,1)} %copy.45) | copy-start | bytes 6684676
  94.4 3.0 %copy-start.4 = (bf16[2,256,2176]{2,1,0:T(8,128)(2,1)S(1)}, bf16[2,256,2176]{2,1,0:T(8,128)(2,1)}, u32[]{:S(2)}) copy-start(bf16[2,256,2176]{2,1,0:T(8,128)(2,1)} %shard_map.28) | copy-start | bytes 6684676
  106.6 2.6 %copy-start.2 = (bf16[2,4,64,2176]{3,2,1,0:T(8,128)(2,1)S(1)}, bf16[2,4,64,2176]{3,2,1,0:T(8,128)(2,1)}, u32[]{:S(2)}) copy-start(bf16[2,4,64,2176]{3,2,1,0:T(8,128)(2,1)} %copy.45) | copy-start | bytes 6684676
  106.6 3.0 %copy-start.3 = (bf16[2,256,2176]{2,1,0:T(8,128)(2,1)S(1)}, bf16[2,256,2176]{2,1,0:T(8,128)(2,1)}, u32[]{:S(2)}) copy-start(bf16[2,256,2176]{2,1,0:T(8,128)(2,1)} %shard_map.29) | copy-start | bytes 6684676
  110.9 10.2 %collective-permute-start.6 = (f32[2,64,512]{2,1,0:T(8,128)S(1)}, f32[2,64,512]{2,1,0:T(8,128)S(1)}, u32[]{:S(2)}, u32[]{:S(2)}) collective-permute-start(f32[2,64,512]{2,1,0:T(8,128)S(1)} %get-tuple-element.50), channel_id=1, source_target_pairs={{0,64},{64,128},{128,192},{192,0},{1,65},{65,129},{129,193},{193,1... | collective-permute-start | bytes 786440 | tf_op jit(solution)/shard_map/ppermute | solution.py:132
  111.5 14.1 %collective-permute-start.7 = (f32[2,64,512]{2,1,0:T(8,128)S(1)}, f32[2,64,512]{2,1,0:T(8,128)S(1)}, u32[]{:S(2)}, u32[]{:S(2)}) collective-permute-start(f32[2,64,512]{2,1,0:T(8,128)S(1)} %get-tuple-element.51), channel_id=1, source_target_pairs={{0,128},{64,192},{128,0},{192,64},{1,129},{65,193},{129,1},{193,65... | collective-permute-start | bytes 786440 | tf_op jit(solution)/shard_map/ppermute | solution.py:132
  113.6 13.7 %collective-permute-start.8 = (f32[2,64,512]{2,1,0:T(8,128)S(1)}, f32[2,64,512]{2,1,0:T(8,128)S(1)}, u32[]{:S(2)}, u32[]{:S(2)}) collective-permute-start(f32[2,64,512]{2,1,0:T(8,128)S(1)} %select_bitcast_fusion), channel_id=1, source_target_pairs={{0,192},{64,0},{128,64},{192,128},{1,193},{65,1},{129,65},{193,129... | collective-permute-start | bytes 786440 | tf_op jit(solution)/shard_map/ppermute | solution.py:132

commit v19 on v17

--- a/solution.py
+++ b/solution.py
@@ -125,15 +125,10 @@
             lax.dot_general(im, fd, dims, preferred_element_type=jnp.float32)
             for fd in fields], axis=1)
         for im in images], axis=0)
-    part = part.reshape(GROUPS, nodes, step, snaps)
-    total = jnp.take(part, me, axis=1)
-    for d in range(1, nodes):
-        blk = jnp.take(part, (me + d) % nodes, axis=1)
-        total = total + lax.ppermute(blk, "node", [(i, (i + d) % nodes) for i in range(nodes)])
-    total = total.reshape(rows, GROUPS, nodes, step).transpose(0, 2, 1, 3)
-    total = total.reshape((rows,) + tuple(sizes) + (snaps // spaces,))
-    total = jnp.moveaxis(total, 3, 0)
-    total = lax.all_to_all(total, SPACE[2], 0, 0, tiled=True).sum(axis=0)
+    part = part.reshape(GROUPS, nodes, step, GROUPS, nodes, step).transpose(1, 0, 2, 4, 3, 5)
+    part = part.reshape((nodes, rows) + tuple(sizes) + (snaps // spaces,))
+    part = jnp.moveaxis(part, 4, 1).reshape(nodes * sizes[2], rows, -1)
+    total = lax.all_to_all(part, ("node", SPACE[2]), 0, 0, tiled=True).sum(axis=0)
     total = total.reshape(rows, sizes[0] * sizes[1], snaps // spaces)
     total = jnp.moveaxis(total, 1, 0)
     total = lax.all_to_all(total, SPACE[:2], 0, 0, tiled=True).sum(axis=0)

time: 156 us -> 161 us (1.032)
  blocking collectives: 24.8 us -> 41.9 us
  waiting for transfers between devices: 47.6 us -> 32.9 us
  local copies, waits for them, and re-layouts: 26.4 us -> 34 us
  starting transfers between devices: 29.1 us -> 24.4 us
    all_to_all x1, blocking collectives: 3.94 us -> 19.7 us  [per_device(): lax.all_to_all(part, ('node', SPACE[2]), 0, 0, tiled=True).sum(axis=0)]
    ppermute x3 -> x0, waiting for transfers between devices: 12.9 us -> none  [per_device(): lax.ppermute(blk, 'node', [(i, (i + d) % nodes) for i in range(nodes)])]
    reshape x1 -> x3, local copies, waits for them, and re-layouts: 0.28 us -> 6.09 us  [the longest x2 3.5 us: per_device(): part.reshape(GROUPS, nodes, step, GROUPS, nodes, step)]
    ppermute x3 -> x0, starting transfers between devices: 3.49 us -> none  [per_device(): lax.ppermute(blk, 'node', [(i, (i + d) % nodes) for i in range(nodes)])]
    ppermute x2, waiting for transfers between devices: 2.01 us -> 0.01 us  [per_device(): above = lax.ppermute(field[0], SPACE, down)]
    ppermute x1, starting transfers between devices: 3.64 us -> 1.91 us  [per_device(): kap_above = lax.ppermute(kap_chunk[0], SPACE, down)]
  transfers between devices with their start and end apart: 11 -> 8, of which waited for: 6 -> 2; matrix products, arithmetic and copies ran while one was open for 14% -> 15% of each run, Pallas kernels for 4% -> 4%
where the time goes in v19:
time: 161 us; the launch traced here: 160 us
  blocking collectives  41.9 us (26%)
  local copies, waits for them, and re-layouts  34 us (21%)
  waiting for transfers between devices  32.9 us (20%)
  starting transfers between devices  24.4 us (15%)
  Pallas kernels  12.9 us (8%)
  matrix products  8.02 us (5%)
  other arithmetic  5.51 us (3%)
    all_to_all x2, waiting for transfers between devices, per_device(): lax.all_to_all(chunked(major, nodes), 'node', 1, 1, tiled=True)  32.8 us
    all_to_all x1, blocking collectives, per_device(): total = lax.all_to_all(total, SPACE[:2], 0, 0, tiled=True).sum(axis=0)  22.1 us
    all_to_all x1, blocking collectives, per_device(): lax.all_to_all(part, ('node', SPACE[2]), 0, 0, tiled=True).sum(axis=0)  19.7 us
    pallas_call x2, Pallas kernels, stencil(): pl.pallas_call(stencil_kernel, grid=(snaps // ROWS,), in_specs=[pl.BlockS...  12.9 us
    all_to_all x2, starting transfers between devices, per_device(): lax.all_to_all(chunked(major, nodes), 'node', 1, 1, tiled=True)  8.76 us
    dot_general x4, matrix products, per_device(): lax.dot_general(im, fd, dims, preferred_element_type=jnp.float32)  8.02 us
    ppermute x2, starting transfers between devices, per_device(): above = lax.ppermute(field[0], SPACE, down)  6.27 us
    slice x1, local copies, waits for them, and re-layouts, per_device(): major = jnp.transpose(snapshots[g * step:(g + 1) * step], (1, 0, 2))  5.04 us
  transfers between devices with their start and end apart: 8, of which 2 were waited for; matrix products, arithmetic and copies ran while one was open for 15% of the time, Pallas kernels for 4%

profile of v19, /device:TPU:8, one launch (start us, length us, event | category | flops | bytes accessed | tf_op | source)
XLA Modules:
  0.0 159.9 jit_solution(10504557256106467716)
XLA Ops:
  0.0 5.0 %fusion.19 = (bf16[64,2,8192]{2,1,0:T(2,128)(2,1)S(1)}, bf16[64,2,8192]{2,1,0:T(2,128)(2,1)S(1)}) fusion(bf16[128,2,8192]{2,1,0:T(2,128)(2,1)} %param.2), kind=kLoop, calls=%fused_computation.71 | loop fusion | bytes 8388608 | tf_op jit(solution)/shard_map/slice | solution.py:108
  5.1 2.7 %copy_bitcast_fusion = (bf16[2,64,8192]{2,1,0:T(8,128)(2,1)S(1)}, bf16[2,64,8192]{2,1,0:T(8,128)(2,1)S(1)}) fusion(bf16[64,2,8192]{2,1,0:T(2,128)(2,1)S(1)} %get-tuple-element.23, bf16[64,2,8192]{2,1,0:T(2,128)(2,1)S(1)} %get-tuple-element.22), kind=kLoop, calls=%fused_computation.2 | loop fusion | bytes 8388608 | tf_op jit(solution)/shard_map/transpose | solution.py:108
  7.8 0.1 fusion.23
  7.9 0.1 fusion.22
  8.0 0.5 copy-done.8
  8.5 0.1 fusion.1
  8.6 0.5 copy-done.4
  9.1 0.1 maximum_bitcast_fusion
  9.2 0.1 maximum_bitcast_fusion.1
  9.3 0.3 concatenate.155
  9.5 1.7 %pad_maximum_fusion = bf16[2,4,64,2176]{3,2,0,1:T(8,128)(2,1)} fusion(bf16[2,1,64,2176]{3,2,0,1:T(8,128)(2,1)S(1)} %bitcast.91, bf16[2,1,64,2176]{3,2,0,1:T(8,128)(2,1)S(1)} %maximum_bitcast_fusion.1, bf16[2,1,64,2176]{3,2,0,1:T(8,128)(2,1)S(1)} %maximum_bitcast_fusion, bf16[2,1,64,2176]{3,2,0,1:T(8,128)(2,1)S(1)} %get-tuple-element.53), kind=kLoop, calls=%fused_computation | loop fusion | flops 3342336 | bytes 4456448 | tf_op jit(solution)/shard_map/stack | solution.py:89
  11.2 4.3 %all-to-all-start = ((bf16[2,4,64,2176]{3,2,0,1:T(8,128)(2,1)}), bf16[2,4,64,2176]{3,2,0,1:T(8,128)(2,1)S(1)}, u32[]{:S(2)}, u32[]{:S(2)}) async-start(bf16[2,4,64,2176]{3,2,0,1:T(8,128)(2,1)} %pad_maximum_fusion), calls=%async_computation | async-start | bytes 4456448 | tf_op jit(solution)/shard_map/all_to_all | solution.py:109
  15.5 0.9 fusion.25
  16.4 1.9 %slice.235 = bf16[2,64,2048]{2,1,0:T(8,128)(2,1)} slice(bf16[2,64,8192]{2,1,0:T(8,128)(2,1)} %copy-done.4), slice={[0:2], [0:64], [6144:8192]} | slice | bytes 1048576 | tf_op jit(solution)/shard_map/slice | solution.py:88
  18.4 1.2 concatenate.175
  19.5 1.3 fusion.24
  20.8 0.1 maximum_bitcast_fusion.2
  20.9 0.1 maximum_bitcast_fusion.3
  21.0 1.7 %pad_maximum_fusion.1 = bf16[2,4,64,2176]{3,2,0,1:T(8,128)(2,1)} fusion(bf16[2,1,64,2176]{3,2,0,1:T(8,128)(2,1)S(1)} %bitcast.90, bf16[2,1,64,2176]{3,2,0,1:T(8,128)(2,1)S(1)} %maximum_bitcast_fusion.3, bf16[2,1,64,2176]{3,2,0,1:T(8,128)(2,1)S(1)} %maximum_bitcast_fusion.2, bf16[2,1,64,2176]{3,2,0,1:T(8,128)(2,1)S(1)} %get-tuple-element.54), kind=kLoop, calls=%fused_computation.1 | loop fusion | flops 3342336 | bytes 4456448 | tf_op jit(solution)/shard_map/stack | solution.py:89
  22.7 20.6 %all-to-all-done = bf16[2,4,64,2176]{3,2,0,1:T(8,128)(2,1)S(1)} async-done(((bf16[2,4,64,2176]{3,2,0,1:T(8,128)(2,1)}), bf16[2,4,64,2176]{3,2,0,1:T(8,128)(2,1)S(1)}, u32[]{:S(2)}, u32[]{:S(2)}) %all-to-all-start) | async-done | bytes 2228256 | tf_op jit(solution)/shard_map/all_to_all | solution.py:109
  43.3 4.5 %all-to-all-start.1 = ((bf16[2,4,64,2176]{3,2,0,1:T(8,128)(2,1)}), bf16[2,4,64,2176]{3,2,0,1:T(8,128)(2,1)}, u32[]{:S(2)}, u32[]{:S(2)}) async-start(bf16[2,4,64,2176]{3,2,0,1:T(8,128)(2,1)} %pad_maximum_fusion.1), calls=%async_computation.1 | async-start | bytes 4456448 | tf_op jit(solution)/shard_map/all_to_all | solution.py:109
  47.8 1.6 copy.30
  49.3 0.1 fusion.27
  49.5 0.1 maximum_bitcast_fusion.4
  49.6 0.1 maximum_bitcast_fusion.5
  49.6 0.1 concatenate.159
  49.8 0.7 slice_reduce_fusion
  50.5 0.6 slice_bitcast_fusion.6
  51.0 1.9 %collective-permute-start.3 = (bf16[2176]{0:T(1024)(128)(2,1)}, bf16[2176]{0:T(1024)(128)(2,1)}, u32[]{:S(2)}, u32[]{:S(2)}) collective-permute-start(bf16[2176]{0:T(1024)(128)(2,1)} %get-tuple-element.18), channel_id=1, source_target_pairs={{1,0},{2,1},{3,2},{4,3},{5,4},{6,5},{7,6},{8,7},{9,8},{10,9},{11,1... | collective-permute-start | bytes 13064 | tf_op jit(solution)/shard_map/ppermute | solution.py:118
  53.0 2.4 %collective-permute-start.2 = (bf16[2176]{0:T(1024)(128)(2,1)}, bf16[2176]{0:T(1024)(128)(2,1)}, u32[]{:S(2)}, u32[]{:S(2)}) collective-permute-start(bf16[2176]{0:T(1024)(128)(2,1)} %get-tuple-element.19), channel_id=1, source_target_pairs={{0,1},{1,2},{2,3},{3,4},{4,5},{5,6},{6,7},{7,8},{8,9},{9,10},{10,1... | collective-permute-start | bytes 13064 | tf_op jit(solution)/shard_map/ppermute | solution.py:117
  55.4 1.2 fusion.20
  56.5 3.1 %collective-permute-start = (bf16[256,2176]{1,0:T(8,128)(2,1)}, bf16[256,2176]{1,0:T(8,128)(2,1)}, u32[]{:S(2)}, u32[]{:S(2)}) collective-permute-start(bf16[256,2176]{1,0:T(8,128)(2,1)} %bitcast.6), channel_id=1, source_target_pairs={{0,1},{1,2},{2,3},{3,4},{4,5},{5,6},{6,7},{7,8},{8,9},{9,10},{10,1... | collective-permute-start | bytes 3342344 | tf_op jit(solution)/shard_map/ppermute | solution.py:110
  59.6 2.5 %collective-permute-start.1 = (bf16[256,2176]{1,0:T(8,128)(2,1)S(1)}, bf16[256,2176]{1,0:T(8,128)(2,1)}, u32[]{:S(2)}, u32[]{:S(2)}) collective-permute-start(bf16[256,2176]{1,0:T(8,128)(2,1)S(1)} %bitcast.92), channel_id=1, source_target_pairs={{1,0},{2,1},{3,2},{4,3},{5,4},{6,5},{7,6},{8,7},{9,8},{10,9},{11,1... | collective-permute-start | bytes 3342344 | tf_op jit(solution)/shard_map/ppermute | solution.py:111
  62.2 0.1 slice_bitcast_fusion.2
  62.3 0.1 slice_bitcast_fusion
  62.4 12.3 %all-to-all-done.1 = bf16[2,4,64,2176]{3,2,0,1:T(8,128)(2,1)} async-done(((bf16[2,4,64,2176]{3,2,0,1:T(8,128)(2,1)}), bf16[2,4,64,2176]{3,2,0,1:T(8,128)(2,1)}, u32[]{:S(2)}, u32[]{:S(2)}) %all-to-all-start.1) | async-done | bytes 2228256 | tf_op jit(solution)/shard_map/all_to_all | solution.py:109
  74.6 3.2 %fusion.21 = (bf16[1,4,64,2176]{3,2,1,0:T(8,128)(2,1)}, bf16[1,4,64,2176]{3,2,1,0:T(8,128)(2,1)}) fusion(bf16[2,4,64,2176]{3,2,0,1:T(8,128)(2,1)} %all-to-all-done.1), kind=kLoop, calls=%fused_computation.73 | loop fusion | bytes 4456448 | tf_op jit(solution)/shard_map/slice | solution.py:111
  77.8 1.9 %collective-permute-start.4 = (bf16[256,2176]{1,0:T(8,128)(2,1)}, bf16[256,2176]{1,0:T(8,128)(2,1)}, u32[]{:S(2)}, u32[]{:S(2)}) collective-permute-start(bf16[256,2176]{1,0:T(8,128)(2,1)} %bitcast.31), channel_id=1, source_target_pairs={{0,1},{1,2},{2,3},{3,4},{4,5},{5,6},{6,7},{7,8},{8,9},{9,10},{10,1... | collective-permute-start | bytes 3342344 | tf_op jit(solution)/shard_map/ppermute | solution.py:110
  79.7 0.1 select_dynamic-update-slice_fusion.1
  79.8 0.1 select_dynamic-update-slice_fusion
  79.9 0.1 constant_dynamic-update-slice_fusion.3
  80.0 0.1 constant_dynamic-update-slice_fusion.2
  80.1 3.2 %copy.36 = bf16[2,4,64,2176]{3,2,1,0:T(8,128)(2,1)} copy(bf16[2,4,64,2176]{3,2,0,1:T(8,128)(2,1)} %all-to-all-done.1) | data formatting | bytes 4456448 | tf_op jit(solution)/shard_map/all_to_all | solution.py:109
  83.3 3.8 %collective-permute-start.5 = (bf16[256,2176]{1,0:T(8,128)(2,1)}, bf16[256,2176]{1,0:T(8,128)(2,1)}, u32[]{:S(2)}, u32[]{:S(2)}) collective-permute-start(bf16[256,2176]{1,0:T(8,128)(2,1)} %bitcast.32), channel_id=1, source_target_pairs={{1,0},{2,1},{3,2},{4,3},{5,4},{6,5},{7,6},{8,7},{9,8},{10,9},{11,1... | collective-permute-start | bytes 3342344 | tf_op jit(solution)/shard_map/ppermute | solution.py:111
  87.1 0.7 reshape.502
  87.9 0.7 reshape.503
  88.6 0.1 add_dynamic-update-slice_fusion.coef_ref
  88.8 0.6 copy-done.6
  89.4 6.5 %shard_map.28 = bf16[2,256,2176]{2,1,0:T(8,128)(2,1)} custom-call(bf16[2,256,2176]{2,1,0:T(8,128)(2,1)} %bitcast.81, bf16[256,2176]{1,0:T(8,128)(2,1)} %collective-permute-done.below_ref, bf16[256,2176]{1,0:T(8,128)(2,1)} %collective-permute-done.1.above_ref, f32[7,2,2176]{2,1,0:T(2,128)} %copy-done.6), custom_call_target="tpu_custom_call" | custom-call | tf_op jit(solution)/shard_map/pallas_call | solution.py:52
  95.9 2.5 %convolution_bitcast_fusion.3 = f32[256,256]{0,1:T(8,128)S(1)} fusion(bf16[2,256,2176]{2,1,0:T(8,128)(2,1)} %shard_map.28, bf16[2,256,2176]{2,1,0:T(8,128)(2,1)S(1)} %bitcast.82), kind=kOutput, calls=%fused_computation.8 | convolution fusion | flops 570425344 | bytes 4718592 | tf_op jit(solution)/shard_map/dot_general | solution.py:125
  98.4 0.4 copy-done.3
  98.8 1.5 convolution_bitcast_fusion.2
  100.3 6.4 %shard_map.29 = bf16[2,256,2176]{2,1,0:T(8,128)(2,1)} custom-call(bf16[2,256,2176]{2,1,0:T(8,128)(2,1)} %bitcast.84, bf16[256,2176]{1,0:T(8,128)(2,1)} %collective-permute-done.4.below_ref, bf16[256,2176]{1,0:T(8,128)(2,1)} %collective-permute-done.5.above_ref, f32[7,2,2176]{2,1,0:T(2,128)} %copy-done.6), custom_call_target="tpu_custom_call" | custom-call | tf_op jit(solution)/shard_map/pallas_call | solution.py:52
  106.7 3.2 %convolution_bitcast_fusion = f32[256,256]{0,1:T(8,128)S(1)} fusion(bf16[2,256,2176]{2,1,0:T(8,128)(2,1)} %shard_map.29, bf16[2,256,2176]{2,1,0:T(8,128)(2,1)} %bitcast.85), kind=kOutput, calls=%fused_computation.5 | convolution fusion | flops 570425344 | bytes 4718592 | tf_op jit(solution)/shard_map/dot_general | solution.py:125
  110.0 0.8 convolution_bitcast_fusion.1
  110.7 0.2 copy-done.5
  110.9 0.1 maximum_maximum_fusion
  111.0 1.1 reshape.467
  112.1 2.4 %copy.50 = f32[2,4,64,2,4,64]{2,0,5,3,4,1:T(2,128)} copy(f32[2,4,64,2,4,64]{2,1,0,5,4,3:T(4,128)S(1)} %reshape.467) | data formatting | bytes 2097152 | tf_op jit(solution)/shard_map/reshape | solution.py:128
  114.5 2.6 %reshape.468 = f32[4,128,8,4,2,8]{1,5,4,3,2,0:T(8,128)S(1)} reshape(f32[4,2,64,4,2,64]{2,1,5,4,3,0:T(2,128)} %bitcast.87) | data formatting | bytes 2097152 | tf_op jit(solution)/shard_map/reshape | solution.py:129
  117.1 0.1 copy.40
  117.3 19.7 %all_to_all.20 = f32[8,128,256]{1,2,0:T(8,128)S(1)} all-to-all(f32[8,128,256]{1,2,0:T(8,128)S(1)} %bitcast.89), channel_id=1, replica_groups=mesh['node'=4,'z'=8,'y'=4,'core'=2] {'node','core'}, dimensions={0} | all-to-all | bytes 2097152 | tf_op jit(solution)/shard_map/all_to_all | solution.py:131
  137.1 22.1 %all_to_all.21 = f32[32,128,8]{1,2,0:T(8,128)S(1)} all-to-all(f32[32,128,8]{1,2,0:T(8,128)S(1)} %bitcast.93), channel_id=1, replica_groups=mesh['node'=4,'z'=8,'y'=4,'core'=2] {'z','y'}, dimensions={0} | all-to-all | bytes 262144 | tf_op jit(solution)/shard_map/all_to_all | solution.py:134
  159.3 0.6 broadcast_multiply_fusion
  (35 shorter events, 0.5 us)
Async XLA Ops:
  7.7 1.3 copy-start.4
  7.7 0.7 copy-start.8
  11.2 32.0 %all-to-all-start = ((bf16[2,4,64,2176]{3,2,0,1:T(8,128)(2,1)}), bf16[2,4,64,2176]{3,2,0,1:T(8,128)(2,1)S(1)}, u32[]{:S(2)}, u32[]{:S(2)}) async-start(bf16[2,4,64,2176]{3,2,0,1:T(8,128)(2,1)} %pad_maximum_fusion), calls=%async_computation | async-start | bytes 4456448 | tf_op jit(solution)/shard_map/all_to_all | solution.py:109
  43.3 31.4 %all-to-all-start.1 = ((bf16[2,4,64,2176]{3,2,0,1:T(8,128)(2,1)}), bf16[2,4,64,2176]{3,2,0,1:T(8,128)(2,1)}, u32[]{:S(2)}, u32[]{:S(2)}) async-start(bf16[2,4,64,2176]{3,2,0,1:T(8,128)(2,1)} %pad_maximum_fusion.1), calls=%async_computation.1 | async-start | bytes 4456448 | tf_op jit(solution)/shard_map/all_to_all | solution.py:109
  47.7 1.6 copy-start.7
  51.0 36.8 %collective-permute-start.3 = (bf16[2176]{0:T(1024)(128)(2,1)}, bf16[2176]{0:T(1024)(128)(2,1)}, u32[]{:S(2)}, u32[]{:S(2)}) collective-permute-start(bf16[2176]{0:T(1024)(128)(2,1)} %get-tuple-element.18), channel_id=1, source_target_pairs={{1,0},{2,1},{3,2},{4,3},{5,4},{6,5},{7,6},{8,7},{9,8},{10,9},{11,1... | collective-permute-start | bytes 13064 | tf_op jit(solution)/shard_map/ppermute | solution.py:118
  53.0 30.4 %collective-permute-start.2 = (bf16[2176]{0:T(1024)(128)(2,1)}, bf16[2176]{0:T(1024)(128)(2,1)}, u32[]{:S(2)}, u32[]{:S(2)}) collective-permute-start(bf16[2176]{0:T(1024)(128)(2,1)} %get-tuple-element.19), channel_id=1, source_target_pairs={{0,1},{1,2},{2,3},{3,4},{4,5},{5,6},{6,7},{7,8},{8,9},{9,10},{10,1... | collective-permute-start | bytes 13064 | tf_op jit(solution)/shard_map/ppermute | solution.py:117
  56.5 32.2 %collective-permute-start = (bf16[256,2176]{1,0:T(8,128)(2,1)}, bf16[256,2176]{1,0:T(8,128)(2,1)}, u32[]{:S(2)}, u32[]{:S(2)}) collective-permute-start(bf16[256,2176]{1,0:T(8,128)(2,1)} %bitcast.6), channel_id=1, source_target_pairs={{0,1},{1,2},{2,3},{3,4},{4,5},{5,6},{6,7},{7,8},{8,9},{9,10},{10,1... | collective-permute-start | bytes 3342344 | tf_op jit(solution)/shard_map/ppermute | solution.py:110
  59.6 29.1 %collective-permute-start.1 = (bf16[256,2176]{1,0:T(8,128)(2,1)S(1)}, bf16[256,2176]{1,0:T(8,128)(2,1)}, u32[]{:S(2)}, u32[]{:S(2)}) collective-permute-start(bf16[256,2176]{1,0:T(8,128)(2,1)S(1)} %bitcast.92), channel_id=1, source_target_pairs={{1,0},{2,1},{3,2},{4,3},{5,4},{6,5},{7,6},{8,7},{9,8},{10,9},{11,1... | collective-permute-start | bytes 3342344 | tf_op jit(solution)/shard_map/ppermute | solution.py:111
  62.4 17.4 %copy-start.9 = (f32[1,2,1]{2,1,0:T(2,128)S(1)}, f32[1,2,1]{2,1,0:T(2,128)}, u32[]{:S(2)}) copy-start(f32[1,2,1]{2,1,0:T(2,128)} %get-tuple-element.48) | copy-start | bytes 28
  77.8 22.5 %collective-permute-start.4 = (bf16[256,2176]{1,0:T(8,128)(2,1)}, bf16[256,2176]{1,0:T(8,128)(2,1)}, u32[]{:S(2)}, u32[]{:S(2)}) collective-permute-start(bf16[256,2176]{1,0:T(8,128)(2,1)} %bitcast.31), channel_id=1, source_target_pairs={{0,1},{1,2},{2,3},{3,4},{4,5},{5,6},{6,7},{7,8},{8,9},{9,10},{10,1... | collective-permute-start | bytes 3342344 | tf_op jit(solution)/shard_map/ppermute | solution.py:110
  83.3 17.0 %collective-permute-start.5 = (bf16[256,2176]{1,0:T(8,128)(2,1)}, bf16[256,2176]{1,0:T(8,128)(2,1)}, u32[]{:S(2)}, u32[]{:S(2)}) collective-permute-start(bf16[256,2176]{1,0:T(8,128)(2,1)} %bitcast.32), channel_id=1, source_target_pairs={{1,0},{2,1},{3,2},{4,3},{5,4},{6,5},{7,6},{8,7},{9,8},{10,9},{11,1... | collective-permute-start | bytes 3342344 | tf_op jit(solution)/shard_map/ppermute | solution.py:111
  88.7 0.7 copy-start.6
  88.7 7.1 %copy-start = (bf16[2,4,64,2176]{3,2,1,0:T(8,128)(2,1)S(1)}, bf16[2,4,64,2176]{3,2,1,0:T(8,128)(2,1)}, u32[]{:S(2)}) copy-start(bf16[2,4,64,2176]{3,2,1,0:T(8,128)(2,1)} %copy.30) | copy-start | bytes 6684676
  95.9 2.6 %copy-start.1 = (bf16[2,4,64,2176]{3,2,1,0:T(8,128)(2,1)S(1)}, bf16[2,4,64,2176]{3,2,1,0:T(8,128)(2,1)}, u32[]{:S(2)}) copy-start(bf16[2,4,64,2176]{3,2,1,0:T(8,128)(2,1)} %copy.36) | copy-start | bytes 6684676
  95.9 3.0 %copy-start.3 = (bf16[2,256,2176]{2,1,0:T(8,128)(2,1)S(1)}, bf16[2,256,2176]{2,1,0:T(8,128)(2,1)}, u32[]{:S(2)}) copy-start(bf16[2,256,2176]{2,1,0:T(8,128)(2,1)} %shard_map.28) | copy-start | bytes 6684676
  106.7 3.2 %copy-start.2 = (bf16[2,256,2176]{2,1,0:T(8,128)(2,1)S(1)}, bf16[2,256,2176]{2,1,0:T(8,128)(2,1)}, u32[]{:S(2)}) copy-start(bf16[2,256,2176]{2,1,0:T(8,128)(2,1)} %shard_map.29) | copy-start | bytes 6684676
  109.9 1.0 copy-start.5

commit v20 on v17

--- a/solution.py
+++ b/solution.py
@@ -125,15 +125,15 @@
             lax.dot_general(im, fd, dims, preferred_element_type=jnp.float32)
             for fd in fields], axis=1)
         for im in images], axis=0)
-    part = part.reshape(GROUPS, nodes, step, snaps)
+    cols = (GROUPS, nodes, sizes[0] // (GROUPS * nodes), sizes[1], sizes[2], snaps // spaces)
+    part = jnp.moveaxis(part.reshape((snaps,) + cols), 5, 0)
+    part = lax.all_to_all(part, SPACE[2], 0, 0, tiled=True).sum(axis=0)
+    part = part.reshape(GROUPS, nodes, step, -1)
     total = jnp.take(part, me, axis=1)
     for d in range(1, nodes):
         blk = jnp.take(part, (me + d) % nodes, axis=1)
         total = total + lax.ppermute(blk, "node", [(i, (i + d) % nodes) for i in range(nodes)])
-    total = total.reshape(rows, GROUPS, nodes, step).transpose(0, 2, 1, 3)
-    total = total.reshape((rows,) + tuple(sizes) + (snaps // spaces,))
-    total = jnp.moveaxis(total, 3, 0)
-    total = lax.all_to_all(total, SPACE[2], 0, 0, tiled=True).sum(axis=0)
+    total = total.reshape((rows,) + cols[:4] + cols[5:]).transpose(0, 2, 1, 3, 4, 5)
     total = total.reshape(rows, sizes[0] * sizes[1], snaps // spaces)
     total = jnp.moveaxis(total, 1, 0)
     total = lax.all_to_all(total, SPACE[:2], 0, 0, tiled=True).sum(axis=0)

time: 156 us -> 159 us (1.019)
  blocking collectives: 24.8 us -> 28.2 us
    all_to_all x1, blocking collectives: 3.94 us -> 5.93 us  [per_device(): part = lax.all_to_all(part, SPACE[2], 0, 0, tiled=True).sum(axis=0)]
  transfers between devices with their start and end apart: 11 -> 11, of which waited for: 6 -> 5; matrix products, arithmetic and copies ran while one was open for 14% -> 13% of each run, Pallas kernels for 4% -> 4%
where the time goes in v20:
time: 159 us; the launch traced here: 158 us
  waiting for transfers between devices  47.2 us (30%)
  starting transfers between devices  29.1 us (18%)
  blocking collectives  28.2 us (18%)
  local copies, waits for them, and re-layouts  26.3 us (17%)
  Pallas kernels  12.8 us (8%)
  other arithmetic  7.09 us (4%)
  matrix products  6.63 us (4%)
    all_to_all x2, waiting for transfers between devices, per_device(): lax.all_to_all(chunked(major, nodes), 'node', 1, 1, tiled=True)  32.7 us
    all_to_all x1, blocking collectives, per_device(): total = lax.all_to_all(total, SPACE[:2], 0, 0, tiled=True).sum(axis=0)  22.2 us
    pallas_call x2, Pallas kernels, stencil(): pl.pallas_call(stencil_kernel, grid=(snaps // ROWS,), in_specs=[pl.BlockS...  12.8 us
    ppermute x3, waiting for transfers between devices, per_device(): lax.ppermute(blk, 'node', [(i, (i + d) % nodes) for i in range(nodes)])  12.5 us
    all_to_all x2, starting transfers between devices, per_device(): lax.all_to_all(chunked(major, nodes), 'node', 1, 1, tiled=True)  8.77 us
    ppermute x2, starting transfers between devices, per_device(): above = lax.ppermute(field[0], SPACE, down)  7.46 us
    dot_general x4, matrix products, per_device(): lax.dot_general(im, fd, dims, preferred_element_type=jnp.float32)  6.63 us
    all_to_all x1, blocking collectives, per_device(): part = lax.all_to_all(part, SPACE[2], 0, 0, tiled=True).sum(axis=0)  5.93 us
  transfers between devices with their start and end apart: 11, of which 5 were waited for; matrix products, arithmetic and copies ran while one was open for 13% of the time, Pallas kernels for 4%

profile of v20, /device:TPU:8, one launch (start us, length us, event | category | flops | bytes accessed | tf_op | source)
XLA Modules:
  0.0 157.7 jit_solution(2869563512136271852)
XLA Ops:
  0.0 5.0 %fusion.21 = (bf16[64,2,8192]{2,1,0:T(2,128)(2,1)S(1)}, bf16[64,2,8192]{2,1,0:T(2,128)(2,1)S(1)}) fusion(bf16[128,2,8192]{2,1,0:T(2,128)(2,1)} %param.4), kind=kLoop, calls=%fused_computation.80 | loop fusion | bytes 8388608 | tf_op jit(solution)/shard_map/slice | solution.py:108
  5.1 2.7 %copy_bitcast_fusion = (bf16[2,64,8192]{2,1,0:T(8,128)(2,1)S(1)}, bf16[2,64,8192]{2,1,0:T(8,128)(2,1)S(1)}) fusion(bf16[64,2,8192]{2,1,0:T(2,128)(2,1)S(1)} %get-tuple-element.35, bf16[64,2,8192]{2,1,0:T(2,128)(2,1)S(1)} %get-tuple-element.34), kind=kLoop, calls=%fused_computation.2 | loop fusion | bytes 8388608 | tf_op jit(solution)/shard_map/transpose | solution.py:108
  7.7 0.1 fusion.25
  7.8 0.1 fusion.24
  8.0 0.1 maximum_bitcast_fusion
  8.1 0.1 maximum_bitcast_fusion.1
  8.2 0.9 copy-done.5
  9.1 0.1 fusion.1
  9.2 0.3 concatenate.155
  9.5 1.7 %pad_maximum_fusion = bf16[2,4,64,2176]{3,2,0,1:T(8,128)(2,1)} fusion(bf16[2,1,64,2176]{3,2,0,1:T(8,128)(2,1)S(1)} %bitcast.106, bf16[2,1,64,2176]{3,2,0,1:T(8,128)(2,1)S(1)} %maximum_bitcast_fusion.1, bf16[2,1,64,2176]{3,2,0,1:T(8,128)(2,1)S(1)} %maximum_bitcast_fusion, bf16[2,1,64,2176]{3,2,0,1:T(8,128)(2,1)S(1)} %get-tuple-element.69), kind=kLoop, calls=%fused_computation | loop fusion | flops 3342336 | bytes 4456448 | tf_op jit(solution)/shard_map/stack | solution.py:89
  11.2 4.3 %all-to-all-start = ((bf16[2,4,64,2176]{3,2,0,1:T(8,128)(2,1)}), bf16[2,4,64,2176]{3,2,0,1:T(8,128)(2,1)S(1)}, u32[]{:S(2)}, u32[]{:S(2)}) async-start(bf16[2,4,64,2176]{3,2,0,1:T(8,128)(2,1)} %pad_maximum_fusion), calls=%async_computation | async-start | bytes 4456448 | tf_op jit(solution)/shard_map/all_to_all | solution.py:109
  15.5 0.9 fusion.27
  16.4 1.9 %slice.246 = bf16[2,64,2048]{2,1,0:T(8,128)(2,1)} slice(bf16[2,64,8192]{2,1,0:T(8,128)(2,1)} %copy-done.5), slice={[0:2], [0:64], [6144:8192]} | slice | bytes 1048576 | tf_op jit(solution)/shard_map/slice | solution.py:88
  18.3 1.2 concatenate.175
  19.5 1.3 fusion.26
  20.8 0.1 maximum_bitcast_fusion.2
  20.9 0.1 maximum_bitcast_fusion.3
  20.9 1.7 %pad_maximum_fusion.1 = bf16[2,4,64,2176]{3,2,0,1:T(8,128)(2,1)} fusion(bf16[2,1,64,2176]{3,2,0,1:T(8,128)(2,1)S(1)} %bitcast.105, bf16[2,1,64,2176]{3,2,0,1:T(8,128)(2,1)S(1)} %maximum_bitcast_fusion.3, bf16[2,1,64,2176]{3,2,0,1:T(8,128)(2,1)S(1)} %maximum_bitcast_fusion.2, bf16[2,1,64,2176]{3,2,0,1:T(8,128)(2,1)S(1)} %get-tuple-element.70), kind=kLoop, calls=%fused_computation.1 | loop fusion | flops 3342336 | bytes 4456448 | tf_op jit(solution)/shard_map/stack | solution.py:89
  22.7 20.5 %all-to-all-done = bf16[2,4,64,2176]{3,2,0,1:T(8,128)(2,1)S(1)} async-done(((bf16[2,4,64,2176]{3,2,0,1:T(8,128)(2,1)}), bf16[2,4,64,2176]{3,2,0,1:T(8,128)(2,1)S(1)}, u32[]{:S(2)}, u32[]{:S(2)}) %all-to-all-start) | async-done | bytes 2228256 | tf_op jit(solution)/shard_map/all_to_all | solution.py:109
  43.2 4.5 %all-to-all-start.1 = ((bf16[2,4,64,2176]{3,2,0,1:T(8,128)(2,1)}), bf16[2,4,64,2176]{3,2,0,1:T(8,128)(2,1)}, u32[]{:S(2)}, u32[]{:S(2)}) async-start(bf16[2,4,64,2176]{3,2,0,1:T(8,128)(2,1)} %pad_maximum_fusion.1), calls=%async_computation.1 | async-start | bytes 4456448 | tf_op jit(solution)/shard_map/all_to_all | solution.py:109
  47.7 1.6 copy.36
  49.6 0.1 concatenate.159
  49.9 1.9 %collective-permute-start.2 = (bf16[2176]{0:T(1024)(128)(2,1)S(1)}, bf16[2176]{0:T(1024)(128)(2,1)S(1)}, u32[]{:S(2)}, u32[]{:S(2)}) collective-permute-start(bf16[2176]{0:T(1024)(128)(2,1)S(1)} %get-tuple-element.31), channel_id=1, source_target_pairs={{0,1},{1,2},{2,3},{3,4},{4,5},{5,6},{6,7},{7,8},{8,9},{9,10},{10,1... | collective-permute-start | bytes 13064 | tf_op jit(solution)/shard_map/ppermute | solution.py:117
  51.8 3.6 %collective-permute-start.3 = (bf16[2176]{0:T(1024)(128)(2,1)S(1)}, bf16[2176]{0:T(1024)(128)(2,1)S(1)}, u32[]{:S(2)}, u32[]{:S(2)}) collective-permute-start(bf16[2176]{0:T(1024)(128)(2,1)S(1)} %get-tuple-element.30), channel_id=1, source_target_pairs={{1,0},{2,1},{3,2},{4,3},{5,4},{6,5},{7,6},{8,7},{9,8},{10,9},{11,1... | collective-permute-start | bytes 13064 | tf_op jit(solution)/shard_map/ppermute | solution.py:118
  55.5 1.2 fusion.22
  56.6 1.9 %collective-permute-start = (bf16[256,2176]{1,0:T(8,128)(2,1)}, bf16[256,2176]{1,0:T(8,128)(2,1)}, u32[]{:S(2)}, u32[]{:S(2)}) collective-permute-start(bf16[256,2176]{1,0:T(8,128)(2,1)} %bitcast.6), channel_id=1, source_target_pairs={{0,1},{1,2},{2,3},{3,4},{4,5},{5,6},{6,7},{7,8},{8,9},{9,10},{10,1... | collective-permute-start | bytes 3342344 | tf_op jit(solution)/shard_map/ppermute | solution.py:110
  58.6 3.6 %collective-permute-start.1 = (bf16[256,2176]{1,0:T(8,128)(2,1)S(1)}, bf16[256,2176]{1,0:T(8,128)(2,1)}, u32[]{:S(2)}, u32[]{:S(2)}) collective-permute-start(bf16[256,2176]{1,0:T(8,128)(2,1)S(1)} %bitcast.107), channel_id=1, source_target_pairs={{1,0},{2,1},{3,2},{4,3},{5,4},{6,5},{7,6},{8,7},{9,8},{10,9},{11,1... | collective-permute-start | bytes 3342344 | tf_op jit(solution)/shard_map/ppermute | solution.py:111
  62.4 12.1 %all-to-all-done.1 = bf16[2,4,64,2176]{3,2,0,1:T(8,128)(2,1)} async-done(((bf16[2,4,64,2176]{3,2,0,1:T(8,128)(2,1)}), bf16[2,4,64,2176]{3,2,0,1:T(8,128)(2,1)}, u32[]{:S(2)}, u32[]{:S(2)}) %all-to-all-start.1) | async-done | bytes 2228256 | tf_op jit(solution)/shard_map/all_to_all | solution.py:109
  74.6 3.2 %fusion.23 = (bf16[1,4,64,2176]{3,2,1,0:T(8,128)(2,1)}, bf16[1,4,64,2176]{3,2,1,0:T(8,128)(2,1)}) fusion(bf16[2,4,64,2176]{3,2,0,1:T(8,128)(2,1)} %all-to-all-done.1), kind=kLoop, calls=%fused_computation.82 | loop fusion | bytes 4456448 | tf_op jit(solution)/shard_map/slice | solution.py:111
  77.8 1.9 %collective-permute-start.4 = (bf16[256,2176]{1,0:T(8,128)(2,1)}, bf16[256,2176]{1,0:T(8,128)(2,1)}, u32[]{:S(2)}, u32[]{:S(2)}) collective-permute-start(bf16[256,2176]{1,0:T(8,128)(2,1)} %bitcast.31), channel_id=1, source_target_pairs={{0,1},{1,2},{2,3},{3,4},{4,5},{5,6},{6,7},{7,8},{8,9},{9,10},{10,1... | collective-permute-start | bytes 3342344 | tf_op jit(solution)/shard_map/ppermute | solution.py:110
  79.7 0.1 select_dynamic-update-slice_fusion.1
  79.8 0.1 select_dynamic-update-slice_fusion
  79.9 0.1 constant_dynamic-update-slice_fusion.3
  80.0 0.1 constant_dynamic-update-slice_fusion.2
  80.1 3.2 %copy.42 = bf16[2,4,64,2176]{3,2,1,0:T(8,128)(2,1)} copy(bf16[2,4,64,2176]{3,2,0,1:T(8,128)(2,1)} %all-to-all-done.1) | data formatting | bytes 4456448 | tf_op jit(solution)/shard_map/all_to_all | solution.py:109
  83.3 3.8 %collective-permute-start.5 = (bf16[256,2176]{1,0:T(8,128)(2,1)}, bf16[256,2176]{1,0:T(8,128)(2,1)}, u32[]{:S(2)}, u32[]{:S(2)}) collective-permute-start(bf16[256,2176]{1,0:T(8,128)(2,1)} %bitcast.32), channel_id=1, source_target_pairs={{1,0},{2,1},{3,2},{4,3},{5,4},{6,5},{7,6},{8,7},{9,8},{10,9},{11,1... | collective-permute-start | bytes 3342344 | tf_op jit(solution)/shard_map/ppermute | solution.py:111
  87.2 0.1 add_dynamic-update-slice_fusion.coef_ref
  87.4 0.6 copy-done.6
  88.0 6.5 %shard_map.28 = bf16[2,256,2176]{2,1,0:T(8,128)(2,1)} custom-call(bf16[2,256,2176]{2,1,0:T(8,128)(2,1)} %bitcast.97, bf16[256,2176]{1,0:T(8,128)(2,1)} %collective-permute-done.below_ref, bf16[256,2176]{1,0:T(8,128)(2,1)} %collective-permute-done.1.above_ref, f32[7,2,2176]{2,1,0:T(2,128)} %copy-done.6), custom_call_target="tpu_custom_call" | custom-call | tf_op jit(solution)/shard_map/pallas_call | solution.py:52
  94.5 2.5 %convolution_bitcast_fusion.3 = f32[256,256]{0,1:T(8,128)S(1)} fusion(bf16[2,256,2176]{2,1,0:T(8,128)(2,1)} %shard_map.28, bf16[2,256,2176]{2,1,0:T(8,128)(2,1)S(1)} %bitcast.98), kind=kOutput, calls=%fused_computation.7 | convolution fusion | flops 570425344 | bytes 4718592 | tf_op jit(solution)/shard_map/dot_general | solution.py:125
  97.0 0.4 copy-done.4
  97.4 0.8 convolution_bitcast_fusion.2
  98.2 2.0 %collective-permute-done.5.above_ref = bf16[256,2176]{1,0:T(8,128)(2,1)} collective-permute-done((bf16[256,2176]{1,0:T(8,128)(2,1)}, bf16[256,2176]{1,0:T(8,128)(2,1)}, u32[]{:S(2)}, u32[]{:S(2)}) %collective-permute-start.5) | collective-permute-done | bytes 1114144 | tf_op jit(solution)/shard_map/ppermute | solution.py:111
  100.2 6.4 %shard_map.29 = bf16[2,256,2176]{2,1,0:T(8,128)(2,1)} custom-call(bf16[2,256,2176]{2,1,0:T(8,128)(2,1)} %bitcast.100, bf16[256,2176]{1,0:T(8,128)(2,1)} %collective-permute-done.4.below_ref, bf16[256,2176]{1,0:T(8,128)(2,1)} %collective-permute-done.5.above_ref, f32[7,2,2176]{2,1,0:T(2,128)} %copy-done.6), custom_call_target="tpu_custom_call" | custom-call | tf_op jit(solution)/shard_map/pallas_call | solution.py:52
  106.6 2.5 %convolution_bitcast_fusion.1 = f32[256,256]{0,1:T(8,128)S(1)} fusion(bf16[2,256,2176]{2,1,0:T(8,128)(2,1)} %shard_map.29, bf16[2,256,2176]{2,1,0:T(8,128)(2,1)S(1)} %bitcast.99), kind=kOutput, calls=%fused_computation.5 | convolution fusion | flops 570425344 | bytes 4718592 | tf_op jit(solution)/shard_map/dot_general | solution.py:125
  109.2 0.4 copy-done.3
  109.6 0.8 convolution_bitcast_fusion
  110.3 0.1 maximum_maximum_fusion
  110.5 0.1 copy.62
  110.6 5.9 %all_to_all.20 = f32[2,512,2,4,1,4,8]{1,6,5,3,2,4,0:T(8,128)S(1)} all-to-all(f32[2,512,2,4,1,4,8]{1,6,5,3,2,4,0:T(8,128)S(1)} %bitcast.104), channel_id=1, replica_groups=mesh['node'=4,'z'=8,'y'=4,'core'=2] {'core'}, dimensions={0} | all-to-all | bytes 2097152 | tf_op jit(solution)/shard_map/all_to_all | solution.py:130
  116.5 0.1 reduce_sum.18
  116.6 0.5 reshape.471
  117.2 1.0 constant_dynamic-slice_fusion.2
  118.2 0.1 select_bitcast_fusion.1
  118.3 0.6 collective-permute-start.6
  118.9 0.1 select_bitcast_fusion
  119.1 2.2 %collective-permute-start.7 = (f32[2,64,256]{1,0,2:T(2,128)S(1)}, f32[2,64,256]{1,0,2:T(2,128)S(1)}, u32[]{:S(2)}, u32[]{:S(2)}) collective-permute-start(f32[2,64,256]{1,0,2:T(2,128)S(1)} %select_bitcast_fusion), channel_id=1, source_target_pairs={{0,128},{64,192},{128,0},{192,64},{1,129},{65,193},{129,1},{193,65... | collective-permute-start | bytes 393224 | tf_op jit(solution)/shard_map/ppermute | solution.py:135
  121.2 0.7 collective-permute-start.8
  121.9 11.6 %collective-permute-done.6 = f32[2,64,256]{1,0,2:T(2,128)S(1)} collective-permute-done((f32[2,64,256]{1,0,2:T(2,128)S(1)}, f32[2,64,256]{1,0,2:T(2,128)S(1)}, u32[]{:S(2)}, u32[]{:S(2)}) %collective-permute-start.6) | collective-permute-done | bytes 131104 | tf_op jit(solution)/shard_map/ppermute | solution.py:135
  133.6 0.8 collective-permute-done.8
  134.4 0.3 fusion.3
  134.7 0.2 reshape.472
  134.8 22.2 %all_to_all.21 = f32[32,128,8]{1,2,0:T(8,128)S(1)} all-to-all(f32[32,128,8]{1,2,0:T(8,128)S(1)} %bitcast.112), channel_id=1, replica_groups=mesh['node'=4,'z'=8,'y'=4,'core'=2] {'z','y'}, dimensions={0} | all-to-all | bytes 262144 | tf_op jit(solution)/shard_map/all_to_all | solution.py:139
  157.1 0.6 broadcast_multiply_fusion
  (43 shorter events, 1.0 us)
Async XLA Ops:
  7.7 1.4 copy-start.5
  7.9 1.1 copy-start.8
  11.2 32.0 %all-to-all-start = ((bf16[2,4,64,2176]{3,2,0,1:T(8,128)(2,1)}), bf16[2,4,64,2176]{3,2,0,1:T(8,128)(2,1)S(1)}, u32[]{:S(2)}, u32[]{:S(2)}) async-start(bf16[2,4,64,2176]{3,2,0,1:T(8,128)(2,1)} %pad_maximum_fusion), calls=%async_computation | async-start | bytes 4456448 | tf_op jit(solution)/shard_map/all_to_all | solution.py:109
  43.2 31.4 %all-to-all-start.1 = ((bf16[2,4,64,2176]{3,2,0,1:T(8,128)(2,1)}), bf16[2,4,64,2176]{3,2,0,1:T(8,128)(2,1)}, u32[]{:S(2)}, u32[]{:S(2)}) async-start(bf16[2,4,64,2176]{3,2,0,1:T(8,128)(2,1)} %pad_maximum_fusion.1), calls=%async_computation.1 | async-start | bytes 4456448 | tf_op jit(solution)/shard_map/all_to_all | solution.py:109
  47.7 1.6 copy-start.7
  49.9 33.4 %collective-permute-start.2 = (bf16[2176]{0:T(1024)(128)(2,1)S(1)}, bf16[2176]{0:T(1024)(128)(2,1)S(1)}, u32[]{:S(2)}, u32[]{:S(2)}) collective-permute-start(bf16[2176]{0:T(1024)(128)(2,1)S(1)} %get-tuple-element.31), channel_id=1, source_target_pairs={{0,1},{1,2},{2,3},{3,4},{4,5},{5,6},{6,7},{7,8},{8,9},{9,10},{10,1... | collective-permute-start | bytes 13064 | tf_op jit(solution)/shard_map/ppermute | solution.py:117
  51.8 35.3 %collective-permute-start.3 = (bf16[2176]{0:T(1024)(128)(2,1)S(1)}, bf16[2176]{0:T(1024)(128)(2,1)S(1)}, u32[]{:S(2)}, u32[]{:S(2)}) collective-permute-start(bf16[2176]{0:T(1024)(128)(2,1)S(1)} %get-tuple-element.30), channel_id=1, source_target_pairs={{1,0},{2,1},{3,2},{4,3},{5,4},{6,5},{7,6},{8,7},{9,8},{10,9},{11,1... | collective-permute-start | bytes 13064 | tf_op jit(solution)/shard_map/ppermute | solution.py:118
  56.6 30.7 %collective-permute-start = (bf16[256,2176]{1,0:T(8,128)(2,1)}, bf16[256,2176]{1,0:T(8,128)(2,1)}, u32[]{:S(2)}, u32[]{:S(2)}) collective-permute-start(bf16[256,2176]{1,0:T(8,128)(2,1)} %bitcast.6), channel_id=1, source_target_pairs={{0,1},{1,2},{2,3},{3,4},{4,5},{5,6},{6,7},{7,8},{8,9},{9,10},{10,1... | collective-permute-start | bytes 3342344 | tf_op jit(solution)/shard_map/ppermute | solution.py:110
  58.6 28.8 %collective-permute-start.1 = (bf16[256,2176]{1,0:T(8,128)(2,1)S(1)}, bf16[256,2176]{1,0:T(8,128)(2,1)}, u32[]{:S(2)}, u32[]{:S(2)}) collective-permute-start(bf16[256,2176]{1,0:T(8,128)(2,1)S(1)} %bitcast.107), channel_id=1, source_target_pairs={{1,0},{2,1},{3,2},{4,3},{5,4},{6,5},{7,6},{8,7},{9,8},{10,9},{11,1... | collective-permute-start | bytes 3342344 | tf_op jit(solution)/shard_map/ppermute | solution.py:111
  77.8 20.5 %collective-permute-start.4 = (bf16[256,2176]{1,0:T(8,128)(2,1)}, bf16[256,2176]{1,0:T(8,128)(2,1)}, u32[]{:S(2)}, u32[]{:S(2)}) collective-permute-start(bf16[256,2176]{1,0:T(8,128)(2,1)} %bitcast.31), channel_id=1, source_target_pairs={{0,1},{1,2},{2,3},{3,4},{4,5},{5,6},{6,7},{7,8},{8,9},{9,10},{10,1... | collective-permute-start | bytes 3342344 | tf_op jit(solution)/shard_map/ppermute | solution.py:110
  83.3 17.0 %collective-permute-start.5 = (bf16[256,2176]{1,0:T(8,128)(2,1)}, bf16[256,2176]{1,0:T(8,128)(2,1)}, u32[]{:S(2)}, u32[]{:S(2)}) collective-permute-start(bf16[256,2176]{1,0:T(8,128)(2,1)} %bitcast.32), channel_id=1, source_target_pairs={{1,0},{2,1},{3,2},{4,3},{5,4},{6,5},{7,6},{8,7},{9,8},{10,9},{11,1... | collective-permute-start | bytes 3342344 | tf_op jit(solution)/shard_map/ppermute | solution.py:111
  87.3 0.7 copy-start.6
  87.4 7.1 %copy-start = (bf16[2,4,64,2176]{3,2,1,0:T(8,128)(2,1)S(1)}, bf16[2,4,64,2176]{3,2,1,0:T(8,128)(2,1)}, u32[]{:S(2)}) copy-start(bf16[2,4,64,2176]{3,2,1,0:T(8,128)(2,1)} %copy.36) | copy-start | bytes 6684676
  94.5 2.6 %copy-start.1 = (bf16[2,4,64,2176]{3,2,1,0:T(8,128)(2,1)S(1)}, bf16[2,4,64,2176]{3,2,1,0:T(8,128)(2,1)}, u32[]{:S(2)}) copy-start(bf16[2,4,64,2176]{3,2,1,0:T(8,128)(2,1)} %copy.42) | copy-start | bytes 6684676
  94.5 3.0 %copy-start.4 = (bf16[2,256,2176]{2,1,0:T(8,128)(2,1)S(1)}, bf16[2,256,2176]{2,1,0:T(8,128)(2,1)}, u32[]{:S(2)}) copy-start(bf16[2,256,2176]{2,1,0:T(8,128)(2,1)} %shard_map.28) | copy-start | bytes 6684676
  106.6 2.6 %copy-start.2 = (bf16[2,4,64,2176]{3,2,1,0:T(8,128)(2,1)S(1)}, bf16[2,4,64,2176]{3,2,1,0:T(8,128)(2,1)}, u32[]{:S(2)}) copy-start(bf16[2,4,64,2176]{3,2,1,0:T(8,128)(2,1)} %copy.42) | copy-start | bytes 6684676
  106.6 3.0 %copy-start.3 = (bf16[2,256,2176]{2,1,0:T(8,128)(2,1)S(1)}, bf16[2,256,2176]{2,1,0:T(8,128)(2,1)}, u32[]{:S(2)}) copy-start(bf16[2,256,2176]{2,1,0:T(8,128)(2,1)} %shard_map.29) | copy-start | bytes 6684676
  118.3 15.3 %collective-permute-start.6 = (f32[2,64,256]{1,0,2:T(2,128)S(1)}, f32[2,64,256]{1,0,2:T(2,128)S(1)}, u32[]{:S(2)}, u32[]{:S(2)}) collective-permute-start(f32[2,64,256]{1,0,2:T(2,128)S(1)} %select_bitcast_fusion.1), channel_id=1, source_target_pairs={{0,64},{64,128},{128,192},{192,0},{1,65},{65,129},{129,193},{193,1... | collective-permute-start | bytes 393224 | tf_op jit(solution)/shard_map/ppermute | solution.py:135
  119.1 14.5 %collective-permute-start.7 = (f32[2,64,256]{1,0,2:T(2,128)S(1)}, f32[2,64,256]{1,0,2:T(2,128)S(1)}, u32[]{:S(2)}, u32[]{:S(2)}) collective-permute-start(f32[2,64,256]{1,0,2:T(2,128)S(1)} %select_bitcast_fusion), channel_id=1, source_target_pairs={{0,128},{64,192},{128,0},{192,64},{1,129},{65,193},{129,1},{193,65... | collective-permute-start | bytes 393224 | tf_op jit(solution)/shard_map/ppermute | solution.py:135
  121.2 13.2 %collective-permute-start.8 = (f32[2,64,256]{1,0,2:T(2,128)S(1)}, f32[2,64,256]{1,0,2:T(2,128)S(1)}, u32[]{:S(2)}, u32[]{:S(2)}) collective-permute-start(f32[2,64,256]{1,0,2:T(2,128)S(1)} %bitcast.113), channel_id=1, source_target_pairs={{0,192},{64,0},{128,64},{192,128},{1,193},{65,1},{129,65},{193,129... | collective-permute-start | bytes 393224 | tf_op jit(solution)/shard_map/ppermute | solution.py:135

commit v21 on v17

--- a/solution.py
+++ b/solution.py
@@ -120,11 +120,8 @@
     for field, (below, above) in zip(fields, fronts):
         images.append(stencil(field, below, above, coef))
     dims = (((0, 2), (0, 2)), ((), ()))
-    part = jnp.concatenate([
-        jnp.concatenate([
-            lax.dot_general(im, fd, dims, preferred_element_type=jnp.float32)
-            for fd in fields], axis=1)
-        for im in images], axis=0)
+    part = lax.dot_general(jnp.concatenate(images, axis=1), jnp.concatenate(fields, axis=1), dims,
+                           preferred_element_type=jnp.float32)
     part = part.reshape(GROUPS, nodes, step, snaps)
     total = jnp.take(part, me, axis=1)
     for d in range(1, nodes):

time: 156 us -> 157 us (level)
  local copies, waits for them, and re-layouts: 26.4 us -> 31 us
  waiting for transfers between devices: 47.6 us -> 45.2 us
    all_to_all x2, waiting for transfers between devices: 32.7 us -> 29.1 us  [per_device(): lax.all_to_all(chunked(major, nodes), 'node', 1, 1, tiled=True)]
    dot_general x4 -> x1, matrix products: 6.63 us -> 5.46 us  [per_device(): lax.dot_general(jnp.concatenate(images, axis=1), jnp.concatenate(fields,...]
  transfers between devices with their start and end apart: 11 -> 11, of which waited for: 6 -> 6; matrix products, arithmetic and copies ran while one was open for 14% -> 15% of each run, Pallas kernels for 4% -> 4%
where the time goes in v21:
time: 157 us; the launch traced here: 155 us
  waiting for transfers between devices  45.2 us (29%)
  local copies, waits for them, and re-layouts  31 us (20%)
  starting transfers between devices  29 us (18%)
  blocking collectives  24.8 us (16%)
  Pallas kernels  12.9 us (8%)
  other arithmetic  6.15 us (4%)
  matrix products  5.46 us (3%)
    all_to_all x2, waiting for transfers between devices, per_device(): lax.all_to_all(chunked(major, nodes), 'node', 1, 1, tiled=True)  29.1 us
    all_to_all x1, blocking collectives, per_device(): total = lax.all_to_all(total, SPACE[:2], 0, 0, tiled=True).sum(axis=0)  20.8 us
    ppermute x3, waiting for transfers between devices, per_device(): lax.ppermute(blk, 'node', [(i, (i + d) % nodes) for i in range(nodes)])  13 us
    pallas_call x2, Pallas kernels, stencil(): pl.pallas_call(stencil_kernel, grid=(snaps // ROWS,), in_specs=[pl.BlockS...  12.9 us
    all_to_all x2, starting transfers between devices, per_device(): lax.all_to_all(chunked(major, nodes), 'node', 1, 1, tiled=True)  8.77 us
    ppermute x2, starting transfers between devices, per_device(): above = lax.ppermute(field[0], SPACE, down)  7.45 us
    dot_general x1, matrix products, per_device(): lax.dot_general(jnp.concatenate(images, axis=1), jnp.concatenate(fields,...  5.46 us
    slice x1, local copies, waits for them, and re-layouts, per_device(): major = jnp.transpose(snapshots[g * step:(g + 1) * step], (1, 0, 2))  5.04 us
  transfers between devices with their start and end apart: 11, of which 6 were waited for; matrix products, arithmetic and copies ran while one was open for 15% of the time, Pallas kernels for 4%

profile of v21, /device:TPU:8, one launch (start us, length us, event | category | flops | bytes accessed | tf_op | source)
XLA Modules:
  0.0 154.9 jit_solution(14247481760067895167)
XLA Ops:
  0.0 5.0 %fusion.34 = (bf16[64,2,8192]{2,1,0:T(2,128)(2,1)S(1)}, bf16[64,2,8192]{2,1,0:T(2,128)(2,1)S(1)}) fusion(bf16[128,2,8192]{2,1,0:T(2,128)(2,1)} %param.4), kind=kLoop, calls=%fused_computation.84 | loop fusion | bytes 8388608 | tf_op jit(solution)/shard_map/slice | solution.py:108
  5.1 2.7 %copy_bitcast_fusion = (bf16[2,64,8192]{2,1,0:T(8,128)(2,1)S(1)}, bf16[2,64,8192]{2,1,0:T(8,128)(2,1)S(1)}) fusion(bf16[64,2,8192]{2,1,0:T(2,128)(2,1)S(1)} %get-tuple-element.35, bf16[64,2,8192]{2,1,0:T(2,128)(2,1)S(1)} %get-tuple-element.34), kind=kLoop, calls=%fused_computation.9 | loop fusion | bytes 8388608 | tf_op jit(solution)/shard_map/transpose | solution.py:108
  7.7 0.1 fusion.38
  7.8 0.1 fusion.37
  8.1 0.1 maximum_bitcast_fusion.1
  8.2 0.9 copy-done
  9.1 0.1 fusion.8
  9.2 0.3 concatenate.152
  9.5 1.7 %pad_maximum_fusion = bf16[2,4,64,2176]{3,2,0,1:T(8,128)(2,1)} fusion(bf16[2,1,64,2176]{3,2,0,1:T(8,128)(2,1)S(1)} %bitcast.104, bf16[2,1,64,2176]{3,2,0,1:T(8,128)(2,1)S(1)} %maximum_bitcast_fusion.1, bf16[2,1,64,2176]{3,2,0,1:T(8,128)(2,1)S(1)} %maximum_bitcast_fusion, bf16[2,1,64,2176]{3,2,0,1:T(8,128)(2,1)S(1)} %get-tuple-element.68), kind=kLoop, calls=%fused_computation.7 | loop fusion | flops 3342336 | bytes 4456448 | tf_op jit(solution)/shard_map/stack | solution.py:89
  11.2 4.3 %all-to-all-start = ((bf16[2,4,64,2176]{3,2,0,1:T(8,128)(2,1)}), bf16[2,4,64,2176]{3,2,0,1:T(8,128)(2,1)S(1)}, u32[]{:S(2)}, u32[]{:S(2)}) async-start(bf16[2,4,64,2176]{3,2,0,1:T(8,128)(2,1)} %pad_maximum_fusion), calls=%async_computation | async-start | bytes 4456448 | tf_op jit(solution)/shard_map/all_to_all | solution.py:109
  15.5 0.6 fusion.24
  16.1 0.9 fusion.40
  17.0 1.9 %slice.246 = bf16[2,64,2048]{2,1,0:T(8,128)(2,1)} slice(bf16[2,64,8192]{2,1,0:T(8,128)(2,1)} %copy-done), slice={[0:2], [0:64], [6144:8192]} | slice | bytes 1048576 | tf_op jit(solution)/shard_map/slice | solution.py:88
  18.9 1.2 concatenate.172
  20.0 1.3 fusion.39
  21.3 0.1 maximum_bitcast_fusion.2
  21.4 0.1 maximum_bitcast_fusion.3
  21.5 1.7 %pad_maximum_fusion.1 = bf16[2,4,64,2176]{3,2,0,1:T(8,128)(2,1)} fusion(bf16[2,1,64,2176]{3,2,0,1:T(8,128)(2,1)S(1)} %bitcast.103, bf16[2,1,64,2176]{3,2,0,1:T(8,128)(2,1)S(1)} %maximum_bitcast_fusion.3, bf16[2,1,64,2176]{3,2,0,1:T(8,128)(2,1)S(1)} %maximum_bitcast_fusion.2, bf16[2,1,64,2176]{3,2,0,1:T(8,128)(2,1)S(1)} %get-tuple-element.69), kind=kLoop, calls=%fused_computation.8 | loop fusion | flops 3342336 | bytes 4456448 | tf_op jit(solution)/shard_map/stack | solution.py:89
  23.2 20.0 %all-to-all-done = bf16[2,4,64,2176]{3,2,0,1:T(8,128)(2,1)S(1)} async-done(((bf16[2,4,64,2176]{3,2,0,1:T(8,128)(2,1)}), bf16[2,4,64,2176]{3,2,0,1:T(8,128)(2,1)S(1)}, u32[]{:S(2)}, u32[]{:S(2)}) %all-to-all-start) | async-done | bytes 2228256 | tf_op jit(solution)/shard_map/all_to_all | solution.py:109
  43.2 4.5 %all-to-all-start.1 = ((bf16[2,4,64,2176]{3,2,0,1:T(8,128)(2,1)}), bf16[2,4,64,2176]{3,2,0,1:T(8,128)(2,1)}, u32[]{:S(2)}, u32[]{:S(2)}) async-start(bf16[2,4,64,2176]{3,2,0,1:T(8,128)(2,1)} %pad_maximum_fusion.1), calls=%async_computation.1 | async-start | bytes 4456448 | tf_op jit(solution)/shard_map/all_to_all | solution.py:109
  47.7 1.6 %copy.41 = bf16[2,4,64,2176]{3,2,1,0:T(8,128)(2,1)} copy(bf16[2,4,64,2176]{3,2,0,1:T(8,128)(2,1)S(1)} %all-to-all-done) | data formatting | bytes 4456448 | tf_op jit(solution)/shard_map/all_to_all | solution.py:109
  49.6 0.1 concatenate.156
  49.8 0.7 slice_reduce_fusion
  50.4 0.6 fusion.43
  51.0 0.7 slice_bitcast_fusion.6
  51.7 1.9 %collective-permute-start.2 = (bf16[2176]{0:T(1024)(128)(2,1)}, bf16[2176]{0:T(1024)(128)(2,1)}, u32[]{:S(2)}, u32[]{:S(2)}) collective-permute-start(bf16[2176]{0:T(1024)(128)(2,1)} %get-tuple-element.31), channel_id=1, source_target_pairs={{0,1},{1,2},{2,3},{3,4},{4,5},{5,6},{6,7},{7,8},{8,9},{9,10},{10,1... | collective-permute-start | bytes 13064 | tf_op jit(solution)/shard_map/ppermute | solution.py:117
  53.6 3.6 %collective-permute-start.3 = (bf16[2176]{0:T(1024)(128)(2,1)}, bf16[2176]{0:T(1024)(128)(2,1)}, u32[]{:S(2)}, u32[]{:S(2)}) collective-permute-start(bf16[2176]{0:T(1024)(128)(2,1)} %get-tuple-element.30), channel_id=1, source_target_pairs={{1,0},{2,1},{3,2},{4,3},{5,4},{6,5},{7,6},{8,7},{9,8},{10,9},{11,1... | collective-permute-start | bytes 13064 | tf_op jit(solution)/shard_map/ppermute | solution.py:118
  57.3 1.2 fusion.35
  58.5 1.9 %collective-permute-start = (bf16[256,2176]{1,0:T(8,128)(2,1)}, bf16[256,2176]{1,0:T(8,128)(2,1)S(1)}, u32[]{:S(2)}, u32[]{:S(2)}) collective-permute-start(bf16[256,2176]{1,0:T(8,128)(2,1)} %bitcast.6), channel_id=1, source_target_pairs={{0,1},{1,2},{2,3},{3,4},{4,5},{5,6},{6,7},{7,8},{8,9},{9,10},{10,1... | collective-permute-start | bytes 3342344 | tf_op jit(solution)/shard_map/ppermute | solution.py:110
  60.4 3.6 %collective-permute-start.1 = (bf16[256,2176]{1,0:T(8,128)(2,1)S(1)}, bf16[256,2176]{1,0:T(8,128)(2,1)S(1)}, u32[]{:S(2)}, u32[]{:S(2)}) collective-permute-start(bf16[256,2176]{1,0:T(8,128)(2,1)S(1)} %bitcast.106), channel_id=1, source_target_pairs={{1,0},{2,1},{3,2},{4,3},{5,4},{6,5},{7,6},{8,7},{9,8},{10,9},{11,1... | collective-permute-start | bytes 3342344 | tf_op jit(solution)/shard_map/ppermute | solution.py:111
  64.0 0.7 slice_bitcast_fusion.4
  64.8 0.7 slice_bitcast_fusion
  65.5 9.1 %all-to-all-done.1 = bf16[2,4,64,2176]{3,2,0,1:T(8,128)(2,1)} async-done(((bf16[2,4,64,2176]{3,2,0,1:T(8,128)(2,1)}), bf16[2,4,64,2176]{3,2,0,1:T(8,128)(2,1)}, u32[]{:S(2)}, u32[]{:S(2)}) %all-to-all-start.1) | async-done | bytes 2228256 | tf_op jit(solution)/shard_map/all_to_all | solution.py:109
  74.6 3.2 %fusion.36 = (bf16[1,4,64,2176]{3,2,1,0:T(8,128)(2,1)}, bf16[1,4,64,2176]{3,2,1,0:T(8,128)(2,1)}) fusion(bf16[2,4,64,2176]{3,2,0,1:T(8,128)(2,1)} %all-to-all-done.1), kind=kLoop, calls=%fused_computation.86 | loop fusion | bytes 4456448 | tf_op jit(solution)/shard_map/slice | solution.py:111
  77.8 1.9 %collective-permute-start.4 = (bf16[256,2176]{1,0:T(8,128)(2,1)}, bf16[256,2176]{1,0:T(8,128)(2,1)}, u32[]{:S(2)}, u32[]{:S(2)}) collective-permute-start(bf16[256,2176]{1,0:T(8,128)(2,1)} %bitcast.29), channel_id=1, source_target_pairs={{0,1},{1,2},{2,3},{3,4},{4,5},{5,6},{6,7},{7,8},{8,9},{9,10},{10,1... | collective-permute-start | bytes 3342344 | tf_op jit(solution)/shard_map/ppermute | solution.py:110
  79.7 0.1 select_dynamic-update-slice_fusion.1
  79.8 0.1 select_dynamic-update-slice_fusion
  80.0 0.1 constant_dynamic-update-slice_fusion.3
  80.1 0.1 constant_dynamic-update-slice_fusion.2
  80.2 3.2 %copy.47 = bf16[2,4,64,2176]{3,2,1,0:T(8,128)(2,1)} copy(bf16[2,4,64,2176]{3,2,0,1:T(8,128)(2,1)} %all-to-all-done.1) | data formatting | bytes 4456448 | tf_op jit(solution)/shard_map/all_to_all | solution.py:109
  83.4 3.8 %collective-permute-start.5 = (bf16[256,2176]{1,0:T(8,128)(2,1)}, bf16[256,2176]{1,0:T(8,128)(2,1)}, u32[]{:S(2)}, u32[]{:S(2)}) collective-permute-start(bf16[256,2176]{1,0:T(8,128)(2,1)} %bitcast.30), channel_id=1, source_target_pairs={{1,0},{2,1},{3,2},{4,3},{5,4},{6,5},{7,6},{8,7},{9,8},{10,9},{11,1... | collective-permute-start | bytes 3342344 | tf_op jit(solution)/shard_map/ppermute | solution.py:111
  87.2 0.7 reshape.568
  87.9 0.7 reshape.569
  88.7 0.1 add_dynamic-update-slice_fusion.coef_ref
  88.8 0.6 copy-done.4
  89.4 0.4 copy-done.2
  89.8 1.0 copy-done.3
  90.9 6.4 %shard_map.28 = bf16[2,256,2176]{2,1,0:T(8,128)(2,1)} custom-call(bf16[2,256,2176]{2,1,0:T(8,128)(2,1)} %bitcast.99, bf16[256,2176]{1,0:T(8,128)(2,1)} %copy-done.2, bf16[256,2176]{1,0:T(8,128)(2,1)} %copy-done.3, f32[7,2,2176]{2,1,0:T(2,128)} %copy-done.4), custom_call_target="tpu_custom_call" | custom-call | tf_op jit(solution)/shard_map/pallas_call | solution.py:52
  97.3 3.1 %collective-permute-done.5.above_ref = bf16[256,2176]{1,0:T(8,128)(2,1)} collective-permute-done((bf16[256,2176]{1,0:T(8,128)(2,1)}, bf16[256,2176]{1,0:T(8,128)(2,1)}, u32[]{:S(2)}, u32[]{:S(2)}) %collective-permute-start.5) | collective-permute-done | bytes 1114144 | tf_op jit(solution)/shard_map/ppermute | solution.py:111
  100.3 6.6 %shard_map.29 = bf16[2,256,2176]{2,1,0:T(8,128)(2,1)} custom-call(bf16[2,256,2176]{2,1,0:T(8,128)(2,1)} %bitcast.101, bf16[256,2176]{1,0:T(8,128)(2,1)} %collective-permute-done.4.below_ref, bf16[256,2176]{1,0:T(8,128)(2,1)} %collective-permute-done.5.above_ref, f32[7,2,2176]{2,1,0:T(2,128)} %copy-done.4), custom_call_target="tpu_custom_call" | custom-call | tf_op jit(solution)/shard_map/pallas_call | solution.py:52
  106.9 5.5 %fusion = f32[512,512,1]{1,0,2:T(8,128)S(1)} fusion(bf16[2,256,2176]{2,1,0:T(8,128)(2,1)} %shard_map.29, bf16[2,256,2176]{2,1,0:T(8,128)(2,1)} %shard_map.28, bf16[2,256,2176]{2,1,0:T(8,128)(2,1)} %bitcast.102, bf16[2,256,2176]{2,1,0:T(8,128)(2,1)S(1)} %bitcast.100), kind=kOutput, calls=%fused_computation | convolution fusion | flops 2299527168 | bytes 9961472 | tf_op jit(solution)/shard_map/dot_general | solution.py:123
  112.4 0.1 fusion.11
  112.5 0.6 collective-permute-start.6
  113.1 2.1 %collective-permute-start.7 = (f32[2,64,512]{2,1,0:T(8,128)S(1)}, f32[2,64,512]{2,1,0:T(8,128)S(1)}, u32[]{:S(2)}, u32[]{:S(2)}) collective-permute-start(f32[2,64,512]{2,1,0:T(8,128)S(1)} %get-tuple-element.51), channel_id=1, source_target_pairs={{0,128},{64,192},{128,0},{192,64},{1,129},{65,193},{129,1},{193,65... | collective-permute-start | bytes 786440 | tf_op jit(solution)/shard_map/ppermute | solution.py:129
  115.2 0.7 collective-permute-start.8
  115.9 6.8 %collective-permute-done.6 = f32[2,64,512]{2,1,0:T(8,128)S(1)} collective-permute-done((f32[2,64,512]{2,1,0:T(8,128)S(1)}, f32[2,64,512]{2,1,0:T(8,128)S(1)}, u32[]{:S(2)}, u32[]{:S(2)}) %collective-permute-start.6) | collective-permute-done | bytes 262176 | tf_op jit(solution)/shard_map/ppermute | solution.py:129
  122.7 4.5 %collective-permute-done.7 = f32[2,64,512]{2,1,0:T(8,128)S(1)} collective-permute-done((f32[2,64,512]{2,1,0:T(8,128)S(1)}, f32[2,64,512]{2,1,0:T(8,128)S(1)}, u32[]{:S(2)}, u32[]{:S(2)}) %collective-permute-start.7) | collective-permute-done | bytes 262176 | tf_op jit(solution)/shard_map/ppermute | solution.py:129
  127.2 1.7 %collective-permute-done.8 = f32[2,64,512]{2,1,0:T(8,128)S(1)} collective-permute-done((f32[2,64,512]{2,1,0:T(8,128)S(1)}, f32[2,64,512]{2,1,0:T(8,128)S(1)}, u32[]{:S(2)}, u32[]{:S(2)}) %collective-permute-start.8) | collective-permute-done | bytes 262176 | tf_op jit(solution)/shard_map/ppermute | solution.py:129
  128.9 0.1 fusion.15
  129.0 0.3 reshape.469
  129.3 0.2 copy.54
  129.5 3.9 %all_to_all.20 = f32[2,128,8,4,8]{1,4,3,2,0:T(8,128)S(1)} all-to-all(f32[2,128,8,4,8]{1,4,3,2,0:T(8,128)S(1)} %copy.55), channel_id=1, replica_groups=mesh['node'=4,'z'=8,'y'=4,'core'=2] {'core'}, dimensions={0} | all-to-all | bytes 524288 | tf_op jit(solution)/shard_map/all_to_all | solution.py:133
  133.5 20.8 %all_to_all.21 = f32[32,128,8]{1,2,0:T(8,128)S(1)} all-to-all(f32[32,128,8]{1,2,0:T(8,128)S(1)} %bitcast.110), channel_id=1, replica_groups=mesh['node'=4,'z'=8,'y'=4,'core'=2] {'z','y'}, dimensions={0} | all-to-all | bytes 262144 | tf_op jit(solution)/shard_map/all_to_all | solution.py:136
  154.3 0.6 broadcast_multiply_fusion
  (46 shorter events, 0.8 us)
Async XLA Ops:
  7.7 1.3 copy-start
  7.9 1.1 copy-start.9
  11.2 32.0 %all-to-all-start = ((bf16[2,4,64,2176]{3,2,0,1:T(8,128)(2,1)}), bf16[2,4,64,2176]{3,2,0,1:T(8,128)(2,1)S(1)}, u32[]{:S(2)}, u32[]{:S(2)}) async-start(bf16[2,4,64,2176]{3,2,0,1:T(8,128)(2,1)} %pad_maximum_fusion), calls=%async_computation | async-start | bytes 4456448 | tf_op jit(solution)/shard_map/all_to_all | solution.py:109
  43.2 31.4 %all-to-all-start.1 = ((bf16[2,4,64,2176]{3,2,0,1:T(8,128)(2,1)}), bf16[2,4,64,2176]{3,2,0,1:T(8,128)(2,1)}, u32[]{:S(2)}, u32[]{:S(2)}) async-start(bf16[2,4,64,2176]{3,2,0,1:T(8,128)(2,1)} %pad_maximum_fusion.1), calls=%async_computation.1 | async-start | bytes 4456448 | tf_op jit(solution)/shard_map/all_to_all | solution.py:109
  47.7 1.6 %copy-start.7 = (bf16[2,8192]{1,0:T(2,128)(2,1)S(1)}, bf16[2,8192]{1,0:T(2,128)(2,1)}, u32[]{:S(2)}) copy-start(bf16[2,8192]{1,0:T(2,128)(2,1)} %param.5) | copy-start | bytes 98308
  51.7 31.7 %collective-permute-start.2 = (bf16[2176]{0:T(1024)(128)(2,1)}, bf16[2176]{0:T(1024)(128)(2,1)}, u32[]{:S(2)}, u32[]{:S(2)}) collective-permute-start(bf16[2176]{0:T(1024)(128)(2,1)} %get-tuple-element.31), channel_id=1, source_target_pairs={{0,1},{1,2},{2,3},{3,4},{4,5},{5,6},{6,7},{7,8},{8,9},{9,10},{10,1... | collective-permute-start | bytes 13064 | tf_op jit(solution)/shard_map/ppermute | solution.py:117
  53.6 34.3 %collective-permute-start.3 = (bf16[2176]{0:T(1024)(128)(2,1)}, bf16[2176]{0:T(1024)(128)(2,1)}, u32[]{:S(2)}, u32[]{:S(2)}) collective-permute-start(bf16[2176]{0:T(1024)(128)(2,1)} %get-tuple-element.30), channel_id=1, source_target_pairs={{1,0},{2,1},{3,2},{4,3},{5,4},{6,5},{7,6},{8,7},{9,8},{10,9},{11,1... | collective-permute-start | bytes 13064 | tf_op jit(solution)/shard_map/ppermute | solution.py:118
  58.5 30.4 %collective-permute-start = (bf16[256,2176]{1,0:T(8,128)(2,1)}, bf16[256,2176]{1,0:T(8,128)(2,1)S(1)}, u32[]{:S(2)}, u32[]{:S(2)}) collective-permute-start(bf16[256,2176]{1,0:T(8,128)(2,1)} %bitcast.6), channel_id=1, source_target_pairs={{0,1},{1,2},{2,3},{3,4},{4,5},{5,6},{6,7},{7,8},{8,9},{9,10},{10,1... | collective-permute-start | bytes 3342344 | tf_op jit(solution)/shard_map/ppermute | solution.py:110
  60.4 28.5 %collective-permute-start.1 = (bf16[256,2176]{1,0:T(8,128)(2,1)S(1)}, bf16[256,2176]{1,0:T(8,128)(2,1)S(1)}, u32[]{:S(2)}, u32[]{:S(2)}) collective-permute-start(bf16[256,2176]{1,0:T(8,128)(2,1)S(1)} %bitcast.106), channel_id=1, source_target_pairs={{1,0},{2,1},{3,2},{4,3},{5,4},{6,5},{7,6},{8,7},{9,8},{10,9},{11,1... | collective-permute-start | bytes 3342344 | tf_op jit(solution)/shard_map/ppermute | solution.py:111
  74.6 5.1 %copy-start.8 = (pred[2176]{0:T(1024)(128)(4,1)S(1)}, pred[2176]{0:T(1024)(128)(4,1)}, u32[]{:S(2)}) copy-start(pred[2176]{0:T(1024)(128)(4,1)} %get-tuple-element.73) | copy-start | bytes 6532
  74.6 5.1 %copy-start.11 = (f32[1,2,1]{2,1,0:T(2,128)S(1)}, f32[1,2,1]{2,1,0:T(2,128)}, u32[]{:S(2)}) copy-start(f32[1,2,1]{2,1,0:T(2,128)} %get-tuple-element.63) | copy-start | bytes 28
  74.6 5.2 %copy-start.10 = (f32[1,2,1]{2,1,0:T(2,128)S(1)}, f32[1,2,1]{2,1,0:T(2,128)}, u32[]{:S(2)}) copy-start(f32[1,2,1]{2,1,0:T(2,128)} %get-tuple-element.62) | copy-start | bytes 28
  74.6 5.3 %copy-start.5 = (f32[1,2,2112]{2,1,0:T(2,128)S(1)}, f32[1,2,2112]{2,1,0:T(2,128)}, u32[]{:S(2)}) copy-start(f32[1,2,2112]{2,1,0:T(2,128)} %get-tuple-element.61) | copy-start | bytes 50692
  74.6 5.3 %copy-start.13 = (f32[1,2,64]{2,1,0:T(2,128)S(1)}, f32[1,2,64]{2,1,0:T(2,128)}, u32[]{:S(2)}) copy-start(f32[1,2,64]{2,1,0:T(2,128)} %get-tuple-element.59) | copy-start | bytes 1540
  74.6 5.4 %copy-start.12 = (f32[1,2,64]{2,1,0:T(2,128)S(1)}, f32[1,2,64]{2,1,0:T(2,128)}, u32[]{:S(2)}) copy-start(f32[1,2,64]{2,1,0:T(2,128)} %get-tuple-element.58) | copy-start | bytes 1540
  77.8 19.4 %collective-permute-start.4 = (bf16[256,2176]{1,0:T(8,128)(2,1)}, bf16[256,2176]{1,0:T(8,128)(2,1)}, u32[]{:S(2)}, u32[]{:S(2)}) collective-permute-start(bf16[256,2176]{1,0:T(8,128)(2,1)} %bitcast.29), channel_id=1, source_target_pairs={{0,1},{1,2},{2,3},{3,4},{4,5},{5,6},{6,7},{7,8},{8,9},{9,10},{10,1... | collective-permute-start | bytes 3342344 | tf_op jit(solution)/shard_map/ppermute | solution.py:110
  80.2 7.7 %copy-start.6 = (f32[1,1,2176]{2,1,0:T(1,128)S(1)}, f32[1,1,2176]{2,1,0:T(1,128)}, u32[]{:S(2)}) copy-start(f32[1,1,2176]{2,1,0:T(1,128)} %get-tuple-element.67) | copy-start | bytes 26116
  83.4 17.0 %collective-permute-start.5 = (bf16[256,2176]{1,0:T(8,128)(2,1)}, bf16[256,2176]{1,0:T(8,128)(2,1)}, u32[]{:S(2)}, u32[]{:S(2)}) collective-permute-start(bf16[256,2176]{1,0:T(8,128)(2,1)} %bitcast.30), channel_id=1, source_target_pairs={{1,0},{2,1},{3,2},{4,3},{5,4},{6,5},{7,6},{8,7},{9,8},{10,9},{11,1... | collective-permute-start | bytes 3342344 | tf_op jit(solution)/shard_map/ppermute | solution.py:111
  88.8 0.6 copy-start.4
  88.8 1.0 copy-start.2
  89.8 1.0 copy-start.3
  100.3 6.6 %copy-start.1 = (bf16[2,4,64,2176]{3,2,1,0:T(8,128)(2,1)S(1)}, bf16[2,4,64,2176]{3,2,1,0:T(8,128)(2,1)}, u32[]{:S(2)}) copy-start(bf16[2,4,64,2176]{3,2,1,0:T(8,128)(2,1)} %copy.41) | copy-start | bytes 6684676
  112.5 10.2 %collective-permute-start.6 = (f32[2,64,512]{2,1,0:T(8,128)S(1)}, f32[2,64,512]{2,1,0:T(8,128)S(1)}, u32[]{:S(2)}, u32[]{:S(2)}) collective-permute-start(f32[2,64,512]{2,1,0:T(8,128)S(1)} %get-tuple-element.50), channel_id=1, source_target_pairs={{0,64},{64,128},{128,192},{192,0},{1,65},{65,129},{129,193},{193,1... | collective-permute-start | bytes 786440 | tf_op jit(solution)/shard_map/ppermute | solution.py:129
  113.1 14.1 %collective-permute-start.7 = (f32[2,64,512]{2,1,0:T(8,128)S(1)}, f32[2,64,512]{2,1,0:T(8,128)S(1)}, u32[]{:S(2)}, u32[]{:S(2)}) collective-permute-start(f32[2,64,512]{2,1,0:T(8,128)S(1)} %get-tuple-element.51), channel_id=1, source_target_pairs={{0,128},{64,192},{128,0},{192,64},{1,129},{65,193},{129,1},{193,65... | collective-permute-start | bytes 786440 | tf_op jit(solution)/shard_map/ppermute | solution.py:129
  115.2 13.7 %collective-permute-start.8 = (f32[2,64,512]{2,1,0:T(8,128)S(1)}, f32[2,64,512]{2,1,0:T(8,128)S(1)}, u32[]{:S(2)}, u32[]{:S(2)}) collective-permute-start(f32[2,64,512]{2,1,0:T(8,128)S(1)} %get-tuple-element.52), channel_id=1, source_target_pairs={{0,192},{64,0},{128,64},{192,128},{1,193},{65,1},{129,65},{193,129... | collective-permute-start | bytes 786440 | tf_op jit(solution)/shard_map/ppermute | solution.py:129

commit v22 on v17

--- a/solution.py
+++ b/solution.py
@@ -132,8 +132,9 @@
         total = total + lax.ppermute(blk, "node", [(i, (i + d) % nodes) for i in range(nodes)])
     total = total.reshape(rows, GROUPS, nodes, step).transpose(0, 2, 1, 3)
     total = total.reshape((rows,) + tuple(sizes) + (snaps // spaces,))
-    total = jnp.moveaxis(total, 3, 0)
-    total = lax.all_to_all(total, SPACE[2], 0, 0, tiled=True).sum(axis=0)
+    core = lax.axis_index(SPACE[2])
+    give = jnp.take(total, 1 - core, axis=3)
+    total = jnp.take(total, core, axis=3) + lax.ppermute(give, SPACE[2], [(0, 1), (1, 0)])
     total = total.reshape(rows, sizes[0] * sizes[1], snaps // spaces)
     total = jnp.moveaxis(total, 1, 0)
     total = lax.all_to_all(total, SPACE[:2], 0, 0, tiled=True).sum(axis=0)

time: 156 us -> 153 us (0.981)
  blocking collectives: 24.8 us -> 20.8 us
    all_to_all x1 -> x0, blocking collectives: 3.94 us -> none  [per_device(): total = lax.all_to_all(total, SPACE[2], 0, 0, tiled=True).sum(axis=0)]
  transfers between devices with their start and end apart: 11 -> 12, of which waited for: 6 -> 7; matrix products, arithmetic and copies ran while one was open for 14% -> 14% of each run, Pallas kernels for 4% -> 4%
where the time goes in v22:
time: 153 us; the launch traced here: 151 us
  waiting for transfers between devices  48.6 us (32%)
  starting transfers between devices  29.5 us (19%)
  local copies, waits for them, and re-layouts  26.3 us (17%)
  blocking collectives  20.8 us (14%)
  Pallas kernels  12.8 us (8%)
  matrix products  6.63 us (4%)
  other arithmetic  5.7 us (4%)
    all_to_all x2, waiting for transfers between devices, per_device(): lax.all_to_all(chunked(major, nodes), 'node', 1, 1, tiled=True)  32.7 us
    all_to_all x1, blocking collectives, per_device(): total = lax.all_to_all(total, SPACE[:2], 0, 0, tiled=True).sum(axis=0)  20.8 us
    ppermute x3, waiting for transfers between devices, per_device(): lax.ppermute(blk, 'node', [(i, (i + d) % nodes) for i in range(nodes)])  12.9 us
    pallas_call x2, Pallas kernels, stencil(): pl.pallas_call(stencil_kernel, grid=(snaps // ROWS,), in_specs=[pl.BlockS...  12.8 us
    all_to_all x2, starting transfers between devices, per_device(): lax.all_to_all(chunked(major, nodes), 'node', 1, 1, tiled=True)  8.76 us
    ppermute x2, starting transfers between devices, per_device(): above = lax.ppermute(field[0], SPACE, down)  7.46 us
    dot_general x4, matrix products, per_device(): lax.dot_general(im, fd, dims, preferred_element_type=jnp.float32)  6.63 us
    slice x1, local copies, waits for them, and re-layouts, per_device(): major = jnp.transpose(snapshots[g * step:(g + 1) * step], (1, 0, 2))  5.04 us
  transfers between devices with their start and end apart: 12, of which 7 were waited for; matrix products, arithmetic and copies ran while one was open for 14% of the time, Pallas kernels for 4%

profile of v22, /device:TPU:8, one launch (start us, length us, event | category | flops | bytes accessed | tf_op | source)
XLA Modules:
  0.0 150.8 jit_solution(357758703185265260)
XLA Ops:
  0.0 5.0 %fusion.27 = (bf16[64,2,8192]{2,1,0:T(2,128)(2,1)S(1)}, bf16[64,2,8192]{2,1,0:T(2,128)(2,1)S(1)}) fusion(bf16[128,2,8192]{2,1,0:T(2,128)(2,1)} %param.6), kind=kLoop, calls=%fused_computation.84 | loop fusion | bytes 8388608 | tf_op jit(solution)/shard_map/slice | solution.py:108
  5.1 2.7 %copy_bitcast_fusion = (bf16[2,64,8192]{2,1,0:T(8,128)(2,1)S(1)}, bf16[2,64,8192]{2,1,0:T(8,128)(2,1)S(1)}) fusion(bf16[64,2,8192]{2,1,0:T(2,128)(2,1)S(1)} %get-tuple-element.47, bf16[64,2,8192]{2,1,0:T(2,128)(2,1)S(1)} %get-tuple-element.46), kind=kLoop, calls=%fused_computation.2 | loop fusion | bytes 8388608 | tf_op jit(solution)/shard_map/transpose | solution.py:108
  7.7 0.1 fusion.31
  7.8 0.1 fusion.30
  8.0 0.1 maximum_bitcast_fusion
  8.1 0.1 maximum_bitcast_fusion.1
  8.2 0.9 copy-done.5
  9.1 0.1 fusion.1
  9.2 0.3 concatenate.155
  9.5 1.7 %pad_maximum_fusion = bf16[2,4,64,2176]{3,2,0,1:T(8,128)(2,1)} fusion(bf16[2,1,64,2176]{3,2,0,1:T(8,128)(2,1)S(1)} %bitcast.129, bf16[2,1,64,2176]{3,2,0,1:T(8,128)(2,1)S(1)} %maximum_bitcast_fusion.1, bf16[2,1,64,2176]{3,2,0,1:T(8,128)(2,1)S(1)} %maximum_bitcast_fusion, bf16[2,1,64,2176]{3,2,0,1:T(8,128)(2,1)S(1)} %get-tuple-element.79), kind=kLoop, calls=%fused_computation | loop fusion | flops 3342336 | bytes 4456448 | tf_op jit(solution)/shard_map/stack | solution.py:89
  11.2 4.3 %all-to-all-start = ((bf16[2,4,64,2176]{3,2,0,1:T(8,128)(2,1)}), bf16[2,4,64,2176]{3,2,0,1:T(8,128)(2,1)S(1)}, u32[]{:S(2)}, u32[]{:S(2)}) async-start(bf16[2,4,64,2176]{3,2,0,1:T(8,128)(2,1)} %pad_maximum_fusion), calls=%async_computation | async-start | bytes 4456448 | tf_op jit(solution)/shard_map/all_to_all | solution.py:109
  15.5 0.9 fusion.33
  16.4 1.9 %slice.259 = bf16[2,64,2048]{2,1,0:T(8,128)(2,1)} slice(bf16[2,64,8192]{2,1,0:T(8,128)(2,1)} %copy-done.5), slice={[0:2], [0:64], [6144:8192]} | slice | bytes 1048576 | tf_op jit(solution)/shard_map/slice | solution.py:88
  18.3 1.2 concatenate.175
  19.5 1.3 fusion.32
  20.8 0.1 maximum_bitcast_fusion.2
  20.9 0.1 maximum_bitcast_fusion.3
  20.9 1.7 %pad_maximum_fusion.1 = bf16[2,4,64,2176]{3,2,0,1:T(8,128)(2,1)} fusion(bf16[2,1,64,2176]{3,2,0,1:T(8,128)(2,1)S(1)} %bitcast.128, bf16[2,1,64,2176]{3,2,0,1:T(8,128)(2,1)S(1)} %maximum_bitcast_fusion.3, bf16[2,1,64,2176]{3,2,0,1:T(8,128)(2,1)S(1)} %maximum_bitcast_fusion.2, bf16[2,1,64,2176]{3,2,0,1:T(8,128)(2,1)S(1)} %get-tuple-element.80), kind=kLoop, calls=%fused_computation.1 | loop fusion | flops 3342336 | bytes 4456448 | tf_op jit(solution)/shard_map/stack | solution.py:89
  22.7 20.5 %all-to-all-done = bf16[2,4,64,2176]{3,2,0,1:T(8,128)(2,1)S(1)} async-done(((bf16[2,4,64,2176]{3,2,0,1:T(8,128)(2,1)}), bf16[2,4,64,2176]{3,2,0,1:T(8,128)(2,1)S(1)}, u32[]{:S(2)}, u32[]{:S(2)}) %all-to-all-start) | async-done | bytes 2228256 | tf_op jit(solution)/shard_map/all_to_all | solution.py:109
  43.2 4.5 %all-to-all-start.1 = ((bf16[2,4,64,2176]{3,2,0,1:T(8,128)(2,1)}), bf16[2,4,64,2176]{3,2,0,1:T(8,128)(2,1)}, u32[]{:S(2)}, u32[]{:S(2)}) async-start(bf16[2,4,64,2176]{3,2,0,1:T(8,128)(2,1)} %pad_maximum_fusion.1), calls=%async_computation.1 | async-start | bytes 4456448 | tf_op jit(solution)/shard_map/all_to_all | solution.py:109
  47.7 1.6 %copy.42 = bf16[2,4,64,2176]{3,2,1,0:T(8,128)(2,1)} copy(bf16[2,4,64,2176]{3,2,0,1:T(8,128)(2,1)S(1)} %all-to-all-done) | data formatting | bytes 4456448 | tf_op jit(solution)/shard_map/all_to_all | solution.py:109
  49.4 0.1 maximum_bitcast_fusion.4
  49.6 0.1 concatenate.159
  49.9 1.9 %collective-permute-start.2 = (bf16[2176]{0:T(1024)(128)(2,1)S(1)}, bf16[2176]{0:T(1024)(128)(2,1)S(1)}, u32[]{:S(2)}, u32[]{:S(2)}) collective-permute-start(bf16[2176]{0:T(1024)(128)(2,1)S(1)} %get-tuple-element.43), channel_id=1, source_target_pairs={{0,1},{1,2},{2,3},{3,4},{4,5},{5,6},{6,7},{7,8},{8,9},{9,10},{10,1... | collective-permute-start | bytes 13064 | tf_op jit(solution)/shard_map/ppermute | solution.py:117
  51.8 3.6 %collective-permute-start.3 = (bf16[2176]{0:T(1024)(128)(2,1)S(1)}, bf16[2176]{0:T(1024)(128)(2,1)S(1)}, u32[]{:S(2)}, u32[]{:S(2)}) collective-permute-start(bf16[2176]{0:T(1024)(128)(2,1)S(1)} %get-tuple-element.42), channel_id=1, source_target_pairs={{1,0},{2,1},{3,2},{4,3},{5,4},{6,5},{7,6},{8,7},{9,8},{10,9},{11,1... | collective-permute-start | bytes 13064 | tf_op jit(solution)/shard_map/ppermute | solution.py:118
  55.5 1.2 fusion.28
  56.6 1.9 %collective-permute-start = (bf16[256,2176]{1,0:T(8,128)(2,1)}, bf16[256,2176]{1,0:T(8,128)(2,1)}, u32[]{:S(2)}, u32[]{:S(2)}) collective-permute-start(bf16[256,2176]{1,0:T(8,128)(2,1)} %bitcast.6), channel_id=1, source_target_pairs={{0,1},{1,2},{2,3},{3,4},{4,5},{5,6},{6,7},{7,8},{8,9},{9,10},{10,1... | collective-permute-start | bytes 3342344 | tf_op jit(solution)/shard_map/ppermute | solution.py:110
  58.6 3.6 %collective-permute-start.1 = (bf16[256,2176]{1,0:T(8,128)(2,1)S(1)}, bf16[256,2176]{1,0:T(8,128)(2,1)}, u32[]{:S(2)}, u32[]{:S(2)}) collective-permute-start(bf16[256,2176]{1,0:T(8,128)(2,1)S(1)} %bitcast.131), channel_id=1, source_target_pairs={{1,0},{2,1},{3,2},{4,3},{5,4},{6,5},{7,6},{8,7},{9,8},{10,9},{11,1... | collective-permute-start | bytes 3342344 | tf_op jit(solution)/shard_map/ppermute | solution.py:111
  62.4 0.1 slice_bitcast_fusion
  62.4 12.1 %all-to-all-done.1 = bf16[2,4,64,2176]{3,2,0,1:T(8,128)(2,1)} async-done(((bf16[2,4,64,2176]{3,2,0,1:T(8,128)(2,1)}), bf16[2,4,64,2176]{3,2,0,1:T(8,128)(2,1)}, u32[]{:S(2)}, u32[]{:S(2)}) %all-to-all-start.1) | async-done | bytes 2228256 | tf_op jit(solution)/shard_map/all_to_all | solution.py:109
  74.6 3.2 %fusion.29 = (bf16[1,4,64,2176]{3,2,1,0:T(8,128)(2,1)}, bf16[1,4,64,2176]{3,2,1,0:T(8,128)(2,1)}) fusion(bf16[2,4,64,2176]{3,2,0,1:T(8,128)(2,1)} %all-to-all-done.1), kind=kLoop, calls=%fused_computation.86 | loop fusion | bytes 4456448 | tf_op jit(solution)/shard_map/slice | solution.py:111
  77.8 1.9 %collective-permute-start.4 = (bf16[256,2176]{1,0:T(8,128)(2,1)}, bf16[256,2176]{1,0:T(8,128)(2,1)}, u32[]{:S(2)}, u32[]{:S(2)}) collective-permute-start(bf16[256,2176]{1,0:T(8,128)(2,1)} %bitcast.31), channel_id=1, source_target_pairs={{0,1},{1,2},{2,3},{3,4},{4,5},{5,6},{6,7},{7,8},{8,9},{9,10},{10,1... | collective-permute-start | bytes 3342344 | tf_op jit(solution)/shard_map/ppermute | solution.py:110
  79.7 0.1 select_dynamic-update-slice_fusion.1
  79.8 0.1 select_dynamic-update-slice_fusion
  79.9 0.1 constant_dynamic-update-slice_fusion.3
  80.0 0.1 constant_dynamic-update-slice_fusion.2
  80.1 3.2 %copy.48 = bf16[2,4,64,2176]{3,2,1,0:T(8,128)(2,1)} copy(bf16[2,4,64,2176]{3,2,0,1:T(8,128)(2,1)} %all-to-all-done.1) | data formatting | bytes 4456448 | tf_op jit(solution)/shard_map/all_to_all | solution.py:109
  83.3 3.8 %collective-permute-start.5 = (bf16[256,2176]{1,0:T(8,128)(2,1)}, bf16[256,2176]{1,0:T(8,128)(2,1)}, u32[]{:S(2)}, u32[]{:S(2)}) collective-permute-start(bf16[256,2176]{1,0:T(8,128)(2,1)} %bitcast.32), channel_id=1, source_target_pairs={{1,0},{2,1},{3,2},{4,3},{5,4},{6,5},{7,6},{8,7},{9,8},{10,9},{11,1... | collective-permute-start | bytes 3342344 | tf_op jit(solution)/shard_map/ppermute | solution.py:111
  87.2 0.1 add_dynamic-update-slice_fusion.coef_ref
  87.4 0.6 copy-done.6
  88.0 6.4 %shard_map.28 = bf16[2,256,2176]{2,1,0:T(8,128)(2,1)} custom-call(bf16[2,256,2176]{2,1,0:T(8,128)(2,1)} %bitcast.119, bf16[256,2176]{1,0:T(8,128)(2,1)} %collective-permute-done.below_ref, bf16[256,2176]{1,0:T(8,128)(2,1)} %collective-permute-done.1.above_ref, f32[7,2,2176]{2,1,0:T(2,128)} %copy-done.6), custom_call_target="tpu_custom_call" | custom-call | tf_op jit(solution)/shard_map/pallas_call | solution.py:52
  94.4 2.5 %convolution_bitcast_fusion.3 = f32[256,256]{0,1:T(8,128)S(1)} fusion(bf16[2,256,2176]{2,1,0:T(8,128)(2,1)} %shard_map.28, bf16[2,256,2176]{2,1,0:T(8,128)(2,1)S(1)} %bitcast.120), kind=kOutput, calls=%fused_computation.7 | convolution fusion | flops 570425344 | bytes 4718592 | tf_op jit(solution)/shard_map/dot_general | solution.py:125
  97.0 0.4 copy-done.4
  97.4 0.8 convolution_bitcast_fusion.2
  98.2 2.0 %collective-permute-done.5.above_ref = bf16[256,2176]{1,0:T(8,128)(2,1)} collective-permute-done((bf16[256,2176]{1,0:T(8,128)(2,1)}, bf16[256,2176]{1,0:T(8,128)(2,1)}, u32[]{:S(2)}, u32[]{:S(2)}) %collective-permute-start.5) | collective-permute-done | bytes 1114144 | tf_op jit(solution)/shard_map/ppermute | solution.py:111
  100.2 6.4 %shard_map.29 = bf16[2,256,2176]{2,1,0:T(8,128)(2,1)} custom-call(bf16[2,256,2176]{2,1,0:T(8,128)(2,1)} %bitcast.122, bf16[256,2176]{1,0:T(8,128)(2,1)} %collective-permute-done.4.below_ref, bf16[256,2176]{1,0:T(8,128)(2,1)} %collective-permute-done.5.above_ref, f32[7,2,2176]{2,1,0:T(2,128)} %copy-done.6), custom_call_target="tpu_custom_call" | custom-call | tf_op jit(solution)/shard_map/pallas_call | solution.py:52
  106.6 2.5 %convolution_bitcast_fusion.1 = f32[256,256]{0,1:T(8,128)S(1)} fusion(bf16[2,256,2176]{2,1,0:T(8,128)(2,1)} %shard_map.29, bf16[2,256,2176]{2,1,0:T(8,128)(2,1)S(1)} %bitcast.121), kind=kOutput, calls=%fused_computation.5 | convolution fusion | flops 570425344 | bytes 4718592 | tf_op jit(solution)/shard_map/dot_general | solution.py:125
  109.1 0.4 copy-done.3
  109.5 0.8 convolution_bitcast_fusion
  110.3 0.1 maximum_maximum_fusion
  110.5 0.3 copy.51
  110.9 0.6 collective-permute-start.6
  111.5 2.1 %collective-permute-start.7 = (f32[2,64,512]{2,1,0:T(8,128)S(1)}, f32[2,64,512]{2,1,0:T(8,128)S(1)}, u32[]{:S(2)}, u32[]{:S(2)}) collective-permute-start(f32[2,64,512]{2,1,0:T(8,128)S(1)} %get-tuple-element.63), channel_id=1, source_target_pairs={{0,128},{64,192},{128,0},{192,64},{1,129},{65,193},{129,1},{193,65... | collective-permute-start | bytes 786440 | tf_op jit(solution)/shard_map/ppermute | solution.py:132
  113.6 0.8 collective-permute-start.8
  114.4 6.7 %collective-permute-done.6 = f32[2,64,512]{2,1,0:T(8,128)S(1)} collective-permute-done((f32[2,64,512]{2,1,0:T(8,128)S(1)}, f32[2,64,512]{2,1,0:T(8,128)S(1)}, u32[]{:S(2)}, u32[]{:S(2)}) %collective-permute-start.6) | collective-permute-done | bytes 262176 | tf_op jit(solution)/shard_map/ppermute | solution.py:132
  121.1 4.5 %collective-permute-done.7 = f32[2,64,512]{2,1,0:T(8,128)S(1)} collective-permute-done((f32[2,64,512]{2,1,0:T(8,128)S(1)}, f32[2,64,512]{2,1,0:T(8,128)S(1)}, u32[]{:S(2)}, u32[]{:S(2)}) %collective-permute-start.7) | collective-permute-done | bytes 262176 | tf_op jit(solution)/shard_map/ppermute | solution.py:132
  125.6 1.7 %collective-permute-done.8 = f32[2,64,512]{2,1,0:T(8,128)S(1)} collective-permute-done((f32[2,64,512]{2,1,0:T(8,128)S(1)}, f32[2,64,512]{2,1,0:T(8,128)S(1)}, u32[]{:S(2)}, u32[]{:S(2)}) %collective-permute-start.8) | collective-permute-done | bytes 262176 | tf_op jit(solution)/shard_map/ppermute | solution.py:132
  127.3 0.1 fusion.7
  127.4 0.3 reshape.470
  127.7 0.2 copy.55
  127.9 0.5 collective-permute-start.9
  128.4 1.0 collective-permute-done.9
  129.4 20.8 %all_to_all.15 = f32[32,128,8]{1,2,0:T(8,128)S(1)} all-to-all(f32[32,128,8]{1,2,0:T(8,128)S(1)} %bitcast.134), channel_id=1, replica_groups=mesh['node'=4,'z'=8,'y'=4,'core'=2] {'z','y'}, dimensions={0} | all-to-all | bytes 262144 | tf_op jit(solution)/shard_map/all_to_all | solution.py:140
  150.2 0.6 broadcast_multiply_fusion
  (43 shorter events, 0.9 us)
Async XLA Ops:
  7.7 1.4 copy-start.5
  7.9 1.1 copy-start.8
  11.2 32.0 %all-to-all-start = ((bf16[2,4,64,2176]{3,2,0,1:T(8,128)(2,1)}), bf16[2,4,64,2176]{3,2,0,1:T(8,128)(2,1)S(1)}, u32[]{:S(2)}, u32[]{:S(2)}) async-start(bf16[2,4,64,2176]{3,2,0,1:T(8,128)(2,1)} %pad_maximum_fusion), calls=%async_computation | async-start | bytes 4456448 | tf_op jit(solution)/shard_map/all_to_all | solution.py:109
  43.2 31.4 %all-to-all-start.1 = ((bf16[2,4,64,2176]{3,2,0,1:T(8,128)(2,1)}), bf16[2,4,64,2176]{3,2,0,1:T(8,128)(2,1)}, u32[]{:S(2)}, u32[]{:S(2)}) async-start(bf16[2,4,64,2176]{3,2,0,1:T(8,128)(2,1)} %pad_maximum_fusion.1), calls=%async_computation.1 | async-start | bytes 4456448 | tf_op jit(solution)/shard_map/all_to_all | solution.py:109
  47.7 1.6 %copy-start.7 = (bf16[2,8192]{1,0:T(2,128)(2,1)S(1)}, bf16[2,8192]{1,0:T(2,128)(2,1)}, u32[]{:S(2)}) copy-start(bf16[2,8192]{1,0:T(2,128)(2,1)} %param.7) | copy-start | bytes 98308
  49.9 33.4 %collective-permute-start.2 = (bf16[2176]{0:T(1024)(128)(2,1)S(1)}, bf16[2176]{0:T(1024)(128)(2,1)S(1)}, u32[]{:S(2)}, u32[]{:S(2)}) collective-permute-start(bf16[2176]{0:T(1024)(128)(2,1)S(1)} %get-tuple-element.43), channel_id=1, source_target_pairs={{0,1},{1,2},{2,3},{3,4},{4,5},{5,6},{6,7},{7,8},{8,9},{9,10},{10,1... | collective-permute-start | bytes 13064 | tf_op jit(solution)/shard_map/ppermute | solution.py:117
  51.8 35.3 %collective-permute-start.3 = (bf16[2176]{0:T(1024)(128)(2,1)S(1)}, bf16[2176]{0:T(1024)(128)(2,1)S(1)}, u32[]{:S(2)}, u32[]{:S(2)}) collective-permute-start(bf16[2176]{0:T(1024)(128)(2,1)S(1)} %get-tuple-element.42), channel_id=1, source_target_pairs={{1,0},{2,1},{3,2},{4,3},{5,4},{6,5},{7,6},{8,7},{9,8},{10,9},{11,1... | collective-permute-start | bytes 13064 | tf_op jit(solution)/shard_map/ppermute | solution.py:118
  56.6 30.7 %collective-permute-start = (bf16[256,2176]{1,0:T(8,128)(2,1)}, bf16[256,2176]{1,0:T(8,128)(2,1)}, u32[]{:S(2)}, u32[]{:S(2)}) collective-permute-start(bf16[256,2176]{1,0:T(8,128)(2,1)} %bitcast.6), channel_id=1, source_target_pairs={{0,1},{1,2},{2,3},{3,4},{4,5},{5,6},{6,7},{7,8},{8,9},{9,10},{10,1... | collective-permute-start | bytes 3342344 | tf_op jit(solution)/shard_map/ppermute | solution.py:110
  58.6 28.8 %collective-permute-start.1 = (bf16[256,2176]{1,0:T(8,128)(2,1)S(1)}, bf16[256,2176]{1,0:T(8,128)(2,1)}, u32[]{:S(2)}, u32[]{:S(2)}) collective-permute-start(bf16[256,2176]{1,0:T(8,128)(2,1)S(1)} %bitcast.131), channel_id=1, source_target_pairs={{1,0},{2,1},{3,2},{4,3},{5,4},{6,5},{7,6},{8,7},{9,8},{10,9},{11,1... | collective-permute-start | bytes 3342344 | tf_op jit(solution)/shard_map/ppermute | solution.py:111
  77.8 20.4 %collective-permute-start.4 = (bf16[256,2176]{1,0:T(8,128)(2,1)}, bf16[256,2176]{1,0:T(8,128)(2,1)}, u32[]{:S(2)}, u32[]{:S(2)}) collective-permute-start(bf16[256,2176]{1,0:T(8,128)(2,1)} %bitcast.31), channel_id=1, source_target_pairs={{0,1},{1,2},{2,3},{3,4},{4,5},{5,6},{6,7},{7,8},{8,9},{9,10},{10,1... | collective-permute-start | bytes 3342344 | tf_op jit(solution)/shard_map/ppermute | solution.py:110
  83.3 17.0 %collective-permute-start.5 = (bf16[256,2176]{1,0:T(8,128)(2,1)}, bf16[256,2176]{1,0:T(8,128)(2,1)}, u32[]{:S(2)}, u32[]{:S(2)}) collective-permute-start(bf16[256,2176]{1,0:T(8,128)(2,1)} %bitcast.32), channel_id=1, source_target_pairs={{1,0},{2,1},{3,2},{4,3},{5,4},{6,5},{7,6},{8,7},{9,8},{10,9},{11,1... | collective-permute-start | bytes 3342344 | tf_op jit(solution)/shard_map/ppermute | solution.py:111
  87.3 0.6 copy-start.6
  87.3 7.1 %copy-start = (bf16[2,4,64,2176]{3,2,1,0:T(8,128)(2,1)S(1)}, bf16[2,4,64,2176]{3,2,1,0:T(8,128)(2,1)}, u32[]{:S(2)}) copy-start(bf16[2,4,64,2176]{3,2,1,0:T(8,128)(2,1)} %copy.42) | copy-start | bytes 6684676
  94.4 2.6 %copy-start.1 = (bf16[2,4,64,2176]{3,2,1,0:T(8,128)(2,1)S(1)}, bf16[2,4,64,2176]{3,2,1,0:T(8,128)(2,1)}, u32[]{:S(2)}) copy-start(bf16[2,4,64,2176]{3,2,1,0:T(8,128)(2,1)} %copy.48) | copy-start | bytes 6684676
  94.4 3.0 %copy-start.4 = (bf16[2,256,2176]{2,1,0:T(8,128)(2,1)S(1)}, bf16[2,256,2176]{2,1,0:T(8,128)(2,1)}, u32[]{:S(2)}) copy-start(bf16[2,256,2176]{2,1,0:T(8,128)(2,1)} %shard_map.28) | copy-start | bytes 6684676
  106.6 2.6 %copy-start.2 = (bf16[2,4,64,2176]{3,2,1,0:T(8,128)(2,1)S(1)}, bf16[2,4,64,2176]{3,2,1,0:T(8,128)(2,1)}, u32[]{:S(2)}) copy-start(bf16[2,4,64,2176]{3,2,1,0:T(8,128)(2,1)} %copy.48) | copy-start | bytes 6684676
  106.6 3.0 %copy-start.3 = (bf16[2,256,2176]{2,1,0:T(8,128)(2,1)S(1)}, bf16[2,256,2176]{2,1,0:T(8,128)(2,1)}, u32[]{:S(2)}) copy-start(bf16[2,256,2176]{2,1,0:T(8,128)(2,1)} %shard_map.29) | copy-start | bytes 6684676
  110.9 10.2 %collective-permute-start.6 = (f32[2,64,512]{2,1,0:T(8,128)S(1)}, f32[2,64,512]{2,1,0:T(8,128)S(1)}, u32[]{:S(2)}, u32[]{:S(2)}) collective-permute-start(f32[2,64,512]{2,1,0:T(8,128)S(1)} %get-tuple-element.62), channel_id=1, source_target_pairs={{0,64},{64,128},{128,192},{192,0},{1,65},{65,129},{129,193},{193,1... | collective-permute-start | bytes 786440 | tf_op jit(solution)/shard_map/ppermute | solution.py:132
  111.5 14.1 %collective-permute-start.7 = (f32[2,64,512]{2,1,0:T(8,128)S(1)}, f32[2,64,512]{2,1,0:T(8,128)S(1)}, u32[]{:S(2)}, u32[]{:S(2)}) collective-permute-start(f32[2,64,512]{2,1,0:T(8,128)S(1)} %get-tuple-element.63), channel_id=1, source_target_pairs={{0,128},{64,192},{128,0},{192,64},{1,129},{65,193},{129,1},{193,65... | collective-permute-start | bytes 786440 | tf_op jit(solution)/shard_map/ppermute | solution.py:132
  113.6 13.7 %collective-permute-start.8 = (f32[2,64,512]{2,1,0:T(8,128)S(1)}, f32[2,64,512]{2,1,0:T(8,128)S(1)}, u32[]{:S(2)}, u32[]{:S(2)}) collective-permute-start(f32[2,64,512]{2,1,0:T(8,128)S(1)} %select_bitcast_fusion), channel_id=1, source_target_pairs={{0,192},{64,0},{128,64},{192,128},{1,193},{65,1},{129,65},{193,129... | collective-permute-start | bytes 786440 | tf_op jit(solution)/shard_map/ppermute | solution.py:132
  127.9 1.4 collective-permute-start.9
